TPU v7x, 512 devices: a whole 4x4x16 slice. The times are simulated.
512 devices in a mesh: chan: 32 (over y, z_lo), inp: 16 (over z_hi, x, core).
Axes of the slice: x: 4, y: 4, z: 16 (z_hi: 2, z_lo: 8; z = z_hi * 8 + z_lo), core: 2. Of those that a mesh axis runs over, the one named last changes fastest.
Arguments:
- voltages: int32 [512, 524288], P('inp', 'chan'), may hold values from -128 to 127
- scales: int32 [512], P('inp'), may hold values from 1 to 5
Outputs:
- visibilities: bfloat16 [2, 1024, 512, 512], P(None, 'chan', 'inp')
All inputs are finite; a program needn't handle non-finite values.
Results may differ from a plain program's by a relative error of at most 0.0069.
Values may be sent and summed in bfloat16 or wider, within the bound.
No kernel may reach another device: no remote copies, remote signals or barrier semaphores. Data moves between devices by JAX's collectives and lax.ppermute only.
A program may use at most 128 MiB of HBM per device.

v0:
```python
import math

import jax
import jax.numpy as jnp
from jax import lax
from jax.sharding import PartitionSpec as P

NFFT = 4096
CHANS = 1024
TAPS = 8


def shifted(block, axis, distance):
    devices = range(lax.axis_size(axis))
    route = [(i - distance, i) for i in devices if i - distance in devices]
    return lax.ppermute(block, axis, route)


def window_table():
    count = TAPS * NFFT
    places = jnp.arange(count).astype(jnp.float32)
    shaping = jnp.sinc((places - count / 2.0) / NFFT)
    taper = 0.5 - 0.5 * jnp.cos(2.0 * math.pi * places / count)
    return (shaping * taper).reshape(TAPS, NFFT)


def dft_table():
    columns = jnp.arange(CHANS, dtype=jnp.int32)
    norm_factor = 1.0 / math.sqrt(NFFT)

    def one_block(start):
        rows_idx = start + jnp.arange(512, dtype=jnp.int32)
        phase = rows_idx[:, None] * columns[None, :] % NFFT
        angle = phase.astype(jnp.float32) * (2.0 * math.pi / NFFT)
        return jnp.stack(
            [jnp.cos(angle) * norm_factor, -jnp.sin(angle) * norm_factor], axis=1
        ).astype(jnp.bfloat16)

    starts = jnp.arange(NFFT // 512, dtype=jnp.int32) * 512
    return lax.map(one_block, starts).reshape(NFFT, 2, CHANS)


def filter_taps(padded, window, spec_count):
    total = jnp.zeros((padded.shape[0], spec_count, NFFT), jnp.float32)
    for tap_index in range(TAPS):
        total = total + window[tap_index] * padded[:, tap_index : tap_index + spec_count]
    return total.astype(jnp.bfloat16)


def shards(voltages, scales):
    inp_count = voltages.shape[0]
    shard_len = voltages.shape[1]
    spec_count = shard_len // NFFT
    history_len = (TAPS - 1) * NFFT
    reach_back = -(-history_len // shard_len)
    samples = voltages.astype(jnp.bfloat16)
    earlier = []
    for distance in range(1, reach_back + 1):
        take_count = min(shard_len, history_len - (distance - 1) * shard_len)
        received = shifted(samples[:, shard_len - take_count :], "chan", distance)
        earlier = [received] + earlier
    joined = jnp.concatenate(earlier + [samples], axis=1).astype(jnp.float32)
    signal = joined * scales.astype(jnp.float32)[:, None] * (1.0 / 256.0)
    padded = signal.reshape(inp_count, TAPS - 1 + spec_count, NFFT)
    filtered = filter_taps(padded, window_table(), spec_count)
    spectra = jnp.einsum(
        "isn,nrc->cirs", filtered, dft_table(), preferred_element_type=jnp.float32
    ).astype(jnp.bfloat16)
    local_block = lax.all_to_all(spectra, "chan", split_axis=0, concat_axis=3, tiled=True)
    chan_count = local_block.shape[0]
    spec_total = local_block.shape[3]
    own_rows = local_block.reshape(chan_count, inp_count, 2 * spec_total)
    swapped = jnp.concatenate([own_rows[..., spec_total:], -own_rows[..., :spec_total]], axis=-1)
    piece = lax.all_gather(own_rows, "inp", axis=1, tiled=True)
    real_part = jnp.einsum("cik,cjk->cij", own_rows, piece, preferred_element_type=jnp.float32)
    imag_part = jnp.einsum("cik,cjk->cij", swapped, piece, preferred_element_type=jnp.float32)
    result = jnp.stack([real_part, imag_part]) * (1.0 / spec_total)
    return result.astype(jnp.bfloat16)


def solution(mesh):
    placed = (P("inp", "chan"), P("inp"))
    return jax.shard_map(
        shards, mesh=mesh, in_specs=placed, out_specs=P(None, "chan", "inp", None), check_vma=False
    )
```

profile of v0, /device:TPU:7, one launch (start us, length us, event | category | flops | bytes accessed | tf_op | source)
XLA Modules:
  0.0 405.5 jit_solution(11215632262744515466)
XLA Ops:
  6.5 0.0 all-gather.2.cloned.1.call-start
  6.5 1.7 convert_element_type.91
  8.2 3.6 collective-permute-start.1
  11.9 0.9 slice.85
  12.8 4.9 %collective-permute-start = (bf16[32,12288]{1,0:T(8,128)(2,1)}, bf16[32,12288]{1,0:T(8,128)(2,1)S(1)}, u32[]{:S(2)}, u32[]{:S(2)}) collective-permute-start(bf16[32,12288]{1,0:T(8,128)(2,1)} %slice.85), channel_id=1, source_target_pairs={{0,32},{16,48},{32,64},{48,80},{64,96},{80,112},{96,128},{112,144}... | collective-permute-start | bytes 2359304 | tf_op jit(solution)/shard_map/ppermute | solution.py:16
  17.7 0.0 copy-start.1
  17.7 95.0 %while.13 = (s32[]{:T(128)}, bf16[8,512,2,1024]{3,1,0,2:T(8,128)(2,1)}, s32[8]{0:T(128)S(1)}, s32[]{:T(128)}) while((s32[]{:T(128)}, bf16[8,512,2,1024]{3,1,0,2:T(8,128)(2,1)}, s32[8]{0:T(128)S(1)}, s32[]{:T(128)}) %tuple.40), condition=%wide.region_1.2_spmd.clone, body=%wide.region_0.1_spmd.clone.sunk | while | flops 14156290 | bytes 6295633 | solution.py:40
  17.7 0.6 dynamic_slice.9
  18.3 0.6 iota_add_fusion.2
  19.0 9.1 %fusion.48 = (bf16[1,512,1,1024]{3,1,2,0:T(8,128)(2,1)S(1)}, bf16[1,512,1,1024]{3,1,2,0:T(8,128)(2,1)S(1)}) fusion(s32[512]{0:T(512)S(1)} %iota_add_fusion.2), kind=kLoop, calls=%fused_computation.15.clone.1 | loop fusion | flops 9961472 | bytes 2099200 | tf_op jit(solution)/shard_map/while/body/eval_jaxpr/stack | solution.py:35
  28.1 1.6 fusion.49
  29.6 0.6 dynamic_slice.9
  30.3 0.6 iota_add_fusion.2
  30.9 9.1 %fusion.48 = (bf16[1,512,1,1024]{3,1,2,0:T(8,128)(2,1)S(1)}, bf16[1,512,1,1024]{3,1,2,0:T(8,128)(2,1)S(1)}) fusion(s32[512]{0:T(512)S(1)} %iota_add_fusion.2), kind=kLoop, calls=%fused_computation.15.clone.1 | loop fusion | flops 9961472 | bytes 2099200 | tf_op jit(solution)/shard_map/while/body/eval_jaxpr/stack | solution.py:35
  40.0 1.5 fusion.49
  41.5 0.6 dynamic_slice.9
  42.1 0.6 iota_add_fusion.2
  42.7 9.1 %fusion.48 = (bf16[1,512,1,1024]{3,1,2,0:T(8,128)(2,1)S(1)}, bf16[1,512,1,1024]{3,1,2,0:T(8,128)(2,1)S(1)}) fusion(s32[512]{0:T(512)S(1)} %iota_add_fusion.2), kind=kLoop, calls=%fused_computation.15.clone.1 | loop fusion | flops 9961472 | bytes 2099200 | tf_op jit(solution)/shard_map/while/body/eval_jaxpr/stack | solution.py:35
  51.8 1.5 fusion.49
  53.4 0.6 dynamic_slice.9
  54.0 0.6 iota_add_fusion.2
  54.6 9.1 %fusion.48 = (bf16[1,512,1,1024]{3,1,2,0:T(8,128)(2,1)S(1)}, bf16[1,512,1,1024]{3,1,2,0:T(8,128)(2,1)S(1)}) fusion(s32[512]{0:T(512)S(1)} %iota_add_fusion.2), kind=kLoop, calls=%fused_computation.15.clone.1 | loop fusion | flops 9961472 | bytes 2099200 | tf_op jit(solution)/shard_map/while/body/eval_jaxpr/stack | solution.py:35
  63.7 1.5 fusion.49
  65.2 0.6 dynamic_slice.9
  65.9 0.6 iota_add_fusion.2
  66.5 9.1 %fusion.48 = (bf16[1,512,1,1024]{3,1,2,0:T(8,128)(2,1)S(1)}, bf16[1,512,1,1024]{3,1,2,0:T(8,128)(2,1)S(1)}) fusion(s32[512]{0:T(512)S(1)} %iota_add_fusion.2), kind=kLoop, calls=%fused_computation.15.clone.1 | loop fusion | flops 9961472 | bytes 2099200 | tf_op jit(solution)/shard_map/while/body/eval_jaxpr/stack | solution.py:35
  75.6 1.5 fusion.49
  77.1 0.6 dynamic_slice.9
  77.8 0.6 iota_add_fusion.2
  78.4 9.1 %fusion.48 = (bf16[1,512,1,1024]{3,1,2,0:T(8,128)(2,1)S(1)}, bf16[1,512,1,1024]{3,1,2,0:T(8,128)(2,1)S(1)}) fusion(s32[512]{0:T(512)S(1)} %iota_add_fusion.2), kind=kLoop, calls=%fused_computation.15.clone.1 | loop fusion | flops 9961472 | bytes 2099200 | tf_op jit(solution)/shard_map/while/body/eval_jaxpr/stack | solution.py:35
  87.5 1.5 fusion.49
  89.0 0.6 dynamic_slice.9
  89.6 0.6 iota_add_fusion.2
  90.2 9.1 %fusion.48 = (bf16[1,512,1,1024]{3,1,2,0:T(8,128)(2,1)S(1)}, bf16[1,512,1,1024]{3,1,2,0:T(8,128)(2,1)S(1)}) fusion(s32[512]{0:T(512)S(1)} %iota_add_fusion.2), kind=kLoop, calls=%fused_computation.15.clone.1 | loop fusion | flops 9961472 | bytes 2099200 | tf_op jit(solution)/shard_map/while/body/eval_jaxpr/stack | solution.py:35
  99.3 1.5 fusion.49
  100.8 0.6 dynamic_slice.9
  101.4 0.6 iota_add_fusion.2
  102.1 9.1 %fusion.48 = (bf16[1,512,1,1024]{3,1,2,0:T(8,128)(2,1)S(1)}, bf16[1,512,1,1024]{3,1,2,0:T(8,128)(2,1)S(1)}) fusion(s32[512]{0:T(512)S(1)} %iota_add_fusion.2), kind=kLoop, calls=%fused_computation.15.clone.1 | loop fusion | flops 9961472 | bytes 2099200 | tf_op jit(solution)/shard_map/while/body/eval_jaxpr/stack | solution.py:35
  111.2 1.5 fusion.49
  112.7 0.0 copy-done.1
  112.7 0.6 fusion.30
  113.3 0.0 collective-permute-done
  113.3 0.0 collective-permute-done.1
  113.3 2.9 maximum_convert_fusion
  116.2 6.8 %reshape.221 = f32[32,11,4096]{2,1,0:T(8,128)} reshape(f32[32,45056]{1,0:T(8,128)} %maximum_convert_fusion) | data formatting | bytes 11534336 | tf_op jit(solution)/shard_map/convert_element_type | solution.py:62
  123.1 8.3 %multiply_multiply_fusion = f32[32,11,4096]{2,1,0:T(8,128)} fusion(f32[32,11,4096]{2,1,0:T(8,128)} %reshape.221, f32[32]{0:T(128)S(1)} %convert_element_type.94), kind=kLoop, calls=%fused_computation.18 | loop fusion | flops 2883584 | bytes 11534464 | tf_op jit(solution)/shard_map/mul | solution.py:63
  131.4 18.0 %fusion.13 = bf16[32,4,4096]{2,1,0:T(4,128)(2,1)S(1)} fusion(f32[32,11,4096]{2,1,0:T(8,128)} %multiply_multiply_fusion, f32[4096]{0:T(1024)S(1)} %get-tuple-element.79, f32[4096]{0:T(1024)S(1)} %get-tuple-element.80, f32[4096]{0:T(1024)S(1)} %get-tuple-element.81, f32[4096]{0:T(1024)S(1)} %get-tuple-element.82, f32[4096]{0:T(1024)S(1)} %get-tuple-element.83, ...), kind=kLoop, calls=%fused_computation.24 | loop fusion | flops 8388608 | bytes 17956864 | tf_op jit(solution)/shard_map/convert_element_type | solution.py:47
  149.4 8.7 %fusion.20 = bf16[1024,32,2,4]{0,1,3,2:T(8,128)(2,1)S(1)} fusion(bf16[4096,2,1024,1]{2,0,3,1:T(8,128)(2,1)} %bitcast.42, bf16[32,4,4096]{2,1,0:T(4,128)(2,1)S(1)} %fusion.13), kind=kOutput, calls=%fused_computation.41 | convolution fusion | flops 2147745792 | bytes 18350080 | tf_op jit(solution)/shard_map/isn,nrc->cirs/dot_general | solution.py:66
  158.0 1.4 copy.22
  159.4 2.0 reshape.224
  161.4 40.3 %all_to_all.15 = bf16[32,2,4096]{2,1,0:T(2,128)(2,1)S(1)} all-to-all(bf16[32,2,4096]{2,1,0:T(2,128)(2,1)S(1)} %reshape.224), channel_id=1, replica_groups=mesh['chan'=32,'inp'=16] {'chan'}, dimensions={0} | all-to-all | bytes 1048576 | tf_op jit(solution)/shard_map/all_to_all | solution.py:69
  201.7 1.0 reshape.225
  202.8 1.9 copy.23
  204.7 3.4 copy.25
  208.1 0.0 all-gather.2.cloned.1.call-update
  208.1 1.1 fusion.40
  209.2 178.7 %all-gather.2.cloned.1.call-done = bf16[32,512,256]{2,1,0:T(8,128)(2,1)} async-done(((bf16[32,32,256]{2,1,0:T(8,128)(2,1)}), bf16[32,512,256]{2,1,0:T(8,128)(2,1)}) %all-gather.2.cloned.1.call-update) | async-done | bytes 8388624 | tf_op jit(solution)/shard_map/all_gather | solution.py:74
  387.9 0.0 copy-start
  387.9 6.2 %convolution_bitcast_fusion.1 = f32[1,32,32,512]{3,2,1,0:T(8,128)S(1)} fusion(bf16[32,32,256]{2,1,0:T(8,128)(2,1)} %copy.25, bf16[32,512,256]{2,1,0:T(8,128)(2,1)} %all-gather.2.cloned.1.call-done), kind=kOutput, calls=%fused_computation.39 | convolution fusion | flops 268435456 | bytes 11010048 | tf_op jit(solution)/shard_map/cik,cjk->cij/dot_general | solution.py:75
  394.1 0.0 copy-done
  394.1 2.5 convolution_bitcast_fusion
  396.7 2.0 fusion.11
  (4 shorter events, 0.0 us)
Async XLA Ops:
  6.5 381.4 %all-gather.2.cloned.1.call-start = ((), (), s32[]{:S(2)}) async-start(), calls=%async_computation.1 | async-start | bytes 8912896 | tf_op jit(solution)/shard_map/all_gather | solution.py:74
  8.2 105.1 %collective-permute-start.1 = (bf16[32,16384]{1,0:T(8,128)(2,1)S(1)}, bf16[32,16384]{1,0:T(8,128)(2,1)S(1)}, u32[]{:S(2)}, u32[]{:S(2)}) collective-permute-start(bf16[32,16384]{1,0:T(8,128)(2,1)S(1)} %convert_element_type.91), channel_id=1, source_target_pairs={{0,16},{16,32},{32,48},{48,64},{64,80},{80,96},{96,112},{112,128},... | collective-permute-start | bytes 3145736 | tf_op jit(solution)/shard_map/ppermute | solution.py:16
  12.8 100.5 %collective-permute-start = (bf16[32,12288]{1,0:T(8,128)(2,1)}, bf16[32,12288]{1,0:T(8,128)(2,1)S(1)}, u32[]{:S(2)}, u32[]{:S(2)}) collective-permute-start(bf16[32,12288]{1,0:T(8,128)(2,1)} %slice.85), channel_id=1, source_target_pairs={{0,32},{16,48},{32,64},{48,80},{64,96},{80,112},{96,128},{112,144}... | collective-permute-start | bytes 2359304 | tf_op jit(solution)/shard_map/ppermute | solution.py:16
  17.7 95.0 %copy-start.1 = (s32[32]{0:T(128)S(1)}, s32[32]{0:T(128)}, u32[]{:S(2)}) copy-start(s32[32]{0:T(128)} %param.5) | copy-start | bytes 388
  387.9 6.2 %copy-start = (bf16[32,512,256]{2,1,0:T(8,128)(2,1)S(1)}, bf16[32,512,256]{2,1,0:T(8,128)(2,1)}, u32[]{:S(2)}) copy-start(bf16[32,512,256]{2,1,0:T(8,128)(2,1)} %all-gather.2.cloned.1.call-done) | copy-start | bytes 25165828
Sparse Core Ops, SparseCore 0:
  208.2 179.6 all-gather.1
where the time goes:
time: 409 us; the launch traced here: 405 us
  waiting for transfers between devices  179 us (44%)
  other arithmetic  124 us (30%)
  blocking collectives  40.3 us (10%)
  local copies, waits for them, and re-layouts  22.7 us (6%)
  matrix products  17.4 us (4%)
  between operations  13.5 us (3%)
  starting transfers between devices  8.48 us (2%)
    all_gather x1, waiting for transfers between devices, shards(): piece = lax.all_gather(own_rows, 'inp', axis=1, tiled=True)  179 us
    another operation x8, other arithmetic, one_block(): jnp.stack([jnp.cos(angle) * norm_factor, -jnp.sin(angle) * norm_factor],...  72.7 us
    all_to_all x1, blocking collectives, shards(): lax.all_to_all(spectra, 'chan', split_axis=0, concat_axis=3, tiled=True)  40.3 us
    convert_element_type x1, other arithmetic, filter_taps(): return total.astype(jnp.bfloat16)  18 us
    dynamic_update_slice x8, other arithmetic, dft_table(): return lax.map(one_block, starts).reshape(NFFT, 2, CHANS)  12 us
    dot_general x1, matrix products, shards(): jnp.einsum('isn,nrc->cirs', filtered, dft_table(), preferred_element_type...  8.68 us
    ppermute x2, starting transfers between devices, shifted(): return lax.ppermute(block, axis, route)  8.48 us
    mul x1, other arithmetic, shards(): signal = joined * scales.astype(jnp.float32)[:, None] * (1.0 / 256.0)  8.31 us
  transfers between devices with their start and end apart: 3, of which 1 were waited for; matrix products, arithmetic and copies ran while one was open for 24% of the time, Pallas kernels for 0%

commit v1 on v0

v1 whole, which is shorter than its diff:
```python
import math

import jax
import jax.numpy as jnp
from jax import lax
from jax.sharding import PartitionSpec as P

NFFT = 4096
CHANS = 1024
TAPS = 8
ROOT = 64


def shifted(block, axis, distance):
    devices = range(lax.axis_size(axis))
    route = [(i - distance, i) for i in devices if i - distance in devices]
    return lax.ppermute(block, axis, route)


def moved(block, mapping):
    return lax.ppermute(block, "inp", [(p, mapping(p)) for p in range(lax.axis_size("inp"))])


def window_table():
    count = TAPS * NFFT
    places = jnp.arange(count).astype(jnp.float32)
    shaping = jnp.sinc((places - count / 2.0) / NFFT)
    taper = 0.5 - 0.5 * jnp.cos(2.0 * math.pi * places / count)
    return (shaping * taper).reshape(TAPS, NFFT)


def dft_table():
    columns = jnp.arange(CHANS, dtype=jnp.int32)
    rows = jnp.arange(ROOT, dtype=jnp.int32)
    step = 2.0 * math.pi / NFFT

    def factor(scale):
        angle = ((scale * rows[:, None] * columns[None, :]) % NFFT).astype(jnp.float32) * step
        return jnp.cos(angle), -jnp.sin(angle)

    hr, hi = factor(ROOT)
    lr, li = factor(1)
    real = hr[:, None, :] * lr[None, :, :] - hi[:, None, :] * li[None, :, :]
    imag = hr[:, None, :] * li[None, :, :] + hi[:, None, :] * lr[None, :, :]
    both = jnp.stack([real, imag], axis=2) * (1.0 / math.sqrt(NFFT))
    return both.astype(jnp.bfloat16).reshape(NFFT, 2 * CHANS)


def gather_inputs(own):
    assert lax.axis_size("inp") == 16
    me = lax.axis_index("inp")
    zh, xx, core = me // 8, (me // 2) % 4, me % 2

    def at(z, x, c):
        return z * 8 + (x % 4) * 2 + c

    def unpack(p):
        return p // 8, (p // 2) % 4, p % 2

    def x_step(d):
        def f(p):
            z, x, c = unpack(p)
            return at(z, x + d, c)
        return f

    cross = moved(own, lambda p: p ^ 8)
    from_left = moved((own, cross), x_step(1))
    from_right = moved((own, cross), x_step(-1))
    far_own = moved(from_left[0], x_step(1))
    far_cross = moved(from_right[1], x_step(-1))
    mine = [
        (0, 0, own), (1, 0, cross),
        (0, -1, from_left[0]), (1, -1, from_left[1]),
        (0, 1, from_right[0]), (1, 1, from_right[1]),
        (0, 2, far_own), (1, 2, far_cross),
    ]
    other = moved(tuple(b for _, _, b in mine), lambda p: p ^ 1)
    width = own.shape[1]
    gathered = jnp.zeros((own.shape[0], 16 * width, own.shape[2]), own.dtype)
    for (dz, dx, block), far in zip(mine, other):
        for dc, piece in ((0, block), (1, far)):
            place = at((zh + dz) % 2, xx + dx + 4, (core + dc) % 2)
            gathered = lax.dynamic_update_slice(gathered, piece, (0, place * width, 0))
    return gathered


def shards(voltages, scales):
    inp_count = voltages.shape[0]
    shard_len = voltages.shape[1]
    spec_count = shard_len // NFFT
    history = TAPS - 1
    samples = voltages.reshape(inp_count, spec_count, NFFT).transpose(1, 0, 2).astype(jnp.bfloat16)
    earlier = []
    need = history
    distance = 1
    while need > 0:
        take = min(spec_count, need)
        earlier = [shifted(samples[spec_count - take :], "chan", distance)] + earlier
        need -= take
        distance += 1
    joined = jnp.concatenate(earlier + [samples], axis=0).astype(jnp.float32)
    signal = joined * (scales.astype(jnp.float32) * (1.0 / 256.0))[None, :, None]
    window = window_table()
    total = jnp.zeros((spec_count, inp_count, NFFT), jnp.float32)
    for tap in range(TAPS):
        total = total + window[tap] * signal[tap : tap + spec_count]
    filtered = total.astype(jnp.bfloat16).reshape(spec_count * inp_count, NFFT)
    spectra = jnp.dot(filtered, dft_table(), preferred_element_type=jnp.float32).astype(jnp.bfloat16)
    spectra = spectra.reshape(spec_count, inp_count, 2, CHANS)
    local_block = lax.all_to_all(spectra, "chan", split_axis=3, concat_axis=0, tiled=True)
    spec_total = local_block.shape[0]
    chan_count = local_block.shape[3]
    own_rows = local_block.transpose(3, 1, 2, 0).reshape(chan_count, inp_count, 2 * spec_total)
    swapped = jnp.concatenate([own_rows[..., spec_total:], -own_rows[..., :spec_total]], axis=-1)
    piece = gather_inputs(own_rows)
    real_part = jnp.einsum("cik,cjk->cij", own_rows, piece, preferred_element_type=jnp.float32)
    imag_part = jnp.einsum("cik,cjk->cij", swapped, piece, preferred_element_type=jnp.float32)
    result = jnp.stack([real_part, imag_part]) * (1.0 / spec_total)
    return result.astype(jnp.bfloat16)


def solution(mesh):
    placed = (P("inp", "chan"), P("inp"))
    return jax.shard_map(
        shards, mesh=mesh, in_specs=placed, out_specs=P(None, "chan", "inp", None), check_vma=False
    )
```

time: 409 us -> 285 us (0.70)
  the two profiles are of different devices: /device:TPU:7 before, /device:TPU:55 now
where the time goes in v1:
time: 285 us; the launch traced here: 284 us
  other arithmetic  95.5 us (34%)
  starting transfers between devices  63 us (22%)
  waiting for transfers between devices  40.7 us (14%)
  local copies, waits for them, and re-layouts  36.2 us (13%)
  blocking collectives  34.9 us (12%)
  matrix products  13.3 us (5%)
    ppermute x15, starting transfers between devices, moved(): lax.ppermute(block, 'inp', [(p, mapping(p)) for p in range(lax.axis_size(...  53.3 us
    ppermute x15, waiting for transfers between devices, moved(): lax.ppermute(block, 'inp', [(p, mapping(p)) for p in range(lax.axis_size(...  40.7 us
    convert_element_type x1, other arithmetic, dft_table(): return both.astype(jnp.bfloat16).reshape(NFFT, 2 * CHANS)  35.1 us
    all_to_all x1, blocking collectives, shards(): lax.all_to_all(spectra, 'chan', split_axis=3, concat_axis=0, tiled=True)  34.9 us
    sub x1, other arithmetic, dft_table(): real = hr[:, None, :] * lr[None, :, :] - hi[:, None, :] * li[None, :, :]  31 us
    unnamed x5, local copies, waits for them, and re-layouts  20.1 us
    convert_element_type x1, other arithmetic, shards(): filtered = total.astype(jnp.bfloat16).reshape(spec_count * inp_count, NFFT)  18.2 us
    ppermute x2, starting transfers between devices, shifted(): return lax.ppermute(block, axis, route)  9.66 us
  transfers between devices with their start and end apart: 17, of which 4 were waited for; matrix products, arithmetic and copies ran while one was open for 32% of the time, Pallas kernels for 0%

profile of v1, /device:TPU:55, one launch (start us, length us, event | category | flops | bytes accessed | tf_op | source)
XLA Modules:
  0.0 284.2 jit_solution(4463776147833942629)
XLA Ops:
  0.0 1.7 convert_element_type.84
  1.7 0.8 convert_element_type.85
  2.5 3.5 %collective-permute-start.1 = (bf16[4,32,4096]{2,0,1:T(4,128)(2,1)S(1)}, bf16[4,32,4096]{2,0,1:T(4,128)(2,1)S(1)}, u32[]{:S(2)}, u32[]{:S(2)}) collective-permute-start(bf16[4,32,4096]{2,0,1:T(4,128)(2,1)S(1)} %bitcast.25), channel_id=1, source_target_pairs={{0,16},{16,32},{32,48},{48,64},{64,80},{80,96},{96,112},{112,128},... | collective-permute-start | bytes 3145736 | tf_op jit(solution)/shard_map/ppermute | solution.py:17
  6.1 0.6 slice.85
  6.7 0.6 copy.9
  7.3 6.1 %collective-permute-start = (bf16[3,32,4096]{2,1,0:T(8,128)(2,1)S(1)}, bf16[3,32,4096]{2,1,0:T(8,128)(2,1)S(1)}, u32[]{:S(2)}, u32[]{:S(2)}) collective-permute-start(bf16[3,32,4096]{2,1,0:T(8,128)(2,1)S(1)} %copy.9), channel_id=1, source_target_pairs={{0,32},{16,48},{32,64},{48,80},{64,96},{80,112},{96,128},{112,144}... | collective-permute-start | bytes 2359304 | tf_op jit(solution)/shard_map/ppermute | solution.py:17
  13.4 1.0 sine_negate_fusion
  14.5 1.1 fusion.34
  15.6 31.0 %multiply_subtract_fusion = (f32[64,64,1,1024]{3,2,1,0:T(1,128)S(1)}, f32[64,64,1,1024]{3,2,1,0:T(1,128)}) fusion(f32[64,1024]{1,0:T(8,128)S(1)} %get-tuple-element.19, f32[64,1024]{1,0:T(8,128)S(1)} %get-tuple-element.18, f32[64,1024]{1,0:T(8,128)S(1)} %get-tuple-element.20, f32[64,1024]{1,0:T(8,128)S(1)} %get-tuple-element.17), kind=kLoop, calls=%fused_computation.3 | loop fusion | flops 25165824 | bytes 34603008 | tf_op jit(solution)/shard_map/sub | solution.py:43
  46.6 35.1 %fusion = bf16[64,64,2,1024]{3,2,1,0:T(2,128)(2,1)} fusion(f32[64,64,1,1024]{3,2,1,0:T(1,128)} %get-tuple-element.6, f32[64,64,1,1024]{3,2,1,0:T(1,128)S(1)} %get-tuple-element.5), kind=kLoop, calls=%fused_computation.1 | loop fusion | flops 25165824 | bytes 50331648 | tf_op jit(solution)/shard_map/convert_element_type | solution.py:46
  81.6 17.1 %copy.18 = bf16[512,8,2,1024]{3,1,2,0:T(8,128)(2,1)} copy(bf16[512,8,2,1024]{3,2,1,0:T(2,128)(2,1)} %bitcast.24) | data formatting | bytes 33554432
  98.7 0.6 fusion.29
  99.4 0.0 collective-permute-done
  99.4 0.7 copy.10
  100.1 0.0 collective-permute-done.1
  100.1 4.7 %convert_multiply_fusion = f32[11,32,4096]{2,0,1:T(8,128)} fusion(bf16[4,32,4096]{2,0,1:T(4,128)(2,1)S(1)} %bitcast.27, bf16[4,32,4096]{2,0,1:T(4,128)(2,1)S(1)} %collective-permute-done.1, bf16[3,32,4096]{2,0,1:T(4,128)(2,1)S(1)} %copy.10, f32[32]{0:T(128)S(1)} %convert_multiply_fusion.1), kind=kLoop, calls=%fused_computation.4 | loop fusion | flops 10092544 | bytes 8650880 | tf_op jit(solution)/shard_map/mul | solution.py:102
  104.7 18.2 %fusion.3 = bf16[4,32,4096]{2,0,1:T(4,128)(2,1)S(1)} fusion(f32[11,32,4096]{2,0,1:T(8,128)} %convert_multiply_fusion, f32[4096]{0:T(1024)S(1)} %get-tuple-element.10, f32[4096]{0:T(1024)S(1)} %get-tuple-element.11, f32[4096]{0:T(1024)S(1)} %get-tuple-element.12, f32[4096]{0:T(1024)S(1)} %get-tuple-element.13, f32[4096]{0:T(1024)S(1)} %get-tuple-element.14, ...), kind=kLoop, calls=%fused_computation.10 | loop fusion | flops 8388608 | bytes 17956864 | tf_op jit(solution)/shard_map/convert_element_type | solution.py:107
  123.0 0.6 copy.11
  123.6 8.2 %convolution_convert_fusion = bf16[128,2048]{1,0:T(8,128)(2,1)S(1)} fusion(bf16[128,4096]{1,0:T(8,128)(2,1)S(1)} %bitcast.31, bf16[4096,2048]{1,0:T(8,128)(2,1)} %bitcast.23), kind=kOutput, calls=%fused_computation.7 | convolution fusion | flops 2147745792 | bytes 18350080 | tf_op jit(solution)/shard_map/dot_general | solution.py:108
  131.7 0.4 reshape.155
  132.1 1.9 copy.12
  134.0 2.0 reshape.157
  136.0 34.9 %all_to_all.18 = bf16[32,2,4096]{2,1,0:T(2,128)(2,1)S(1)} all-to-all(bf16[32,2,4096]{2,1,0:T(2,128)(2,1)S(1)} %reshape.157), channel_id=1, replica_groups=mesh['chan'=32,'inp'=16] {'chan'}, dimensions={0} | all-to-all | bytes 1048576 | tf_op jit(solution)/shard_map/all_to_all | solution.py:110
  170.9 1.0 reshape.158
  172.0 3.8 %copy.17 = bf16[4,32,2,32,32]{4,1,2,0,3:T(8,128)(2,1)} copy(bf16[4,32,2,32,32]{1,2,0,4,3:T(2,128)(2,1)S(1)} %bitcast.29) | data formatting | bytes 1048576 | tf_op jit(solution)/shard_map/all_to_all | solution.py:110
  175.8 3.7 %copy.15 = bf16[32,32,2,128]{3,2,1,0:T(2,128)(2,1)S(1)} copy(bf16[32,32,2,128]{0,1,2,3:T(8,128)(2,1)} %bitcast.30) | data formatting | bytes 1048576 | tf_op jit(solution)/shard_map/transpose | solution.py:113
  179.4 0.3 reshape.156
  179.8 13.0 %collective-permute-start.3 = (bf16[32,32,256]{2,1,0:T(8,128)(2,1)S(1)}, bf16[32,32,256]{2,1,0:T(8,128)(2,1)S(1)}, u32[]{:S(2)}, u32[]{:S(2)}) collective-permute-start(bf16[32,32,256]{2,1,0:T(8,128)(2,1)S(1)} %reshape.156), channel_id=1, source_target_pairs={{0,8},{1,9},{2,10},{3,11},{4,12},{5,13},{6,14},{7,15},{8,0},{9,1},... | collective-permute-start | bytes 1572872 | tf_op jit(solution)/shard_map/ppermute | solution.py:21
  192.8 5.5 %collective-permute-start.2 = (bf16[32,32,256]{2,1,0:T(8,128)(2,1)S(1)}, bf16[32,32,256]{2,1,0:T(8,128)(2,1)}, u32[]{:S(2)}, u32[]{:S(2)}) collective-permute-start(bf16[32,32,256]{2,1,0:T(8,128)(2,1)S(1)} %reshape.156), channel_id=1, source_target_pairs={{0,1},{1,0},{2,3},{3,2},{4,5},{5,4},{6,7},{7,6},{8,9},{9,8},{10,11... | collective-permute-start | bytes 1572872 | tf_op jit(solution)/shard_map/ppermute | solution.py:21
  198.3 2.1 collective-permute-start.5
  200.4 3.2 %collective-permute-start.9 = (bf16[32,32,256]{2,1,0:T(8,128)(2,1)S(1)}, bf16[32,32,256]{2,1,0:T(8,128)(2,1)S(1)}, u32[]{:S(2)}, u32[]{:S(2)}) collective-permute-start(bf16[32,32,256]{2,1,0:T(8,128)(2,1)S(1)} %reshape.156), channel_id=1, source_target_pairs={{0,6},{1,7},{2,0},{3,1},{4,2},{5,3},{6,4},{7,5},{8,14},{9,15},{10,... | collective-permute-start | bytes 1572872 | tf_op jit(solution)/shard_map/ppermute | solution.py:21
  203.6 33.7 %collective-permute-done.3 = bf16[32,32,256]{2,1,0:T(8,128)(2,1)S(1)} collective-permute-done((bf16[32,32,256]{2,1,0:T(8,128)(2,1)S(1)}, bf16[32,32,256]{2,1,0:T(8,128)(2,1)S(1)}, u32[]{:S(2)}, u32[]{:S(2)}) %collective-permute-start.3) | collective-permute-done | bytes 524320 | tf_op jit(solution)/shard_map/ppermute | solution.py:21
  237.3 2.1 collective-permute-start.7
  239.4 3.2 %collective-permute-start.11 = (bf16[32,32,256]{2,1,0:T(8,128)(2,1)S(1)}, bf16[32,32,256]{2,1,0:T(8,128)(2,1)S(1)}, u32[]{:S(2)}, u32[]{:S(2)}) collective-permute-start(bf16[32,32,256]{2,1,0:T(8,128)(2,1)S(1)} %collective-permute-done.3), channel_id=1, source_target_pairs={{0,6},{1,7},{2,0},{3,1},{4,2},{5,3},{6,4},{7,5},{8,14},{9,15},{10,... | collective-permute-start | bytes 1572872 | tf_op jit(solution)/shard_map/ppermute | solution.py:21
  242.9 0.0 collective-permute-done.2
  242.9 3.3 %collective-permute-start.4 = (bf16[32,32,256]{2,1,0:T(8,128)(2,1)S(1)}, bf16[32,32,256]{2,1,0:T(8,128)(2,1)S(1)}, u32[]{:S(2)}, u32[]{:S(2)}) collective-permute-start(bf16[32,32,256]{2,1,0:T(8,128)(2,1)S(1)} %collective-permute-done.3), channel_id=1, source_target_pairs={{0,1},{1,0},{2,3},{3,2},{4,5},{5,4},{6,7},{7,6},{8,9},{9,8},{10,11... | collective-permute-start | bytes 1572872 | tf_op jit(solution)/shard_map/ppermute | solution.py:21
  246.1 0.1 fusion.41
  246.2 0.0 collective-permute-done.5
  246.2 1.9 collective-permute-start.6
  248.1 0.0 collective-permute-done.9
  248.2 3.3 %collective-permute-start.13 = (bf16[32,32,256]{2,1,0:T(8,128)(2,1)S(1)}, bf16[32,32,256]{2,1,0:T(8,128)(2,1)S(1)}, u32[]{:S(2)}, u32[]{:S(2)}) collective-permute-start(bf16[32,32,256]{2,1,0:T(8,128)(2,1)S(1)} %collective-permute-done.5), channel_id=1, source_target_pairs={{0,2},{1,3},{2,4},{3,5},{4,6},{5,7},{6,0},{7,1},{8,10},{9,11},{10,... | collective-permute-start | bytes 1572872 | tf_op jit(solution)/shard_map/ppermute | solution.py:21
  251.5 0.9 broadcast_in_dim.7
  252.5 1.1 constant_dynamic-update-slice_fusion.14
  253.6 0.0 collective-permute-done.7
  253.6 2.7 collective-permute-start.8
  256.3 2.0 collective-permute-start.15
  258.3 2.8 collective-permute-start.10
  261.1 0.1 constant_dynamic-update-slice_fusion.12
  261.2 1.9 collective-permute-start.12
  263.1 0.7 collective-permute-done.13
  263.8 2.9 %collective-permute-start.14 = (bf16[32,32,256]{2,1,0:T(8,128)(2,1)S(1)}, bf16[32,32,256]{2,1,0:T(8,128)(2,1)S(1)}, u32[]{:S(2)}, u32[]{:S(2)}) collective-permute-start(bf16[32,32,256]{2,1,0:T(8,128)(2,1)S(1)} %collective-permute-done.13), channel_id=1, source_target_pairs={{0,1},{1,0},{2,3},{3,2},{4,5},{5,4},{6,7},{7,6},{8,9},{9,8},{10,11... | collective-permute-start | bytes 1572872 | tf_op jit(solution)/shard_map/ppermute | solution.py:21
  266.7 0.1 constant_dynamic-update-slice_fusion.10
  266.8 5.5 %collective-permute-done.15 = bf16[32,32,256]{2,1,0:T(8,128)(2,1)S(1)} collective-permute-done((bf16[32,32,256]{2,1,0:T(8,128)(2,1)S(1)}, bf16[32,32,256]{2,1,0:T(8,128)(2,1)S(1)}, u32[]{:S(2)}, u32[]{:S(2)}) %collective-permute-start.15) | collective-permute-done | bytes 524320 | tf_op jit(solution)/shard_map/ppermute | solution.py:21
  272.3 3.6 %collective-permute-start.16 = (bf16[32,32,256]{2,1,0:T(8,128)(2,1)S(1)}, bf16[32,32,256]{2,1,0:T(8,128)(2,1)S(1)}, u32[]{:S(2)}, u32[]{:S(2)}) collective-permute-start(bf16[32,32,256]{2,1,0:T(8,128)(2,1)S(1)} %collective-permute-done.15), channel_id=1, source_target_pairs={{0,1},{1,0},{2,3},{3,2},{4,5},{5,4},{6,7},{7,6},{8,9},{9,8},{10,11... | collective-permute-start | bytes 1572872 | tf_op jit(solution)/shard_map/ppermute | solution.py:21
  275.9 0.0 collective-permute-done.8
  275.9 0.1 constant_dynamic-update-slice_fusion.8
  276.0 0.0 collective-permute-done.10
  276.0 0.1 constant_dynamic-update-slice_fusion.6
  276.1 0.1 constant_dynamic-update-slice_fusion.4
  276.2 0.1 constant_dynamic-update-slice_fusion.2
  276.3 0.8 collective-permute-done.16
  277.2 2.5 convolution_bitcast_fusion.1
  279.7 2.5 convolution_bitcast_fusion
  282.3 2.0 fusion.1
  (19 shorter events, 0.4 us)
Async XLA Ops:
  2.5 97.5 %collective-permute-start.1 = (bf16[4,32,4096]{2,0,1:T(4,128)(2,1)S(1)}, bf16[4,32,4096]{2,0,1:T(4,128)(2,1)S(1)}, u32[]{:S(2)}, u32[]{:S(2)}) collective-permute-start(bf16[4,32,4096]{2,0,1:T(4,128)(2,1)S(1)} %bitcast.25), channel_id=1, source_target_pairs={{0,16},{16,32},{32,48},{48,64},{64,80},{80,96},{96,112},{112,128},... | collective-permute-start | bytes 3145736 | tf_op jit(solution)/shard_map/ppermute | solution.py:17
  7.3 92.1 %collective-permute-start = (bf16[3,32,4096]{2,1,0:T(8,128)(2,1)S(1)}, bf16[3,32,4096]{2,1,0:T(8,128)(2,1)S(1)}, u32[]{:S(2)}, u32[]{:S(2)}) collective-permute-start(bf16[3,32,4096]{2,1,0:T(8,128)(2,1)S(1)} %copy.9), channel_id=1, source_target_pairs={{0,32},{16,48},{32,64},{48,80},{64,96},{80,112},{96,128},{112,144}... | collective-permute-start | bytes 2359304 | tf_op jit(solution)/shard_map/ppermute | solution.py:17
  46.6 35.1 %copy-start = (s32[32]{0:T(128)S(1)}, s32[32]{0:T(128)}, u32[]{:S(2)}) copy-start(s32[32]{0:T(128)} %param.3) | copy-start | bytes 388
  179.8 57.5 %collective-permute-start.3 = (bf16[32,32,256]{2,1,0:T(8,128)(2,1)S(1)}, bf16[32,32,256]{2,1,0:T(8,128)(2,1)S(1)}, u32[]{:S(2)}, u32[]{:S(2)}) collective-permute-start(bf16[32,32,256]{2,1,0:T(8,128)(2,1)S(1)} %reshape.156), channel_id=1, source_target_pairs={{0,8},{1,9},{2,10},{3,11},{4,12},{5,13},{6,14},{7,15},{8,0},{9,1},... | collective-permute-start | bytes 1572872 | tf_op jit(solution)/shard_map/ppermute | solution.py:21
  192.8 50.1 %collective-permute-start.2 = (bf16[32,32,256]{2,1,0:T(8,128)(2,1)S(1)}, bf16[32,32,256]{2,1,0:T(8,128)(2,1)}, u32[]{:S(2)}, u32[]{:S(2)}) collective-permute-start(bf16[32,32,256]{2,1,0:T(8,128)(2,1)S(1)} %reshape.156), channel_id=1, source_target_pairs={{0,1},{1,0},{2,3},{3,2},{4,5},{5,4},{6,7},{7,6},{8,9},{9,8},{10,11... | collective-permute-start | bytes 1572872 | tf_op jit(solution)/shard_map/ppermute | solution.py:21
  198.3 47.9 %collective-permute-start.5 = (bf16[32,32,256]{2,1,0:T(8,128)(2,1)S(1)}, bf16[32,32,256]{2,1,0:T(8,128)(2,1)S(1)}, u32[]{:S(2)}, u32[]{:S(2)}) collective-permute-start(bf16[32,32,256]{2,1,0:T(8,128)(2,1)S(1)} %reshape.156), channel_id=1, source_target_pairs={{0,2},{1,3},{2,4},{3,5},{4,6},{5,7},{6,0},{7,1},{8,10},{9,11},{10,... | collective-permute-start | bytes 1572872 | tf_op jit(solution)/shard_map/ppermute | solution.py:21
  200.4 47.7 %collective-permute-start.9 = (bf16[32,32,256]{2,1,0:T(8,128)(2,1)S(1)}, bf16[32,32,256]{2,1,0:T(8,128)(2,1)S(1)}, u32[]{:S(2)}, u32[]{:S(2)}) collective-permute-start(bf16[32,32,256]{2,1,0:T(8,128)(2,1)S(1)} %reshape.156), channel_id=1, source_target_pairs={{0,6},{1,7},{2,0},{3,1},{4,2},{5,3},{6,4},{7,5},{8,14},{9,15},{10,... | collective-permute-start | bytes 1572872 | tf_op jit(solution)/shard_map/ppermute | solution.py:21
  237.3 16.2 %collective-permute-start.7 = (bf16[32,32,256]{2,1,0:T(8,128)(2,1)S(1)}, bf16[32,32,256]{2,1,0:T(8,128)(2,1)S(1)}, u32[]{:S(2)}, u32[]{:S(2)}) collective-permute-start(bf16[32,32,256]{2,1,0:T(8,128)(2,1)S(1)} %collective-permute-done.3), channel_id=1, source_target_pairs={{0,2},{1,3},{2,4},{3,5},{4,6},{5,7},{6,0},{7,1},{8,10},{9,11},{10,... | collective-permute-start | bytes 1572872 | tf_op jit(solution)/shard_map/ppermute | solution.py:21
  239.4 16.8 %collective-permute-start.11 = (bf16[32,32,256]{2,1,0:T(8,128)(2,1)S(1)}, bf16[32,32,256]{2,1,0:T(8,128)(2,1)S(1)}, u32[]{:S(2)}, u32[]{:S(2)}) collective-permute-start(bf16[32,32,256]{2,1,0:T(8,128)(2,1)S(1)} %collective-permute-done.3), channel_id=1, source_target_pairs={{0,6},{1,7},{2,0},{3,1},{4,2},{5,3},{6,4},{7,5},{8,14},{9,15},{10,... | collective-permute-start | bytes 1572872 | tf_op jit(solution)/shard_map/ppermute | solution.py:21
  242.9 15.5 %collective-permute-start.4 = (bf16[32,32,256]{2,1,0:T(8,128)(2,1)S(1)}, bf16[32,32,256]{2,1,0:T(8,128)(2,1)S(1)}, u32[]{:S(2)}, u32[]{:S(2)}) collective-permute-start(bf16[32,32,256]{2,1,0:T(8,128)(2,1)S(1)} %collective-permute-done.3), channel_id=1, source_target_pairs={{0,1},{1,0},{2,3},{3,2},{4,5},{5,4},{6,7},{7,6},{8,9},{9,8},{10,11... | collective-permute-start | bytes 1572872 | tf_op jit(solution)/shard_map/ppermute | solution.py:21
  246.2 15.0 %collective-permute-start.6 = (bf16[32,32,256]{2,1,0:T(8,128)(2,1)S(1)}, bf16[32,32,256]{2,1,0:T(8,128)(2,1)S(1)}, u32[]{:S(2)}, u32[]{:S(2)}) collective-permute-start(bf16[32,32,256]{2,1,0:T(8,128)(2,1)S(1)} %collective-permute-done.5), channel_id=1, source_target_pairs={{0,1},{1,0},{2,3},{3,2},{4,5},{5,4},{6,7},{7,6},{8,9},{9,8},{10,11... | collective-permute-start | bytes 1572872 | tf_op jit(solution)/shard_map/ppermute | solution.py:21
  248.2 15.7 %collective-permute-start.13 = (bf16[32,32,256]{2,1,0:T(8,128)(2,1)S(1)}, bf16[32,32,256]{2,1,0:T(8,128)(2,1)S(1)}, u32[]{:S(2)}, u32[]{:S(2)}) collective-permute-start(bf16[32,32,256]{2,1,0:T(8,128)(2,1)S(1)} %collective-permute-done.5), channel_id=1, source_target_pairs={{0,2},{1,3},{2,4},{3,5},{4,6},{5,7},{6,0},{7,1},{8,10},{9,11},{10,... | collective-permute-start | bytes 1572872 | tf_op jit(solution)/shard_map/ppermute | solution.py:21
  253.6 22.3 %collective-permute-start.8 = (bf16[32,32,256]{2,1,0:T(8,128)(2,1)S(1)}, bf16[32,32,256]{2,1,0:T(8,128)(2,1)S(1)}, u32[]{:S(2)}, u32[]{:S(2)}) collective-permute-start(bf16[32,32,256]{2,1,0:T(8,128)(2,1)S(1)} %collective-permute-done.7), channel_id=1, source_target_pairs={{0,1},{1,0},{2,3},{3,2},{4,5},{5,4},{6,7},{7,6},{8,9},{9,8},{10,11... | collective-permute-start | bytes 1572872 | tf_op jit(solution)/shard_map/ppermute | solution.py:21
  256.3 16.0 %collective-permute-start.15 = (bf16[32,32,256]{2,1,0:T(8,128)(2,1)S(1)}, bf16[32,32,256]{2,1,0:T(8,128)(2,1)S(1)}, u32[]{:S(2)}, u32[]{:S(2)}) collective-permute-start(bf16[32,32,256]{2,1,0:T(8,128)(2,1)S(1)} %collective-permute-done.11), channel_id=1, source_target_pairs={{0,6},{1,7},{2,0},{3,1},{4,2},{5,3},{6,4},{7,5},{8,14},{9,15},{10,... | collective-permute-start | bytes 1572872 | tf_op jit(solution)/shard_map/ppermute | solution.py:21
  258.3 17.7 %collective-permute-start.10 = (bf16[32,32,256]{2,1,0:T(8,128)(2,1)S(1)}, bf16[32,32,256]{2,1,0:T(8,128)(2,1)S(1)}, u32[]{:S(2)}, u32[]{:S(2)}) collective-permute-start(bf16[32,32,256]{2,1,0:T(8,128)(2,1)S(1)} %collective-permute-done.9), channel_id=1, source_target_pairs={{0,1},{1,0},{2,3},{3,2},{4,5},{5,4},{6,7},{7,6},{8,9},{9,8},{10,11... | collective-permute-start | bytes 1572872 | tf_op jit(solution)/shard_map/ppermute | solution.py:21
  261.2 14.9 %collective-permute-start.12 = (bf16[32,32,256]{2,1,0:T(8,128)(2,1)S(1)}, bf16[32,32,256]{2,1,0:T(8,128)(2,1)S(1)}, u32[]{:S(2)}, u32[]{:S(2)}) collective-permute-start(bf16[32,32,256]{2,1,0:T(8,128)(2,1)S(1)} %collective-permute-done.11), channel_id=1, source_target_pairs={{0,1},{1,0},{2,3},{3,2},{4,5},{5,4},{6,7},{7,6},{8,9},{9,8},{10,11... | collective-permute-start | bytes 1572872 | tf_op jit(solution)/shard_map/ppermute | solution.py:21
  263.8 12.4 %collective-permute-start.14 = (bf16[32,32,256]{2,1,0:T(8,128)(2,1)S(1)}, bf16[32,32,256]{2,1,0:T(8,128)(2,1)S(1)}, u32[]{:S(2)}, u32[]{:S(2)}) collective-permute-start(bf16[32,32,256]{2,1,0:T(8,128)(2,1)S(1)} %collective-permute-done.13), channel_id=1, source_target_pairs={{0,1},{1,0},{2,3},{3,2},{4,5},{5,4},{6,7},{7,6},{8,9},{9,8},{10,11... | collective-permute-start | bytes 1572872 | tf_op jit(solution)/shard_map/ppermute | solution.py:21
  272.3 4.9 %collective-permute-start.16 = (bf16[32,32,256]{2,1,0:T(8,128)(2,1)S(1)}, bf16[32,32,256]{2,1,0:T(8,128)(2,1)S(1)}, u32[]{:S(2)}, u32[]{:S(2)}) collective-permute-start(bf16[32,32,256]{2,1,0:T(8,128)(2,1)S(1)} %collective-permute-done.15), channel_id=1, source_target_pairs={{0,1},{1,0},{2,3},{3,2},{4,5},{5,4},{6,7},{7,6},{8,9},{9,8},{10,11... | collective-permute-start | bytes 1572872 | tf_op jit(solution)/shard_map/ppermute | solution.py:21

commit v2 on v1

--- a/solution.py
+++ b/solution.py
@@ -1,8 +1,10 @@
+import functools
 import math
 
 import jax
 import jax.numpy as jnp
 from jax import lax
+from jax.experimental import pallas as pl
 from jax.sharding import PartitionSpec as P
 
 NFFT = 4096
@@ -38,12 +40,41 @@
         angle = ((scale * rows[:, None] * columns[None, :]) % NFFT).astype(jnp.float32) * step
         return jnp.cos(angle), -jnp.sin(angle)
 
-    hr, hi = factor(ROOT)
-    lr, li = factor(1)
-    real = hr[:, None, :] * lr[None, :, :] - hi[:, None, :] * li[None, :, :]
-    imag = hr[:, None, :] * li[None, :, :] + hi[:, None, :] * lr[None, :, :]
-    both = jnp.stack([real, imag], axis=2) * (1.0 / math.sqrt(NFFT))
-    return both.astype(jnp.bfloat16).reshape(NFFT, 2 * CHANS)
+    def spread(part, axis):
+        grown = jnp.broadcast_to(jnp.expand_dims(part, axis), (ROOT, ROOT, CHANS))
+        return grown.reshape(NFFT, CHANS)
+
+    hr, hi = (spread(t, 1) for t in factor(ROOT))
+    lr, li = (spread(t, 0) for t in factor(1))
+    real = hr * lr - hi * li
+    imag = hr * li + hi * lr
+    both = jnp.concatenate([real, imag], axis=1) * (1.0 / math.sqrt(NFFT))
+    return lax.optimization_barrier(both.astype(jnp.bfloat16))
+
+
+def polyphase_kernel(spec_count, x_ref, w_ref, g_ref, o_ref):
+    gain = g_ref[...]
+    for s in range(spec_count):
+        total = jnp.zeros(o_ref.shape[1:], jnp.float32)
+        for tap in range(TAPS):
+            total = total + w_ref[tap : tap + 1, :] * (x_ref[s + tap].astype(jnp.float32) * gain)
+        o_ref[s] = total.astype(o_ref.dtype)
+
+
+def polyphase(joined, window, gain, spec_count):
+    rows, inputs, length = joined.shape
+    lanes = 512
+    return pl.pallas_call(
+        functools.partial(polyphase_kernel, spec_count),
+        out_shape=jax.ShapeDtypeStruct((spec_count, inputs, length), jnp.bfloat16),
+        grid=(length // lanes,),
+        in_specs=[
+            pl.BlockSpec((rows, inputs, lanes), lambda k: (0, 0, k)),
+            pl.BlockSpec((TAPS, lanes), lambda k: (0, k)),
+            pl.BlockSpec((inputs, 1), lambda k: (0, 0)),
+        ],
+        out_specs=pl.BlockSpec((spec_count, inputs, lanes), lambda k: (0, 0, k)),
+    )(joined, window, gain)
 
 
 def gather_inputs(own):
@@ -98,13 +129,9 @@
         earlier = [shifted(samples[spec_count - take :], "chan", distance)] + earlier
         need -= take
         distance += 1
-    joined = jnp.concatenate(earlier + [samples], axis=0).astype(jnp.float32)
-    signal = joined * (scales.astype(jnp.float32) * (1.0 / 256.0))[None, :, None]
-    window = window_table()
-    total = jnp.zeros((spec_count, inp_count, NFFT), jnp.float32)
-    for tap in range(TAPS):
-        total = total + window[tap] * signal[tap : tap + spec_count]
-    filtered = total.astype(jnp.bfloat16).reshape(spec_count * inp_count, NFFT)
+    joined = jnp.concatenate(earlier + [samples], axis=0)
+    gain = (scales.astype(jnp.float32) * (1.0 / 256.0)).reshape(inp_count, 1)
+    filtered = polyphase(joined, window_table(), gain, spec_count).reshape(spec_count * inp_count, NFFT)
     spectra = jnp.dot(filtered, dft_table(), preferred_element_type=jnp.float32).astype(jnp.bfloat16)
     spectra = spectra.reshape(spec_count, inp_count, 2, CHANS)
     local_block = lax.all_to_all(spectra, "chan", split_axis=3, concat_axis=0, tiled=True)

time: 285 us -> 239 us (0.84)
  other arithmetic: 95.5 us -> 23.3 us
  waiting for transfers between devices: 40.7 us -> 72.5 us
  local copies, waits for them, and re-layouts: 36.2 us -> 17.5 us
  Pallas kernels: 0 us -> 6.81 us
  blocking collectives: 34.9 us -> 40.6 us
    convert_element_type x2 -> x1, other arithmetic: 53.3 us -> 8.04 us  [dft_table(): return lax.optimization_barrier(both.astype(jnp.bfloat16))]
    ppermute x2, waiting for transfers between devices: 0.01 us -> 31.6 us  [shifted(): return lax.ppermute(block, axis, route)]
    sub x1, other arithmetic: 31 us -> 4.79 us  [dft_table(): real = hr * lr - hi * li]
    unnamed x5 -> x4, local copies, waits for them, and re-layouts: 20.1 us -> 3.03 us
    pallas_call x0 -> x1, Pallas kernels: none -> 6.81 us  [polyphase(): pl.pallas_call(functools.partial(polyphase_kernel, spec_count), out_shape...]
    all_to_all x1, blocking collectives: 34.9 us -> 40.6 us  [shards(): lax.all_to_all(spectra, 'chan', split_axis=3, concat_axis=0, tiled=True)]
    mul x2 -> x0, other arithmetic: 4.68 us -> none  [the longest x1 4.68 us: shards(): joined * (scales.astype(jnp.float32) * (1.0 / 256.0))[None, :, None]]
    concatenate x0 -> x1, other arithmetic: none -> 3.33 us  [shards(): joined = jnp.concatenate(earlier + [samples], axis=0)]
  transfers between devices with their start and end apart: 17 -> 17, of which waited for: 4 -> 5; matrix products, arithmetic and copies ran while one was open for 32% -> 9% of each run, Pallas kernels for 0% -> 0%
where the time goes in v2:
time: 239 us; the launch traced here: 238 us
  waiting for transfers between devices  72.5 us (30%)
  starting transfers between devices  63.5 us (27%)
  blocking collectives  40.6 us (17%)
  other arithmetic  23.3 us (10%)
  local copies, waits for them, and re-layouts  17.5 us (7%)
  matrix products  13.5 us (6%)
  Pallas kernels  6.81 us (3%)
    ppermute x15, starting transfers between devices, moved(): lax.ppermute(block, 'inp', [(p, mapping(p)) for p in range(lax.axis_size(...  53.9 us
    ppermute x15, waiting for transfers between devices, moved(): lax.ppermute(block, 'inp', [(p, mapping(p)) for p in range(lax.axis_size(...  40.9 us
    all_to_all x1, blocking collectives, shards(): lax.all_to_all(spectra, 'chan', split_axis=3, concat_axis=0, tiled=True)  40.6 us
    ppermute x2, waiting for transfers between devices, shifted(): return lax.ppermute(block, axis, route)  31.6 us
    ppermute x2, starting transfers between devices, shifted(): return lax.ppermute(block, axis, route)  9.65 us
    dot_general x1, matrix products, shards(): jnp.dot(filtered, dft_table(), preferred_element_type=jnp.float32)  8.44 us
    convert_element_type x1, other arithmetic, dft_table(): return lax.optimization_barrier(both.astype(jnp.bfloat16))  8.04 us
    pallas_call x1, Pallas kernels, polyphase(): pl.pallas_call(functools.partial(polyphase_kernel, spec_count), out_shape...  6.81 us
  transfers between devices with their start and end apart: 17, of which 5 were waited for; matrix products, arithmetic and copies ran while one was open for 9% of the time, Pallas kernels for 0%

profile of v2, /device:TPU:55, one launch (start us, length us, event | category | flops | bytes accessed | tf_op | source)
XLA Modules:
  0.0 238.5 jit_solution(13918790312768933223)
XLA Ops:
  0.0 1.7 convert_element_type.54
  1.7 0.1 copy.23
  1.8 3.5 %collective-permute-start.1 = (bf16[4,32,4096]{2,1,0:T(8,128)(2,1)S(1)}, bf16[4,32,4096]{2,1,0:T(8,128)(2,1)}, u32[]{:S(2)}, u32[]{:S(2)}) collective-permute-start(bf16[4,32,4096]{2,1,0:T(8,128)(2,1)S(1)} %bitcast.35), channel_id=1, source_target_pairs={{0,16},{16,32},{32,48},{48,64},{64,80},{80,96},{96,112},{112,128},... | collective-permute-start | bytes 3145736 | tf_op jit(solution)/shard_map/ppermute | solution.py:19
  5.3 0.9 slice.12
  6.3 6.1 %collective-permute-start = (bf16[3,32,4096]{2,1,0:T(8,128)(2,1)}, bf16[3,32,4096]{2,1,0:T(8,128)(2,1)}, u32[]{:S(2)}, u32[]{:S(2)}) collective-permute-start(bf16[3,32,4096]{2,1,0:T(8,128)(2,1)} %slice.12), channel_id=1, source_target_pairs={{0,32},{16,48},{32,64},{48,80},{64,96},{80,112},{96,128},{112,144}... | collective-permute-start | bytes 2359304 | tf_op jit(solution)/shard_map/ppermute | solution.py:19
  12.4 1.0 sine_negate_fusion
  13.4 1.1 fusion.26
  14.5 4.8 %multiply_subtract_fusion = (f32[64,64,1024]{2,1,0:T(8,128)S(1)}, f32[64,64,1024]{2,1,0:T(8,128)S(1)}) fusion(f32[64,1024]{1,0:T(8,128)S(1)} %get-tuple-element.11, f32[64,1024]{1,0:T(8,128)S(1)} %get-tuple-element.10, f32[64,1024]{1,0:T(8,128)S(1)} %get-tuple-element.12, f32[64,1024]{1,0:T(8,128)S(1)} %get-tuple-element.9), kind=kLoop, calls=%fused_computation.3 | loop fusion | flops 25165824 | bytes 34603008 | tf_op jit(solution)/shard_map/sub | solution.py:49
  19.3 0.0 copy-start
  19.4 8.0 %fusion = bf16[4096,2048]{1,0:T(8,128)(2,1)} fusion(f32[4096,1024]{1,0:T(8,128)S(1)} %bitcast.31, f32[4096,1024]{1,0:T(8,128)S(1)} %bitcast.30), kind=kLoop, calls=%fused_computation.1 | loop fusion | flops 25165824 | bytes 50331648 | tf_op jit(solution)/shard_map/convert_element_type | solution.py:52
  27.4 0.7 copy.14.g_ref
  28.1 1.3 fusion.21.w_ref
  29.4 31.6 %collective-permute-done = bf16[3,32,4096]{2,1,0:T(8,128)(2,1)} collective-permute-done((bf16[3,32,4096]{2,1,0:T(8,128)(2,1)}, bf16[3,32,4096]{2,1,0:T(8,128)(2,1)}, u32[]{:S(2)}, u32[]{:S(2)}) %collective-permute-start) | collective-permute-done | bytes 786464 | tf_op jit(solution)/shard_map/ppermute | solution.py:19
  61.0 0.0 collective-permute-done.1
  61.0 3.3 %pad_maximum_fusion.x_ref = bf16[11,32,4096]{2,1,0:T(8,128)(2,1)} fusion(bf16[4,32,4096]{2,1,0:T(8,128)(2,1)S(1)} %bitcast.37, bf16[4,32,4096]{2,1,0:T(8,128)(2,1)} %collective-permute-done.1, bf16[3,32,4096]{2,1,0:T(8,128)(2,1)} %collective-permute-done), kind=kLoop, calls=%fused_computation.6 | loop fusion | flops 2883584 | bytes 5767168 | tf_op jit(solution)/shard_map/concatenate | solution.py:132
  64.3 6.8 %shard_map.28 = bf16[4,32,4096]{2,1,0:T(8,128)(2,1)} custom-call(bf16[11,32,4096]{2,1,0:T(8,128)(2,1)} %pad_maximum_fusion.x_ref, f32[8,4096]{1,0:T(8,128)} %fusion.21.w_ref, f32[32,1]{1,0:T(8,128)} %copy.14.g_ref), custom_call_target="tpu_custom_call" | custom-call | tf_op jit(solution)/shard_map/pallas_call | solution.py:67
  71.1 8.4 %convolution_convert_fusion = bf16[128,2048]{1,0:T(8,128)(2,1)S(1)} fusion(bf16[128,4096]{1,0:T(8,128)(2,1)} %bitcast.38, bf16[4096,2048]{1,0:T(8,128)(2,1)} %fusion), kind=kOutput, calls=%fused_computation.7 | convolution fusion | flops 2147745792 | bytes 18350080 | tf_op jit(solution)/shard_map/dot_general | solution.py:135
  79.6 0.4 reshape.118
  80.0 1.9 copy.15
  81.9 2.0 reshape.120
  83.9 40.6 %all_to_all.18 = bf16[32,2,4096]{2,1,0:T(2,128)(2,1)S(1)} all-to-all(bf16[32,2,4096]{2,1,0:T(2,128)(2,1)S(1)} %reshape.120), channel_id=1, replica_groups=mesh['chan'=32,'inp'=16] {'chan'}, dimensions={0} | all-to-all | bytes 1048576 | tf_op jit(solution)/shard_map/all_to_all | solution.py:137
  124.4 1.0 reshape.121
  125.5 3.8 %copy.20 = bf16[4,32,2,32,32]{4,1,2,0,3:T(8,128)(2,1)} copy(bf16[4,32,2,32,32]{1,2,0,4,3:T(2,128)(2,1)S(1)} %bitcast.33) | data formatting | bytes 1048576 | tf_op jit(solution)/shard_map/all_to_all | solution.py:137
  129.3 3.7 %copy.18 = bf16[32,32,2,128]{3,2,1,0:T(2,128)(2,1)S(1)} copy(bf16[32,32,2,128]{0,1,2,3:T(8,128)(2,1)} %bitcast.34) | data formatting | bytes 1048576 | tf_op jit(solution)/shard_map/transpose | solution.py:140
  133.0 0.3 reshape.119
  133.3 13.8 %collective-permute-start.3 = (bf16[32,32,256]{2,1,0:T(8,128)(2,1)S(1)}, bf16[32,32,256]{2,1,0:T(8,128)(2,1)S(1)}, u32[]{:S(2)}, u32[]{:S(2)}) collective-permute-start(bf16[32,32,256]{2,1,0:T(8,128)(2,1)S(1)} %reshape.119), channel_id=1, source_target_pairs={{0,8},{1,9},{2,10},{3,11},{4,12},{5,13},{6,14},{7,15},{8,0},{9,1},... | collective-permute-start | bytes 1572872 | tf_op jit(solution)/shard_map/ppermute | solution.py:23
  147.1 5.2 %collective-permute-start.2 = (bf16[32,32,256]{2,1,0:T(8,128)(2,1)S(1)}, bf16[32,32,256]{2,1,0:T(8,128)(2,1)}, u32[]{:S(2)}, u32[]{:S(2)}) collective-permute-start(bf16[32,32,256]{2,1,0:T(8,128)(2,1)S(1)} %reshape.119), channel_id=1, source_target_pairs={{0,1},{1,0},{2,3},{3,2},{4,5},{5,4},{6,7},{7,6},{8,9},{9,8},{10,11... | collective-permute-start | bytes 1572872 | tf_op jit(solution)/shard_map/ppermute | solution.py:23
  152.3 2.1 collective-permute-start.5
  154.4 3.2 %collective-permute-start.9 = (bf16[32,32,256]{2,1,0:T(8,128)(2,1)S(1)}, bf16[32,32,256]{2,1,0:T(8,128)(2,1)S(1)}, u32[]{:S(2)}, u32[]{:S(2)}) collective-permute-start(bf16[32,32,256]{2,1,0:T(8,128)(2,1)S(1)} %reshape.119), channel_id=1, source_target_pairs={{0,6},{1,7},{2,0},{3,1},{4,2},{5,3},{6,4},{7,5},{8,14},{9,15},{10,... | collective-permute-start | bytes 1572872 | tf_op jit(solution)/shard_map/ppermute | solution.py:23
  157.6 33.8 %collective-permute-done.3 = bf16[32,32,256]{2,1,0:T(8,128)(2,1)S(1)} collective-permute-done((bf16[32,32,256]{2,1,0:T(8,128)(2,1)S(1)}, bf16[32,32,256]{2,1,0:T(8,128)(2,1)S(1)}, u32[]{:S(2)}, u32[]{:S(2)}) %collective-permute-start.3) | collective-permute-done | bytes 524320 | tf_op jit(solution)/shard_map/ppermute | solution.py:23
  191.4 2.1 collective-permute-start.7
  193.5 3.4 %collective-permute-start.11 = (bf16[32,32,256]{2,1,0:T(8,128)(2,1)S(1)}, bf16[32,32,256]{2,1,0:T(8,128)(2,1)S(1)}, u32[]{:S(2)}, u32[]{:S(2)}) collective-permute-start(bf16[32,32,256]{2,1,0:T(8,128)(2,1)S(1)} %collective-permute-done.3), channel_id=1, source_target_pairs={{0,6},{1,7},{2,0},{3,1},{4,2},{5,3},{6,4},{7,5},{8,14},{9,15},{10,... | collective-permute-start | bytes 1572872 | tf_op jit(solution)/shard_map/ppermute | solution.py:23
  197.1 0.0 collective-permute-done.2
  197.1 3.3 %collective-permute-start.4 = (bf16[32,32,256]{2,1,0:T(8,128)(2,1)S(1)}, bf16[32,32,256]{2,1,0:T(8,128)(2,1)S(1)}, u32[]{:S(2)}, u32[]{:S(2)}) collective-permute-start(bf16[32,32,256]{2,1,0:T(8,128)(2,1)S(1)} %collective-permute-done.3), channel_id=1, source_target_pairs={{0,1},{1,0},{2,3},{3,2},{4,5},{5,4},{6,7},{7,6},{8,9},{9,8},{10,11... | collective-permute-start | bytes 1572872 | tf_op jit(solution)/shard_map/ppermute | solution.py:23
  200.4 0.1 fusion.33
  200.5 1.9 collective-permute-start.6
  202.4 3.3 %collective-permute-start.13 = (bf16[32,32,256]{2,1,0:T(8,128)(2,1)S(1)}, bf16[32,32,256]{2,1,0:T(8,128)(2,1)S(1)}, u32[]{:S(2)}, u32[]{:S(2)}) collective-permute-start(bf16[32,32,256]{2,1,0:T(8,128)(2,1)S(1)} %collective-permute-done.5), channel_id=1, source_target_pairs={{0,2},{1,3},{2,4},{3,5},{4,6},{5,7},{6,0},{7,1},{8,10},{9,11},{10,... | collective-permute-start | bytes 1572872 | tf_op jit(solution)/shard_map/ppermute | solution.py:23
  205.7 0.9 broadcast_in_dim.48
  206.7 1.1 constant_dynamic-update-slice_fusion.14
  207.8 0.0 collective-permute-done.7
  207.8 2.7 %collective-permute-start.8 = (bf16[32,32,256]{2,1,0:T(8,128)(2,1)S(1)}, bf16[32,32,256]{2,1,0:T(8,128)(2,1)S(1)}, u32[]{:S(2)}, u32[]{:S(2)}) collective-permute-start(bf16[32,32,256]{2,1,0:T(8,128)(2,1)S(1)} %collective-permute-done.7), channel_id=1, source_target_pairs={{0,1},{1,0},{2,3},{3,2},{4,5},{5,4},{6,7},{7,6},{8,9},{9,8},{10,11... | collective-permute-start | bytes 1572872 | tf_op jit(solution)/shard_map/ppermute | solution.py:23
  210.5 0.0 collective-permute-done.11
  210.5 2.0 collective-permute-start.15
  212.6 0.0 collective-permute-done.4
  212.6 2.8 %collective-permute-start.10 = (bf16[32,32,256]{2,1,0:T(8,128)(2,1)S(1)}, bf16[32,32,256]{2,1,0:T(8,128)(2,1)S(1)}, u32[]{:S(2)}, u32[]{:S(2)}) collective-permute-start(bf16[32,32,256]{2,1,0:T(8,128)(2,1)S(1)} %collective-permute-done.9), channel_id=1, source_target_pairs={{0,1},{1,0},{2,3},{3,2},{4,5},{5,4},{6,7},{7,6},{8,9},{9,8},{10,11... | collective-permute-start | bytes 1572872 | tf_op jit(solution)/shard_map/ppermute | solution.py:23
  215.4 0.1 constant_dynamic-update-slice_fusion.12
  215.5 0.0 collective-permute-done.6
  215.5 1.9 collective-permute-start.12
  217.4 0.3 collective-permute-done.13
  217.7 3.0 %collective-permute-start.14 = (bf16[32,32,256]{2,1,0:T(8,128)(2,1)S(1)}, bf16[32,32,256]{2,1,0:T(8,128)(2,1)S(1)}, u32[]{:S(2)}, u32[]{:S(2)}) collective-permute-start(bf16[32,32,256]{2,1,0:T(8,128)(2,1)S(1)} %collective-permute-done.13), channel_id=1, source_target_pairs={{0,1},{1,0},{2,3},{3,2},{4,5},{5,4},{6,7},{7,6},{8,9},{9,8},{10,11... | collective-permute-start | bytes 1572872 | tf_op jit(solution)/shard_map/ppermute | solution.py:23
  220.8 0.1 constant_dynamic-update-slice_fusion.10
  220.9 5.7 %collective-permute-done.15 = bf16[32,32,256]{2,1,0:T(8,128)(2,1)S(1)} collective-permute-done((bf16[32,32,256]{2,1,0:T(8,128)(2,1)S(1)}, bf16[32,32,256]{2,1,0:T(8,128)(2,1)S(1)}, u32[]{:S(2)}, u32[]{:S(2)}) %collective-permute-start.15) | collective-permute-done | bytes 524320 | tf_op jit(solution)/shard_map/ppermute | solution.py:23
  226.5 3.3 %collective-permute-start.16 = (bf16[32,32,256]{2,1,0:T(8,128)(2,1)S(1)}, bf16[32,32,256]{2,1,0:T(8,128)(2,1)S(1)}, u32[]{:S(2)}, u32[]{:S(2)}) collective-permute-start(bf16[32,32,256]{2,1,0:T(8,128)(2,1)S(1)} %collective-permute-done.15), channel_id=1, source_target_pairs={{0,1},{1,0},{2,3},{3,2},{4,5},{5,4},{6,7},{7,6},{8,9},{9,8},{10,11... | collective-permute-start | bytes 1572872 | tf_op jit(solution)/shard_map/ppermute | solution.py:23
  229.9 0.1 constant_dynamic-update-slice_fusion.8
  230.0 0.0 collective-permute-done.10
  230.0 0.1 constant_dynamic-update-slice_fusion.6
  230.1 0.0 collective-permute-done.12
  230.1 0.1 constant_dynamic-update-slice_fusion.4
  230.3 0.0 collective-permute-done.14
  230.3 0.1 constant_dynamic-update-slice_fusion.2
  230.4 1.0 collective-permute-done.16
  231.5 2.5 %convolution_bitcast_fusion.1 = f32[1,32,32,512]{3,2,1,0:T(8,128)S(1)} fusion(bf16[32,32,256]{2,1,0:T(8,128)(2,1)S(1)} %reshape.119, bf16[32,512,256]{2,1,0:T(8,128)(2,1)S(1)} %constant_dynamic-update-slice_fusion), kind=kOutput, calls=%fused_computation.9 | convolution fusion | flops 268435456 | bytes 11010048 | tf_op jit(solution)/shard_map/cik,cjk->cij/dot_general | solution.py:143
  234.0 2.5 %convolution_bitcast_fusion = f32[1,32,32,512]{3,2,1,0:T(8,128)S(1)} fusion(bf16[32,512,256]{2,1,0:T(8,128)(2,1)S(1)} %constant_dynamic-update-slice_fusion, bf16[32,32,128]{2,1,0:T(8,128)(2,1)S(1)} %get-tuple-element.8, bf16[32,32,128]{2,1,0:T(8,128)(2,1)S(1)} %get-tuple-element.7), kind=kOutput, calls=%fused_computation.8 | convolution fusion | flops 269484032 | bytes 11010048 | tf_op jit(solution)/shard_map/cik,cjk->cij/dot_general | solution.py:144
  236.5 2.0 fusion.1
  (15 shorter events, 0.4 us)
Async XLA Ops:
  1.8 59.2 %collective-permute-start.1 = (bf16[4,32,4096]{2,1,0:T(8,128)(2,1)S(1)}, bf16[4,32,4096]{2,1,0:T(8,128)(2,1)}, u32[]{:S(2)}, u32[]{:S(2)}) collective-permute-start(bf16[4,32,4096]{2,1,0:T(8,128)(2,1)S(1)} %bitcast.35), channel_id=1, source_target_pairs={{0,16},{16,32},{32,48},{48,64},{64,80},{80,96},{96,112},{112,128},... | collective-permute-start | bytes 3145736 | tf_op jit(solution)/shard_map/ppermute | solution.py:19
  6.3 54.7 %collective-permute-start = (bf16[3,32,4096]{2,1,0:T(8,128)(2,1)}, bf16[3,32,4096]{2,1,0:T(8,128)(2,1)}, u32[]{:S(2)}, u32[]{:S(2)}) collective-permute-start(bf16[3,32,4096]{2,1,0:T(8,128)(2,1)} %slice.12), channel_id=1, source_target_pairs={{0,32},{16,48},{32,64},{48,80},{64,96},{80,112},{96,128},{112,144}... | collective-permute-start | bytes 2359304 | tf_op jit(solution)/shard_map/ppermute | solution.py:19
  19.3 8.1 %copy-start = (s32[32]{0:T(128)S(1)}, s32[32]{0:T(128)}, u32[]{:S(2)}) copy-start(s32[32]{0:T(128)} %param.3) | copy-start | bytes 388
  133.3 58.1 %collective-permute-start.3 = (bf16[32,32,256]{2,1,0:T(8,128)(2,1)S(1)}, bf16[32,32,256]{2,1,0:T(8,128)(2,1)S(1)}, u32[]{:S(2)}, u32[]{:S(2)}) collective-permute-start(bf16[32,32,256]{2,1,0:T(8,128)(2,1)S(1)} %reshape.119), channel_id=1, source_target_pairs={{0,8},{1,9},{2,10},{3,11},{4,12},{5,13},{6,14},{7,15},{8,0},{9,1},... | collective-permute-start | bytes 1572872 | tf_op jit(solution)/shard_map/ppermute | solution.py:23
  147.1 50.0 %collective-permute-start.2 = (bf16[32,32,256]{2,1,0:T(8,128)(2,1)S(1)}, bf16[32,32,256]{2,1,0:T(8,128)(2,1)}, u32[]{:S(2)}, u32[]{:S(2)}) collective-permute-start(bf16[32,32,256]{2,1,0:T(8,128)(2,1)S(1)} %reshape.119), channel_id=1, source_target_pairs={{0,1},{1,0},{2,3},{3,2},{4,5},{5,4},{6,7},{7,6},{8,9},{9,8},{10,11... | collective-permute-start | bytes 1572872 | tf_op jit(solution)/shard_map/ppermute | solution.py:23
  152.3 48.2 %collective-permute-start.5 = (bf16[32,32,256]{2,1,0:T(8,128)(2,1)S(1)}, bf16[32,32,256]{2,1,0:T(8,128)(2,1)S(1)}, u32[]{:S(2)}, u32[]{:S(2)}) collective-permute-start(bf16[32,32,256]{2,1,0:T(8,128)(2,1)S(1)} %reshape.119), channel_id=1, source_target_pairs={{0,2},{1,3},{2,4},{3,5},{4,6},{5,7},{6,0},{7,1},{8,10},{9,11},{10,... | collective-permute-start | bytes 1572872 | tf_op jit(solution)/shard_map/ppermute | solution.py:23
  154.4 48.0 %collective-permute-start.9 = (bf16[32,32,256]{2,1,0:T(8,128)(2,1)S(1)}, bf16[32,32,256]{2,1,0:T(8,128)(2,1)S(1)}, u32[]{:S(2)}, u32[]{:S(2)}) collective-permute-start(bf16[32,32,256]{2,1,0:T(8,128)(2,1)S(1)} %reshape.119), channel_id=1, source_target_pairs={{0,6},{1,7},{2,0},{3,1},{4,2},{5,3},{6,4},{7,5},{8,14},{9,15},{10,... | collective-permute-start | bytes 1572872 | tf_op jit(solution)/shard_map/ppermute | solution.py:23
  191.4 16.4 %collective-permute-start.7 = (bf16[32,32,256]{2,1,0:T(8,128)(2,1)S(1)}, bf16[32,32,256]{2,1,0:T(8,128)(2,1)S(1)}, u32[]{:S(2)}, u32[]{:S(2)}) collective-permute-start(bf16[32,32,256]{2,1,0:T(8,128)(2,1)S(1)} %collective-permute-done.3), channel_id=1, source_target_pairs={{0,2},{1,3},{2,4},{3,5},{4,6},{5,7},{6,0},{7,1},{8,10},{9,11},{10,... | collective-permute-start | bytes 1572872 | tf_op jit(solution)/shard_map/ppermute | solution.py:23
  193.5 17.0 %collective-permute-start.11 = (bf16[32,32,256]{2,1,0:T(8,128)(2,1)S(1)}, bf16[32,32,256]{2,1,0:T(8,128)(2,1)S(1)}, u32[]{:S(2)}, u32[]{:S(2)}) collective-permute-start(bf16[32,32,256]{2,1,0:T(8,128)(2,1)S(1)} %collective-permute-done.3), channel_id=1, source_target_pairs={{0,6},{1,7},{2,0},{3,1},{4,2},{5,3},{6,4},{7,5},{8,14},{9,15},{10,... | collective-permute-start | bytes 1572872 | tf_op jit(solution)/shard_map/ppermute | solution.py:23
  197.1 15.4 %collective-permute-start.4 = (bf16[32,32,256]{2,1,0:T(8,128)(2,1)S(1)}, bf16[32,32,256]{2,1,0:T(8,128)(2,1)S(1)}, u32[]{:S(2)}, u32[]{:S(2)}) collective-permute-start(bf16[32,32,256]{2,1,0:T(8,128)(2,1)S(1)} %collective-permute-done.3), channel_id=1, source_target_pairs={{0,1},{1,0},{2,3},{3,2},{4,5},{5,4},{6,7},{7,6},{8,9},{9,8},{10,11... | collective-permute-start | bytes 1572872 | tf_op jit(solution)/shard_map/ppermute | solution.py:23
  200.5 15.0 %collective-permute-start.6 = (bf16[32,32,256]{2,1,0:T(8,128)(2,1)S(1)}, bf16[32,32,256]{2,1,0:T(8,128)(2,1)S(1)}, u32[]{:S(2)}, u32[]{:S(2)}) collective-permute-start(bf16[32,32,256]{2,1,0:T(8,128)(2,1)S(1)} %collective-permute-done.5), channel_id=1, source_target_pairs={{0,1},{1,0},{2,3},{3,2},{4,5},{5,4},{6,7},{7,6},{8,9},{9,8},{10,11... | collective-permute-start | bytes 1572872 | tf_op jit(solution)/shard_map/ppermute | solution.py:23
  202.4 15.3 %collective-permute-start.13 = (bf16[32,32,256]{2,1,0:T(8,128)(2,1)S(1)}, bf16[32,32,256]{2,1,0:T(8,128)(2,1)S(1)}, u32[]{:S(2)}, u32[]{:S(2)}) collective-permute-start(bf16[32,32,256]{2,1,0:T(8,128)(2,1)S(1)} %collective-permute-done.5), channel_id=1, source_target_pairs={{0,2},{1,3},{2,4},{3,5},{4,6},{5,7},{6,0},{7,1},{8,10},{9,11},{10,... | collective-permute-start | bytes 1572872 | tf_op jit(solution)/shard_map/ppermute | solution.py:23
  207.8 22.1 %collective-permute-start.8 = (bf16[32,32,256]{2,1,0:T(8,128)(2,1)S(1)}, bf16[32,32,256]{2,1,0:T(8,128)(2,1)S(1)}, u32[]{:S(2)}, u32[]{:S(2)}) collective-permute-start(bf16[32,32,256]{2,1,0:T(8,128)(2,1)S(1)} %collective-permute-done.7), channel_id=1, source_target_pairs={{0,1},{1,0},{2,3},{3,2},{4,5},{5,4},{6,7},{7,6},{8,9},{9,8},{10,11... | collective-permute-start | bytes 1572872 | tf_op jit(solution)/shard_map/ppermute | solution.py:23
  210.5 16.0 %collective-permute-start.15 = (bf16[32,32,256]{2,1,0:T(8,128)(2,1)S(1)}, bf16[32,32,256]{2,1,0:T(8,128)(2,1)S(1)}, u32[]{:S(2)}, u32[]{:S(2)}) collective-permute-start(bf16[32,32,256]{2,1,0:T(8,128)(2,1)S(1)} %collective-permute-done.11), channel_id=1, source_target_pairs={{0,6},{1,7},{2,0},{3,1},{4,2},{5,3},{6,4},{7,5},{8,14},{9,15},{10,... | collective-permute-start | bytes 1572872 | tf_op jit(solution)/shard_map/ppermute | solution.py:23
  212.6 17.4 %collective-permute-start.10 = (bf16[32,32,256]{2,1,0:T(8,128)(2,1)S(1)}, bf16[32,32,256]{2,1,0:T(8,128)(2,1)S(1)}, u32[]{:S(2)}, u32[]{:S(2)}) collective-permute-start(bf16[32,32,256]{2,1,0:T(8,128)(2,1)S(1)} %collective-permute-done.9), channel_id=1, source_target_pairs={{0,1},{1,0},{2,3},{3,2},{4,5},{5,4},{6,7},{7,6},{8,9},{9,8},{10,11... | collective-permute-start | bytes 1572872 | tf_op jit(solution)/shard_map/ppermute | solution.py:23
  215.5 14.7 %collective-permute-start.12 = (bf16[32,32,256]{2,1,0:T(8,128)(2,1)S(1)}, bf16[32,32,256]{2,1,0:T(8,128)(2,1)S(1)}, u32[]{:S(2)}, u32[]{:S(2)}) collective-permute-start(bf16[32,32,256]{2,1,0:T(8,128)(2,1)S(1)} %collective-permute-done.11), channel_id=1, source_target_pairs={{0,1},{1,0},{2,3},{3,2},{4,5},{5,4},{6,7},{7,6},{8,9},{9,8},{10,11... | collective-permute-start | bytes 1572872 | tf_op jit(solution)/shard_map/ppermute | solution.py:23
  217.7 12.5 %collective-permute-start.14 = (bf16[32,32,256]{2,1,0:T(8,128)(2,1)S(1)}, bf16[32,32,256]{2,1,0:T(8,128)(2,1)S(1)}, u32[]{:S(2)}, u32[]{:S(2)}) collective-permute-start(bf16[32,32,256]{2,1,0:T(8,128)(2,1)S(1)} %collective-permute-done.13), channel_id=1, source_target_pairs={{0,1},{1,0},{2,3},{3,2},{4,5},{5,4},{6,7},{7,6},{8,9},{9,8},{10,11... | collective-permute-start | bytes 1572872 | tf_op jit(solution)/shard_map/ppermute | solution.py:23
  226.5 4.9 %collective-permute-start.16 = (bf16[32,32,256]{2,1,0:T(8,128)(2,1)S(1)}, bf16[32,32,256]{2,1,0:T(8,128)(2,1)S(1)}, u32[]{:S(2)}, u32[]{:S(2)}) collective-permute-start(bf16[32,32,256]{2,1,0:T(8,128)(2,1)S(1)} %collective-permute-done.15), channel_id=1, source_target_pairs={{0,1},{1,0},{2,3},{3,2},{4,5},{5,4},{6,7},{7,6},{8,9},{9,8},{10,11... | collective-permute-start | bytes 1572872 | tf_op jit(solution)/shard_map/ppermute | solution.py:23

commit v3 on v2

--- a/solution.py
+++ b/solution.py
@@ -77,42 +77,33 @@
     )(joined, window, gain)
 
 
-def gather_inputs(own):
+def place_of():
     assert lax.axis_size("inp") == 16
     me = lax.axis_index("inp")
-    zh, xx, core = me // 8, (me // 2) % 4, me % 2
+    return me // 8, (me // 2) % 4, me % 2
 
-    def at(z, x, c):
-        return z * 8 + (x % 4) * 2 + c
 
-    def unpack(p):
-        return p // 8, (p // 2) % 4, p % 2
+def x_step(d):
+    return lambda p: (p // 8) * 8 + ((p // 2 + d) % 4) * 2 + p % 2
 
-    def x_step(d):
-        def f(p):
-            z, x, c = unpack(p)
-            return at(z, x + d, c)
-        return f
 
-    cross = moved(own, lambda p: p ^ 8)
-    from_left = moved((own, cross), x_step(1))
-    from_right = moved((own, cross), x_step(-1))
-    far_own = moved(from_left[0], x_step(1))
-    far_cross = moved(from_right[1], x_step(-1))
-    mine = [
-        (0, 0, own), (1, 0, cross),
-        (0, -1, from_left[0]), (1, -1, from_left[1]),
-        (0, 1, from_right[0]), (1, 1, from_right[1]),
-        (0, 2, far_own), (1, 2, far_cross),
+def column_blocks(pair, zh, xx):
+    chans, width, depth = pair.shape[0], pair.shape[1] // 2, pair.shape[2]
+    from_left = moved(pair, x_step(1))
+    from_right = moved(pair, x_step(-1))
+    far_low = moved(from_left[:, :width], x_step(1))
+    far_high = moved(from_right[:, width:], x_step(-1))
+    pieces = [
+        (0, 0, pair[:, :width]), (1, 0, pair[:, width:]),
+        (0, -1, from_left[:, :width]), (1, -1, from_left[:, width:]),
+        (0, 1, from_right[:, :width]), (1, 1, from_right[:, width:]),
+        (0, 2, far_low), (1, 2, far_high),
     ]
-    other = moved(tuple(b for _, _, b in mine), lambda p: p ^ 1)
-    width = own.shape[1]
-    gathered = jnp.zeros((own.shape[0], 16 * width, own.shape[2]), own.dtype)
-    for (dz, dx, block), far in zip(mine, other):
-        for dc, piece in ((0, block), (1, far)):
-            place = at((zh + dz) % 2, xx + dx + 4, (core + dc) % 2)
-            gathered = lax.dynamic_update_slice(gathered, piece, (0, place * width, 0))
-    return gathered
+    column = jnp.zeros((chans, 8 * width, depth), pair.dtype)
+    for z, dx, piece in pieces:
+        slot = z * 4 + (xx + dx + 4) % 4
+        column = lax.dynamic_update_slice(column, piece, (0, slot * width, 0))
+    return column
 
 
 def shards(voltages, scales):
@@ -120,6 +111,7 @@
     shard_len = voltages.shape[1]
     spec_count = shard_len // NFFT
     history = TAPS - 1
+    zh, xx, core = place_of()
     samples = voltages.reshape(inp_count, spec_count, NFFT).transpose(1, 0, 2).astype(jnp.bfloat16)
     earlier = []
     need = history
@@ -134,15 +126,31 @@
     filtered = polyphase(joined, window_table(), gain, spec_count).reshape(spec_count * inp_count, NFFT)
     spectra = jnp.dot(filtered, dft_table(), preferred_element_type=jnp.float32).astype(jnp.bfloat16)
     spectra = spectra.reshape(spec_count, inp_count, 2, CHANS)
-    local_block = lax.all_to_all(spectra, "chan", split_axis=3, concat_axis=0, tiled=True)
+    crossed = moved(spectra, lambda p: p ^ 8)
+    low_first = zh == 0
+    both = jnp.concatenate(
+        [jnp.where(low_first, spectra, crossed), jnp.where(low_first, crossed, spectra)], axis=1
+    )
+    local_block = lax.all_to_all(both, "chan", split_axis=3, concat_axis=0, tiled=True)
     spec_total = local_block.shape[0]
     chan_count = local_block.shape[3]
-    own_rows = local_block.transpose(3, 1, 2, 0).reshape(chan_count, inp_count, 2 * spec_total)
+    pair = local_block.transpose(3, 1, 2, 0).reshape(chan_count, 2 * inp_count, 2 * spec_total)
+    own_rows = lax.dynamic_slice_in_dim(pair, zh * inp_count, inp_count, axis=1)
     swapped = jnp.concatenate([own_rows[..., spec_total:], -own_rows[..., :spec_total]], axis=-1)
-    piece = gather_inputs(own_rows)
-    real_part = jnp.einsum("cik,cjk->cij", own_rows, piece, preferred_element_type=jnp.float32)
-    imag_part = jnp.einsum("cik,cjk->cij", swapped, piece, preferred_element_type=jnp.float32)
-    result = jnp.stack([real_part, imag_part]) * (1.0 / spec_total)
+    lhs = jnp.stack([own_rows, swapped])
+    mine = column_blocks(pair, zh, xx)
+    theirs = moved(mine, lambda p: p ^ 1)
+
+    def correlate(column):
+        return jnp.einsum("rcik,cjk->rcij", lhs, column, preferred_element_type=jnp.float32)
+
+    part_mine = correlate(mine)
+    part_theirs = correlate(theirs)
+    first = jnp.where(core == 0, part_mine, part_theirs)
+    second = jnp.where(core == 0, part_theirs, part_mine)
+    shape = first.shape[:3] + (8, inp_count)
+    result = jnp.stack([first.reshape(shape), second.reshape(shape)], axis=4)
+    result = result.reshape(first.shape[:3] + (16 * inp_count,)) * (1.0 / spec_total)
     return result.astype(jnp.bfloat16)
 
 

time: 239 us -> 337 us (1.41)
  the two profiles are of different devices: /device:TPU:55 before, /device:TPU:7 now
where the time goes in v3:
time: 337 us; the launch traced here: 336 us
  blocking collectives  113 us (34%)
  local copies, waits for them, and re-layouts  72.5 us (22%)
  waiting for transfers between devices  57.5 us (17%)
  starting transfers between devices  40.3 us (12%)
  other arithmetic  28.8 us (9%)
  matrix products  16.9 us (5%)
  Pallas kernels  6.81 us (2%)
    all_to_all x1, blocking collectives, shards(): lax.all_to_all(both, 'chan', split_axis=3, concat_axis=0, tiled=True)  113 us
    ppermute x6, waiting for transfers between devices, moved(): lax.ppermute(block, 'inp', [(p, mapping(p)) for p in range(lax.axis_size(...  42.3 us
    convert_element_type x2, local copies, waits for them, and re-layouts, shards(): return result.astype(jnp.bfloat16)  34.9 us
    ppermute x6, starting transfers between devices, moved(): lax.ppermute(block, 'inp', [(p, mapping(p)) for p in range(lax.axis_size(...  31 us
    ppermute x2, waiting for transfers between devices, shifted(): return lax.ppermute(block, axis, route)  15.1 us
    another operation x2, local copies, waits for them, and re-layouts, shards(): result = jnp.stack([first.reshape(shape), second.reshape(shape)], axis=4)  10.3 us
    ppermute x2, starting transfers between devices, shifted(): return lax.ppermute(block, axis, route)  9.33 us
    dot_general x2, matrix products, correlate(): jnp.einsum('rcik,cjk->rcij', lhs, column, preferred_element_type=jnp.floa...  8.49 us
  transfers between devices with their start and end apart: 8, of which 6 were waited for; matrix products, arithmetic and copies ran while one was open for 9% of the time, Pallas kernels for 0%

profile of v3, /device:TPU:7, one launch (start us, length us, event | category | flops | bytes accessed | tf_op | source)
XLA Modules:
  0.0 335.7 jit_solution(5357530748694944954)
XLA Ops:
  0.0 1.7 convert_element_type.57
  1.7 0.1 copy.30
  1.8 4.5 %collective-permute-start.1 = (bf16[4,32,4096]{2,1,0:T(8,128)(2,1)S(1)}, bf16[4,32,4096]{2,1,0:T(8,128)(2,1)}, u32[]{:S(2)}, u32[]{:S(2)}) collective-permute-start(bf16[4,32,4096]{2,1,0:T(8,128)(2,1)S(1)} %bitcast.56), channel_id=1, source_target_pairs={{0,16},{16,32},{32,48},{48,64},{64,80},{80,96},{96,112},{112,128},... | collective-permute-start | bytes 3145736 | tf_op jit(solution)/shard_map/ppermute | solution.py:19
  6.3 0.9 slice.38
  7.2 4.8 %collective-permute-start = (bf16[3,32,4096]{2,1,0:T(8,128)(2,1)}, bf16[3,32,4096]{2,1,0:T(8,128)(2,1)}, u32[]{:S(2)}, u32[]{:S(2)}) collective-permute-start(bf16[3,32,4096]{2,1,0:T(8,128)(2,1)} %slice.38), channel_id=1, source_target_pairs={{0,32},{16,48},{32,64},{48,80},{64,96},{80,112},{96,128},{112,144}... | collective-permute-start | bytes 2359304 | tf_op jit(solution)/shard_map/ppermute | solution.py:19
  12.1 1.0 sine_negate_fusion
  13.1 1.1 fusion.27
  14.2 4.8 %multiply_subtract_fusion = (f32[64,64,1024]{2,1,0:T(8,128)S(1)}, f32[64,64,1024]{2,1,0:T(8,128)S(1)}) fusion(f32[64,1024]{1,0:T(8,128)S(1)} %get-tuple-element.21, f32[64,1024]{1,0:T(8,128)S(1)} %get-tuple-element.20, f32[64,1024]{1,0:T(8,128)S(1)} %get-tuple-element.22, f32[64,1024]{1,0:T(8,128)S(1)} %get-tuple-element.19), kind=kLoop, calls=%fused_computation.5 | loop fusion | flops 25165824 | bytes 34603008 | tf_op jit(solution)/shard_map/sub | solution.py:49
  19.0 0.0 copy-start
  19.0 8.0 %fusion = bf16[4096,2048]{1,0:T(8,128)(2,1)} fusion(f32[4096,1024]{1,0:T(8,128)S(1)} %bitcast.51, f32[4096,1024]{1,0:T(8,128)S(1)} %bitcast.50), kind=kLoop, calls=%fused_computation.1 | loop fusion | flops 25165824 | bytes 50331648 | tf_op jit(solution)/shard_map/convert_element_type | solution.py:52
  27.0 0.0 copy-done
  27.0 0.7 copy.15.g_ref
  27.7 1.3 fusion.22.w_ref
  29.0 15.1 %collective-permute-done = bf16[3,32,4096]{2,1,0:T(8,128)(2,1)} collective-permute-done((bf16[3,32,4096]{2,1,0:T(8,128)(2,1)}, bf16[3,32,4096]{2,1,0:T(8,128)(2,1)}, u32[]{:S(2)}, u32[]{:S(2)}) %collective-permute-start) | collective-permute-done | bytes 786464 | tf_op jit(solution)/shard_map/ppermute | solution.py:19
  44.1 0.0 collective-permute-done.1
  44.1 3.3 pad_maximum_fusion.x_ref
  47.5 6.8 %shard_map.28 = bf16[4,32,4096]{2,1,0:T(8,128)(2,1)} custom-call(bf16[11,32,4096]{2,1,0:T(8,128)(2,1)} %pad_maximum_fusion.x_ref, f32[8,4096]{1,0:T(8,128)} %fusion.22.w_ref, f32[32,1]{1,0:T(8,128)} %copy.15.g_ref), custom_call_target="tpu_custom_call" | custom-call | tf_op jit(solution)/shard_map/pallas_call | solution.py:67
  54.3 8.4 %convolution_convert_fusion = bf16[128,2048]{1,0:T(8,128)(2,1)S(1)} fusion(bf16[128,4096]{1,0:T(8,128)(2,1)} %bitcast.59, bf16[4096,2048]{1,0:T(8,128)(2,1)} %fusion), kind=kOutput, calls=%fused_computation.11 | convolution fusion | flops 2147745792 | bytes 18350080 | tf_op jit(solution)/shard_map/dot_general | solution.py:127
  62.7 0.4 reshape.122
  63.1 0.1 copy.17
  63.2 14.5 %collective-permute-start.2 = (bf16[4,32,2,1024]{3,1,2,0:T(8,128)(2,1)S(1)}, bf16[4,32,2,1024]{3,1,2,0:T(8,128)(2,1)S(1)}, u32[]{:S(2)}, u32[]{:S(2)}) collective-permute-start(bf16[4,32,2,1024]{3,1,2,0:T(8,128)(2,1)S(1)} %copy.17), channel_id=1, source_target_pairs={{0,8},{1,9},{2,10},{3,11},{4,12},{5,13},{6,14},{7,15},{8,0},{9,1},... | collective-permute-start | bytes 1572872 | tf_op jit(solution)/shard_map/ppermute | solution.py:23
  77.8 10.7 %collective-permute-done.2 = bf16[4,32,2,1024]{3,1,2,0:T(8,128)(2,1)S(1)} collective-permute-done((bf16[4,32,2,1024]{3,1,2,0:T(8,128)(2,1)S(1)}, bf16[4,32,2,1024]{3,1,2,0:T(8,128)(2,1)S(1)}, u32[]{:S(2)}, u32[]{:S(2)}) %collective-permute-start.2) | collective-permute-done | bytes 524320 | tf_op jit(solution)/shard_map/ppermute | solution.py:23
  88.5 0.1 broadcast_select_fusion.1
  88.6 0.1 pad_maximum_fusion.1
  88.7 1.7 copy.19
  90.4 1.5 reshape.126
  91.9 112.5 %all_to_all.18 = bf16[32,2,8192]{2,1,0:T(2,128)(2,1)} all-to-all(bf16[32,2,8192]{2,1,0:T(2,128)(2,1)S(1)} %reshape.126), channel_id=1, replica_groups=mesh['chan'=32,'inp'=16] {'chan'}, dimensions={0} | all-to-all | bytes 2097152 | tf_op jit(solution)/shard_map/all_to_all | solution.py:134
  204.4 5.0 %reshape.127 = bf16[1024,4,2,64]{3,2,1,0:T(2,128)(2,1)S(1)} reshape(bf16[32,2,8192]{2,1,0:T(2,128)(2,1)} %all_to_all.18) | data formatting | bytes 2097152
  209.4 0.3 copy.20
  209.7 0.7 copy.21
  210.4 2.2 copy.22
  212.6 0.7 reshape.123
  213.3 2.0 collective-permute-start.3
  215.3 3.3 collective-permute-start.4
  218.7 2.4 broadcast_in_dim.44
  221.1 0.9 slice_dynamic-update-slice_fusion.3
  222.0 0.9 dynamic-slice_bitcast_fusion
  223.0 15.1 %collective-permute-done.3 = bf16[32,64,256]{2,1,0:T(8,128)(2,1)} collective-permute-done((bf16[32,64,256]{2,1,0:T(8,128)(2,1)S(1)}, bf16[32,64,256]{2,1,0:T(8,128)(2,1)}, u32[]{:S(2)}, u32[]{:S(2)}) %collective-permute-start.3) | collective-permute-done | bytes 1048608 | tf_op jit(solution)/shard_map/ppermute | solution.py:23
  238.1 2.0 fusion.36
  240.1 3.2 collective-permute-start.5
  243.3 1.9 slice_dynamic-update-slice_fusion.1
  245.2 0.0 collective-permute-done.4
  245.2 0.9 slice_dynamic-update-slice_fusion
  246.1 1.1 fusion.35
  247.3 2.1 collective-permute-start.6
  249.4 3.4 collective-permute-done.5
  252.7 1.9 constant_dynamic-update-slice_fusion.1
  254.6 6.3 %collective-permute-done.6 = bf16[32,32,256]{2,1,0:T(8,128)(2,1)S(1)} collective-permute-done((bf16[32,32,256]{2,1,0:T(8,128)(2,1)}, bf16[32,32,256]{2,1,0:T(8,128)(2,1)S(1)}, u32[]{:S(2)}, u32[]{:S(2)}) %collective-permute-start.6) | collective-permute-done | bytes 524320 | tf_op jit(solution)/shard_map/ppermute | solution.py:23
  260.9 0.9 constant_dynamic-update-slice_fusion
  261.8 5.9 %collective-permute-start.7 = (bf16[32,256,256]{2,1,0:T(8,128)(2,1)}, bf16[32,256,256]{2,1,0:T(8,128)(2,1)}, u32[]{:S(2)}, u32[]{:S(2)}) collective-permute-start(bf16[32,256,256]{2,1,0:T(8,128)(2,1)} %constant_dynamic-update-slice_fusion), channel_id=1, source_target_pairs={{0,1},{1,0},{2,3},{3,2},{4,5},{5,4},{6,7},{7,6},{8,9},{9,8},{10,11... | collective-permute-start | bytes 12582920 | tf_op jit(solution)/shard_map/ppermute | solution.py:23
  267.7 0.1 constant_dynamic-slice_fusion
  267.8 0.1 maximum_bitcast_fusion
  267.9 6.9 %collective-permute-done.7 = bf16[32,256,256]{2,1,0:T(8,128)(2,1)} collective-permute-done((bf16[32,256,256]{2,1,0:T(8,128)(2,1)}, bf16[32,256,256]{2,1,0:T(8,128)(2,1)}, u32[]{:S(2)}, u32[]{:S(2)}) %collective-permute-start.7) | collective-permute-done | bytes 4194336 | tf_op jit(solution)/shard_map/ppermute | solution.py:23
  274.8 3.6 %fusion.2 = f32[32,256,2,32]{1,3,2,0:T(8,128)S(1)} fusion(bf16[32,256,256]{2,1,0:T(8,128)(2,1)} %collective-permute-done.7, bf16[1,32,32,256]{3,2,0,1:T(8,128)(2,1)S(1)} %maximum_bitcast_fusion, bf16[1,32,32,256]{3,2,0,1:T(8,128)(2,1)S(1)} %get-tuple-element.7), kind=kOutput, calls=%fused_computation.6 | convolution fusion | flops 270532608 | bytes 7340032 | tf_op jit(solution)/shard_map/rcik,cjk->rcij/dot_general | solution.py:145
  278.3 4.9 %select_bitcast_fusion.1 = (f32[2,32,32,256]{3,2,0,1:T(8,128)}, f32[2,32,32,256]{3,2,0,1:T(8,128)S(1)}) fusion(f32[32,256,2,32]{1,3,2,0:T(8,128)S(1)} %fusion.2, pred[]{:T(512)S(6)} %eq.40, bf16[1,32,32,256]{3,2,0,1:T(8,128)(2,1)S(1)} %maximum_bitcast_fusion, bf16[1,32,32,256]{3,2,0,1:T(8,128)(2,1)S(1)} %get-tuple-element.7, ...), kind=kOutput, calls=%fused_computation.13 | convolution fusion | flops 271581184 | bytes 11534337 | tf_op jit(solution)/shard_map/rcik,cjk->rcij/dot_general | solution.py:145
  283.3 6.0 %stack_reshape.6 = f32[2,32,32,8,1,32]{5,3,2,0,1,4:T(8,128)} reshape(f32[2,32,32,256]{3,2,0,1:T(8,128)} %get-tuple-element.5) | data formatting | bytes 4194304 | tf_op jit(solution)/shard_map/stack;reshape | solution.py:152
  289.3 4.3 %stack_reshape.7 = f32[2,32,32,8,1,32]{5,3,2,0,1,4:T(8,128)} reshape(f32[2,32,32,256]{3,2,0,1:T(8,128)S(1)} %get-tuple-element.6) | data formatting | bytes 4194304 | tf_op jit(solution)/shard_map/stack;reshape | solution.py:152
  293.6 7.2 %fusion.1 = bf16[2,32,32,8,2,32]{5,3,2,0,1,4:T(8,128)(2,1)S(1)} fusion(f32[2,32,32,8,1,32]{5,3,2,0,1,4:T(8,128)} %stack_reshape.7, f32[2,32,32,8,1,32]{5,3,2,0,1,4:T(8,128)} %stack_reshape.6), kind=kLoop, calls=%fused_computation.3 | loop fusion | flops 3145728 | bytes 6291456 | tf_op jit(solution)/shard_map/convert_element_type | solution.py:154
  300.7 13.3 %copy.23 = bf16[2,32,32,8,2,32]{5,4,3,2,1,0:T(2,128)(2,1)} copy(bf16[2,32,32,8,2,32]{5,3,2,0,1,4:T(8,128)(2,1)S(1)} %fusion.1) | data formatting | bytes 4194304 | tf_op jit(solution)/shard_map/convert_element_type | solution.py:154
  314.0 21.7 %convert_element_type.67 = bf16[2,32,32,512]{3,2,1,0:T(8,128)(2,1)} reshape(bf16[2,32,32,8,2,32]{5,4,3,2,1,0:T(2,128)(2,1)} %copy.23) | data formatting | bytes 4194304 | tf_op jit(solution)/shard_map/convert_element_type | solution.py:154
  (2 shorter events, 0.0 us)
Async XLA Ops:
  1.8 42.4 %collective-permute-start.1 = (bf16[4,32,4096]{2,1,0:T(8,128)(2,1)S(1)}, bf16[4,32,4096]{2,1,0:T(8,128)(2,1)}, u32[]{:S(2)}, u32[]{:S(2)}) collective-permute-start(bf16[4,32,4096]{2,1,0:T(8,128)(2,1)S(1)} %bitcast.56), channel_id=1, source_target_pairs={{0,16},{16,32},{32,48},{48,64},{64,80},{80,96},{96,112},{112,128},... | collective-permute-start | bytes 3145736 | tf_op jit(solution)/shard_map/ppermute | solution.py:19
  7.2 36.9 %collective-permute-start = (bf16[3,32,4096]{2,1,0:T(8,128)(2,1)}, bf16[3,32,4096]{2,1,0:T(8,128)(2,1)}, u32[]{:S(2)}, u32[]{:S(2)}) collective-permute-start(bf16[3,32,4096]{2,1,0:T(8,128)(2,1)} %slice.38), channel_id=1, source_target_pairs={{0,32},{16,48},{32,64},{48,80},{64,96},{80,112},{96,128},{112,144}... | collective-permute-start | bytes 2359304 | tf_op jit(solution)/shard_map/ppermute | solution.py:19
  19.0 8.0 %copy-start = (s32[32]{0:T(128)S(1)}, s32[32]{0:T(128)}, u32[]{:S(2)}) copy-start(s32[32]{0:T(128)} %param.3) | copy-start | bytes 388
  63.2 25.2 %collective-permute-start.2 = (bf16[4,32,2,1024]{3,1,2,0:T(8,128)(2,1)S(1)}, bf16[4,32,2,1024]{3,1,2,0:T(8,128)(2,1)S(1)}, u32[]{:S(2)}, u32[]{:S(2)}) collective-permute-start(bf16[4,32,2,1024]{3,1,2,0:T(8,128)(2,1)S(1)} %copy.17), channel_id=1, source_target_pairs={{0,8},{1,9},{2,10},{3,11},{4,12},{5,13},{6,14},{7,15},{8,0},{9,1},... | collective-permute-start | bytes 1572872 | tf_op jit(solution)/shard_map/ppermute | solution.py:23
  213.3 24.8 %collective-permute-start.3 = (bf16[32,64,256]{2,1,0:T(8,128)(2,1)S(1)}, bf16[32,64,256]{2,1,0:T(8,128)(2,1)}, u32[]{:S(2)}, u32[]{:S(2)}) collective-permute-start(bf16[32,64,256]{2,1,0:T(8,128)(2,1)S(1)} %reshape.123), channel_id=1, source_target_pairs={{0,2},{1,3},{2,4},{3,5},{4,6},{5,7},{6,0},{7,1},{8,10},{9,11},{10,... | collective-permute-start | bytes 3145736 | tf_op jit(solution)/shard_map/ppermute | solution.py:23
  215.3 30.0 %collective-permute-start.4 = (bf16[32,64,256]{2,1,0:T(8,128)(2,1)S(1)}, bf16[32,64,256]{2,1,0:T(8,128)(2,1)S(1)}, u32[]{:S(2)}, u32[]{:S(2)}) collective-permute-start(bf16[32,64,256]{2,1,0:T(8,128)(2,1)S(1)} %reshape.123), channel_id=1, source_target_pairs={{0,6},{1,7},{2,0},{3,1},{4,2},{5,3},{6,4},{7,5},{8,14},{9,15},{10,... | collective-permute-start | bytes 3145736 | tf_op jit(solution)/shard_map/ppermute | solution.py:23
  240.1 12.6 %collective-permute-start.5 = (bf16[32,32,256]{2,1,0:T(8,128)(2,1)S(1)}, bf16[32,32,256]{2,1,0:T(8,128)(2,1)}, u32[]{:S(2)}, u32[]{:S(2)}) collective-permute-start(bf16[32,32,256]{2,1,0:T(8,128)(2,1)S(1)} %get-tuple-element.13), channel_id=1, source_target_pairs={{0,2},{1,3},{2,4},{3,5},{4,6},{5,7},{6,0},{7,1},{8,10},{9,11},{10,... | collective-permute-start | bytes 1572872 | tf_op jit(solution)/shard_map/ppermute | solution.py:23
  247.3 13.7 %collective-permute-start.6 = (bf16[32,32,256]{2,1,0:T(8,128)(2,1)}, bf16[32,32,256]{2,1,0:T(8,128)(2,1)S(1)}, u32[]{:S(2)}, u32[]{:S(2)}) collective-permute-start(bf16[32,32,256]{2,1,0:T(8,128)(2,1)} %get-tuple-element.11), channel_id=1, source_target_pairs={{0,6},{1,7},{2,0},{3,1},{4,2},{5,3},{6,4},{7,5},{8,14},{9,15},{10,... | collective-permute-start | bytes 1572872 | tf_op jit(solution)/shard_map/ppermute | solution.py:23
  261.8 13.0 %collective-permute-start.7 = (bf16[32,256,256]{2,1,0:T(8,128)(2,1)}, bf16[32,256,256]{2,1,0:T(8,128)(2,1)}, u32[]{:S(2)}, u32[]{:S(2)}) collective-permute-start(bf16[32,256,256]{2,1,0:T(8,128)(2,1)} %constant_dynamic-update-slice_fusion), channel_id=1, source_target_pairs={{0,1},{1,0},{2,3},{3,2},{4,5},{5,4},{6,7},{7,6},{8,9},{9,8},{10,11... | collective-permute-start | bytes 12582920 | tf_op jit(solution)/shard_map/ppermute | solution.py:23

commit v4 on v2

--- a/solution.py
+++ b/solution.py
@@ -5,12 +5,16 @@
 import jax.numpy as jnp
 from jax import lax
 from jax.experimental import pallas as pl
-from jax.sharding import PartitionSpec as P
+from jax.sharding import Mesh, NamedSharding, PartitionSpec as P
 
 NFFT = 4096
 CHANS = 1024
 TAPS = 8
 ROOT = 64
+
+
+TIME = ("y", "zl")
+INPUT = ("zh", "x", "core")
 
 
 def shifted(block, axis, distance):
@@ -20,7 +24,7 @@
 
 
 def moved(block, mapping):
-    return lax.ppermute(block, "inp", [(p, mapping(p)) for p in range(lax.axis_size("inp"))])
+    return lax.ppermute(block, INPUT, [(p, mapping(p)) for p in range(lax.axis_size(INPUT))])
 
 
 def window_table():
@@ -78,8 +82,8 @@
 
 
 def gather_inputs(own):
-    assert lax.axis_size("inp") == 16
-    me = lax.axis_index("inp")
+    assert lax.axis_size(INPUT) == 16
+    me = lax.axis_index(INPUT)
     zh, xx, core = me // 8, (me // 2) % 4, me % 2
 
     def at(z, x, c):
@@ -126,17 +130,20 @@
     distance = 1
     while need > 0:
         take = min(spec_count, need)
-        earlier = [shifted(samples[spec_count - take :], "chan", distance)] + earlier
+        earlier = [shifted(samples[spec_count - take :], TIME, distance)] + earlier
         need -= take
         distance += 1
     joined = jnp.concatenate(earlier + [samples], axis=0)
     gain = (scales.astype(jnp.float32) * (1.0 / 256.0)).reshape(inp_count, 1)
     filtered = polyphase(joined, window_table(), gain, spec_count).reshape(spec_count * inp_count, NFFT)
     spectra = jnp.dot(filtered, dft_table(), preferred_element_type=jnp.float32).astype(jnp.bfloat16)
-    spectra = spectra.reshape(spec_count, inp_count, 2, CHANS)
-    local_block = lax.all_to_all(spectra, "chan", split_axis=3, concat_axis=0, tiled=True)
-    spec_total = local_block.shape[0]
-    chan_count = local_block.shape[3]
+    rows_y, rows_z = lax.axis_size("y"), lax.axis_size("zl")
+    spectra = spectra.reshape(spec_count, inp_count, 2, rows_y, rows_z, CHANS // (rows_y * rows_z))
+    step_z = lax.all_to_all(spectra, "zl", split_axis=4, concat_axis=0, tiled=True)
+    step_y = lax.all_to_all(step_z, "y", split_axis=3, concat_axis=0, tiled=True)
+    spec_total = step_y.shape[0]
+    chan_count = step_y.shape[5]
+    local_block = step_y.reshape(spec_total, inp_count, 2, chan_count)
     own_rows = local_block.transpose(3, 1, 2, 0).reshape(chan_count, inp_count, 2 * spec_total)
     swapped = jnp.concatenate([own_rows[..., spec_total:], -own_rows[..., :spec_total]], axis=-1)
     piece = gather_inputs(own_rows)
@@ -147,7 +154,14 @@
 
 
 def solution(mesh):
-    placed = (P("inp", "chan"), P("inp"))
-    return jax.shard_map(
-        shards, mesh=mesh, in_specs=placed, out_specs=P(None, "chan", "inp", None), check_vma=False
+    fine = Mesh(mesh.devices.reshape(4, 8, 2, 4, 2), TIME + INPUT)
+    placed = (P(INPUT, TIME), P(INPUT))
+    inner = jax.shard_map(
+        shards, mesh=fine, in_specs=placed, out_specs=P(None, TIME, INPUT, None), check_vma=False
     )
+    target = NamedSharding(mesh, P(None, "chan", "inp", None))
+
+    def run(voltages, scales):
+        return jax.lax.with_sharding_constraint(inner(voltages, scales), target)
+
+    return run

time: 239 us -> 255 us (1.067)
  the two profiles are of different devices: /device:TPU:55 before, /device:TPU:7 now
where the time goes in v4:
time: 255 us; the launch traced here: 252 us
  starting transfers between devices  95.4 us (37%)
  blocking collectives  66.7 us (26%)
  other arithmetic  23.3 us (9%)
  local copies, waits for them, and re-layouts  23 us (9%)
  waiting for transfers between devices  23 us (9%)
  matrix products  13.5 us (5%)
  Pallas kernels  6.81 us (3%)
    ppermute x15, starting transfers between devices, moved(): lax.ppermute(block, INPUT, [(p, mapping(p)) for p in range(lax.axis_size(...  86.1 us
    all_to_all x1, blocking collectives, shards(): lax.all_to_all(spectra, 'zl', split_axis=4, concat_axis=0, tiled=True)  51.7 us
    ppermute x2, waiting for transfers between devices, shifted(): return lax.ppermute(block, axis, route)  15.1 us
    all_to_all x1, blocking collectives, shards(): lax.all_to_all(step_z, 'y', split_axis=3, concat_axis=0, tiled=True)  15 us
    unnamed x6, local copies, waits for them, and re-layouts  9.65 us
    ppermute x2, starting transfers between devices, shifted(): return lax.ppermute(block, axis, route)  9.34 us
    dot_general x1, matrix products, shards(): jnp.dot(filtered, dft_table(), preferred_element_type=jnp.float32)  8.44 us
    convert_element_type x1, other arithmetic, dft_table(): return lax.optimization_barrier(both.astype(jnp.bfloat16))  8.04 us
  transfers between devices with their start and end apart: 17, of which 4 were waited for; matrix products, arithmetic and copies ran while one was open for 8% of the time, Pallas kernels for 0%

profile of v4, /device:TPU:7, one launch (start us, length us, event | category | flops | bytes accessed | tf_op | source)
XLA Modules:
  0.0 252.4 jit_solution(17405235306518312482)
XLA Ops:
  0.0 1.7 convert_element_type.54
  1.7 0.1 copy.24
  1.8 4.5 %collective-permute-start.1 = (bf16[4,32,4096]{2,1,0:T(8,128)(2,1)S(1)}, bf16[4,32,4096]{2,1,0:T(8,128)(2,1)}, u32[]{:S(2)}, u32[]{:S(2)}) collective-permute-start(bf16[4,32,4096]{2,1,0:T(8,128)(2,1)S(1)} %bitcast.48), channel_id=1, source_target_pairs={{0,16},{16,32},{32,48},{48,64},{64,80},{80,96},{96,112},{112,128},... | collective-permute-start | bytes 3145736 | tf_op jit(solution)/shard_map/ppermute | solution.py:23
  6.3 0.9 slice.12
  7.2 4.8 %collective-permute-start = (bf16[3,32,4096]{2,1,0:T(8,128)(2,1)}, bf16[3,32,4096]{2,1,0:T(8,128)(2,1)}, u32[]{:S(2)}, u32[]{:S(2)}) collective-permute-start(bf16[3,32,4096]{2,1,0:T(8,128)(2,1)} %slice.12), channel_id=1, source_target_pairs={{0,32},{16,48},{32,64},{48,80},{64,96},{80,112},{96,128},{112,144}... | collective-permute-start | bytes 2359304 | tf_op jit(solution)/shard_map/ppermute | solution.py:23
  12.1 1.0 sine_negate_fusion
  13.1 1.1 fusion.26
  14.2 4.8 %multiply_subtract_fusion = (f32[64,64,1024]{2,1,0:T(8,128)S(1)}, f32[64,64,1024]{2,1,0:T(8,128)S(1)}) fusion(f32[64,1024]{1,0:T(8,128)S(1)} %get-tuple-element.11, f32[64,1024]{1,0:T(8,128)S(1)} %get-tuple-element.10, f32[64,1024]{1,0:T(8,128)S(1)} %get-tuple-element.12, f32[64,1024]{1,0:T(8,128)S(1)} %get-tuple-element.9), kind=kLoop, calls=%fused_computation.3 | loop fusion | flops 25165824 | bytes 34603008 | tf_op jit(solution)/shard_map/sub | solution.py:53
  19.0 0.0 copy-start
  19.0 8.0 %fusion = bf16[4096,2048]{1,0:T(8,128)(2,1)} fusion(f32[4096,1024]{1,0:T(8,128)S(1)} %bitcast.43, f32[4096,1024]{1,0:T(8,128)S(1)} %bitcast.42), kind=kLoop, calls=%fused_computation.1 | loop fusion | flops 25165824 | bytes 50331648 | tf_op jit(solution)/shard_map/convert_element_type | solution.py:56
  27.1 0.7 copy.13.g_ref
  27.8 1.3 fusion.21.w_ref
  29.0 15.1 %collective-permute-done = bf16[3,32,4096]{2,1,0:T(8,128)(2,1)} collective-permute-done((bf16[3,32,4096]{2,1,0:T(8,128)(2,1)}, bf16[3,32,4096]{2,1,0:T(8,128)(2,1)}, u32[]{:S(2)}, u32[]{:S(2)}) %collective-permute-start) | collective-permute-done | bytes 786464 | tf_op jit(solution)/shard_map/ppermute | solution.py:23
  44.1 0.0 collective-permute-done.1
  44.1 3.3 %pad_maximum_fusion.x_ref = bf16[11,32,4096]{2,1,0:T(8,128)(2,1)} fusion(bf16[4,32,4096]{2,1,0:T(8,128)(2,1)S(1)} %bitcast.50, bf16[4,32,4096]{2,1,0:T(8,128)(2,1)} %collective-permute-done.1, bf16[3,32,4096]{2,1,0:T(8,128)(2,1)} %collective-permute-done), kind=kLoop, calls=%fused_computation.6 | loop fusion | flops 2883584 | bytes 5767168 | tf_op jit(solution)/shard_map/concatenate | solution.py:136
  47.5 6.8 %shard_map.28 = bf16[4,32,4096]{2,1,0:T(8,128)(2,1)} custom-call(bf16[11,32,4096]{2,1,0:T(8,128)(2,1)} %pad_maximum_fusion.x_ref, f32[8,4096]{1,0:T(8,128)} %fusion.21.w_ref, f32[32,1]{1,0:T(8,128)} %copy.13.g_ref), custom_call_target="tpu_custom_call" | custom-call | tf_op jit(solution)/shard_map/pallas_call | solution.py:71
  54.3 8.4 %convolution_convert_fusion = bf16[128,2048]{1,0:T(8,128)(2,1)S(1)} fusion(bf16[128,4096]{1,0:T(8,128)(2,1)} %bitcast.51, bf16[4096,2048]{1,0:T(8,128)(2,1)} %fusion), kind=kOutput, calls=%fused_computation.7 | convolution fusion | flops 2147745792 | bytes 18350080 | tf_op jit(solution)/shard_map/dot_general | solution.py:139
  62.7 1.6 reshape.122
  64.4 2.7 %copy.26 = bf16[4,32,2,4,8,32]{5,1,3,2,0,4:T(8,128)(2,1)} copy(bf16[4,32,2,4,8,32]{5,4,3,2,1,0:T(8,128)(2,1)S(1)} %reshape.122) | data formatting | bytes 1048576 | tf_op jit(solution)/shard_map/reshape | solution.py:141
  67.1 3.8 %reshape.125 = bf16[8,2,16384]{2,1,0:T(2,128)(2,1)S(1)} reshape(bf16[8,4,2,4,32,32]{5,4,3,2,1,0:T(8,128)(2,1)} %bitcast.45) | data formatting | bytes 1048576
  70.9 51.7 %all_to_all.33 = bf16[8,2,16384]{2,1,0:T(2,128)(2,1)S(1)} all-to-all(bf16[8,2,16384]{2,1,0:T(2,128)(2,1)S(1)} %reshape.125), channel_id=1, replica_groups=mesh['y'=4,'zl'=8,'zh'=2,'x'=4,'core'=2] {'zl'}, dimensions={0} | all-to-all | bytes 1048576 | tf_op jit(solution)/shard_map/all_to_all | solution.py:142
  122.5 1.0 reshape.126
  123.6 2.0 copy.25
  125.5 3.7 %reshape.127 = bf16[4,2,32768]{2,1,0:T(2,128)(2,1)S(1)} reshape(bf16[4,32,2,1,32,32]{5,4,3,2,1,0:T(8,128)(2,1)} %bitcast.47) | data formatting | bytes 1048576
  129.3 15.0 %all_to_all.34 = bf16[4,2,32768]{2,1,0:T(2,128)(2,1)S(1)} all-to-all(bf16[4,2,32768]{2,1,0:T(2,128)(2,1)S(1)} %reshape.127), channel_id=1, replica_groups=mesh['y'=4,'zl'=8,'zh'=2,'x'=4,'core'=2] {'y'}, dimensions={0} | all-to-all | bytes 1048576 | tf_op jit(solution)/shard_map/all_to_all | solution.py:143
  144.3 1.1 reshape.128
  145.4 2.3 copy.17
  147.7 0.3 reshape.124
  148.1 13.4 %collective-permute-start.3 = (bf16[32,32,256]{2,1,0:T(8,128)(2,1)S(1)}, bf16[32,32,256]{2,1,0:T(8,128)(2,1)S(1)}, u32[]{:S(2)}, u32[]{:S(2)}) collective-permute-start(bf16[32,32,256]{2,1,0:T(8,128)(2,1)S(1)} %reshape.124), channel_id=1, source_target_pairs={{0,8},{1,9},{2,10},{3,11},{4,12},{5,13},{6,14},{7,15},{8,0},{9,1},... | collective-permute-start | bytes 1572872 | tf_op jit(solution)/shard_map/ppermute | solution.py:27
  161.5 7.9 %collective-permute-start.2 = (bf16[32,32,256]{2,1,0:T(8,128)(2,1)S(1)}, bf16[32,32,256]{2,1,0:T(8,128)(2,1)}, u32[]{:S(2)}, u32[]{:S(2)}) collective-permute-start(bf16[32,32,256]{2,1,0:T(8,128)(2,1)S(1)} %reshape.124), channel_id=1, source_target_pairs={{0,1},{1,0},{2,3},{3,2},{4,5},{5,4},{6,7},{7,6},{8,9},{9,8},{10,11... | collective-permute-start | bytes 1572872 | tf_op jit(solution)/shard_map/ppermute | solution.py:27
  169.4 2.1 collective-permute-start.5
  171.5 3.2 %collective-permute-start.9 = (bf16[32,32,256]{2,1,0:T(8,128)(2,1)S(1)}, bf16[32,32,256]{2,1,0:T(8,128)(2,1)S(1)}, u32[]{:S(2)}, u32[]{:S(2)}) collective-permute-start(bf16[32,32,256]{2,1,0:T(8,128)(2,1)S(1)} %reshape.124), channel_id=1, source_target_pairs={{0,6},{1,7},{2,0},{3,1},{4,2},{5,3},{6,4},{7,5},{8,14},{9,15},{10,... | collective-permute-start | bytes 1572872 | tf_op jit(solution)/shard_map/ppermute | solution.py:27
  174.7 3.3 %collective-permute-start.7 = (bf16[32,32,256]{2,1,0:T(8,128)(2,1)S(1)}, bf16[32,32,256]{2,1,0:T(8,128)(2,1)S(1)}, u32[]{:S(2)}, u32[]{:S(2)}) collective-permute-start(bf16[32,32,256]{2,1,0:T(8,128)(2,1)S(1)} %collective-permute-done.3), channel_id=1, source_target_pairs={{0,2},{1,3},{2,4},{3,5},{4,6},{5,7},{6,0},{7,1},{8,10},{9,11},{10,... | collective-permute-start | bytes 1572872 | tf_op jit(solution)/shard_map/ppermute | solution.py:27
  178.0 2.0 collective-permute-start.11
  180.2 34.1 %collective-permute-start.4 = (bf16[32,32,256]{2,1,0:T(8,128)(2,1)S(1)}, bf16[32,32,256]{2,1,0:T(8,128)(2,1)S(1)}, u32[]{:S(2)}, u32[]{:S(2)}) collective-permute-start(bf16[32,32,256]{2,1,0:T(8,128)(2,1)S(1)} %collective-permute-done.3), channel_id=1, source_target_pairs={{0,1},{1,0},{2,3},{3,2},{4,5},{5,4},{6,7},{7,6},{8,9},{9,8},{10,11... | collective-permute-start | bytes 1572872 | tf_op jit(solution)/shard_map/ppermute | solution.py:27
  214.3 0.1 fusion.33
  214.4 0.0 collective-permute-done.5
  214.4 1.9 collective-permute-start.6
  216.3 3.3 %collective-permute-start.13 = (bf16[32,32,256]{2,1,0:T(8,128)(2,1)S(1)}, bf16[32,32,256]{2,1,0:T(8,128)(2,1)S(1)}, u32[]{:S(2)}, u32[]{:S(2)}) collective-permute-start(bf16[32,32,256]{2,1,0:T(8,128)(2,1)S(1)} %collective-permute-done.5), channel_id=1, source_target_pairs={{0,2},{1,3},{2,4},{3,5},{4,6},{5,7},{6,0},{7,1},{8,10},{9,11},{10,... | collective-permute-start | bytes 1572872 | tf_op jit(solution)/shard_map/ppermute | solution.py:27
  219.7 0.9 broadcast_in_dim.48
  220.7 1.1 constant_dynamic-update-slice_fusion.14
  221.7 0.0 collective-permute-done.7
  221.8 2.7 %collective-permute-start.8 = (bf16[32,32,256]{2,1,0:T(8,128)(2,1)S(1)}, bf16[32,32,256]{2,1,0:T(8,128)(2,1)S(1)}, u32[]{:S(2)}, u32[]{:S(2)}) collective-permute-start(bf16[32,32,256]{2,1,0:T(8,128)(2,1)S(1)} %collective-permute-done.7), channel_id=1, source_target_pairs={{0,1},{1,0},{2,3},{3,2},{4,5},{5,4},{6,7},{7,6},{8,9},{9,8},{10,11... | collective-permute-start | bytes 1572872 | tf_op jit(solution)/shard_map/ppermute | solution.py:27
  224.4 0.0 collective-permute-done.11
  224.5 2.0 collective-permute-start.15
  226.5 2.2 collective-permute-start.10
  228.7 0.1 constant_dynamic-update-slice_fusion.12
  228.8 0.0 collective-permute-done.6
  228.8 2.1 collective-permute-start.12
  231.0 0.3 collective-permute-done.13
  231.2 3.2 %collective-permute-start.14 = (bf16[32,32,256]{2,1,0:T(8,128)(2,1)S(1)}, bf16[32,32,256]{2,1,0:T(8,128)(2,1)S(1)}, u32[]{:S(2)}, u32[]{:S(2)}) collective-permute-start(bf16[32,32,256]{2,1,0:T(8,128)(2,1)S(1)} %collective-permute-done.13), channel_id=1, source_target_pairs={{0,1},{1,0},{2,3},{3,2},{4,5},{5,4},{6,7},{7,6},{8,9},{9,8},{10,11... | collective-permute-start | bytes 1572872 | tf_op jit(solution)/shard_map/ppermute | solution.py:27
  234.5 0.1 constant_dynamic-update-slice_fusion.10
  234.6 6.5 %collective-permute-done.15 = bf16[32,32,256]{2,1,0:T(8,128)(2,1)S(1)} collective-permute-done((bf16[32,32,256]{2,1,0:T(8,128)(2,1)S(1)}, bf16[32,32,256]{2,1,0:T(8,128)(2,1)S(1)}, u32[]{:S(2)}, u32[]{:S(2)}) %collective-permute-start.15) | collective-permute-done | bytes 524320 | tf_op jit(solution)/shard_map/ppermute | solution.py:27
  241.1 2.7 %collective-permute-start.16 = (bf16[32,32,256]{2,1,0:T(8,128)(2,1)S(1)}, bf16[32,32,256]{2,1,0:T(8,128)(2,1)S(1)}, u32[]{:S(2)}, u32[]{:S(2)}) collective-permute-start(bf16[32,32,256]{2,1,0:T(8,128)(2,1)S(1)} %collective-permute-done.15), channel_id=1, source_target_pairs={{0,1},{1,0},{2,3},{3,2},{4,5},{5,4},{6,7},{7,6},{8,9},{9,8},{10,11... | collective-permute-start | bytes 1572872 | tf_op jit(solution)/shard_map/ppermute | solution.py:27
  243.8 0.0 collective-permute-done.8
  243.8 0.1 constant_dynamic-update-slice_fusion.8
  243.9 0.0 collective-permute-done.10
  243.9 0.1 constant_dynamic-update-slice_fusion.6
  244.1 0.1 constant_dynamic-update-slice_fusion.4
  244.2 0.1 constant_dynamic-update-slice_fusion.2
  244.3 1.0 collective-permute-done.16
  245.4 2.5 convolution_bitcast_fusion.1
  247.9 2.5 %convolution_bitcast_fusion = f32[1,32,32,512]{3,2,1,0:T(8,128)S(1)} fusion(bf16[32,512,256]{2,1,0:T(8,128)(2,1)S(1)} %constant_dynamic-update-slice_fusion, bf16[32,32,128]{2,1,0:T(8,128)(2,1)S(1)} %get-tuple-element.8, bf16[32,32,128]{2,1,0:T(8,128)(2,1)S(1)} %get-tuple-element.7), kind=kOutput, calls=%fused_computation.8 | convolution fusion | flops 269484032 | bytes 11010048 | tf_op jit(solution)/shard_map/cik,cjk->cij/dot_general | solution.py:151
  250.4 2.0 fusion.1
  (18 shorter events, 0.4 us)
Async XLA Ops:
  1.8 42.4 %collective-permute-start.1 = (bf16[4,32,4096]{2,1,0:T(8,128)(2,1)S(1)}, bf16[4,32,4096]{2,1,0:T(8,128)(2,1)}, u32[]{:S(2)}, u32[]{:S(2)}) collective-permute-start(bf16[4,32,4096]{2,1,0:T(8,128)(2,1)S(1)} %bitcast.48), channel_id=1, source_target_pairs={{0,16},{16,32},{32,48},{48,64},{64,80},{80,96},{96,112},{112,128},... | collective-permute-start | bytes 3145736 | tf_op jit(solution)/shard_map/ppermute | solution.py:23
  7.2 36.9 %collective-permute-start = (bf16[3,32,4096]{2,1,0:T(8,128)(2,1)}, bf16[3,32,4096]{2,1,0:T(8,128)(2,1)}, u32[]{:S(2)}, u32[]{:S(2)}) collective-permute-start(bf16[3,32,4096]{2,1,0:T(8,128)(2,1)} %slice.12), channel_id=1, source_target_pairs={{0,32},{16,48},{32,64},{48,80},{64,96},{80,112},{96,128},{112,144}... | collective-permute-start | bytes 2359304 | tf_op jit(solution)/shard_map/ppermute | solution.py:23
  19.0 8.1 %copy-start = (s32[32]{0:T(128)S(1)}, s32[32]{0:T(128)}, u32[]{:S(2)}) copy-start(s32[32]{0:T(128)} %param.3) | copy-start | bytes 388
  148.1 26.6 %collective-permute-start.3 = (bf16[32,32,256]{2,1,0:T(8,128)(2,1)S(1)}, bf16[32,32,256]{2,1,0:T(8,128)(2,1)S(1)}, u32[]{:S(2)}, u32[]{:S(2)}) collective-permute-start(bf16[32,32,256]{2,1,0:T(8,128)(2,1)S(1)} %reshape.124), channel_id=1, source_target_pairs={{0,8},{1,9},{2,10},{3,11},{4,12},{5,13},{6,14},{7,15},{8,0},{9,1},... | collective-permute-start | bytes 1572872 | tf_op jit(solution)/shard_map/ppermute | solution.py:27
  161.5 18.7 %collective-permute-start.2 = (bf16[32,32,256]{2,1,0:T(8,128)(2,1)S(1)}, bf16[32,32,256]{2,1,0:T(8,128)(2,1)}, u32[]{:S(2)}, u32[]{:S(2)}) collective-permute-start(bf16[32,32,256]{2,1,0:T(8,128)(2,1)S(1)} %reshape.124), channel_id=1, source_target_pairs={{0,1},{1,0},{2,3},{3,2},{4,5},{5,4},{6,7},{7,6},{8,9},{9,8},{10,11... | collective-permute-start | bytes 1572872 | tf_op jit(solution)/shard_map/ppermute | solution.py:27
  169.4 45.0 %collective-permute-start.5 = (bf16[32,32,256]{2,1,0:T(8,128)(2,1)S(1)}, bf16[32,32,256]{2,1,0:T(8,128)(2,1)S(1)}, u32[]{:S(2)}, u32[]{:S(2)}) collective-permute-start(bf16[32,32,256]{2,1,0:T(8,128)(2,1)S(1)} %reshape.124), channel_id=1, source_target_pairs={{0,2},{1,3},{2,4},{3,5},{4,6},{5,7},{6,0},{7,1},{8,10},{9,11},{10,... | collective-permute-start | bytes 1572872 | tf_op jit(solution)/shard_map/ppermute | solution.py:27
  171.5 44.8 %collective-permute-start.9 = (bf16[32,32,256]{2,1,0:T(8,128)(2,1)S(1)}, bf16[32,32,256]{2,1,0:T(8,128)(2,1)S(1)}, u32[]{:S(2)}, u32[]{:S(2)}) collective-permute-start(bf16[32,32,256]{2,1,0:T(8,128)(2,1)S(1)} %reshape.124), channel_id=1, source_target_pairs={{0,6},{1,7},{2,0},{3,1},{4,2},{5,3},{6,4},{7,5},{8,14},{9,15},{10,... | collective-permute-start | bytes 1572872 | tf_op jit(solution)/shard_map/ppermute | solution.py:27
  174.7 47.1 %collective-permute-start.7 = (bf16[32,32,256]{2,1,0:T(8,128)(2,1)S(1)}, bf16[32,32,256]{2,1,0:T(8,128)(2,1)S(1)}, u32[]{:S(2)}, u32[]{:S(2)}) collective-permute-start(bf16[32,32,256]{2,1,0:T(8,128)(2,1)S(1)} %collective-permute-done.3), channel_id=1, source_target_pairs={{0,2},{1,3},{2,4},{3,5},{4,6},{5,7},{6,0},{7,1},{8,10},{9,11},{10,... | collective-permute-start | bytes 1572872 | tf_op jit(solution)/shard_map/ppermute | solution.py:27
  178.0 46.5 %collective-permute-start.11 = (bf16[32,32,256]{2,1,0:T(8,128)(2,1)S(1)}, bf16[32,32,256]{2,1,0:T(8,128)(2,1)S(1)}, u32[]{:S(2)}, u32[]{:S(2)}) collective-permute-start(bf16[32,32,256]{2,1,0:T(8,128)(2,1)S(1)} %collective-permute-done.3), channel_id=1, source_target_pairs={{0,6},{1,7},{2,0},{3,1},{4,2},{5,3},{6,4},{7,5},{8,14},{9,15},{10,... | collective-permute-start | bytes 1572872 | tf_op jit(solution)/shard_map/ppermute | solution.py:27
  180.2 46.3 %collective-permute-start.4 = (bf16[32,32,256]{2,1,0:T(8,128)(2,1)S(1)}, bf16[32,32,256]{2,1,0:T(8,128)(2,1)S(1)}, u32[]{:S(2)}, u32[]{:S(2)}) collective-permute-start(bf16[32,32,256]{2,1,0:T(8,128)(2,1)S(1)} %collective-permute-done.3), channel_id=1, source_target_pairs={{0,1},{1,0},{2,3},{3,2},{4,5},{5,4},{6,7},{7,6},{8,9},{9,8},{10,11... | collective-permute-start | bytes 1572872 | tf_op jit(solution)/shard_map/ppermute | solution.py:27
  214.4 14.4 %collective-permute-start.6 = (bf16[32,32,256]{2,1,0:T(8,128)(2,1)S(1)}, bf16[32,32,256]{2,1,0:T(8,128)(2,1)S(1)}, u32[]{:S(2)}, u32[]{:S(2)}) collective-permute-start(bf16[32,32,256]{2,1,0:T(8,128)(2,1)S(1)} %collective-permute-done.5), channel_id=1, source_target_pairs={{0,1},{1,0},{2,3},{3,2},{4,5},{5,4},{6,7},{7,6},{8,9},{9,8},{10,11... | collective-permute-start | bytes 1572872 | tf_op jit(solution)/shard_map/ppermute | solution.py:27
  216.3 14.9 %collective-permute-start.13 = (bf16[32,32,256]{2,1,0:T(8,128)(2,1)S(1)}, bf16[32,32,256]{2,1,0:T(8,128)(2,1)S(1)}, u32[]{:S(2)}, u32[]{:S(2)}) collective-permute-start(bf16[32,32,256]{2,1,0:T(8,128)(2,1)S(1)} %collective-permute-done.5), channel_id=1, source_target_pairs={{0,2},{1,3},{2,4},{3,5},{4,6},{5,7},{6,0},{7,1},{8,10},{9,11},{10,... | collective-permute-start | bytes 1572872 | tf_op jit(solution)/shard_map/ppermute | solution.py:27
  221.8 22.1 %collective-permute-start.8 = (bf16[32,32,256]{2,1,0:T(8,128)(2,1)S(1)}, bf16[32,32,256]{2,1,0:T(8,128)(2,1)S(1)}, u32[]{:S(2)}, u32[]{:S(2)}) collective-permute-start(bf16[32,32,256]{2,1,0:T(8,128)(2,1)S(1)} %collective-permute-done.7), channel_id=1, source_target_pairs={{0,1},{1,0},{2,3},{3,2},{4,5},{5,4},{6,7},{7,6},{8,9},{9,8},{10,11... | collective-permute-start | bytes 1572872 | tf_op jit(solution)/shard_map/ppermute | solution.py:27
  224.5 16.6 %collective-permute-start.15 = (bf16[32,32,256]{2,1,0:T(8,128)(2,1)S(1)}, bf16[32,32,256]{2,1,0:T(8,128)(2,1)S(1)}, u32[]{:S(2)}, u32[]{:S(2)}) collective-permute-start(bf16[32,32,256]{2,1,0:T(8,128)(2,1)S(1)} %collective-permute-done.11), channel_id=1, source_target_pairs={{0,6},{1,7},{2,0},{3,1},{4,2},{5,3},{6,4},{7,5},{8,14},{9,15},{10,... | collective-permute-start | bytes 1572872 | tf_op jit(solution)/shard_map/ppermute | solution.py:27
  226.5 17.4 %collective-permute-start.10 = (bf16[32,32,256]{2,1,0:T(8,128)(2,1)S(1)}, bf16[32,32,256]{2,1,0:T(8,128)(2,1)S(1)}, u32[]{:S(2)}, u32[]{:S(2)}) collective-permute-start(bf16[32,32,256]{2,1,0:T(8,128)(2,1)S(1)} %collective-permute-done.9), channel_id=1, source_target_pairs={{0,1},{1,0},{2,3},{3,2},{4,5},{5,4},{6,7},{7,6},{8,9},{9,8},{10,11... | collective-permute-start | bytes 1572872 | tf_op jit(solution)/shard_map/ppermute | solution.py:27
  228.8 15.2 %collective-permute-start.12 = (bf16[32,32,256]{2,1,0:T(8,128)(2,1)S(1)}, bf16[32,32,256]{2,1,0:T(8,128)(2,1)S(1)}, u32[]{:S(2)}, u32[]{:S(2)}) collective-permute-start(bf16[32,32,256]{2,1,0:T(8,128)(2,1)S(1)} %collective-permute-done.11), channel_id=1, source_target_pairs={{0,1},{1,0},{2,3},{3,2},{4,5},{5,4},{6,7},{7,6},{8,9},{9,8},{10,11... | collective-permute-start | bytes 1572872 | tf_op jit(solution)/shard_map/ppermute | solution.py:27
  231.2 13.0 %collective-permute-start.14 = (bf16[32,32,256]{2,1,0:T(8,128)(2,1)S(1)}, bf16[32,32,256]{2,1,0:T(8,128)(2,1)S(1)}, u32[]{:S(2)}, u32[]{:S(2)}) collective-permute-start(bf16[32,32,256]{2,1,0:T(8,128)(2,1)S(1)} %collective-permute-done.13), channel_id=1, source_target_pairs={{0,1},{1,0},{2,3},{3,2},{4,5},{5,4},{6,7},{7,6},{8,9},{9,8},{10,11... | collective-permute-start | bytes 1572872 | tf_op jit(solution)/shard_map/ppermute | solution.py:27
  241.1 4.2 %collective-permute-start.16 = (bf16[32,32,256]{2,1,0:T(8,128)(2,1)S(1)}, bf16[32,32,256]{2,1,0:T(8,128)(2,1)S(1)}, u32[]{:S(2)}, u32[]{:S(2)}) collective-permute-start(bf16[32,32,256]{2,1,0:T(8,128)(2,1)S(1)} %collective-permute-done.15), channel_id=1, source_target_pairs={{0,1},{1,0},{2,3},{3,2},{4,5},{5,4},{6,7},{7,6},{8,9},{9,8},{10,11... | collective-permute-start | bytes 1572872 | tf_op jit(solution)/shard_map/ppermute | solution.py:27

commit v5 on v2

--- a/solution.py
+++ b/solution.py
@@ -85,33 +85,27 @@
     def at(z, x, c):
         return z * 8 + (x % 4) * 2 + c
 
-    def unpack(p):
-        return p // 8, (p // 2) % 4, p % 2
-
     def x_step(d):
-        def f(p):
-            z, x, c = unpack(p)
-            return at(z, x + d, c)
-        return f
+        return lambda p: at(p // 8, (p // 2) % 4 + d, p % 2)
 
     cross = moved(own, lambda p: p ^ 8)
-    from_left = moved((own, cross), x_step(1))
-    from_right = moved((own, cross), x_step(-1))
-    far_own = moved(from_left[0], x_step(1))
-    far_cross = moved(from_right[1], x_step(-1))
-    mine = [
-        (0, 0, own), (1, 0, cross),
-        (0, -1, from_left[0]), (1, -1, from_left[1]),
-        (0, 1, from_right[0]), (1, 1, from_right[1]),
-        (0, 2, far_own), (1, 2, far_cross),
-    ]
-    other = moved(tuple(b for _, _, b in mine), lambda p: p ^ 1)
+    left_own = moved(own, x_step(1))
+    right_own = moved(own, x_step(-1))
+    far_own = moved(left_own, x_step(1))
+    near = jnp.stack([own, left_own, right_own, far_own])
+    near_other = moved(near, lambda p: p ^ 1)
+    left_cross = moved(cross, x_step(1))
+    right_cross = moved(cross, x_step(-1))
+    far_cross = moved(right_cross, x_step(-1))
+    far = jnp.stack([cross, left_cross, right_cross, far_cross])
+    far_other = moved(far, lambda p: p ^ 1)
     width = own.shape[1]
     gathered = jnp.zeros((own.shape[0], 16 * width, own.shape[2]), own.dtype)
-    for (dz, dx, block), far in zip(mine, other):
-        for dc, piece in ((0, block), (1, far)):
+    sets = ((0, 0, near), (0, 1, near_other), (1, 0, far), (1, 1, far_other))
+    for dz, dc, blocks in sets:
+        for slot, dx in enumerate((0, -1, 1, 2)):
             place = at((zh + dz) % 2, xx + dx + 4, (core + dc) % 2)
-            gathered = lax.dynamic_update_slice(gathered, piece, (0, place * width, 0))
+            gathered = lax.dynamic_update_slice(gathered, blocks[slot], (0, place * width, 0))
     return gathered
 
 
@@ -121,14 +115,10 @@
     spec_count = shard_len // NFFT
     history = TAPS - 1
     samples = voltages.reshape(inp_count, spec_count, NFFT).transpose(1, 0, 2).astype(jnp.bfloat16)
-    earlier = []
-    need = history
-    distance = 1
-    while need > 0:
-        take = min(spec_count, need)
-        earlier = [shifted(samples[spec_count - take :], "chan", distance)] + earlier
-        need -= take
-        distance += 1
+    assert history <= 2 * spec_count
+    recent = shifted(samples, "chan", 1)
+    older = shifted(recent[2 * spec_count - history :], "chan", 1)
+    earlier = [older, recent]
     joined = jnp.concatenate(earlier + [samples], axis=0)
     gain = (scales.astype(jnp.float32) * (1.0 / 256.0)).reshape(inp_count, 1)
     filtered = polyphase(joined, window_table(), gain, spec_count).reshape(spec_count * inp_count, NFFT)

time: 239 us -> 256 us (1.071)
  the two profiles are of different devices: /device:TPU:55 before, /device:TPU:455 now
where the time goes in v5:
time: 256 us; the launch traced here: 255 us
  waiting for transfers between devices  100 us (39%)
  blocking collectives  44.5 us (17%)
  starting transfers between devices  37 us (14%)
  other arithmetic  26.5 us (10%)
  local copies, waits for them, and re-layouts  26 us (10%)
  matrix products  13.5 us (5%)
  Pallas kernels  6.81 us (3%)
    ppermute x9, waiting for transfers between devices, moved(): lax.ppermute(block, 'inp', [(p, mapping(p)) for p in range(lax.axis_size(...  78.2 us
    all_to_all x1, blocking collectives, shards(): lax.all_to_all(spectra, 'chan', split_axis=3, concat_axis=0, tiled=True)  44.5 us
    ppermute x9, starting transfers between devices, moved(): lax.ppermute(block, 'inp', [(p, mapping(p)) for p in range(lax.axis_size(...  28.4 us
    ppermute x2, waiting for transfers between devices, shifted(): return lax.ppermute(block, axis, route)  22 us
    ppermute x2, starting transfers between devices, shifted(): return lax.ppermute(block, axis, route)  8.59 us
    dot_general x1, matrix products, shards(): jnp.dot(filtered, dft_table(), preferred_element_type=jnp.float32)  8.44 us
    convert_element_type x1, other arithmetic, dft_table(): return lax.optimization_barrier(both.astype(jnp.bfloat16))  8.04 us
    dynamic_update_slice x16, local copies, waits for them, and re-layouts, gather_inputs(): lax.dynamic_update_slice(gathered, blocks[slot], (0, place * width, 0))  8.02 us
  transfers between devices with their start and end apart: 11, of which 7 were waited for; matrix products, arithmetic and copies ran while one was open for 11% of the time, Pallas kernels for 0%

profile of v5, /device:TPU:455, one launch (start us, length us, event | category | flops | bytes accessed | tf_op | source)
XLA Modules:
  0.0 255.2 jit_solution(7137580986030076836)
XLA Ops:
  0.0 1.7 convert_element_type.54
  1.7 0.1 copy.26
  1.8 2.6 %collective-permute-start = (bf16[4,32,4096]{2,1,0:T(8,128)(2,1)S(1)}, bf16[4,32,4096]{2,1,0:T(8,128)(2,1)}, u32[]{:S(2)}, u32[]{:S(2)}) collective-permute-start(bf16[4,32,4096]{2,1,0:T(8,128)(2,1)S(1)} %bitcast.76), channel_id=1, source_target_pairs={{0,16},{16,32},{32,48},{48,64},{64,80},{80,96},{96,112},{112,128},... | collective-permute-start | bytes 3145736 | tf_op jit(solution)/shard_map/ppermute | solution.py:19
  4.4 1.0 sine_negate_fusion
  5.5 1.1 fusion.34
  6.6 4.8 %multiply_subtract_fusion = (f32[64,64,1024]{2,1,0:T(8,128)S(1)}, f32[64,64,1024]{2,1,0:T(8,128)S(1)}) fusion(f32[64,1024]{1,0:T(8,128)S(1)} %get-tuple-element.11, f32[64,1024]{1,0:T(8,128)S(1)} %get-tuple-element.10, f32[64,1024]{1,0:T(8,128)S(1)} %get-tuple-element.12, f32[64,1024]{1,0:T(8,128)S(1)} %get-tuple-element.9), kind=kLoop, calls=%fused_computation.3 | loop fusion | flops 25165824 | bytes 34603008 | tf_op jit(solution)/shard_map/sub | solution.py:49
  11.4 16.4 %collective-permute-done = bf16[4,32,4096]{2,1,0:T(8,128)(2,1)} collective-permute-done((bf16[4,32,4096]{2,1,0:T(8,128)(2,1)S(1)}, bf16[4,32,4096]{2,1,0:T(8,128)(2,1)}, u32[]{:S(2)}, u32[]{:S(2)}) %collective-permute-start) | collective-permute-done | bytes 1048608 | tf_op jit(solution)/shard_map/ppermute | solution.py:19
  27.8 2.1 slice.44
  29.9 5.9 %collective-permute-start.1 = (bf16[3,32,4096]{2,1,0:T(8,128)(2,1)}, bf16[3,32,4096]{2,1,0:T(8,128)(2,1)}, u32[]{:S(2)}, u32[]{:S(2)}) collective-permute-start(bf16[3,32,4096]{2,1,0:T(8,128)(2,1)} %slice.44), channel_id=1, source_target_pairs={{0,16},{16,32},{32,48},{48,64},{64,80},{80,96},{96,112},{112,128},... | collective-permute-start | bytes 2359304 | tf_op jit(solution)/shard_map/ppermute | solution.py:19
  35.8 0.0 copy-start.6
  35.8 8.0 %fusion = bf16[4096,2048]{1,0:T(8,128)(2,1)} fusion(f32[4096,1024]{1,0:T(8,128)S(1)} %bitcast.70, f32[4096,1024]{1,0:T(8,128)S(1)} %bitcast.69), kind=kLoop, calls=%fused_computation.1 | loop fusion | flops 25165824 | bytes 50331648 | tf_op jit(solution)/shard_map/convert_element_type | solution.py:52
  43.9 0.7 copy.16.g_ref
  44.6 1.3 fusion.29.w_ref
  45.8 5.6 %collective-permute-done.1 = bf16[3,32,4096]{2,1,0:T(8,128)(2,1)} collective-permute-done((bf16[3,32,4096]{2,1,0:T(8,128)(2,1)}, bf16[3,32,4096]{2,1,0:T(8,128)(2,1)}, u32[]{:S(2)}, u32[]{:S(2)}) %collective-permute-start.1) | collective-permute-done | bytes 786464 | tf_op jit(solution)/shard_map/ppermute | solution.py:19
  51.4 3.3 %pad_maximum_fusion.x_ref = bf16[11,32,4096]{2,1,0:T(8,128)(2,1)} fusion(bf16[4,32,4096]{2,1,0:T(8,128)(2,1)S(1)} %bitcast.77, bf16[4,32,4096]{2,1,0:T(8,128)(2,1)} %collective-permute-done, bf16[3,32,4096]{2,1,0:T(8,128)(2,1)} %collective-permute-done.1), kind=kLoop, calls=%fused_computation.6 | loop fusion | flops 2883584 | bytes 5767168 | tf_op jit(solution)/shard_map/concatenate | solution.py:122
  54.7 6.8 %shard_map.28 = bf16[4,32,4096]{2,1,0:T(8,128)(2,1)} custom-call(bf16[11,32,4096]{2,1,0:T(8,128)(2,1)} %pad_maximum_fusion.x_ref, f32[8,4096]{1,0:T(8,128)} %fusion.29.w_ref, f32[32,1]{1,0:T(8,128)} %copy.16.g_ref), custom_call_target="tpu_custom_call" | custom-call | tf_op jit(solution)/shard_map/pallas_call | solution.py:67
  61.5 8.4 %convolution_convert_fusion = bf16[128,2048]{1,0:T(8,128)(2,1)S(1)} fusion(bf16[128,4096]{1,0:T(8,128)(2,1)} %bitcast.74, bf16[4096,2048]{1,0:T(8,128)(2,1)} %fusion), kind=kOutput, calls=%fused_computation.7 | convolution fusion | flops 2147745792 | bytes 18350080 | tf_op jit(solution)/shard_map/dot_general | solution.py:125
  70.0 0.4 reshape.118
  70.4 1.9 copy.17
  72.3 2.0 reshape.120
  74.3 44.5 %all_to_all.18 = bf16[32,2,4096]{2,1,0:T(2,128)(2,1)S(1)} all-to-all(bf16[32,2,4096]{2,1,0:T(2,128)(2,1)S(1)} %reshape.120), channel_id=1, replica_groups=mesh['chan'=32,'inp'=16] {'chan'}, dimensions={0} | all-to-all | bytes 1048576 | tf_op jit(solution)/shard_map/all_to_all | solution.py:127
  118.8 1.0 reshape.121
  119.8 3.8 %copy.23 = bf16[4,32,2,32,32]{4,1,2,0,3:T(8,128)(2,1)} copy(bf16[4,32,2,32,32]{1,2,0,4,3:T(2,128)(2,1)S(1)} %bitcast.72) | data formatting | bytes 1048576 | tf_op jit(solution)/shard_map/all_to_all | solution.py:127
  123.6 3.7 %copy.20 = bf16[32,32,2,128]{3,2,1,0:T(2,128)(2,1)S(1)} copy(bf16[32,32,2,128]{0,1,2,3:T(8,128)(2,1)} %bitcast.73) | data formatting | bytes 1048576 | tf_op jit(solution)/shard_map/transpose | solution.py:130
  127.3 0.3 reshape.119
  127.6 2.1 collective-permute-start.2
  129.7 3.2 %collective-permute-start.3 = (bf16[32,32,256]{2,1,0:T(8,128)(2,1)S(1)}, bf16[32,32,256]{2,1,0:T(8,128)(2,1)S(1)}, u32[]{:S(2)}, u32[]{:S(2)}) collective-permute-start(bf16[32,32,256]{2,1,0:T(8,128)(2,1)S(1)} %reshape.119), channel_id=1, source_target_pairs={{0,6},{1,7},{2,0},{3,1},{4,2},{5,3},{6,4},{7,5},{8,14},{9,15},{10,... | collective-permute-start | bytes 1572872 | tf_op jit(solution)/shard_map/ppermute | solution.py:23
  132.9 8.7 %collective-permute-done.2 = bf16[32,32,256]{2,1,0:T(8,128)(2,1)S(1)} collective-permute-done((bf16[32,32,256]{2,1,0:T(8,128)(2,1)S(1)}, bf16[32,32,256]{2,1,0:T(8,128)(2,1)S(1)}, u32[]{:S(2)}, u32[]{:S(2)}) %collective-permute-start.2) | collective-permute-done | bytes 524320 | tf_op jit(solution)/shard_map/ppermute | solution.py:23
  141.6 3.3 %collective-permute-start.4 = (bf16[32,32,256]{2,1,0:T(8,128)(2,1)S(1)}, bf16[32,32,256]{2,1,0:T(8,128)(2,1)S(1)}, u32[]{:S(2)}, u32[]{:S(2)}) collective-permute-start(bf16[32,32,256]{2,1,0:T(8,128)(2,1)S(1)} %collective-permute-done.2), channel_id=1, source_target_pairs={{0,2},{1,3},{2,4},{3,5},{4,6},{5,7},{6,0},{7,1},{8,10},{9,11},{10,... | collective-permute-start | bytes 1572872 | tf_op jit(solution)/shard_map/ppermute | solution.py:23
  144.9 2.1 collective-permute-start.6
  147.1 0.3 stack_reshape.3
  147.4 0.0 collective-permute-done.3
  147.4 7.3 %collective-permute-done.4 = bf16[32,32,256]{2,1,0:T(8,128)(2,1)S(1)} collective-permute-done((bf16[32,32,256]{2,1,0:T(8,128)(2,1)S(1)}, bf16[32,32,256]{2,1,0:T(8,128)(2,1)S(1)}, u32[]{:S(2)}, u32[]{:S(2)}) %collective-permute-start.4) | collective-permute-done | bytes 524320 | tf_op jit(solution)/shard_map/ppermute | solution.py:23
  154.7 0.8 copy-done.4
  155.5 1.6 pad_maximum_fusion.1
  157.1 5.1 %collective-permute-start.5 = (bf16[4,32,32,256]{3,2,1,0:T(8,128)(2,1)S(1)}, bf16[4,32,32,256]{3,2,1,0:T(8,128)(2,1)}, u32[]{:S(2)}, u32[]{:S(2)}) collective-permute-start(bf16[4,32,32,256]{3,2,1,0:T(8,128)(2,1)S(1)} %pad_maximum_fusion.1), channel_id=1, source_target_pairs={{0,1},{1,0},{2,3},{3,2},{4,5},{5,4},{6,7},{7,6},{8,9},{9,8},{10,11... | collective-permute-start | bytes 6291464 | tf_op jit(solution)/shard_map/ppermute | solution.py:23
  162.2 40.5 %collective-permute-done.6 = bf16[32,32,256]{2,1,0:T(8,128)(2,1)} collective-permute-done((bf16[32,32,256]{2,1,0:T(8,128)(2,1)S(1)}, bf16[32,32,256]{2,1,0:T(8,128)(2,1)}, u32[]{:S(2)}, u32[]{:S(2)}) %collective-permute-start.6) | collective-permute-done | bytes 524320 | tf_op jit(solution)/shard_map/ppermute | solution.py:23
  202.7 1.9 collective-permute-start.8
  204.6 4.5 %collective-permute-start.7 = (bf16[32,32,256]{2,1,0:T(8,128)(2,1)}, bf16[32,32,256]{2,1,0:T(8,128)(2,1)}, u32[]{:S(2)}, u32[]{:S(2)}) collective-permute-start(bf16[32,32,256]{2,1,0:T(8,128)(2,1)} %collective-permute-done.6), channel_id=1, source_target_pairs={{0,2},{1,3},{2,4},{3,5},{4,6},{5,7},{6,0},{7,1},{8,10},{9,11},{10,... | collective-permute-start | bytes 1572872 | tf_op jit(solution)/shard_map/ppermute | solution.py:23
  209.2 9.7 %collective-permute-done.8 = bf16[32,32,256]{2,1,0:T(8,128)(2,1)S(1)} collective-permute-done((bf16[32,32,256]{2,1,0:T(8,128)(2,1)}, bf16[32,32,256]{2,1,0:T(8,128)(2,1)S(1)}, u32[]{:S(2)}, u32[]{:S(2)}) %collective-permute-start.8) | collective-permute-done | bytes 524320 | tf_op jit(solution)/shard_map/ppermute | solution.py:23
  218.9 1.9 collective-permute-start.9
  221.0 0.0 copy-start.1
  221.1 0.9 broadcast_in_dim.48
  222.1 0.0 collective-permute-done.7
  222.1 12.0 %collective-permute-done.9 = bf16[32,32,256]{2,1,0:T(8,128)(2,1)} collective-permute-done((bf16[32,32,256]{2,1,0:T(8,128)(2,1)S(1)}, bf16[32,32,256]{2,1,0:T(8,128)(2,1)}, u32[]{:S(2)}, u32[]{:S(2)}) %collective-permute-start.9) | collective-permute-done | bytes 524320 | tf_op jit(solution)/shard_map/ppermute | solution.py:23
  234.1 1.6 pad_maximum_fusion.2
  235.7 4.2 %collective-permute-start.10 = (bf16[4,32,32,256]{3,2,1,0:T(8,128)(2,1)S(1)}, bf16[4,32,32,256]{3,2,1,0:T(8,128)(2,1)S(1)}, u32[]{:S(2)}, u32[]{:S(2)}) collective-permute-start(bf16[4,32,32,256]{3,2,1,0:T(8,128)(2,1)S(1)} %pad_maximum_fusion.2), channel_id=1, source_target_pairs={{0,1},{1,0},{2,3},{3,2},{4,5},{5,4},{6,7},{7,6},{8,9},{9,8},{10,11... | collective-permute-start | bytes 6291464 | tf_op jit(solution)/shard_map/ppermute | solution.py:23
  240.0 0.1 fusion.41
  240.2 0.0 collective-permute-done.5
  240.3 1.1 fusion.9
  241.3 1.1 fusion.8
  242.4 1.1 fusion.7
  243.5 1.1 fusion.6
  244.6 1.1 constant_dynamic-update-slice_fusion.3
  245.7 1.1 constant_dynamic-update-slice_fusion.2
  246.9 1.1 constant_dynamic-update-slice_fusion
  247.9 0.0 collective-permute-done.10
  248.0 0.1 fusion.5
  248.0 0.1 fusion.4
  248.1 0.1 fusion.3
  248.1 0.1 fusion.2
  248.2 2.5 convolution_bitcast_fusion.1
  250.7 2.5 convolution_bitcast_fusion
  253.3 2.0 fusion.1
  (18 shorter events, 0.3 us)
Async XLA Ops:
  1.8 26.0 %collective-permute-start = (bf16[4,32,4096]{2,1,0:T(8,128)(2,1)S(1)}, bf16[4,32,4096]{2,1,0:T(8,128)(2,1)}, u32[]{:S(2)}, u32[]{:S(2)}) collective-permute-start(bf16[4,32,4096]{2,1,0:T(8,128)(2,1)S(1)} %bitcast.76), channel_id=1, source_target_pairs={{0,16},{16,32},{32,48},{48,64},{64,80},{80,96},{96,112},{112,128},... | collective-permute-start | bytes 3145736 | tf_op jit(solution)/shard_map/ppermute | solution.py:19
  29.9 21.5 %collective-permute-start.1 = (bf16[3,32,4096]{2,1,0:T(8,128)(2,1)}, bf16[3,32,4096]{2,1,0:T(8,128)(2,1)}, u32[]{:S(2)}, u32[]{:S(2)}) collective-permute-start(bf16[3,32,4096]{2,1,0:T(8,128)(2,1)} %slice.44), channel_id=1, source_target_pairs={{0,16},{16,32},{32,48},{48,64},{64,80},{80,96},{96,112},{112,128},... | collective-permute-start | bytes 2359304 | tf_op jit(solution)/shard_map/ppermute | solution.py:19
  35.8 8.1 %copy-start.6 = (s32[32]{0:T(128)S(1)}, s32[32]{0:T(128)}, u32[]{:S(2)}) copy-start(s32[32]{0:T(128)} %param.3) | copy-start | bytes 388
  127.6 14.0 %collective-permute-start.2 = (bf16[32,32,256]{2,1,0:T(8,128)(2,1)S(1)}, bf16[32,32,256]{2,1,0:T(8,128)(2,1)S(1)}, u32[]{:S(2)}, u32[]{:S(2)}) collective-permute-start(bf16[32,32,256]{2,1,0:T(8,128)(2,1)S(1)} %reshape.119), channel_id=1, source_target_pairs={{0,2},{1,3},{2,4},{3,5},{4,6},{5,7},{6,0},{7,1},{8,10},{9,11},{10,... | collective-permute-start | bytes 1572872 | tf_op jit(solution)/shard_map/ppermute | solution.py:23
  129.7 17.7 %collective-permute-start.3 = (bf16[32,32,256]{2,1,0:T(8,128)(2,1)S(1)}, bf16[32,32,256]{2,1,0:T(8,128)(2,1)S(1)}, u32[]{:S(2)}, u32[]{:S(2)}) collective-permute-start(bf16[32,32,256]{2,1,0:T(8,128)(2,1)S(1)} %reshape.119), channel_id=1, source_target_pairs={{0,6},{1,7},{2,0},{3,1},{4,2},{5,3},{6,4},{7,5},{8,14},{9,15},{10,... | collective-permute-start | bytes 1572872 | tf_op jit(solution)/shard_map/ppermute | solution.py:23
  141.6 13.1 %copy-start = (bf16[32,32,256]{2,1,0:T(8,128)(2,1)}, bf16[32,32,256]{2,1,0:T(8,128)(2,1)S(1)}, u32[]{:S(2)}) copy-start(bf16[32,32,256]{2,1,0:T(8,128)(2,1)S(1)} %collective-permute-done.2) | copy-start | bytes 1572868
  141.6 13.1 %collective-permute-start.4 = (bf16[32,32,256]{2,1,0:T(8,128)(2,1)S(1)}, bf16[32,32,256]{2,1,0:T(8,128)(2,1)S(1)}, u32[]{:S(2)}, u32[]{:S(2)}) collective-permute-start(bf16[32,32,256]{2,1,0:T(8,128)(2,1)S(1)} %collective-permute-done.2), channel_id=1, source_target_pairs={{0,2},{1,3},{2,4},{3,5},{4,6},{5,7},{6,0},{7,1},{8,10},{9,11},{10,... | collective-permute-start | bytes 1572872 | tf_op jit(solution)/shard_map/ppermute | solution.py:23
  144.9 57.7 %collective-permute-start.6 = (bf16[32,32,256]{2,1,0:T(8,128)(2,1)S(1)}, bf16[32,32,256]{2,1,0:T(8,128)(2,1)}, u32[]{:S(2)}, u32[]{:S(2)}) collective-permute-start(bf16[32,32,256]{2,1,0:T(8,128)(2,1)S(1)} %reshape.119), channel_id=1, source_target_pairs={{0,8},{1,9},{2,10},{3,11},{4,12},{5,13},{6,14},{7,15},{8,0},{9,1},... | collective-permute-start | bytes 1572872 | tf_op jit(solution)/shard_map/ppermute | solution.py:23
  147.4 7.3 %copy-start.2 = (bf16[32,32,256]{2,1,0:T(8,128)(2,1)}, bf16[32,32,256]{2,1,0:T(8,128)(2,1)S(1)}, u32[]{:S(2)}) copy-start(bf16[32,32,256]{2,1,0:T(8,128)(2,1)S(1)} %collective-permute-done.3) | copy-start | bytes 1572868
  154.7 0.8 copy-start.4
  157.1 83.1 %collective-permute-start.5 = (bf16[4,32,32,256]{3,2,1,0:T(8,128)(2,1)S(1)}, bf16[4,32,32,256]{3,2,1,0:T(8,128)(2,1)}, u32[]{:S(2)}, u32[]{:S(2)}) collective-permute-start(bf16[4,32,32,256]{3,2,1,0:T(8,128)(2,1)S(1)} %pad_maximum_fusion.1), channel_id=1, source_target_pairs={{0,1},{1,0},{2,3},{3,2},{4,5},{5,4},{6,7},{7,6},{8,9},{9,8},{10,11... | collective-permute-start | bytes 6291464 | tf_op jit(solution)/shard_map/ppermute | solution.py:23
  202.7 16.2 %collective-permute-start.8 = (bf16[32,32,256]{2,1,0:T(8,128)(2,1)}, bf16[32,32,256]{2,1,0:T(8,128)(2,1)S(1)}, u32[]{:S(2)}, u32[]{:S(2)}) collective-permute-start(bf16[32,32,256]{2,1,0:T(8,128)(2,1)} %collective-permute-done.6), channel_id=1, source_target_pairs={{0,6},{1,7},{2,0},{3,1},{4,2},{5,3},{6,4},{7,5},{8,14},{9,15},{10,... | collective-permute-start | bytes 1572872 | tf_op jit(solution)/shard_map/ppermute | solution.py:23
  204.6 17.5 %collective-permute-start.7 = (bf16[32,32,256]{2,1,0:T(8,128)(2,1)}, bf16[32,32,256]{2,1,0:T(8,128)(2,1)}, u32[]{:S(2)}, u32[]{:S(2)}) collective-permute-start(bf16[32,32,256]{2,1,0:T(8,128)(2,1)} %collective-permute-done.6), channel_id=1, source_target_pairs={{0,2},{1,3},{2,4},{3,5},{4,6},{5,7},{6,0},{7,1},{8,10},{9,11},{10,... | collective-permute-start | bytes 1572872 | tf_op jit(solution)/shard_map/ppermute | solution.py:23
  218.9 15.2 %collective-permute-start.9 = (bf16[32,32,256]{2,1,0:T(8,128)(2,1)S(1)}, bf16[32,32,256]{2,1,0:T(8,128)(2,1)}, u32[]{:S(2)}, u32[]{:S(2)}) collective-permute-start(bf16[32,32,256]{2,1,0:T(8,128)(2,1)S(1)} %collective-permute-done.8), channel_id=1, source_target_pairs={{0,6},{1,7},{2,0},{3,1},{4,2},{5,3},{6,4},{7,5},{8,14},{9,15},{10,... | collective-permute-start | bytes 1572872 | tf_op jit(solution)/shard_map/ppermute | solution.py:23
  221.0 19.0 %copy-start.1 = (bf16[32,32,256]{2,1,0:T(8,128)(2,1)S(1)}, bf16[32,32,256]{2,1,0:T(8,128)(2,1)}, u32[]{:S(2)}) copy-start(bf16[32,32,256]{2,1,0:T(8,128)(2,1)} %copy-done) | copy-start | bytes 1572868
  221.1 19.1 %copy-start.3 = (bf16[32,32,256]{2,1,0:T(8,128)(2,1)S(1)}, bf16[32,32,256]{2,1,0:T(8,128)(2,1)}, u32[]{:S(2)}) copy-start(bf16[32,32,256]{2,1,0:T(8,128)(2,1)} %copy-done.2) | copy-start | bytes 1572868
  221.1 19.1 %copy-start.5 = (bf16[32,32,256]{2,1,0:T(8,128)(2,1)S(1)}, bf16[32,32,256]{2,1,0:T(8,128)(2,1)}, u32[]{:S(2)}) copy-start(bf16[32,32,256]{2,1,0:T(8,128)(2,1)} %copy-done.4) | copy-start | bytes 1572868
  235.7 12.2 %collective-permute-start.10 = (bf16[4,32,32,256]{3,2,1,0:T(8,128)(2,1)S(1)}, bf16[4,32,32,256]{3,2,1,0:T(8,128)(2,1)S(1)}, u32[]{:S(2)}, u32[]{:S(2)}) collective-permute-start(bf16[4,32,32,256]{3,2,1,0:T(8,128)(2,1)S(1)} %pad_maximum_fusion.2), channel_id=1, source_target_pairs={{0,1},{1,0},{2,3},{3,2},{4,5},{5,4},{6,7},{7,6},{8,9},{9,8},{10,11... | collective-permute-start | bytes 6291464 | tf_op jit(solution)/shard_map/ppermute | solution.py:23

commit v6 on v4

--- a/solution.py
+++ b/solution.py
@@ -82,41 +82,15 @@
 
 
 def gather_inputs(own):
-    assert lax.axis_size(INPUT) == 16
-    me = lax.axis_index(INPUT)
-    zh, xx, core = me // 8, (me // 2) % 4, me % 2
-
-    def at(z, x, c):
-        return z * 8 + (x % 4) * 2 + c
-
-    def unpack(p):
-        return p // 8, (p // 2) % 4, p % 2
-
-    def x_step(d):
-        def f(p):
-            z, x, c = unpack(p)
-            return at(z, x + d, c)
-        return f
-
-    cross = moved(own, lambda p: p ^ 8)
-    from_left = moved((own, cross), x_step(1))
-    from_right = moved((own, cross), x_step(-1))
-    far_own = moved(from_left[0], x_step(1))
-    far_cross = moved(from_right[1], x_step(-1))
-    mine = [
-        (0, 0, own), (1, 0, cross),
-        (0, -1, from_left[0]), (1, -1, from_left[1]),
-        (0, 1, from_right[0]), (1, 1, from_right[1]),
-        (0, 2, far_own), (1, 2, far_cross),
-    ]
-    other = moved(tuple(b for _, _, b in mine), lambda p: p ^ 1)
-    width = own.shape[1]
-    gathered = jnp.zeros((own.shape[0], 16 * width, own.shape[2]), own.dtype)
-    for (dz, dx, block), far in zip(mine, other):
-        for dc, piece in ((0, block), (1, far)):
-            place = at((zh + dz) % 2, xx + dx + 4, (core + dc) % 2)
-            gathered = lax.dynamic_update_slice(gathered, piece, (0, place * width, 0))
-    return gathered
+    zh = lax.axis_index("zh")
+    cross = lax.ppermute(own, "zh", [(0, 1), (1, 0)])
+    low_first = zh == 0
+    pair = jnp.concatenate([jnp.where(low_first, own, cross), jnp.where(low_first, cross, own)], axis=1)
+    everyone = lax.all_gather(pair, ("x", "core"), axis=1, tiled=True)
+    chans, depth = own.shape[0], own.shape[2]
+    groups = lax.axis_size(("x", "core"))
+    ordered = everyone.reshape(chans, groups, 2, own.shape[1], depth).transpose(0, 2, 1, 3, 4)
+    return ordered.reshape(chans, 2 * groups * own.shape[1], depth)
 
 
 def shards(voltages, scales):
@@ -137,13 +111,10 @@
     gain = (scales.astype(jnp.float32) * (1.0 / 256.0)).reshape(inp_count, 1)
     filtered = polyphase(joined, window_table(), gain, spec_count).reshape(spec_count * inp_count, NFFT)
     spectra = jnp.dot(filtered, dft_table(), preferred_element_type=jnp.float32).astype(jnp.bfloat16)
-    rows_y, rows_z = lax.axis_size("y"), lax.axis_size("zl")
-    spectra = spectra.reshape(spec_count, inp_count, 2, rows_y, rows_z, CHANS // (rows_y * rows_z))
-    step_z = lax.all_to_all(spectra, "zl", split_axis=4, concat_axis=0, tiled=True)
-    step_y = lax.all_to_all(step_z, "y", split_axis=3, concat_axis=0, tiled=True)
-    spec_total = step_y.shape[0]
-    chan_count = step_y.shape[5]
-    local_block = step_y.reshape(spec_total, inp_count, 2, chan_count)
+    spectra = spectra.reshape(spec_count, inp_count, 2, CHANS)
+    local_block = lax.all_to_all(spectra, TIME, split_axis=3, concat_axis=0, tiled=True)
+    spec_total = local_block.shape[0]
+    chan_count = local_block.shape[3]
     own_rows = local_block.transpose(3, 1, 2, 0).reshape(chan_count, inp_count, 2 * spec_total)
     swapped = jnp.concatenate([own_rows[..., spec_total:], -own_rows[..., :spec_total]], axis=-1)
     piece = gather_inputs(own_rows)

time: 255 us -> 285 us (1.12)
  waiting for transfers between devices: 23 us -> 113 us
  starting transfers between devices: 95.4 us -> 23 us
  between operations: 0.71 us -> 13.5 us
  blocking collectives: 66.7 us -> 61.6 us
  matrix products: 13.5 us -> 17 us
    all_gather x0 -> x1, waiting for transfers between devices: none -> 74.2 us  [gather_inputs(): everyone = lax.all_gather(pair, ('x', 'core'), axis=1, tiled=True)]
    ppermute x15 -> x1, starting transfers between devices: 86.1 us -> 13.6 us  [gather_inputs(): cross = lax.ppermute(own, 'zh', [(0, 1), (1, 0)])]
    ppermute x15 -> x1, waiting for transfers between devices: 7.84 us -> 23.4 us  [gather_inputs(): cross = lax.ppermute(own, 'zh', [(0, 1), (1, 0)])]
    unnamed x6, local copies, waits for them, and re-layouts: 9.65 us -> 3.03 us
    reshape x2 -> x3, local copies, waits for them, and re-layouts: 4.31 us -> 10.4 us  [the longest x1 8.09 us: gather_inputs(): everyone.reshape(chans, groups, 2, own.shape[1], depth)]
    all_to_all x2 -> x1, blocking collectives: 66.7 us -> 61.6 us  [shards(): lax.all_to_all(spectra, TIME, split_axis=3, concat_axis=0, tiled=True)]
    dot_general x1, matrix products: 2.52 us -> 6.05 us  [shards(): jnp.einsum('cik,cjk->cij', own_rows, piece, preferred_element_type=jnp.fl...]
  transfers between devices with their start and end apart: 17 -> 4, of which waited for: 4 -> 3; matrix products, arithmetic and copies ran while one was open for 8% -> 6% of each run, Pallas kernels for 0% -> 0%
where the time goes in v6:
time: 285 us; the launch traced here: 282 us
  waiting for transfers between devices  113 us (40%)
  blocking collectives  61.6 us (22%)
  other arithmetic  24.4 us (9%)
  starting transfers between devices  23 us (8%)
  local copies, waits for them, and re-layouts  22.9 us (8%)
  matrix products  17 us (6%)
  between operations  13.5 us (5%)
  Pallas kernels  6.81 us (2%)
    all_gather x1, waiting for transfers between devices, gather_inputs(): everyone = lax.all_gather(pair, ('x', 'core'), axis=1, tiled=True)  74.2 us
    all_to_all x1, blocking collectives, shards(): lax.all_to_all(spectra, TIME, split_axis=3, concat_axis=0, tiled=True)  61.6 us
    ppermute x1, waiting for transfers between devices, gather_inputs(): cross = lax.ppermute(own, 'zh', [(0, 1), (1, 0)])  23.4 us
    ppermute x2, waiting for transfers between devices, shifted(): return lax.ppermute(block, axis, route)  15.2 us
    ppermute x1, starting transfers between devices, gather_inputs(): cross = lax.ppermute(own, 'zh', [(0, 1), (1, 0)])  13.6 us
    ppermute x2, starting transfers between devices, shifted(): return lax.ppermute(block, axis, route)  9.32 us
    dot_general x1, matrix products, shards(): jnp.dot(filtered, dft_table(), preferred_element_type=jnp.float32)  8.44 us
    reshape x1, local copies, waits for them, and re-layouts, gather_inputs(): everyone.reshape(chans, groups, 2, own.shape[1], depth)  8.09 us
  transfers between devices with their start and end apart: 4, of which 3 were waited for; matrix products, arithmetic and copies ran while one was open for 6% of the time, Pallas kernels for 0%

profile of v6, /device:TPU:7, one launch (start us, length us, event | category | flops | bytes accessed | tf_op | source)
XLA Modules:
  0.0 282.1 jit_solution(6158203827926171329)
XLA Ops:
  6.5 0.0 all-gather.2.cloned.1.call-start
  6.5 1.7 convert_element_type.54
  8.2 0.1 copy.27
  8.3 4.5 %collective-permute-start.1 = (bf16[4,32,4096]{2,1,0:T(8,128)(2,1)S(1)}, bf16[4,32,4096]{2,1,0:T(8,128)(2,1)}, u32[]{:S(2)}, u32[]{:S(2)}) collective-permute-start(bf16[4,32,4096]{2,1,0:T(8,128)(2,1)S(1)} %bitcast.42), channel_id=1, source_target_pairs={{0,16},{16,32},{32,48},{48,64},{64,80},{80,96},{96,112},{112,128},... | collective-permute-start | bytes 3145736 | tf_op jit(solution)/shard_map/ppermute | solution.py:23
  12.8 0.9 slice.12
  13.8 4.8 %collective-permute-start = (bf16[3,32,4096]{2,1,0:T(8,128)(2,1)}, bf16[3,32,4096]{2,1,0:T(8,128)(2,1)}, u32[]{:S(2)}, u32[]{:S(2)}) collective-permute-start(bf16[3,32,4096]{2,1,0:T(8,128)(2,1)} %slice.12), channel_id=1, source_target_pairs={{0,32},{16,48},{32,64},{48,80},{64,96},{80,112},{96,128},{112,144}... | collective-permute-start | bytes 2359304 | tf_op jit(solution)/shard_map/ppermute | solution.py:23
  18.6 1.0 sine_negate_fusion
  19.6 1.1 fusion.26
  20.7 4.8 %multiply_subtract_fusion = (f32[64,64,1024]{2,1,0:T(8,128)S(1)}, f32[64,64,1024]{2,1,0:T(8,128)S(1)}) fusion(f32[64,1024]{1,0:T(8,128)S(1)} %get-tuple-element.13, f32[64,1024]{1,0:T(8,128)S(1)} %get-tuple-element.12, f32[64,1024]{1,0:T(8,128)S(1)} %get-tuple-element.14, f32[64,1024]{1,0:T(8,128)S(1)} %get-tuple-element.11), kind=kLoop, calls=%fused_computation.3 | loop fusion | flops 25165824 | bytes 34603008 | tf_op jit(solution)/shard_map/sub | solution.py:53
  25.5 0.0 copy-start.1
  25.5 8.0 %fusion = bf16[4096,2048]{1,0:T(8,128)(2,1)} fusion(f32[4096,1024]{1,0:T(8,128)S(1)} %bitcast.37, f32[4096,1024]{1,0:T(8,128)S(1)} %bitcast.36), kind=kLoop, calls=%fused_computation.1 | loop fusion | flops 25165824 | bytes 50331648 | tf_op jit(solution)/shard_map/convert_element_type | solution.py:56
  33.5 0.0 copy-done.1
  33.5 0.7 copy.17.g_ref
  34.2 1.3 fusion.21.w_ref
  35.5 15.2 %collective-permute-done = bf16[3,32,4096]{2,1,0:T(8,128)(2,1)} collective-permute-done((bf16[3,32,4096]{2,1,0:T(8,128)(2,1)}, bf16[3,32,4096]{2,1,0:T(8,128)(2,1)}, u32[]{:S(2)}, u32[]{:S(2)}) %collective-permute-start) | collective-permute-done | bytes 786464 | tf_op jit(solution)/shard_map/ppermute | solution.py:23
  50.7 0.0 collective-permute-done.1
  50.7 3.3 %pad_maximum_fusion.x_ref = bf16[11,32,4096]{2,1,0:T(8,128)(2,1)} fusion(bf16[4,32,4096]{2,1,0:T(8,128)(2,1)S(1)} %bitcast.44, bf16[4,32,4096]{2,1,0:T(8,128)(2,1)} %collective-permute-done.1, bf16[3,32,4096]{2,1,0:T(8,128)(2,1)} %collective-permute-done), kind=kLoop, calls=%fused_computation.6 | loop fusion | flops 2883584 | bytes 5767168 | tf_op jit(solution)/shard_map/concatenate | solution.py:110
  54.0 6.8 %shard_map.28 = bf16[4,32,4096]{2,1,0:T(8,128)(2,1)} custom-call(bf16[11,32,4096]{2,1,0:T(8,128)(2,1)} %pad_maximum_fusion.x_ref, f32[8,4096]{1,0:T(8,128)} %fusion.21.w_ref, f32[32,1]{1,0:T(8,128)} %copy.17.g_ref), custom_call_target="tpu_custom_call" | custom-call | tf_op jit(solution)/shard_map/pallas_call | solution.py:71
  60.8 8.4 %convolution_convert_fusion = bf16[128,2048]{1,0:T(8,128)(2,1)S(1)} fusion(bf16[128,4096]{1,0:T(8,128)(2,1)} %bitcast.45, bf16[4096,2048]{1,0:T(8,128)(2,1)} %fusion), kind=kOutput, calls=%fused_computation.7 | convolution fusion | flops 2147745792 | bytes 18350080 | tf_op jit(solution)/shard_map/dot_general | solution.py:113
  69.3 0.4 reshape.124
  69.7 1.9 copy.18
  71.6 2.0 reshape.128
  73.6 61.6 %all_to_all.18 = bf16[32,2,4096]{2,1,0:T(2,128)(2,1)S(1)} all-to-all(bf16[32,2,4096]{2,1,0:T(2,128)(2,1)S(1)} %reshape.128), channel_id=1, replica_groups=mesh['y'=4,'zl'=8,'zh'=2,'x'=4,'core'=2] {'y','zl'}, dimensions={0} | all-to-all | bytes 1048576 | tf_op jit(solution)/shard_map/all_to_all | solution.py:115
  135.2 1.0 reshape.129
  136.2 3.8 %copy.24 = bf16[4,32,2,32,32]{4,1,2,0,3:T(8,128)(2,1)} copy(bf16[4,32,2,32,32]{1,2,0,4,3:T(2,128)(2,1)S(1)} %bitcast.39) | data formatting | bytes 1048576 | tf_op jit(solution)/shard_map/all_to_all | solution.py:115
  140.1 3.7 %copy.21 = bf16[32,32,2,128]{3,2,1,0:T(2,128)(2,1)S(1)} copy(bf16[32,32,2,128]{0,1,2,3:T(8,128)(2,1)} %bitcast.40) | data formatting | bytes 1048576 | tf_op jit(solution)/shard_map/transpose | solution.py:118
  143.7 0.3 reshape.125
  144.1 13.6 %collective-permute-start.2 = (bf16[32,32,256]{2,1,0:T(8,128)(2,1)S(1)}, bf16[32,32,256]{2,1,0:T(8,128)(2,1)S(1)}, u32[]{:S(2)}, u32[]{:S(2)}) collective-permute-start(bf16[32,32,256]{2,1,0:T(8,128)(2,1)S(1)} %reshape.125), channel_id=1, source_target_pairs={{0,8},{8,0},{1,9},{9,1},{2,10},{10,2},{3,11},{11,3},{4,12},{12,4},... | collective-permute-start | bytes 1572872 | tf_op jit(solution)/shard_map/ppermute | solution.py:86
  157.7 23.4 %collective-permute-done.2 = bf16[32,32,256]{2,1,0:T(8,128)(2,1)S(1)} collective-permute-done((bf16[32,32,256]{2,1,0:T(8,128)(2,1)S(1)}, bf16[32,32,256]{2,1,0:T(8,128)(2,1)S(1)}, u32[]{:S(2)}, u32[]{:S(2)}) %collective-permute-start.2) | collective-permute-done | bytes 524320 | tf_op jit(solution)/shard_map/ppermute | solution.py:86
  181.2 0.1 broadcast_select_fusion.1
  181.2 1.1 pad_maximum_fusion.1
  182.3 0.0 all-gather.2.cloned.1.call-update
  182.3 0.1 fusion.33
  182.4 74.2 %all-gather.2.cloned.1.call-done = bf16[32,512,256]{2,1,0:T(8,128)(2,1)} async-done(((bf16[32,64,256]{2,1,0:T(8,128)(2,1)}), bf16[32,512,256]{2,1,0:T(8,128)(2,1)}) %all-gather.2.cloned.1.call-update) | async-done | bytes 8388624 | tf_op jit(solution)/shard_map/all_gather | solution.py:89
  256.6 8.1 %copy.22 = bf16[32,8,2,32,256]{4,3,1,2,0:T(8,128)(2,1)} copy(bf16[32,8,2,32,256]{4,3,2,1,0:T(8,128)(2,1)} %bitcast.41) | data formatting | bytes 16777216 | tf_op jit(solution)/shard_map/reshape | solution.py:92
  264.7 0.0 copy-start
  264.7 6.1 %convolution_bitcast_fusion.1 = f32[1,32,32,512]{3,2,1,0:T(8,128)S(1)} fusion(bf16[32,32,256]{2,1,0:T(8,128)(2,1)S(1)} %reshape.125, bf16[32,512,256]{2,1,0:T(8,128)(2,1)} %bitcast.34), kind=kOutput, calls=%fused_computation.9 | convolution fusion | flops 268435456 | bytes 11010048 | tf_op jit(solution)/shard_map/cik,cjk->cij/dot_general | solution.py:121
  270.7 0.0 copy-done
  270.7 2.5 convolution_bitcast_fusion
  273.3 2.0 fusion.1
  (2 shorter events, 0.0 us)
Async XLA Ops:
  6.5 250.0 %all-gather.2.cloned.1.call-start = ((), (), s32[]{:S(2)}) async-start(), calls=%async_computation.1 | async-start | bytes 9437184 | tf_op jit(solution)/shard_map/all_gather | solution.py:89
  8.3 42.4 %collective-permute-start.1 = (bf16[4,32,4096]{2,1,0:T(8,128)(2,1)S(1)}, bf16[4,32,4096]{2,1,0:T(8,128)(2,1)}, u32[]{:S(2)}, u32[]{:S(2)}) collective-permute-start(bf16[4,32,4096]{2,1,0:T(8,128)(2,1)S(1)} %bitcast.42), channel_id=1, source_target_pairs={{0,16},{16,32},{32,48},{48,64},{64,80},{80,96},{96,112},{112,128},... | collective-permute-start | bytes 3145736 | tf_op jit(solution)/shard_map/ppermute | solution.py:23
  13.8 36.9 %collective-permute-start = (bf16[3,32,4096]{2,1,0:T(8,128)(2,1)}, bf16[3,32,4096]{2,1,0:T(8,128)(2,1)}, u32[]{:S(2)}, u32[]{:S(2)}) collective-permute-start(bf16[3,32,4096]{2,1,0:T(8,128)(2,1)} %slice.12), channel_id=1, source_target_pairs={{0,32},{16,48},{32,64},{48,80},{64,96},{80,112},{96,128},{112,144}... | collective-permute-start | bytes 2359304 | tf_op jit(solution)/shard_map/ppermute | solution.py:23
  25.5 8.0 %copy-start.1 = (s32[32]{0:T(128)S(1)}, s32[32]{0:T(128)}, u32[]{:S(2)}) copy-start(s32[32]{0:T(128)} %param.3) | copy-start | bytes 388
  144.1 37.1 %collective-permute-start.2 = (bf16[32,32,256]{2,1,0:T(8,128)(2,1)S(1)}, bf16[32,32,256]{2,1,0:T(8,128)(2,1)S(1)}, u32[]{:S(2)}, u32[]{:S(2)}) collective-permute-start(bf16[32,32,256]{2,1,0:T(8,128)(2,1)S(1)} %reshape.125), channel_id=1, source_target_pairs={{0,8},{8,0},{1,9},{9,1},{2,10},{10,2},{3,11},{11,3},{4,12},{12,4},... | collective-permute-start | bytes 1572872 | tf_op jit(solution)/shard_map/ppermute | solution.py:86
  264.7 6.1 %copy-start = (bf16[32,8,2,32,256]{4,3,1,2,0:T(8,128)(2,1)S(1)}, bf16[32,8,2,32,256]{4,3,1,2,0:T(8,128)(2,1)}, u32[]{:S(2)}) copy-start(bf16[32,8,2,32,256]{4,3,1,2,0:T(8,128)(2,1)} %copy.22) | copy-start | bytes 25165828
Sparse Core Ops, SparseCore 0:
  182.4 74.0 all-gather.1

commit v7 on v2

--- a/solution.py
+++ b/solution.py
@@ -52,29 +52,31 @@
     return lax.optimization_barrier(both.astype(jnp.bfloat16))
 
 
-def polyphase_kernel(spec_count, x_ref, w_ref, g_ref, o_ref):
+def polyphase_kernel(spec_count, *refs):
+    pieces, (w_ref, g_ref, o_ref) = refs[:-3], refs[-3:]
     gain = g_ref[...]
+    rows = [p[k].astype(jnp.float32) * gain for p in pieces for k in range(p.shape[0])]
     for s in range(spec_count):
         total = jnp.zeros(o_ref.shape[1:], jnp.float32)
         for tap in range(TAPS):
-            total = total + w_ref[tap : tap + 1, :] * (x_ref[s + tap].astype(jnp.float32) * gain)
+            total = total + w_ref[tap : tap + 1, :] * rows[s + tap]
         o_ref[s] = total.astype(o_ref.dtype)
 
 
-def polyphase(joined, window, gain, spec_count):
-    rows, inputs, length = joined.shape
+def polyphase(pieces, window, gain, spec_count):
+    inputs, length = pieces[0].shape[1:]
     lanes = 512
     return pl.pallas_call(
         functools.partial(polyphase_kernel, spec_count),
         out_shape=jax.ShapeDtypeStruct((spec_count, inputs, length), jnp.bfloat16),
         grid=(length // lanes,),
-        in_specs=[
-            pl.BlockSpec((rows, inputs, lanes), lambda k: (0, 0, k)),
+        in_specs=[pl.BlockSpec((p.shape[0], inputs, lanes), lambda k: (0, 0, k)) for p in pieces]
+        + [
             pl.BlockSpec((TAPS, lanes), lambda k: (0, k)),
             pl.BlockSpec((inputs, 1), lambda k: (0, 0)),
         ],
         out_specs=pl.BlockSpec((spec_count, inputs, lanes), lambda k: (0, 0, k)),
-    )(joined, window, gain)
+    )(*pieces, window, gain)
 
 
 def gather_inputs(own):
@@ -129,9 +131,9 @@
         earlier = [shifted(samples[spec_count - take :], "chan", distance)] + earlier
         need -= take
         distance += 1
-    joined = jnp.concatenate(earlier + [samples], axis=0)
     gain = (scales.astype(jnp.float32) * (1.0 / 256.0)).reshape(inp_count, 1)
-    filtered = polyphase(joined, window_table(), gain, spec_count).reshape(spec_count * inp_count, NFFT)
+    filtered = polyphase(earlier + [samples], window_table(), gain, spec_count)
+    filtered = filtered.reshape(spec_count * inp_count, NFFT)
     spectra = jnp.dot(filtered, dft_table(), preferred_element_type=jnp.float32).astype(jnp.bfloat16)
     spectra = spectra.reshape(spec_count, inp_count, 2, CHANS)
     local_block = lax.all_to_all(spectra, "chan", split_axis=3, concat_axis=0, tiled=True)

time: 239 us -> 236 us (0.987)
  other arithmetic: 23.3 us -> 20 us
    concatenate x1 -> x0, other arithmetic: 3.33 us -> none  [shards(): joined = jnp.concatenate(earlier + [samples], axis=0)]
where the time goes in v7:
time: 236 us; the launch traced here: 235 us
  waiting for transfers between devices  72.9 us (31%)
  starting transfers between devices  63.2 us (27%)
  blocking collectives  40.6 us (17%)
  other arithmetic  20 us (8%)
  local copies, waits for them, and re-layouts  17.6 us (7%)
  matrix products  13.5 us (6%)
  Pallas kernels  6.74 us (3%)
    ppermute x15, starting transfers between devices, moved(): lax.ppermute(block, 'inp', [(p, mapping(p)) for p in range(lax.axis_size(...  53.5 us
    ppermute x15, waiting for transfers between devices, moved(): lax.ppermute(block, 'inp', [(p, mapping(p)) for p in range(lax.axis_size(...  41.3 us
    all_to_all x1, blocking collectives, shards(): lax.all_to_all(spectra, 'chan', split_axis=3, concat_axis=0, tiled=True)  40.6 us
    ppermute x2, waiting for transfers between devices, shifted(): return lax.ppermute(block, axis, route)  31.6 us
    ppermute x2, starting transfers between devices, shifted(): return lax.ppermute(block, axis, route)  9.65 us
    dot_general x1, matrix products, shards(): jnp.dot(filtered, dft_table(), preferred_element_type=jnp.float32)  8.44 us
    convert_element_type x1, other arithmetic, dft_table(): return lax.optimization_barrier(both.astype(jnp.bfloat16))  8.02 us
    pallas_call x1, Pallas kernels, polyphase(): pl.pallas_call(functools.partial(polyphase_kernel, spec_count), out_shape...  6.74 us
  transfers between devices with their start and end apart: 17, of which 5 were waited for; matrix products, arithmetic and copies ran while one was open for 9% of the time, Pallas kernels for 0%

profile of v7, /device:TPU:55, one launch (start us, length us, event | category | flops | bytes accessed | tf_op | source)
XLA Modules:
  0.0 235.1 jit_solution(14021962745027665613)
XLA Ops:
  0.0 1.7 convert_element_type.52
  1.7 0.1 copy.23
  1.8 0.0 copy-start
  1.8 3.5 %collective-permute-start.1 = (bf16[4,32,4096]{2,1,0:T(8,128)(2,1)S(1)}, bf16[4,32,4096]{2,1,0:T(8,128)(2,1)}, u32[]{:S(2)}, u32[]{:S(2)}) collective-permute-start(bf16[4,32,4096]{2,1,0:T(8,128)(2,1)S(1)} %bitcast.35), channel_id=1, source_target_pairs={{0,16},{16,32},{32,48},{48,64},{64,80},{80,96},{96,112},{112,128},... | collective-permute-start | bytes 3145736 | tf_op jit(solution)/shard_map/ppermute | solution.py:19
  5.3 1.0 slice.12
  6.3 6.1 %collective-permute-start = (bf16[3,32,4096]{2,1,0:T(8,128)(2,1)}, bf16[3,32,4096]{2,1,0:T(8,128)(2,1)}, u32[]{:S(2)}, u32[]{:S(2)}) collective-permute-start(bf16[3,32,4096]{2,1,0:T(8,128)(2,1)} %slice.12), channel_id=1, source_target_pairs={{0,32},{16,48},{32,64},{48,80},{64,96},{80,112},{96,128},{112,144}... | collective-permute-start | bytes 2359304 | tf_op jit(solution)/shard_map/ppermute | solution.py:19
  12.4 1.0 sine_negate_fusion
  13.5 1.1 fusion.26
  14.6 4.8 %multiply_subtract_fusion = (f32[64,64,1024]{2,1,0:T(8,128)S(1)}, f32[64,64,1024]{2,1,0:T(8,128)S(1)}) fusion(f32[64,1024]{1,0:T(8,128)S(1)} %get-tuple-element.11, f32[64,1024]{1,0:T(8,128)S(1)} %get-tuple-element.10, f32[64,1024]{1,0:T(8,128)S(1)} %get-tuple-element.12, f32[64,1024]{1,0:T(8,128)S(1)} %get-tuple-element.9), kind=kLoop, calls=%fused_computation.3 | loop fusion | flops 25165824 | bytes 34603008 | tf_op jit(solution)/shard_map/sub | solution.py:49
  19.4 0.0 copy-start.1
  19.4 8.0 %fusion = bf16[4096,2048]{1,0:T(8,128)(2,1)} fusion(f32[4096,1024]{1,0:T(8,128)S(1)} %bitcast.31, f32[4096,1024]{1,0:T(8,128)S(1)} %bitcast.30), kind=kLoop, calls=%fused_computation.1 | loop fusion | flops 25165824 | bytes 50331648 | tf_op jit(solution)/shard_map/convert_element_type | solution.py:52
  27.4 0.7 copy.14.refs_4_
  28.1 1.3 fusion.21.refs_3_
  29.4 31.6 %collective-permute-done.refs_0_ = bf16[3,32,4096]{2,1,0:T(8,128)(2,1)} collective-permute-done((bf16[3,32,4096]{2,1,0:T(8,128)(2,1)}, bf16[3,32,4096]{2,1,0:T(8,128)(2,1)}, u32[]{:S(2)}, u32[]{:S(2)}) %collective-permute-start) | collective-permute-done | bytes 786464 | tf_op jit(solution)/shard_map/ppermute | solution.py:19
  61.0 0.0 collective-permute-done.1.refs_1_
  61.0 6.7 %shard_map.28 = bf16[4,32,4096]{2,1,0:T(8,128)(2,1)} custom-call(bf16[3,32,4096]{2,1,0:T(8,128)(2,1)} %collective-permute-done.refs_0_, bf16[4,32,4096]{2,1,0:T(8,128)(2,1)} %collective-permute-done.1.refs_1_, bf16[4,32,4096]{2,1,0:T(8,128)(2,1)} %bitcast.37, f32[8,4096]{1,0:T(8,128)} %fusion.21.refs_3_, f32[32,1]{1,0:T(8,128)} %copy.14.refs_4_), custom_call_target="tpu_custom_call" | custom-call | tf_op jit(solution)/shard_map/pallas_call | solution.py:69
  67.7 8.4 %convolution_convert_fusion = bf16[128,2048]{1,0:T(8,128)(2,1)S(1)} fusion(bf16[128,4096]{1,0:T(8,128)(2,1)} %bitcast.38, bf16[4096,2048]{1,0:T(8,128)(2,1)} %fusion), kind=kOutput, calls=%fused_computation.6 | convolution fusion | flops 2147745792 | bytes 18350080 | tf_op jit(solution)/shard_map/dot_general | solution.py:137
  76.2 0.4 reshape.118
  76.6 1.9 copy.15
  78.5 2.0 reshape.120
  80.5 40.6 %all_to_all.18 = bf16[32,2,4096]{2,1,0:T(2,128)(2,1)S(1)} all-to-all(bf16[32,2,4096]{2,1,0:T(2,128)(2,1)S(1)} %reshape.120), channel_id=1, replica_groups=mesh['chan'=32,'inp'=16] {'chan'}, dimensions={0} | all-to-all | bytes 1048576 | tf_op jit(solution)/shard_map/all_to_all | solution.py:139
  121.1 1.0 reshape.121
  122.1 3.8 %copy.20 = bf16[4,32,2,32,32]{4,1,2,0,3:T(8,128)(2,1)} copy(bf16[4,32,2,32,32]{1,2,0,4,3:T(2,128)(2,1)S(1)} %bitcast.33) | data formatting | bytes 1048576 | tf_op jit(solution)/shard_map/all_to_all | solution.py:139
  125.9 3.7 %copy.18 = bf16[32,32,2,128]{3,2,1,0:T(2,128)(2,1)S(1)} copy(bf16[32,32,2,128]{0,1,2,3:T(8,128)(2,1)} %bitcast.34) | data formatting | bytes 1048576 | tf_op jit(solution)/shard_map/transpose | solution.py:142
  129.6 0.3 reshape.119
  129.9 13.8 %collective-permute-start.3 = (bf16[32,32,256]{2,1,0:T(8,128)(2,1)S(1)}, bf16[32,32,256]{2,1,0:T(8,128)(2,1)S(1)}, u32[]{:S(2)}, u32[]{:S(2)}) collective-permute-start(bf16[32,32,256]{2,1,0:T(8,128)(2,1)S(1)} %reshape.119), channel_id=1, source_target_pairs={{0,8},{1,9},{2,10},{3,11},{4,12},{5,13},{6,14},{7,15},{8,0},{9,1},... | collective-permute-start | bytes 1572872 | tf_op jit(solution)/shard_map/ppermute | solution.py:23
  143.7 5.2 %collective-permute-start.2 = (bf16[32,32,256]{2,1,0:T(8,128)(2,1)S(1)}, bf16[32,32,256]{2,1,0:T(8,128)(2,1)}, u32[]{:S(2)}, u32[]{:S(2)}) collective-permute-start(bf16[32,32,256]{2,1,0:T(8,128)(2,1)S(1)} %reshape.119), channel_id=1, source_target_pairs={{0,1},{1,0},{2,3},{3,2},{4,5},{5,4},{6,7},{7,6},{8,9},{9,8},{10,11... | collective-permute-start | bytes 1572872 | tf_op jit(solution)/shard_map/ppermute | solution.py:23
  148.9 2.1 collective-permute-start.5
  151.0 3.2 %collective-permute-start.9 = (bf16[32,32,256]{2,1,0:T(8,128)(2,1)S(1)}, bf16[32,32,256]{2,1,0:T(8,128)(2,1)S(1)}, u32[]{:S(2)}, u32[]{:S(2)}) collective-permute-start(bf16[32,32,256]{2,1,0:T(8,128)(2,1)S(1)} %reshape.119), channel_id=1, source_target_pairs={{0,6},{1,7},{2,0},{3,1},{4,2},{5,3},{6,4},{7,5},{8,14},{9,15},{10,... | collective-permute-start | bytes 1572872 | tf_op jit(solution)/shard_map/ppermute | solution.py:23
  154.2 33.8 %collective-permute-done.3 = bf16[32,32,256]{2,1,0:T(8,128)(2,1)S(1)} collective-permute-done((bf16[32,32,256]{2,1,0:T(8,128)(2,1)S(1)}, bf16[32,32,256]{2,1,0:T(8,128)(2,1)S(1)}, u32[]{:S(2)}, u32[]{:S(2)}) %collective-permute-start.3) | collective-permute-done | bytes 524320 | tf_op jit(solution)/shard_map/ppermute | solution.py:23
  188.0 2.1 collective-permute-start.7
  190.1 3.2 %collective-permute-start.11 = (bf16[32,32,256]{2,1,0:T(8,128)(2,1)S(1)}, bf16[32,32,256]{2,1,0:T(8,128)(2,1)S(1)}, u32[]{:S(2)}, u32[]{:S(2)}) collective-permute-start(bf16[32,32,256]{2,1,0:T(8,128)(2,1)S(1)} %collective-permute-done.3), channel_id=1, source_target_pairs={{0,6},{1,7},{2,0},{3,1},{4,2},{5,3},{6,4},{7,5},{8,14},{9,15},{10,... | collective-permute-start | bytes 1572872 | tf_op jit(solution)/shard_map/ppermute | solution.py:23
  193.5 0.0 collective-permute-done.2
  193.6 3.4 %collective-permute-start.4 = (bf16[32,32,256]{2,1,0:T(8,128)(2,1)S(1)}, bf16[32,32,256]{2,1,0:T(8,128)(2,1)S(1)}, u32[]{:S(2)}, u32[]{:S(2)}) collective-permute-start(bf16[32,32,256]{2,1,0:T(8,128)(2,1)S(1)} %collective-permute-done.3), channel_id=1, source_target_pairs={{0,1},{1,0},{2,3},{3,2},{4,5},{5,4},{6,7},{7,6},{8,9},{9,8},{10,11... | collective-permute-start | bytes 1572872 | tf_op jit(solution)/shard_map/ppermute | solution.py:23
  197.0 0.1 fusion.33
  197.1 1.9 collective-permute-start.6
  199.0 0.0 collective-permute-done.9
  199.0 3.3 %collective-permute-start.13 = (bf16[32,32,256]{2,1,0:T(8,128)(2,1)S(1)}, bf16[32,32,256]{2,1,0:T(8,128)(2,1)S(1)}, u32[]{:S(2)}, u32[]{:S(2)}) collective-permute-start(bf16[32,32,256]{2,1,0:T(8,128)(2,1)S(1)} %collective-permute-done.5), channel_id=1, source_target_pairs={{0,2},{1,3},{2,4},{3,5},{4,6},{5,7},{6,0},{7,1},{8,10},{9,11},{10,... | collective-permute-start | bytes 1572872 | tf_op jit(solution)/shard_map/ppermute | solution.py:23
  202.3 0.9 broadcast_in_dim.48
  203.3 1.1 constant_dynamic-update-slice_fusion.14
  204.4 2.7 %collective-permute-start.8 = (bf16[32,32,256]{2,1,0:T(8,128)(2,1)S(1)}, bf16[32,32,256]{2,1,0:T(8,128)(2,1)S(1)}, u32[]{:S(2)}, u32[]{:S(2)}) collective-permute-start(bf16[32,32,256]{2,1,0:T(8,128)(2,1)S(1)} %collective-permute-done.7), channel_id=1, source_target_pairs={{0,1},{1,0},{2,3},{3,2},{4,5},{5,4},{6,7},{7,6},{8,9},{9,8},{10,11... | collective-permute-start | bytes 1572872 | tf_op jit(solution)/shard_map/ppermute | solution.py:23
  207.1 0.0 collective-permute-done.11
  207.2 2.0 collective-permute-start.15
  209.2 0.0 collective-permute-done.4
  209.2 2.6 %collective-permute-start.10 = (bf16[32,32,256]{2,1,0:T(8,128)(2,1)S(1)}, bf16[32,32,256]{2,1,0:T(8,128)(2,1)S(1)}, u32[]{:S(2)}, u32[]{:S(2)}) collective-permute-start(bf16[32,32,256]{2,1,0:T(8,128)(2,1)S(1)} %collective-permute-done.9), channel_id=1, source_target_pairs={{0,1},{1,0},{2,3},{3,2},{4,5},{5,4},{6,7},{7,6},{8,9},{9,8},{10,11... | collective-permute-start | bytes 1572872 | tf_op jit(solution)/shard_map/ppermute | solution.py:23
  211.8 0.1 constant_dynamic-update-slice_fusion.12
  211.9 0.0 collective-permute-done.6
  211.9 1.9 collective-permute-start.12
  213.8 0.5 collective-permute-done.13
  214.3 3.0 %collective-permute-start.14 = (bf16[32,32,256]{2,1,0:T(8,128)(2,1)S(1)}, bf16[32,32,256]{2,1,0:T(8,128)(2,1)S(1)}, u32[]{:S(2)}, u32[]{:S(2)}) collective-permute-start(bf16[32,32,256]{2,1,0:T(8,128)(2,1)S(1)} %collective-permute-done.13), channel_id=1, source_target_pairs={{0,1},{1,0},{2,3},{3,2},{4,5},{5,4},{6,7},{7,6},{8,9},{9,8},{10,11... | collective-permute-start | bytes 1572872 | tf_op jit(solution)/shard_map/ppermute | solution.py:23
  217.4 0.1 constant_dynamic-update-slice_fusion.10
  217.5 5.9 %collective-permute-done.15 = bf16[32,32,256]{2,1,0:T(8,128)(2,1)S(1)} collective-permute-done((bf16[32,32,256]{2,1,0:T(8,128)(2,1)S(1)}, bf16[32,32,256]{2,1,0:T(8,128)(2,1)S(1)}, u32[]{:S(2)}, u32[]{:S(2)}) %collective-permute-start.15) | collective-permute-done | bytes 524320 | tf_op jit(solution)/shard_map/ppermute | solution.py:23
  223.4 3.1 %collective-permute-start.16 = (bf16[32,32,256]{2,1,0:T(8,128)(2,1)S(1)}, bf16[32,32,256]{2,1,0:T(8,128)(2,1)S(1)}, u32[]{:S(2)}, u32[]{:S(2)}) collective-permute-start(bf16[32,32,256]{2,1,0:T(8,128)(2,1)S(1)} %collective-permute-done.15), channel_id=1, source_target_pairs={{0,1},{1,0},{2,3},{3,2},{4,5},{5,4},{6,7},{7,6},{8,9},{9,8},{10,11... | collective-permute-start | bytes 1572872 | tf_op jit(solution)/shard_map/ppermute | solution.py:23
  226.5 0.1 constant_dynamic-update-slice_fusion.8
  226.6 0.0 collective-permute-done.10
  226.6 0.1 constant_dynamic-update-slice_fusion.6
  226.7 0.0 collective-permute-done.12
  226.8 0.1 constant_dynamic-update-slice_fusion.4
  226.9 0.0 collective-permute-done.14
  226.9 0.1 constant_dynamic-update-slice_fusion.2
  227.0 1.0 collective-permute-done.16
  228.1 2.5 %convolution_bitcast_fusion.1 = f32[1,32,32,512]{3,2,1,0:T(8,128)S(1)} fusion(bf16[32,32,256]{2,1,0:T(8,128)(2,1)S(1)} %reshape.119, bf16[32,512,256]{2,1,0:T(8,128)(2,1)S(1)} %constant_dynamic-update-slice_fusion), kind=kOutput, calls=%fused_computation.8 | convolution fusion | flops 268435456 | bytes 11010048 | tf_op jit(solution)/shard_map/cik,cjk->cij/dot_general | solution.py:145
  230.6 2.5 %convolution_bitcast_fusion = f32[1,32,32,512]{3,2,1,0:T(8,128)S(1)} fusion(bf16[32,512,256]{2,1,0:T(8,128)(2,1)S(1)} %constant_dynamic-update-slice_fusion, bf16[32,32,128]{2,1,0:T(8,128)(2,1)S(1)} %get-tuple-element.8, bf16[32,32,128]{2,1,0:T(8,128)(2,1)S(1)} %get-tuple-element.7), kind=kOutput, calls=%fused_computation.7 | convolution fusion | flops 269484032 | bytes 11010048 | tf_op jit(solution)/shard_map/cik,cjk->cij/dot_general | solution.py:146
  233.1 2.0 fusion.1
  (16 shorter events, 0.4 us)
Async XLA Ops:
  1.8 17.6 %copy-start = (bf16[4,4,8,4096]{3,2,0,1:T(8,128)(2,1)}, bf16[4,4,8,4096]{3,2,0,1:T(8,128)(2,1)S(1)}, u32[]{:S(2)}) copy-start(bf16[4,4,8,4096]{3,2,0,1:T(8,128)(2,1)S(1)} %copy.23) | copy-start | bytes 3145732
  1.8 59.2 %collective-permute-start.1 = (bf16[4,32,4096]{2,1,0:T(8,128)(2,1)S(1)}, bf16[4,32,4096]{2,1,0:T(8,128)(2,1)}, u32[]{:S(2)}, u32[]{:S(2)}) collective-permute-start(bf16[4,32,4096]{2,1,0:T(8,128)(2,1)S(1)} %bitcast.35), channel_id=1, source_target_pairs={{0,16},{16,32},{32,48},{48,64},{64,80},{80,96},{96,112},{112,128},... | collective-permute-start | bytes 3145736 | tf_op jit(solution)/shard_map/ppermute | solution.py:19
  6.3 54.7 %collective-permute-start = (bf16[3,32,4096]{2,1,0:T(8,128)(2,1)}, bf16[3,32,4096]{2,1,0:T(8,128)(2,1)}, u32[]{:S(2)}, u32[]{:S(2)}) collective-permute-start(bf16[3,32,4096]{2,1,0:T(8,128)(2,1)} %slice.12), channel_id=1, source_target_pairs={{0,32},{16,48},{32,64},{48,80},{64,96},{80,112},{96,128},{112,144}... | collective-permute-start | bytes 2359304 | tf_op jit(solution)/shard_map/ppermute | solution.py:19
  19.4 8.0 %copy-start.1 = (s32[32]{0:T(128)S(1)}, s32[32]{0:T(128)}, u32[]{:S(2)}) copy-start(s32[32]{0:T(128)} %param.3) | copy-start | bytes 388
  129.9 58.1 %collective-permute-start.3 = (bf16[32,32,256]{2,1,0:T(8,128)(2,1)S(1)}, bf16[32,32,256]{2,1,0:T(8,128)(2,1)S(1)}, u32[]{:S(2)}, u32[]{:S(2)}) collective-permute-start(bf16[32,32,256]{2,1,0:T(8,128)(2,1)S(1)} %reshape.119), channel_id=1, source_target_pairs={{0,8},{1,9},{2,10},{3,11},{4,12},{5,13},{6,14},{7,15},{8,0},{9,1},... | collective-permute-start | bytes 1572872 | tf_op jit(solution)/shard_map/ppermute | solution.py:23
  143.7 49.9 %collective-permute-start.2 = (bf16[32,32,256]{2,1,0:T(8,128)(2,1)S(1)}, bf16[32,32,256]{2,1,0:T(8,128)(2,1)}, u32[]{:S(2)}, u32[]{:S(2)}) collective-permute-start(bf16[32,32,256]{2,1,0:T(8,128)(2,1)S(1)} %reshape.119), channel_id=1, source_target_pairs={{0,1},{1,0},{2,3},{3,2},{4,5},{5,4},{6,7},{7,6},{8,9},{9,8},{10,11... | collective-permute-start | bytes 1572872 | tf_op jit(solution)/shard_map/ppermute | solution.py:23
  148.9 48.2 %collective-permute-start.5 = (bf16[32,32,256]{2,1,0:T(8,128)(2,1)S(1)}, bf16[32,32,256]{2,1,0:T(8,128)(2,1)S(1)}, u32[]{:S(2)}, u32[]{:S(2)}) collective-permute-start(bf16[32,32,256]{2,1,0:T(8,128)(2,1)S(1)} %reshape.119), channel_id=1, source_target_pairs={{0,2},{1,3},{2,4},{3,5},{4,6},{5,7},{6,0},{7,1},{8,10},{9,11},{10,... | collective-permute-start | bytes 1572872 | tf_op jit(solution)/shard_map/ppermute | solution.py:23
  151.0 48.0 %collective-permute-start.9 = (bf16[32,32,256]{2,1,0:T(8,128)(2,1)S(1)}, bf16[32,32,256]{2,1,0:T(8,128)(2,1)S(1)}, u32[]{:S(2)}, u32[]{:S(2)}) collective-permute-start(bf16[32,32,256]{2,1,0:T(8,128)(2,1)S(1)} %reshape.119), channel_id=1, source_target_pairs={{0,6},{1,7},{2,0},{3,1},{4,2},{5,3},{6,4},{7,5},{8,14},{9,15},{10,... | collective-permute-start | bytes 1572872 | tf_op jit(solution)/shard_map/ppermute | solution.py:23
  188.0 16.4 %collective-permute-start.7 = (bf16[32,32,256]{2,1,0:T(8,128)(2,1)S(1)}, bf16[32,32,256]{2,1,0:T(8,128)(2,1)S(1)}, u32[]{:S(2)}, u32[]{:S(2)}) collective-permute-start(bf16[32,32,256]{2,1,0:T(8,128)(2,1)S(1)} %collective-permute-done.3), channel_id=1, source_target_pairs={{0,2},{1,3},{2,4},{3,5},{4,6},{5,7},{6,0},{7,1},{8,10},{9,11},{10,... | collective-permute-start | bytes 1572872 | tf_op jit(solution)/shard_map/ppermute | solution.py:23
  190.1 17.0 %collective-permute-start.11 = (bf16[32,32,256]{2,1,0:T(8,128)(2,1)S(1)}, bf16[32,32,256]{2,1,0:T(8,128)(2,1)S(1)}, u32[]{:S(2)}, u32[]{:S(2)}) collective-permute-start(bf16[32,32,256]{2,1,0:T(8,128)(2,1)S(1)} %collective-permute-done.3), channel_id=1, source_target_pairs={{0,6},{1,7},{2,0},{3,1},{4,2},{5,3},{6,4},{7,5},{8,14},{9,15},{10,... | collective-permute-start | bytes 1572872 | tf_op jit(solution)/shard_map/ppermute | solution.py:23
  193.6 15.6 %collective-permute-start.4 = (bf16[32,32,256]{2,1,0:T(8,128)(2,1)S(1)}, bf16[32,32,256]{2,1,0:T(8,128)(2,1)S(1)}, u32[]{:S(2)}, u32[]{:S(2)}) collective-permute-start(bf16[32,32,256]{2,1,0:T(8,128)(2,1)S(1)} %collective-permute-done.3), channel_id=1, source_target_pairs={{0,1},{1,0},{2,3},{3,2},{4,5},{5,4},{6,7},{7,6},{8,9},{9,8},{10,11... | collective-permute-start | bytes 1572872 | tf_op jit(solution)/shard_map/ppermute | solution.py:23
  197.1 14.8 %collective-permute-start.6 = (bf16[32,32,256]{2,1,0:T(8,128)(2,1)S(1)}, bf16[32,32,256]{2,1,0:T(8,128)(2,1)S(1)}, u32[]{:S(2)}, u32[]{:S(2)}) collective-permute-start(bf16[32,32,256]{2,1,0:T(8,128)(2,1)S(1)} %collective-permute-done.5), channel_id=1, source_target_pairs={{0,1},{1,0},{2,3},{3,2},{4,5},{5,4},{6,7},{7,6},{8,9},{9,8},{10,11... | collective-permute-start | bytes 1572872 | tf_op jit(solution)/shard_map/ppermute | solution.py:23
  199.0 15.3 %collective-permute-start.13 = (bf16[32,32,256]{2,1,0:T(8,128)(2,1)S(1)}, bf16[32,32,256]{2,1,0:T(8,128)(2,1)S(1)}, u32[]{:S(2)}, u32[]{:S(2)}) collective-permute-start(bf16[32,32,256]{2,1,0:T(8,128)(2,1)S(1)} %collective-permute-done.5), channel_id=1, source_target_pairs={{0,2},{1,3},{2,4},{3,5},{4,6},{5,7},{6,0},{7,1},{8,10},{9,11},{10,... | collective-permute-start | bytes 1572872 | tf_op jit(solution)/shard_map/ppermute | solution.py:23
  204.4 22.1 %collective-permute-start.8 = (bf16[32,32,256]{2,1,0:T(8,128)(2,1)S(1)}, bf16[32,32,256]{2,1,0:T(8,128)(2,1)S(1)}, u32[]{:S(2)}, u32[]{:S(2)}) collective-permute-start(bf16[32,32,256]{2,1,0:T(8,128)(2,1)S(1)} %collective-permute-done.7), channel_id=1, source_target_pairs={{0,1},{1,0},{2,3},{3,2},{4,5},{5,4},{6,7},{7,6},{8,9},{9,8},{10,11... | collective-permute-start | bytes 1572872 | tf_op jit(solution)/shard_map/ppermute | solution.py:23
  207.2 16.2 %collective-permute-start.15 = (bf16[32,32,256]{2,1,0:T(8,128)(2,1)S(1)}, bf16[32,32,256]{2,1,0:T(8,128)(2,1)S(1)}, u32[]{:S(2)}, u32[]{:S(2)}) collective-permute-start(bf16[32,32,256]{2,1,0:T(8,128)(2,1)S(1)} %collective-permute-done.11), channel_id=1, source_target_pairs={{0,6},{1,7},{2,0},{3,1},{4,2},{5,3},{6,4},{7,5},{8,14},{9,15},{10,... | collective-permute-start | bytes 1572872 | tf_op jit(solution)/shard_map/ppermute | solution.py:23
  209.2 17.4 %collective-permute-start.10 = (bf16[32,32,256]{2,1,0:T(8,128)(2,1)S(1)}, bf16[32,32,256]{2,1,0:T(8,128)(2,1)S(1)}, u32[]{:S(2)}, u32[]{:S(2)}) collective-permute-start(bf16[32,32,256]{2,1,0:T(8,128)(2,1)S(1)} %collective-permute-done.9), channel_id=1, source_target_pairs={{0,1},{1,0},{2,3},{3,2},{4,5},{5,4},{6,7},{7,6},{8,9},{9,8},{10,11... | collective-permute-start | bytes 1572872 | tf_op jit(solution)/shard_map/ppermute | solution.py:23
  211.9 14.8 %collective-permute-start.12 = (bf16[32,32,256]{2,1,0:T(8,128)(2,1)S(1)}, bf16[32,32,256]{2,1,0:T(8,128)(2,1)S(1)}, u32[]{:S(2)}, u32[]{:S(2)}) collective-permute-start(bf16[32,32,256]{2,1,0:T(8,128)(2,1)S(1)} %collective-permute-done.11), channel_id=1, source_target_pairs={{0,1},{1,0},{2,3},{3,2},{4,5},{5,4},{6,7},{7,6},{8,9},{9,8},{10,11... | collective-permute-start | bytes 1572872 | tf_op jit(solution)/shard_map/ppermute | solution.py:23
  214.3 12.5 %collective-permute-start.14 = (bf16[32,32,256]{2,1,0:T(8,128)(2,1)S(1)}, bf16[32,32,256]{2,1,0:T(8,128)(2,1)S(1)}, u32[]{:S(2)}, u32[]{:S(2)}) collective-permute-start(bf16[32,32,256]{2,1,0:T(8,128)(2,1)S(1)} %collective-permute-done.13), channel_id=1, source_target_pairs={{0,1},{1,0},{2,3},{3,2},{4,5},{5,4},{6,7},{7,6},{8,9},{9,8},{10,11... | collective-permute-start | bytes 1572872 | tf_op jit(solution)/shard_map/ppermute | solution.py:23
  223.4 4.7 %collective-permute-start.16 = (bf16[32,32,256]{2,1,0:T(8,128)(2,1)S(1)}, bf16[32,32,256]{2,1,0:T(8,128)(2,1)S(1)}, u32[]{:S(2)}, u32[]{:S(2)}) collective-permute-start(bf16[32,32,256]{2,1,0:T(8,128)(2,1)S(1)} %collective-permute-done.15), channel_id=1, source_target_pairs={{0,1},{1,0},{2,3},{3,2},{4,5},{5,4},{6,7},{7,6},{8,9},{9,8},{10,11... | collective-permute-start | bytes 1572872 | tf_op jit(solution)/shard_map/ppermute | solution.py:23

commit v8 on v7

--- a/solution.py
+++ b/solution.py
@@ -123,14 +123,14 @@
     spec_count = shard_len // NFFT
     history = TAPS - 1
     samples = voltages.reshape(inp_count, spec_count, NFFT).transpose(1, 0, 2).astype(jnp.bfloat16)
-    earlier = []
-    need = history
-    distance = 1
-    while need > 0:
-        take = min(spec_count, need)
-        earlier = [shifted(samples[spec_count - take :], "chan", distance)] + earlier
-        need -= take
-        distance += 1
+    behind = history - spec_count
+    assert 0 <= behind <= spec_count
+    count = lax.axis_size("chan")
+    last = lax.axis_index("chan") == count - 1
+    from_prev = shifted(samples[spec_count - behind :], "chan", 1)
+    from_next = lax.ppermute(samples, "chan", [(i, (i - 1) % count) for i in range(count)])
+    earlier = [jnp.where(last, jnp.zeros_like(from_prev), from_prev), jnp.where(last, jnp.zeros_like(samples), samples)]
+    samples = from_next
     gain = (scales.astype(jnp.float32) * (1.0 / 256.0)).reshape(inp_count, 1)
     filtered = polyphase(earlier + [samples], window_table(), gain, spec_count)
     filtered = filtered.reshape(spec_count * inp_count, NFFT)

time: 236 us -> 230 us (0.975)
  the two profiles are of different devices: /device:TPU:55 before, /device:TPU:7 now
where the time goes in v8:
time: 230 us; the launch traced here: 229 us
  starting transfers between devices  65.2 us (28%)
  waiting for transfers between devices  60.8 us (26%)
  blocking collectives  36.9 us (16%)
  other arithmetic  25.1 us (11%)
  local copies, waits for them, and re-layouts  19.7 us (9%)
  matrix products  13.5 us (6%)
  Pallas kernels  6.69 us (3%)
    ppermute x15, starting transfers between devices, moved(): lax.ppermute(block, 'inp', [(p, mapping(p)) for p in range(lax.axis_size(...  47.7 us
    ppermute x15, waiting for transfers between devices, moved(): lax.ppermute(block, 'inp', [(p, mapping(p)) for p in range(lax.axis_size(...  46 us
    all_to_all x1, blocking collectives, shards(): lax.all_to_all(spectra, 'chan', split_axis=3, concat_axis=0, tiled=True)  36.9 us
    ppermute x1, starting transfers between devices, shards(): lax.ppermute(samples, 'chan', [(i, (i - 1) % count) for i in range(count)])  15.3 us
    ppermute x1, waiting for transfers between devices, shifted(): return lax.ppermute(block, axis, route)  14.8 us
    dot_general x1, matrix products, shards(): jnp.dot(filtered, dft_table(), preferred_element_type=jnp.float32)  8.44 us
    convert_element_type x1, other arithmetic, dft_table(): return lax.optimization_barrier(both.astype(jnp.bfloat16))  8.04 us
    pallas_call x1, Pallas kernels, polyphase(): pl.pallas_call(functools.partial(polyphase_kernel, spec_count), out_shape...  6.69 us
  transfers between devices with their start and end apart: 17, of which 5 were waited for; matrix products, arithmetic and copies ran while one was open for 12% of the time, Pallas kernels for 0%

profile of v8, /device:TPU:7, one launch (start us, length us, event | category | flops | bytes accessed | tf_op | source)
XLA Modules:
  0.0 228.6 jit_solution(6862494807662633241)
XLA Ops:
  0.0 1.7 convert_element_type.54
  1.7 1.1 copy.25
  2.8 15.3 %collective-permute-start.1 = (bf16[4,32,4096]{2,1,0:T(8,128)(2,1)}, bf16[4,32,4096]{2,1,0:T(8,128)(2,1)}, u32[]{:S(2)}, u32[]{:S(2)}) collective-permute-start(bf16[4,32,4096]{2,1,0:T(8,128)(2,1)} %bitcast.33), channel_id=1, source_target_pairs={{0,496},{16,0},{32,16},{48,32},{64,48},{80,64},{96,80},{112,96},{1... | collective-permute-start | bytes 3145736 | tf_op jit(solution)/shard_map/ppermute | solution.py:131
  18.1 2.1 slice.12
  20.2 2.2 collective-permute-start
  22.3 1.8 sine_negate_fusion
  24.1 1.1 fusion.26
  25.2 6.1 %multiply_subtract_fusion = (f32[64,64,1024]{2,1,0:T(8,128)S(1)}, f32[64,64,1024]{2,1,0:T(8,128)S(1)}) fusion(f32[64,1024]{1,0:T(8,128)} %get-tuple-element.11, f32[64,1024]{1,0:T(8,128)S(1)} %get-tuple-element.10, f32[64,1024]{1,0:T(8,128)} %get-tuple-element.12, f32[64,1024]{1,0:T(8,128)S(1)} %get-tuple-element.9), kind=kLoop, calls=%fused_computation.3 | loop fusion | flops 25165824 | bytes 34603008 | tf_op jit(solution)/shard_map/sub | solution.py:49
  31.3 0.0 copy-start
  31.3 8.0 %fusion = bf16[4096,2048]{1,0:T(8,128)(2,1)} fusion(f32[4096,1024]{1,0:T(8,128)S(1)} %bitcast.35, f32[4096,1024]{1,0:T(8,128)S(1)} %bitcast.34), kind=kLoop, calls=%fused_computation.1 | loop fusion | flops 25165824 | bytes 50331648 | tf_op jit(solution)/shard_map/convert_element_type | solution.py:52
  39.4 1.0 broadcast_select_fusion.refs_1_
  40.4 1.3 fusion.21.refs_3_
  41.7 0.7 copy.14.refs_4_
  42.4 14.8 %collective-permute-done = bf16[3,32,4096]{2,1,0:T(8,128)(2,1)} collective-permute-done((bf16[3,32,4096]{2,1,0:T(8,128)(2,1)}, bf16[3,32,4096]{2,1,0:T(8,128)(2,1)}, u32[]{:S(2)}, u32[]{:S(2)}) %collective-permute-start) | collective-permute-done | bytes 786464 | tf_op jit(solution)/shard_map/ppermute | solution.py:19
  57.2 2.1 broadcast_select_fusion.1.refs_0_
  59.2 0.0 collective-permute-done.1.refs_2_
  59.2 6.7 %shard_map.28 = bf16[4,32,4096]{2,1,0:T(8,128)(2,1)} custom-call(bf16[3,32,4096]{2,1,0:T(8,128)(2,1)} %broadcast_select_fusion.1.refs_0_, bf16[4,32,4096]{2,1,0:T(8,128)(2,1)} %broadcast_select_fusion.refs_1_, bf16[4,32,4096]{2,1,0:T(8,128)(2,1)} %collective-permute-done.1.refs_2_, f32[8,4096]{1,0:T(8,128)} %fusion.21.refs_3_, f32[32,1]{1,0:T(8,128)} %copy.14.refs_4_), custom_call_target="tpu_custom_call" | custom-call | tf_op jit(solution)/shard_map/pallas_call | solution.py:69
  65.9 8.4 %convolution_convert_fusion = bf16[128,2048]{1,0:T(8,128)(2,1)S(1)} fusion(bf16[128,4096]{1,0:T(8,128)(2,1)} %bitcast.41, bf16[4096,2048]{1,0:T(8,128)(2,1)} %fusion), kind=kOutput, calls=%fused_computation.6 | convolution fusion | flops 2147745792 | bytes 18350080 | tf_op jit(solution)/shard_map/dot_general | solution.py:137
  74.4 0.4 reshape.118
  74.7 1.9 copy.15
  76.7 2.0 reshape.120
  78.7 36.9 %all_to_all.18 = bf16[32,2,4096]{2,1,0:T(2,128)(2,1)S(1)} all-to-all(bf16[32,2,4096]{2,1,0:T(2,128)(2,1)S(1)} %reshape.120), channel_id=1, replica_groups=mesh['chan'=32,'inp'=16] {'chan'}, dimensions={0} | all-to-all | bytes 1048576 | tf_op jit(solution)/shard_map/all_to_all | solution.py:139
  115.6 1.0 reshape.121
  116.6 3.8 %copy.20 = bf16[4,32,2,32,32]{4,1,2,0,3:T(8,128)(2,1)} copy(bf16[4,32,2,32,32]{1,2,0,4,3:T(2,128)(2,1)S(1)} %bitcast.39) | data formatting | bytes 1048576 | tf_op jit(solution)/shard_map/all_to_all | solution.py:139
  120.4 3.7 %copy.18 = bf16[32,32,2,128]{3,2,1,0:T(2,128)(2,1)S(1)} copy(bf16[32,32,2,128]{0,1,2,3:T(8,128)(2,1)} %bitcast.40) | data formatting | bytes 1048576 | tf_op jit(solution)/shard_map/transpose | solution.py:142
  124.1 0.3 reshape.119
  124.4 9.1 %collective-permute-start.3 = (bf16[32,32,256]{2,1,0:T(8,128)(2,1)S(1)}, bf16[32,32,256]{2,1,0:T(8,128)(2,1)S(1)}, u32[]{:S(2)}, u32[]{:S(2)}) collective-permute-start(bf16[32,32,256]{2,1,0:T(8,128)(2,1)S(1)} %reshape.119), channel_id=1, source_target_pairs={{0,8},{1,9},{2,10},{3,11},{4,12},{5,13},{6,14},{7,15},{8,0},{9,1},... | collective-permute-start | bytes 1572872 | tf_op jit(solution)/shard_map/ppermute | solution.py:23
  133.5 4.0 %collective-permute-start.2 = (bf16[32,32,256]{2,1,0:T(8,128)(2,1)S(1)}, bf16[32,32,256]{2,1,0:T(8,128)(2,1)}, u32[]{:S(2)}, u32[]{:S(2)}) collective-permute-start(bf16[32,32,256]{2,1,0:T(8,128)(2,1)S(1)} %reshape.119), channel_id=1, source_target_pairs={{0,1},{1,0},{2,3},{3,2},{4,5},{5,4},{6,7},{7,6},{8,9},{9,8},{10,11... | collective-permute-start | bytes 1572872 | tf_op jit(solution)/shard_map/ppermute | solution.py:23
  137.5 2.1 collective-permute-start.5
  139.6 3.2 %collective-permute-start.9 = (bf16[32,32,256]{2,1,0:T(8,128)(2,1)S(1)}, bf16[32,32,256]{2,1,0:T(8,128)(2,1)S(1)}, u32[]{:S(2)}, u32[]{:S(2)}) collective-permute-start(bf16[32,32,256]{2,1,0:T(8,128)(2,1)S(1)} %reshape.119), channel_id=1, source_target_pairs={{0,6},{1,7},{2,0},{3,1},{4,2},{5,3},{6,4},{7,5},{8,14},{9,15},{10,... | collective-permute-start | bytes 1572872 | tf_op jit(solution)/shard_map/ppermute | solution.py:23
  142.8 38.2 %collective-permute-done.3 = bf16[32,32,256]{2,1,0:T(8,128)(2,1)S(1)} collective-permute-done((bf16[32,32,256]{2,1,0:T(8,128)(2,1)S(1)}, bf16[32,32,256]{2,1,0:T(8,128)(2,1)S(1)}, u32[]{:S(2)}, u32[]{:S(2)}) %collective-permute-start.3) | collective-permute-done | bytes 524320 | tf_op jit(solution)/shard_map/ppermute | solution.py:23
  181.0 2.1 collective-permute-start.7
  183.1 3.2 %collective-permute-start.11 = (bf16[32,32,256]{2,1,0:T(8,128)(2,1)S(1)}, bf16[32,32,256]{2,1,0:T(8,128)(2,1)S(1)}, u32[]{:S(2)}, u32[]{:S(2)}) collective-permute-start(bf16[32,32,256]{2,1,0:T(8,128)(2,1)S(1)} %collective-permute-done.3), channel_id=1, source_target_pairs={{0,6},{1,7},{2,0},{3,1},{4,2},{5,3},{6,4},{7,5},{8,14},{9,15},{10,... | collective-permute-start | bytes 1572872 | tf_op jit(solution)/shard_map/ppermute | solution.py:23
  186.6 3.7 %collective-permute-start.4 = (bf16[32,32,256]{2,1,0:T(8,128)(2,1)S(1)}, bf16[32,32,256]{2,1,0:T(8,128)(2,1)S(1)}, u32[]{:S(2)}, u32[]{:S(2)}) collective-permute-start(bf16[32,32,256]{2,1,0:T(8,128)(2,1)S(1)} %collective-permute-done.3), channel_id=1, source_target_pairs={{0,1},{1,0},{2,3},{3,2},{4,5},{5,4},{6,7},{7,6},{8,9},{9,8},{10,11... | collective-permute-start | bytes 1572872 | tf_op jit(solution)/shard_map/ppermute | solution.py:23
  190.3 0.1 fusion.33
  190.4 0.0 collective-permute-done.5
  190.4 1.9 collective-permute-start.6
  192.3 3.5 %collective-permute-start.13 = (bf16[32,32,256]{2,1,0:T(8,128)(2,1)S(1)}, bf16[32,32,256]{2,1,0:T(8,128)(2,1)S(1)}, u32[]{:S(2)}, u32[]{:S(2)}) collective-permute-start(bf16[32,32,256]{2,1,0:T(8,128)(2,1)S(1)} %collective-permute-done.5), channel_id=1, source_target_pairs={{0,2},{1,3},{2,4},{3,5},{4,6},{5,7},{6,0},{7,1},{8,10},{9,11},{10,... | collective-permute-start | bytes 1572872 | tf_op jit(solution)/shard_map/ppermute | solution.py:23
  195.8 0.9 broadcast_in_dim.56
  196.8 1.1 constant_dynamic-update-slice_fusion.14
  197.9 2.7 %collective-permute-start.8 = (bf16[32,32,256]{2,1,0:T(8,128)(2,1)S(1)}, bf16[32,32,256]{2,1,0:T(8,128)(2,1)S(1)}, u32[]{:S(2)}, u32[]{:S(2)}) collective-permute-start(bf16[32,32,256]{2,1,0:T(8,128)(2,1)S(1)} %collective-permute-done.7), channel_id=1, source_target_pairs={{0,1},{1,0},{2,3},{3,2},{4,5},{5,4},{6,7},{7,6},{8,9},{9,8},{10,11... | collective-permute-start | bytes 1572872 | tf_op jit(solution)/shard_map/ppermute | solution.py:23
  200.6 0.0 collective-permute-done.11
  200.6 2.0 collective-permute-start.15
  202.7 0.0 collective-permute-done.4
  202.7 2.2 collective-permute-start.10
  204.9 0.1 constant_dynamic-update-slice_fusion.12
  205.0 0.0 collective-permute-done.6
  205.0 2.1 collective-permute-start.12
  207.1 0.1 collective-permute-done.13
  207.2 3.2 %collective-permute-start.14 = (bf16[32,32,256]{2,1,0:T(8,128)(2,1)S(1)}, bf16[32,32,256]{2,1,0:T(8,128)(2,1)S(1)}, u32[]{:S(2)}, u32[]{:S(2)}) collective-permute-start(bf16[32,32,256]{2,1,0:T(8,128)(2,1)S(1)} %collective-permute-done.13), channel_id=1, source_target_pairs={{0,1},{1,0},{2,3},{3,2},{4,5},{5,4},{6,7},{7,6},{8,9},{9,8},{10,11... | collective-permute-start | bytes 1572872 | tf_op jit(solution)/shard_map/ppermute | solution.py:23
  210.5 0.1 constant_dynamic-update-slice_fusion.10
  210.6 6.7 %collective-permute-done.15 = bf16[32,32,256]{2,1,0:T(8,128)(2,1)S(1)} collective-permute-done((bf16[32,32,256]{2,1,0:T(8,128)(2,1)S(1)}, bf16[32,32,256]{2,1,0:T(8,128)(2,1)S(1)}, u32[]{:S(2)}, u32[]{:S(2)}) %collective-permute-start.15) | collective-permute-done | bytes 524320 | tf_op jit(solution)/shard_map/ppermute | solution.py:23
  217.3 2.7 %collective-permute-start.16 = (bf16[32,32,256]{2,1,0:T(8,128)(2,1)S(1)}, bf16[32,32,256]{2,1,0:T(8,128)(2,1)S(1)}, u32[]{:S(2)}, u32[]{:S(2)}) collective-permute-start(bf16[32,32,256]{2,1,0:T(8,128)(2,1)S(1)} %collective-permute-done.15), channel_id=1, source_target_pairs={{0,1},{1,0},{2,3},{3,2},{4,5},{5,4},{6,7},{7,6},{8,9},{9,8},{10,11... | collective-permute-start | bytes 1572872 | tf_op jit(solution)/shard_map/ppermute | solution.py:23
  220.0 0.1 constant_dynamic-update-slice_fusion.8
  220.1 0.0 collective-permute-done.10
  220.1 0.1 constant_dynamic-update-slice_fusion.6
  220.2 0.0 collective-permute-done.12
  220.2 0.1 constant_dynamic-update-slice_fusion.4
  220.3 0.0 collective-permute-done.14
  220.4 0.1 constant_dynamic-update-slice_fusion.2
  220.5 1.0 collective-permute-done.16
  221.6 2.5 %convolution_bitcast_fusion.1 = f32[1,32,32,512]{3,2,1,0:T(8,128)S(1)} fusion(bf16[32,32,256]{2,1,0:T(8,128)(2,1)S(1)} %reshape.119, bf16[32,512,256]{2,1,0:T(8,128)(2,1)S(1)} %constant_dynamic-update-slice_fusion), kind=kOutput, calls=%fused_computation.8 | convolution fusion | flops 268435456 | bytes 11010048 | tf_op jit(solution)/shard_map/cik,cjk->cij/dot_general | solution.py:145
  224.1 2.5 %convolution_bitcast_fusion = f32[1,32,32,512]{3,2,1,0:T(8,128)S(1)} fusion(bf16[32,512,256]{2,1,0:T(8,128)(2,1)S(1)} %constant_dynamic-update-slice_fusion, bf16[32,32,128]{2,1,0:T(8,128)(2,1)S(1)} %get-tuple-element.8, bf16[32,32,128]{2,1,0:T(8,128)(2,1)S(1)} %get-tuple-element.7), kind=kOutput, calls=%fused_computation.7 | convolution fusion | flops 269484032 | bytes 11010048 | tf_op jit(solution)/shard_map/cik,cjk->cij/dot_general | solution.py:146
  226.6 2.0 fusion.1
  (16 shorter events, 0.4 us)
Async XLA Ops:
  2.8 56.5 %collective-permute-start.1 = (bf16[4,32,4096]{2,1,0:T(8,128)(2,1)}, bf16[4,32,4096]{2,1,0:T(8,128)(2,1)}, u32[]{:S(2)}, u32[]{:S(2)}) collective-permute-start(bf16[4,32,4096]{2,1,0:T(8,128)(2,1)} %bitcast.33), channel_id=1, source_target_pairs={{0,496},{16,0},{32,16},{48,32},{64,48},{80,64},{96,80},{112,96},{1... | collective-permute-start | bytes 3145736 | tf_op jit(solution)/shard_map/ppermute | solution.py:131
  20.2 37.0 %collective-permute-start = (bf16[3,32,4096]{2,1,0:T(8,128)(2,1)}, bf16[3,32,4096]{2,1,0:T(8,128)(2,1)}, u32[]{:S(2)}, u32[]{:S(2)}) collective-permute-start(bf16[3,32,4096]{2,1,0:T(8,128)(2,1)} %slice.12), channel_id=1, source_target_pairs={{0,16},{16,32},{32,48},{48,64},{64,80},{80,96},{96,112},{112,128},... | collective-permute-start | bytes 2359304 | tf_op jit(solution)/shard_map/ppermute | solution.py:19
  31.3 10.4 %copy-start = (s32[32]{0:T(128)S(1)}, s32[32]{0:T(128)}, u32[]{:S(2)}) copy-start(s32[32]{0:T(128)} %param.3) | copy-start | bytes 388
  124.4 56.6 %collective-permute-start.3 = (bf16[32,32,256]{2,1,0:T(8,128)(2,1)S(1)}, bf16[32,32,256]{2,1,0:T(8,128)(2,1)S(1)}, u32[]{:S(2)}, u32[]{:S(2)}) collective-permute-start(bf16[32,32,256]{2,1,0:T(8,128)(2,1)S(1)} %reshape.119), channel_id=1, source_target_pairs={{0,8},{1,9},{2,10},{3,11},{4,12},{5,13},{6,14},{7,15},{8,0},{9,1},... | collective-permute-start | bytes 1572872 | tf_op jit(solution)/shard_map/ppermute | solution.py:23
  133.5 53.0 %collective-permute-start.2 = (bf16[32,32,256]{2,1,0:T(8,128)(2,1)S(1)}, bf16[32,32,256]{2,1,0:T(8,128)(2,1)}, u32[]{:S(2)}, u32[]{:S(2)}) collective-permute-start(bf16[32,32,256]{2,1,0:T(8,128)(2,1)S(1)} %reshape.119), channel_id=1, source_target_pairs={{0,1},{1,0},{2,3},{3,2},{4,5},{5,4},{6,7},{7,6},{8,9},{9,8},{10,11... | collective-permute-start | bytes 1572872 | tf_op jit(solution)/shard_map/ppermute | solution.py:23
  137.5 52.8 %collective-permute-start.5 = (bf16[32,32,256]{2,1,0:T(8,128)(2,1)S(1)}, bf16[32,32,256]{2,1,0:T(8,128)(2,1)S(1)}, u32[]{:S(2)}, u32[]{:S(2)}) collective-permute-start(bf16[32,32,256]{2,1,0:T(8,128)(2,1)S(1)} %reshape.119), channel_id=1, source_target_pairs={{0,2},{1,3},{2,4},{3,5},{4,6},{5,7},{6,0},{7,1},{8,10},{9,11},{10,... | collective-permute-start | bytes 1572872 | tf_op jit(solution)/shard_map/ppermute | solution.py:23
  139.6 52.7 %collective-permute-start.9 = (bf16[32,32,256]{2,1,0:T(8,128)(2,1)S(1)}, bf16[32,32,256]{2,1,0:T(8,128)(2,1)S(1)}, u32[]{:S(2)}, u32[]{:S(2)}) collective-permute-start(bf16[32,32,256]{2,1,0:T(8,128)(2,1)S(1)} %reshape.119), channel_id=1, source_target_pairs={{0,6},{1,7},{2,0},{3,1},{4,2},{5,3},{6,4},{7,5},{8,14},{9,15},{10,... | collective-permute-start | bytes 1572872 | tf_op jit(solution)/shard_map/ppermute | solution.py:23
  181.0 16.9 %collective-permute-start.7 = (bf16[32,32,256]{2,1,0:T(8,128)(2,1)S(1)}, bf16[32,32,256]{2,1,0:T(8,128)(2,1)S(1)}, u32[]{:S(2)}, u32[]{:S(2)}) collective-permute-start(bf16[32,32,256]{2,1,0:T(8,128)(2,1)S(1)} %collective-permute-done.3), channel_id=1, source_target_pairs={{0,2},{1,3},{2,4},{3,5},{4,6},{5,7},{6,0},{7,1},{8,10},{9,11},{10,... | collective-permute-start | bytes 1572872 | tf_op jit(solution)/shard_map/ppermute | solution.py:23
  183.1 17.5 %collective-permute-start.11 = (bf16[32,32,256]{2,1,0:T(8,128)(2,1)S(1)}, bf16[32,32,256]{2,1,0:T(8,128)(2,1)S(1)}, u32[]{:S(2)}, u32[]{:S(2)}) collective-permute-start(bf16[32,32,256]{2,1,0:T(8,128)(2,1)S(1)} %collective-permute-done.3), channel_id=1, source_target_pairs={{0,6},{1,7},{2,0},{3,1},{4,2},{5,3},{6,4},{7,5},{8,14},{9,15},{10,... | collective-permute-start | bytes 1572872 | tf_op jit(solution)/shard_map/ppermute | solution.py:23
  186.6 16.1 %collective-permute-start.4 = (bf16[32,32,256]{2,1,0:T(8,128)(2,1)S(1)}, bf16[32,32,256]{2,1,0:T(8,128)(2,1)S(1)}, u32[]{:S(2)}, u32[]{:S(2)}) collective-permute-start(bf16[32,32,256]{2,1,0:T(8,128)(2,1)S(1)} %collective-permute-done.3), channel_id=1, source_target_pairs={{0,1},{1,0},{2,3},{3,2},{4,5},{5,4},{6,7},{7,6},{8,9},{9,8},{10,11... | collective-permute-start | bytes 1572872 | tf_op jit(solution)/shard_map/ppermute | solution.py:23
  190.4 14.6 %collective-permute-start.6 = (bf16[32,32,256]{2,1,0:T(8,128)(2,1)S(1)}, bf16[32,32,256]{2,1,0:T(8,128)(2,1)S(1)}, u32[]{:S(2)}, u32[]{:S(2)}) collective-permute-start(bf16[32,32,256]{2,1,0:T(8,128)(2,1)S(1)} %collective-permute-done.5), channel_id=1, source_target_pairs={{0,1},{1,0},{2,3},{3,2},{4,5},{5,4},{6,7},{7,6},{8,9},{9,8},{10,11... | collective-permute-start | bytes 1572872 | tf_op jit(solution)/shard_map/ppermute | solution.py:23
  192.3 14.9 %collective-permute-start.13 = (bf16[32,32,256]{2,1,0:T(8,128)(2,1)S(1)}, bf16[32,32,256]{2,1,0:T(8,128)(2,1)S(1)}, u32[]{:S(2)}, u32[]{:S(2)}) collective-permute-start(bf16[32,32,256]{2,1,0:T(8,128)(2,1)S(1)} %collective-permute-done.5), channel_id=1, source_target_pairs={{0,2},{1,3},{2,4},{3,5},{4,6},{5,7},{6,0},{7,1},{8,10},{9,11},{10,... | collective-permute-start | bytes 1572872 | tf_op jit(solution)/shard_map/ppermute | solution.py:23
  197.9 22.1 %collective-permute-start.8 = (bf16[32,32,256]{2,1,0:T(8,128)(2,1)S(1)}, bf16[32,32,256]{2,1,0:T(8,128)(2,1)S(1)}, u32[]{:S(2)}, u32[]{:S(2)}) collective-permute-start(bf16[32,32,256]{2,1,0:T(8,128)(2,1)S(1)} %collective-permute-done.7), channel_id=1, source_target_pairs={{0,1},{1,0},{2,3},{3,2},{4,5},{5,4},{6,7},{7,6},{8,9},{9,8},{10,11... | collective-permute-start | bytes 1572872 | tf_op jit(solution)/shard_map/ppermute | solution.py:23
  200.6 16.6 %collective-permute-start.15 = (bf16[32,32,256]{2,1,0:T(8,128)(2,1)S(1)}, bf16[32,32,256]{2,1,0:T(8,128)(2,1)S(1)}, u32[]{:S(2)}, u32[]{:S(2)}) collective-permute-start(bf16[32,32,256]{2,1,0:T(8,128)(2,1)S(1)} %collective-permute-done.11), channel_id=1, source_target_pairs={{0,6},{1,7},{2,0},{3,1},{4,2},{5,3},{6,4},{7,5},{8,14},{9,15},{10,... | collective-permute-start | bytes 1572872 | tf_op jit(solution)/shard_map/ppermute | solution.py:23
  202.7 17.4 %collective-permute-start.10 = (bf16[32,32,256]{2,1,0:T(8,128)(2,1)S(1)}, bf16[32,32,256]{2,1,0:T(8,128)(2,1)S(1)}, u32[]{:S(2)}, u32[]{:S(2)}) collective-permute-start(bf16[32,32,256]{2,1,0:T(8,128)(2,1)S(1)} %collective-permute-done.9), channel_id=1, source_target_pairs={{0,1},{1,0},{2,3},{3,2},{4,5},{5,4},{6,7},{7,6},{8,9},{9,8},{10,11... | collective-permute-start | bytes 1572872 | tf_op jit(solution)/shard_map/ppermute | solution.py:23
  205.0 15.2 %collective-permute-start.12 = (bf16[32,32,256]{2,1,0:T(8,128)(2,1)S(1)}, bf16[32,32,256]{2,1,0:T(8,128)(2,1)S(1)}, u32[]{:S(2)}, u32[]{:S(2)}) collective-permute-start(bf16[32,32,256]{2,1,0:T(8,128)(2,1)S(1)} %collective-permute-done.11), channel_id=1, source_target_pairs={{0,1},{1,0},{2,3},{3,2},{4,5},{5,4},{6,7},{7,6},{8,9},{9,8},{10,11... | collective-permute-start | bytes 1572872 | tf_op jit(solution)/shard_map/ppermute | solution.py:23
  207.2 13.1 %collective-permute-start.14 = (bf16[32,32,256]{2,1,0:T(8,128)(2,1)S(1)}, bf16[32,32,256]{2,1,0:T(8,128)(2,1)S(1)}, u32[]{:S(2)}, u32[]{:S(2)}) collective-permute-start(bf16[32,32,256]{2,1,0:T(8,128)(2,1)S(1)} %collective-permute-done.13), channel_id=1, source_target_pairs={{0,1},{1,0},{2,3},{3,2},{4,5},{5,4},{6,7},{7,6},{8,9},{9,8},{10,11... | collective-permute-start | bytes 1572872 | tf_op jit(solution)/shard_map/ppermute | solution.py:23
  217.3 4.2 %collective-permute-start.16 = (bf16[32,32,256]{2,1,0:T(8,128)(2,1)S(1)}, bf16[32,32,256]{2,1,0:T(8,128)(2,1)S(1)}, u32[]{:S(2)}, u32[]{:S(2)}) collective-permute-start(bf16[32,32,256]{2,1,0:T(8,128)(2,1)S(1)} %collective-permute-done.15), channel_id=1, source_target_pairs={{0,1},{1,0},{2,3},{3,2},{4,5},{5,4},{6,7},{7,6},{8,9},{9,8},{10,11... | collective-permute-start | bytes 1572872 | tf_op jit(solution)/shard_map/ppermute | solution.py:23

commit v9 on v8

--- a/solution.py
+++ b/solution.py
@@ -79,7 +79,7 @@
     )(*pieces, window, gain)
 
 
-def gather_inputs(own):
+def gather_inputs(own, cross):
     assert lax.axis_size("inp") == 16
     me = lax.axis_index("inp")
     zh, xx, core = me // 8, (me // 2) % 4, me % 2
@@ -87,16 +87,9 @@
     def at(z, x, c):
         return z * 8 + (x % 4) * 2 + c
 
-    def unpack(p):
-        return p // 8, (p // 2) % 4, p % 2
+    def x_step(d):
+        return lambda p: at(p // 8, (p // 2) % 4 + d, p % 2)
 
-    def x_step(d):
-        def f(p):
-            z, x, c = unpack(p)
-            return at(z, x + d, c)
-        return f
-
-    cross = moved(own, lambda p: p ^ 8)
     from_left = moved((own, cross), x_step(1))
     from_right = moved((own, cross), x_step(-1))
     far_own = moved(from_left[0], x_step(1))
@@ -136,12 +129,16 @@
     filtered = filtered.reshape(spec_count * inp_count, NFFT)
     spectra = jnp.dot(filtered, dft_table(), preferred_element_type=jnp.float32).astype(jnp.bfloat16)
     spectra = spectra.reshape(spec_count, inp_count, 2, CHANS)
-    local_block = lax.all_to_all(spectra, "chan", split_axis=3, concat_axis=0, tiled=True)
-    spec_total = local_block.shape[0]
-    chan_count = local_block.shape[3]
-    own_rows = local_block.transpose(3, 1, 2, 0).reshape(chan_count, inp_count, 2 * spec_total)
+    crossed = moved(spectra, lambda p: p ^ 8)
+
+    def corner_turn(block):
+        turned = lax.all_to_all(block, "chan", split_axis=3, concat_axis=0, tiled=True)
+        return turned.transpose(3, 1, 2, 0).reshape(turned.shape[3], inp_count, 2 * turned.shape[0])
+
+    own_rows = corner_turn(spectra)
+    spec_total = own_rows.shape[2] // 2
     swapped = jnp.concatenate([own_rows[..., spec_total:], -own_rows[..., :spec_total]], axis=-1)
-    piece = gather_inputs(own_rows)
+    piece = gather_inputs(own_rows, corner_turn(crossed))
     real_part = jnp.einsum("cik,cjk->cij", own_rows, piece, preferred_element_type=jnp.float32)
     imag_part = jnp.einsum("cik,cjk->cij", swapped, piece, preferred_element_type=jnp.float32)
     result = jnp.stack([real_part, imag_part]) * (1.0 / spec_total)

time: 230 us -> 263 us (1.14)
  blocking collectives: 36.9 us -> 0 us
  starting transfers between devices: 65.2 us -> 101 us
  local copies, waits for them, and re-layouts: 19.7 us -> 39.8 us
  waiting for transfers between devices: 60.8 us -> 74.8 us
    all_to_all x1 -> x0, blocking collectives: 36.9 us -> none  [shards(): lax.all_to_all(spectra, 'chan', split_axis=3, concat_axis=0, tiled=True)]
    all_to_all x0 -> x2, starting transfers between devices: none -> 35.8 us  [corner_turn(): lax.all_to_all(block, 'chan', split_axis=3, concat_axis=0, tiled=True)]
    all_to_all x0 -> x2, waiting for transfers between devices: none -> 33.2 us  [corner_turn(): lax.all_to_all(block, 'chan', split_axis=3, concat_axis=0, tiled=True)]
    ppermute x15, waiting for transfers between devices: 46 us -> 26.9 us  [moved(): lax.ppermute(block, 'inp', [(p, mapping(p)) for p in range(lax.axis_size(...]
    unnamed x4 -> x6, local copies, waits for them, and re-layouts: 3.03 us -> 11.6 us
    all_to_all x1 -> x2, local copies, waits for them, and re-layouts: 3.82 us -> 7.63 us  [corner_turn(): lax.all_to_all(block, 'chan', split_axis=3, concat_axis=0, tiled=True)]
    transpose x1 -> x2, local copies, waits for them, and re-layouts: 3.65 us -> 7.31 us  [corner_turn(): turned.transpose(3, 1, 2, 0)]
  transfers between devices with their start and end apart: 17 -> 19, of which waited for: 5 -> 5; matrix products, arithmetic and copies ran while one was open for 12% -> 21% of each run, Pallas kernels for 0% -> 0%
where the time goes in v9:
time: 263 us; the launch traced here: 261 us
  starting transfers between devices  101 us (38%)
  waiting for transfers between devices  74.8 us (28%)
  local copies, waits for them, and re-layouts  39.8 us (15%)
  other arithmetic  25.2 us (10%)
  matrix products  13.5 us (5%)
  Pallas kernels  6.69 us (3%)
    ppermute x15, starting transfers between devices, moved(): lax.ppermute(block, 'inp', [(p, mapping(p)) for p in range(lax.axis_size(...  47.2 us
    all_to_all x2, starting transfers between devices, corner_turn(): lax.all_to_all(block, 'chan', split_axis=3, concat_axis=0, tiled=True)  35.8 us
    all_to_all x2, waiting for transfers between devices, corner_turn(): lax.all_to_all(block, 'chan', split_axis=3, concat_axis=0, tiled=True)  33.2 us
    ppermute x15, waiting for transfers between devices, moved(): lax.ppermute(block, 'inp', [(p, mapping(p)) for p in range(lax.axis_size(...  26.9 us
    ppermute x1, starting transfers between devices, shards(): lax.ppermute(samples, 'chan', [(i, (i - 1) % count) for i in range(count)])  15.3 us
    ppermute x1, waiting for transfers between devices, shifted(): return lax.ppermute(block, axis, route)  14.7 us
    unnamed x6, local copies, waits for them, and re-layouts  11.6 us
    dot_general x1, matrix products, shards(): jnp.dot(filtered, dft_table(), preferred_element_type=jnp.float32)  8.44 us
  transfers between devices with their start and end apart: 19, of which 5 were waited for; matrix products, arithmetic and copies ran while one was open for 21% of the time, Pallas kernels for 0%

profile of v9, /device:TPU:7, one launch (start us, length us, event | category | flops | bytes accessed | tf_op | source)
XLA Modules:
  0.0 261.3 jit_solution(11983476691087704228)
XLA Ops:
  0.0 1.7 convert_element_type.54
  1.7 1.1 copy.46
  2.8 15.3 %collective-permute-start.1 = (bf16[4,32,4096]{2,1,0:T(8,128)(2,1)}, bf16[4,32,4096]{2,1,0:T(8,128)(2,1)}, u32[]{:S(2)}, u32[]{:S(2)}) collective-permute-start(bf16[4,32,4096]{2,1,0:T(8,128)(2,1)} %bitcast.42), channel_id=1, source_target_pairs={{0,496},{16,0},{32,16},{48,32},{64,48},{80,64},{96,80},{112,96},{1... | collective-permute-start | bytes 3145736 | tf_op jit(solution)/shard_map/ppermute | solution.py:124
  18.1 2.1 slice.12
  20.2 2.2 collective-permute-start
  22.3 1.8 sine_negate_fusion
  24.1 1.1 fusion.26
  25.2 6.1 %multiply_subtract_fusion = (f32[64,64,1024]{2,1,0:T(8,128)S(1)}, f32[64,64,1024]{2,1,0:T(8,128)S(1)}) fusion(f32[64,1024]{1,0:T(8,128)} %get-tuple-element.11, f32[64,1024]{1,0:T(8,128)S(1)} %get-tuple-element.10, f32[64,1024]{1,0:T(8,128)} %get-tuple-element.12, f32[64,1024]{1,0:T(8,128)S(1)} %get-tuple-element.9), kind=kLoop, calls=%fused_computation.3 | loop fusion | flops 25165824 | bytes 34603008 | tf_op jit(solution)/shard_map/sub | solution.py:49
  31.4 8.0 %fusion = bf16[4096,2048]{1,0:T(8,128)(2,1)} fusion(f32[4096,1024]{1,0:T(8,128)S(1)} %bitcast.44, f32[4096,1024]{1,0:T(8,128)S(1)} %bitcast.43), kind=kLoop, calls=%fused_computation.1 | loop fusion | flops 25165824 | bytes 50331648 | tf_op jit(solution)/shard_map/convert_element_type | solution.py:52
  39.4 1.0 broadcast_select_fusion.refs_1_
  40.5 1.3 fusion.21.refs_3_
  41.7 0.7 copy.28.refs_4_
  42.4 14.7 %collective-permute-done = bf16[3,32,4096]{2,1,0:T(8,128)(2,1)} collective-permute-done((bf16[3,32,4096]{2,1,0:T(8,128)(2,1)}, bf16[3,32,4096]{2,1,0:T(8,128)(2,1)}, u32[]{:S(2)}, u32[]{:S(2)}) %collective-permute-start) | collective-permute-done | bytes 786464 | tf_op jit(solution)/shard_map/ppermute | solution.py:19
  57.2 2.1 broadcast_select_fusion.1.refs_0_
  59.2 6.7 %shard_map.28 = bf16[4,32,4096]{2,1,0:T(8,128)(2,1)} custom-call(bf16[3,32,4096]{2,1,0:T(8,128)(2,1)} %broadcast_select_fusion.1.refs_0_, bf16[4,32,4096]{2,1,0:T(8,128)(2,1)} %broadcast_select_fusion.refs_1_, bf16[4,32,4096]{2,1,0:T(8,128)(2,1)} %collective-permute-done.1.refs_2_, f32[8,4096]{1,0:T(8,128)} %fusion.21.refs_3_, f32[32,1]{1,0:T(8,128)} %copy.28.refs_4_), custom_call_target="tpu_custom_call" | custom-call | tf_op jit(solution)/shard_map/pallas_call | solution.py:69
  65.9 8.4 %convolution_convert_fusion = bf16[128,2048]{1,0:T(8,128)(2,1)S(1)} fusion(bf16[128,4096]{1,0:T(8,128)(2,1)} %bitcast.53, bf16[4096,2048]{1,0:T(8,128)(2,1)} %fusion), kind=kOutput, calls=%fused_computation.6 | convolution fusion | flops 2147745792 | bytes 18350080 | tf_op jit(solution)/shard_map/dot_general | solution.py:130
  74.4 0.4 reshape.121
  74.8 1.9 copy.29
  76.7 2.7 %reshape.124 = bf16[32,2,4096]{2,1,0:T(2,128)(2,1)} reshape(bf16[1024,4,2,32]{3,2,1,0:T(2,128)(2,1)S(1)} %bitcast.48) | data formatting | bytes 1048576
  79.4 8.0 %all-to-all-start = ((bf16[32,2,4096]{2,1,0:T(2,128)(2,1)}), bf16[32,2,4096]{2,1,0:T(2,128)(2,1)}, u32[]{:S(2)}, u32[]{:S(2)}) async-start(bf16[32,2,4096]{2,1,0:T(2,128)(2,1)} %reshape.124), calls=%async_computation | async-start | bytes 1048576 | tf_op jit(solution)/shard_map/all_to_all | solution.py:135
  87.4 0.1 copy.33
  87.5 9.0 %collective-permute-start.3 = (bf16[4,32,2,1024]{3,1,2,0:T(8,128)(2,1)S(1)}, bf16[4,32,2,1024]{3,1,2,0:T(8,128)(2,1)S(1)}, u32[]{:S(2)}, u32[]{:S(2)}) collective-permute-start(bf16[4,32,2,1024]{3,1,2,0:T(8,128)(2,1)S(1)} %copy.33), channel_id=1, source_target_pairs={{0,8},{1,9},{2,10},{3,11},{4,12},{5,13},{6,14},{7,15},{8,0},{9,1},... | collective-permute-start | bytes 1572872 | tf_op jit(solution)/shard_map/ppermute | solution.py:23
  96.5 20.6 %collective-permute-done.3 = bf16[4,32,2,1024]{3,1,2,0:T(8,128)(2,1)S(1)} collective-permute-done((bf16[4,32,2,1024]{3,1,2,0:T(8,128)(2,1)S(1)}, bf16[4,32,2,1024]{3,1,2,0:T(8,128)(2,1)S(1)}, u32[]{:S(2)}, u32[]{:S(2)}) %collective-permute-start.3) | collective-permute-done | bytes 524320 | tf_op jit(solution)/shard_map/ppermute | solution.py:23
  117.1 1.6 copy.34
  118.7 2.7 %reshape.126 = bf16[32,2,4096]{2,1,0:T(2,128)(2,1)} reshape(bf16[1024,4,2,32]{3,2,1,0:T(2,128)(2,1)S(1)} %bitcast.47) | data formatting | bytes 1048576
  121.4 26.0 %all-to-all-done = bf16[32,2,4096]{2,1,0:T(2,128)(2,1)} async-done(((bf16[32,2,4096]{2,1,0:T(2,128)(2,1)}), bf16[32,2,4096]{2,1,0:T(2,128)(2,1)}, u32[]{:S(2)}, u32[]{:S(2)}) %all-to-all-start) | async-done | bytes 524320 | tf_op jit(solution)/shard_map/all_to_all | solution.py:135
  147.4 27.9 %all-to-all-start.1 = ((bf16[32,2,4096]{2,1,0:T(2,128)(2,1)}), bf16[32,2,4096]{2,1,0:T(2,128)(2,1)S(1)}, u32[]{:S(2)}, u32[]{:S(2)}) async-start(bf16[32,2,4096]{2,1,0:T(2,128)(2,1)} %reshape.126), calls=%async_computation.1 | async-start | bytes 1048576 | tf_op jit(solution)/shard_map/all_to_all | solution.py:135
  175.3 5.1 %reshape.125 = bf16[1024,4,2,32]{3,2,1,0:T(2,128)(2,1)S(1)} reshape(bf16[32,2,4096]{2,1,0:T(2,128)(2,1)} %all-to-all-done) | data formatting | bytes 1048576
  180.4 3.8 %copy.39 = bf16[4,32,2,32,32]{4,1,2,0,3:T(8,128)(2,1)} copy(bf16[4,32,2,32,32]{1,2,0,4,3:T(2,128)(2,1)S(1)} %bitcast.49) | data formatting | bytes 1048576 | tf_op jit(solution)/shard_map/all_to_all | solution.py:135
  184.3 3.7 %copy.32 = bf16[32,32,2,128]{3,2,1,0:T(2,128)(2,1)S(1)} copy(bf16[32,32,2,128]{0,1,2,3:T(8,128)(2,1)} %bitcast.50) | data formatting | bytes 1048576 | tf_op jit(solution)/shard_map/transpose | solution.py:136
  187.9 0.3 reshape.122
  188.3 3.7 %collective-permute-start.2 = (bf16[32,32,256]{2,1,0:T(8,128)(2,1)S(1)}, bf16[32,32,256]{2,1,0:T(8,128)(2,1)}, u32[]{:S(2)}, u32[]{:S(2)}) collective-permute-start(bf16[32,32,256]{2,1,0:T(8,128)(2,1)S(1)} %reshape.122), channel_id=1, source_target_pairs={{0,1},{1,0},{2,3},{3,2},{4,5},{5,4},{6,7},{7,6},{8,9},{9,8},{10,11... | collective-permute-start | bytes 1572872 | tf_op jit(solution)/shard_map/ppermute | solution.py:23
  192.0 2.1 collective-permute-start.5
  194.1 3.2 %collective-permute-start.9 = (bf16[32,32,256]{2,1,0:T(8,128)(2,1)S(1)}, bf16[32,32,256]{2,1,0:T(8,128)(2,1)}, u32[]{:S(2)}, u32[]{:S(2)}) collective-permute-start(bf16[32,32,256]{2,1,0:T(8,128)(2,1)S(1)} %reshape.122), channel_id=1, source_target_pairs={{0,6},{1,7},{2,0},{3,1},{4,2},{5,3},{6,4},{7,5},{8,14},{9,15},{10,... | collective-permute-start | bytes 1572872 | tf_op jit(solution)/shard_map/ppermute | solution.py:23
  197.3 7.2 %all-to-all-done.1 = bf16[32,2,4096]{2,1,0:T(2,128)(2,1)S(1)} async-done(((bf16[32,2,4096]{2,1,0:T(2,128)(2,1)}), bf16[32,2,4096]{2,1,0:T(2,128)(2,1)S(1)}, u32[]{:S(2)}, u32[]{:S(2)}) %all-to-all-start.1) | async-done | bytes 524320 | tf_op jit(solution)/shard_map/all_to_all | solution.py:135
  204.4 1.0 reshape.127
  205.5 3.8 %copy.41 = bf16[4,32,2,32,32]{4,1,2,0,3:T(8,128)(2,1)} copy(bf16[4,32,2,32,32]{1,2,0,4,3:T(2,128)(2,1)S(1)} %bitcast.51) | data formatting | bytes 1048576 | tf_op jit(solution)/shard_map/all_to_all | solution.py:135
  209.3 3.7 %copy.37 = bf16[32,32,2,128]{3,2,1,0:T(2,128)(2,1)S(1)} copy(bf16[32,32,2,128]{0,1,2,3:T(8,128)(2,1)} %bitcast.52) | data formatting | bytes 1048576 | tf_op jit(solution)/shard_map/transpose | solution.py:136
  213.0 0.3 reshape.123
  213.3 2.1 collective-permute-start.7
  215.4 3.2 %collective-permute-start.11 = (bf16[32,32,256]{2,1,0:T(8,128)(2,1)S(1)}, bf16[32,32,256]{2,1,0:T(8,128)(2,1)S(1)}, u32[]{:S(2)}, u32[]{:S(2)}) collective-permute-start(bf16[32,32,256]{2,1,0:T(8,128)(2,1)S(1)} %reshape.123), channel_id=1, source_target_pairs={{0,6},{1,7},{2,0},{3,1},{4,2},{5,3},{6,4},{7,5},{8,14},{9,15},{10,... | collective-permute-start | bytes 1572872 | tf_op jit(solution)/shard_map/ppermute | solution.py:23
  218.8 4.3 %collective-permute-start.4 = (bf16[32,32,256]{2,1,0:T(8,128)(2,1)S(1)}, bf16[32,32,256]{2,1,0:T(8,128)(2,1)S(1)}, u32[]{:S(2)}, u32[]{:S(2)}) collective-permute-start(bf16[32,32,256]{2,1,0:T(8,128)(2,1)S(1)} %reshape.123), channel_id=1, source_target_pairs={{0,1},{1,0},{2,3},{3,2},{4,5},{5,4},{6,7},{7,6},{8,9},{9,8},{10,11... | collective-permute-start | bytes 1572872 | tf_op jit(solution)/shard_map/ppermute | solution.py:23
  223.1 0.1 fusion.33
  223.2 1.9 collective-permute-start.6
  225.2 3.3 %collective-permute-start.13 = (bf16[32,32,256]{2,1,0:T(8,128)(2,1)}, bf16[32,32,256]{2,1,0:T(8,128)(2,1)S(1)}, u32[]{:S(2)}, u32[]{:S(2)}) collective-permute-start(bf16[32,32,256]{2,1,0:T(8,128)(2,1)} %collective-permute-done.5), channel_id=1, source_target_pairs={{0,2},{1,3},{2,4},{3,5},{4,6},{5,7},{6,0},{7,1},{8,10},{9,11},{10,... | collective-permute-start | bytes 1572872 | tf_op jit(solution)/shard_map/ppermute | solution.py:23
  228.5 0.9 broadcast_in_dim.56
  229.5 1.1 constant_dynamic-update-slice_fusion.14
  230.6 2.7 %collective-permute-start.8 = (bf16[32,32,256]{2,1,0:T(8,128)(2,1)S(1)}, bf16[32,32,256]{2,1,0:T(8,128)(2,1)S(1)}, u32[]{:S(2)}, u32[]{:S(2)}) collective-permute-start(bf16[32,32,256]{2,1,0:T(8,128)(2,1)S(1)} %collective-permute-done.7), channel_id=1, source_target_pairs={{0,1},{1,0},{2,3},{3,2},{4,5},{5,4},{6,7},{7,6},{8,9},{9,8},{10,11... | collective-permute-start | bytes 1572872 | tf_op jit(solution)/shard_map/ppermute | solution.py:23
  233.3 2.0 collective-permute-start.15
  235.3 2.2 collective-permute-start.10
  237.5 0.1 constant_dynamic-update-slice_fusion.12
  237.6 1.1 constant_dynamic-update-slice_fusion.11
  238.7 2.1 collective-permute-start.12
  240.8 2.7 %collective-permute-start.14 = (bf16[32,32,256]{2,1,0:T(8,128)(2,1)S(1)}, bf16[32,32,256]{2,1,0:T(8,128)(2,1)S(1)}, u32[]{:S(2)}, u32[]{:S(2)}) collective-permute-start(bf16[32,32,256]{2,1,0:T(8,128)(2,1)S(1)} %collective-permute-done.13), channel_id=1, source_target_pairs={{0,1},{1,0},{2,3},{3,2},{4,5},{5,4},{6,7},{7,6},{8,9},{9,8},{10,11... | collective-permute-start | bytes 1572872 | tf_op jit(solution)/shard_map/ppermute | solution.py:23
  243.5 0.1 constant_dynamic-update-slice_fusion.10
  243.6 6.3 %collective-permute-done.15 = bf16[32,32,256]{2,1,0:T(8,128)(2,1)S(1)} collective-permute-done((bf16[32,32,256]{2,1,0:T(8,128)(2,1)S(1)}, bf16[32,32,256]{2,1,0:T(8,128)(2,1)S(1)}, u32[]{:S(2)}, u32[]{:S(2)}) %collective-permute-start.15) | collective-permute-done | bytes 524320 | tf_op jit(solution)/shard_map/ppermute | solution.py:23
  249.9 2.7 %collective-permute-start.16 = (bf16[32,32,256]{2,1,0:T(8,128)(2,1)S(1)}, bf16[32,32,256]{2,1,0:T(8,128)(2,1)S(1)}, u32[]{:S(2)}, u32[]{:S(2)}) collective-permute-start(bf16[32,32,256]{2,1,0:T(8,128)(2,1)S(1)} %collective-permute-done.15), channel_id=1, source_target_pairs={{0,1},{1,0},{2,3},{3,2},{4,5},{5,4},{6,7},{7,6},{8,9},{9,8},{10,11... | collective-permute-start | bytes 1572872 | tf_op jit(solution)/shard_map/ppermute | solution.py:23
  252.6 0.1 constant_dynamic-update-slice_fusion.8
  252.7 1.1 constant_dynamic-update-slice_fusion.7
  253.9 0.1 constant_dynamic-update-slice_fusion.4
  254.0 0.1 constant_dynamic-update-slice_fusion.2
  254.2 2.5 convolution_bitcast_fusion.1
  256.8 2.5 convolution_bitcast_fusion
  259.3 2.0 fusion.1
  (26 shorter events, 0.4 us)
Async XLA Ops:
  2.8 56.5 %collective-permute-start.1 = (bf16[4,32,4096]{2,1,0:T(8,128)(2,1)}, bf16[4,32,4096]{2,1,0:T(8,128)(2,1)}, u32[]{:S(2)}, u32[]{:S(2)}) collective-permute-start(bf16[4,32,4096]{2,1,0:T(8,128)(2,1)} %bitcast.42), channel_id=1, source_target_pairs={{0,496},{16,0},{32,16},{48,32},{64,48},{80,64},{96,80},{112,96},{1... | collective-permute-start | bytes 3145736 | tf_op jit(solution)/shard_map/ppermute | solution.py:124
  20.2 37.0 %collective-permute-start = (bf16[3,32,4096]{2,1,0:T(8,128)(2,1)}, bf16[3,32,4096]{2,1,0:T(8,128)(2,1)}, u32[]{:S(2)}, u32[]{:S(2)}) collective-permute-start(bf16[3,32,4096]{2,1,0:T(8,128)(2,1)} %slice.12), channel_id=1, source_target_pairs={{0,16},{16,32},{32,48},{48,64},{64,80},{80,96},{96,112},{112,128},... | collective-permute-start | bytes 2359304 | tf_op jit(solution)/shard_map/ppermute | solution.py:19
  31.4 10.4 %copy-start = (s32[32]{0:T(128)S(1)}, s32[32]{0:T(128)}, u32[]{:S(2)}) copy-start(s32[32]{0:T(128)} %param.3) | copy-start | bytes 388
  79.4 68.1 %all-to-all-start = ((bf16[32,2,4096]{2,1,0:T(2,128)(2,1)}), bf16[32,2,4096]{2,1,0:T(2,128)(2,1)}, u32[]{:S(2)}, u32[]{:S(2)}) async-start(bf16[32,2,4096]{2,1,0:T(2,128)(2,1)} %reshape.124), calls=%async_computation | async-start | bytes 1048576 | tf_op jit(solution)/shard_map/all_to_all | solution.py:135
  87.5 29.6 %collective-permute-start.3 = (bf16[4,32,2,1024]{3,1,2,0:T(8,128)(2,1)S(1)}, bf16[4,32,2,1024]{3,1,2,0:T(8,128)(2,1)S(1)}, u32[]{:S(2)}, u32[]{:S(2)}) collective-permute-start(bf16[4,32,2,1024]{3,1,2,0:T(8,128)(2,1)S(1)} %copy.33), channel_id=1, source_target_pairs={{0,8},{1,9},{2,10},{3,11},{4,12},{5,13},{6,14},{7,15},{8,0},{9,1},... | collective-permute-start | bytes 1572872 | tf_op jit(solution)/shard_map/ppermute | solution.py:23
  147.4 57.0 %all-to-all-start.1 = ((bf16[32,2,4096]{2,1,0:T(2,128)(2,1)}), bf16[32,2,4096]{2,1,0:T(2,128)(2,1)S(1)}, u32[]{:S(2)}, u32[]{:S(2)}) async-start(bf16[32,2,4096]{2,1,0:T(2,128)(2,1)} %reshape.126), calls=%async_computation.1 | async-start | bytes 1048576 | tf_op jit(solution)/shard_map/all_to_all | solution.py:135
  188.3 30.6 %collective-permute-start.2 = (bf16[32,32,256]{2,1,0:T(8,128)(2,1)S(1)}, bf16[32,32,256]{2,1,0:T(8,128)(2,1)}, u32[]{:S(2)}, u32[]{:S(2)}) collective-permute-start(bf16[32,32,256]{2,1,0:T(8,128)(2,1)S(1)} %reshape.122), channel_id=1, source_target_pairs={{0,1},{1,0},{2,3},{3,2},{4,5},{5,4},{6,7},{7,6},{8,9},{9,8},{10,11... | collective-permute-start | bytes 1572872 | tf_op jit(solution)/shard_map/ppermute | solution.py:23
  192.0 31.2 %collective-permute-start.5 = (bf16[32,32,256]{2,1,0:T(8,128)(2,1)S(1)}, bf16[32,32,256]{2,1,0:T(8,128)(2,1)}, u32[]{:S(2)}, u32[]{:S(2)}) collective-permute-start(bf16[32,32,256]{2,1,0:T(8,128)(2,1)S(1)} %reshape.122), channel_id=1, source_target_pairs={{0,2},{1,3},{2,4},{3,5},{4,6},{5,7},{6,0},{7,1},{8,10},{9,11},{10,... | collective-permute-start | bytes 1572872 | tf_op jit(solution)/shard_map/ppermute | solution.py:23
  194.1 31.1 %collective-permute-start.9 = (bf16[32,32,256]{2,1,0:T(8,128)(2,1)S(1)}, bf16[32,32,256]{2,1,0:T(8,128)(2,1)}, u32[]{:S(2)}, u32[]{:S(2)}) collective-permute-start(bf16[32,32,256]{2,1,0:T(8,128)(2,1)S(1)} %reshape.122), channel_id=1, source_target_pairs={{0,6},{1,7},{2,0},{3,1},{4,2},{5,3},{6,4},{7,5},{8,14},{9,15},{10,... | collective-permute-start | bytes 1572872 | tf_op jit(solution)/shard_map/ppermute | solution.py:23
  213.3 17.3 %collective-permute-start.7 = (bf16[32,32,256]{2,1,0:T(8,128)(2,1)S(1)}, bf16[32,32,256]{2,1,0:T(8,128)(2,1)S(1)}, u32[]{:S(2)}, u32[]{:S(2)}) collective-permute-start(bf16[32,32,256]{2,1,0:T(8,128)(2,1)S(1)} %reshape.123), channel_id=1, source_target_pairs={{0,2},{1,3},{2,4},{3,5},{4,6},{5,7},{6,0},{7,1},{8,10},{9,11},{10,... | collective-permute-start | bytes 1572872 | tf_op jit(solution)/shard_map/ppermute | solution.py:23
  215.4 17.9 %collective-permute-start.11 = (bf16[32,32,256]{2,1,0:T(8,128)(2,1)S(1)}, bf16[32,32,256]{2,1,0:T(8,128)(2,1)S(1)}, u32[]{:S(2)}, u32[]{:S(2)}) collective-permute-start(bf16[32,32,256]{2,1,0:T(8,128)(2,1)S(1)} %reshape.123), channel_id=1, source_target_pairs={{0,6},{1,7},{2,0},{3,1},{4,2},{5,3},{6,4},{7,5},{8,14},{9,15},{10,... | collective-permute-start | bytes 1572872 | tf_op jit(solution)/shard_map/ppermute | solution.py:23
  218.8 16.5 %collective-permute-start.4 = (bf16[32,32,256]{2,1,0:T(8,128)(2,1)S(1)}, bf16[32,32,256]{2,1,0:T(8,128)(2,1)S(1)}, u32[]{:S(2)}, u32[]{:S(2)}) collective-permute-start(bf16[32,32,256]{2,1,0:T(8,128)(2,1)S(1)} %reshape.123), channel_id=1, source_target_pairs={{0,1},{1,0},{2,3},{3,2},{4,5},{5,4},{6,7},{7,6},{8,9},{9,8},{10,11... | collective-permute-start | bytes 1572872 | tf_op jit(solution)/shard_map/ppermute | solution.py:23
  223.2 15.5 %collective-permute-start.6 = (bf16[32,32,256]{2,1,0:T(8,128)(2,1)}, bf16[32,32,256]{2,1,0:T(8,128)(2,1)S(1)}, u32[]{:S(2)}, u32[]{:S(2)}) collective-permute-start(bf16[32,32,256]{2,1,0:T(8,128)(2,1)} %collective-permute-done.5), channel_id=1, source_target_pairs={{0,1},{1,0},{2,3},{3,2},{4,5},{5,4},{6,7},{7,6},{8,9},{9,8},{10,11... | collective-permute-start | bytes 1572872 | tf_op jit(solution)/shard_map/ppermute | solution.py:23
  225.2 15.7 %collective-permute-start.13 = (bf16[32,32,256]{2,1,0:T(8,128)(2,1)}, bf16[32,32,256]{2,1,0:T(8,128)(2,1)S(1)}, u32[]{:S(2)}, u32[]{:S(2)}) collective-permute-start(bf16[32,32,256]{2,1,0:T(8,128)(2,1)} %collective-permute-done.5), channel_id=1, source_target_pairs={{0,2},{1,3},{2,4},{3,5},{4,6},{5,7},{6,0},{7,1},{8,10},{9,11},{10,... | collective-permute-start | bytes 1572872 | tf_op jit(solution)/shard_map/ppermute | solution.py:23
  230.6 22.1 %collective-permute-start.8 = (bf16[32,32,256]{2,1,0:T(8,128)(2,1)S(1)}, bf16[32,32,256]{2,1,0:T(8,128)(2,1)S(1)}, u32[]{:S(2)}, u32[]{:S(2)}) collective-permute-start(bf16[32,32,256]{2,1,0:T(8,128)(2,1)S(1)} %collective-permute-done.7), channel_id=1, source_target_pairs={{0,1},{1,0},{2,3},{3,2},{4,5},{5,4},{6,7},{7,6},{8,9},{9,8},{10,11... | collective-permute-start | bytes 1572872 | tf_op jit(solution)/shard_map/ppermute | solution.py:23
  233.3 16.6 %collective-permute-start.15 = (bf16[32,32,256]{2,1,0:T(8,128)(2,1)S(1)}, bf16[32,32,256]{2,1,0:T(8,128)(2,1)S(1)}, u32[]{:S(2)}, u32[]{:S(2)}) collective-permute-start(bf16[32,32,256]{2,1,0:T(8,128)(2,1)S(1)} %collective-permute-done.11), channel_id=1, source_target_pairs={{0,6},{1,7},{2,0},{3,1},{4,2},{5,3},{6,4},{7,5},{8,14},{9,15},{10,... | collective-permute-start | bytes 1572872 | tf_op jit(solution)/shard_map/ppermute | solution.py:23
  235.3 18.5 %collective-permute-start.10 = (bf16[32,32,256]{2,1,0:T(8,128)(2,1)}, bf16[32,32,256]{2,1,0:T(8,128)(2,1)S(1)}, u32[]{:S(2)}, u32[]{:S(2)}) collective-permute-start(bf16[32,32,256]{2,1,0:T(8,128)(2,1)} %collective-permute-done.9), channel_id=1, source_target_pairs={{0,1},{1,0},{2,3},{3,2},{4,5},{5,4},{6,7},{7,6},{8,9},{9,8},{10,11... | collective-permute-start | bytes 1572872 | tf_op jit(solution)/shard_map/ppermute | solution.py:23
  238.7 15.2 %collective-permute-start.12 = (bf16[32,32,256]{2,1,0:T(8,128)(2,1)S(1)}, bf16[32,32,256]{2,1,0:T(8,128)(2,1)S(1)}, u32[]{:S(2)}, u32[]{:S(2)}) collective-permute-start(bf16[32,32,256]{2,1,0:T(8,128)(2,1)S(1)} %collective-permute-done.11), channel_id=1, source_target_pairs={{0,1},{1,0},{2,3},{3,2},{4,5},{5,4},{6,7},{7,6},{8,9},{9,8},{10,11... | collective-permute-start | bytes 1572872 | tf_op jit(solution)/shard_map/ppermute | solution.py:23
  240.8 13.2 %collective-permute-start.14 = (bf16[32,32,256]{2,1,0:T(8,128)(2,1)S(1)}, bf16[32,32,256]{2,1,0:T(8,128)(2,1)S(1)}, u32[]{:S(2)}, u32[]{:S(2)}) collective-permute-start(bf16[32,32,256]{2,1,0:T(8,128)(2,1)S(1)} %collective-permute-done.13), channel_id=1, source_target_pairs={{0,1},{1,0},{2,3},{3,2},{4,5},{5,4},{6,7},{7,6},{8,9},{9,8},{10,11... | collective-permute-start | bytes 1572872 | tf_op jit(solution)/shard_map/ppermute | solution.py:23
  249.9 4.2 %collective-permute-start.16 = (bf16[32,32,256]{2,1,0:T(8,128)(2,1)S(1)}, bf16[32,32,256]{2,1,0:T(8,128)(2,1)S(1)}, u32[]{:S(2)}, u32[]{:S(2)}) collective-permute-start(bf16[32,32,256]{2,1,0:T(8,128)(2,1)S(1)} %collective-permute-done.15), channel_id=1, source_target_pairs={{0,1},{1,0},{2,3},{3,2},{4,5},{5,4},{6,7},{7,6},{8,9},{9,8},{10,11... | collective-permute-start | bytes 1572872 | tf_op jit(solution)/shard_map/ppermute | solution.py:23

commit v10 on v8

--- a/solution.py
+++ b/solution.py
@@ -96,25 +96,24 @@
             return at(z, x + d, c)
         return f
 
+    width = own.shape[1]
+
+    def place(gathered, blocks, dz, dc):
+        for block, dx in zip(blocks, (0, -1, 1, 2)):
+            slot = at((zh + dz) % 2, xx + dx + 4, (core + dc) % 2)
+            gathered = lax.dynamic_update_slice(gathered, block, (0, slot * width, 0))
+        return gathered
+
     cross = moved(own, lambda p: p ^ 8)
-    from_left = moved((own, cross), x_step(1))
-    from_right = moved((own, cross), x_step(-1))
-    far_own = moved(from_left[0], x_step(1))
-    far_cross = moved(from_right[1], x_step(-1))
-    mine = [
-        (0, 0, own), (1, 0, cross),
-        (0, -1, from_left[0]), (1, -1, from_left[1]),
-        (0, 1, from_right[0]), (1, 1, from_right[1]),
-        (0, 2, far_own), (1, 2, far_cross),
-    ]
-    other = moved(tuple(b for _, _, b in mine), lambda p: p ^ 1)
-    width = own.shape[1]
+    left_own = moved(own, x_step(1))
+    right_own = moved(own, x_step(-1))
+    near = (own, left_own, right_own, moved(left_own, x_step(1)))
     gathered = jnp.zeros((own.shape[0], 16 * width, own.shape[2]), own.dtype)
-    for (dz, dx, block), far in zip(mine, other):
-        for dc, piece in ((0, block), (1, far)):
-            place = at((zh + dz) % 2, xx + dx + 4, (core + dc) % 2)
-            gathered = lax.dynamic_update_slice(gathered, piece, (0, place * width, 0))
-    return gathered
+    gathered = place(place(gathered, near, 0, 0), moved(near, lambda p: p ^ 1), 0, 1)
+    gathered, cross = lax.optimization_barrier((gathered, cross))
+    right_cross = moved(cross, x_step(-1))
+    far = (cross, moved(cross, x_step(1)), right_cross, moved(right_cross, x_step(-1)))
+    return place(place(gathered, far, 1, 0), moved(far, lambda p: p ^ 1), 1, 1)
 
 
 def shards(voltages, scales):

time: 230 us -> 258 us (1.12)
  local copies, waits for them, and re-layouts: 19.7 us -> 34.8 us
  matrix products: 13.5 us -> 20.3 us
  waiting for transfers between devices: 60.8 us -> 65.3 us
    dynamic_update_slice x16, local copies, waits for them, and re-layouts: 1.8 us -> 13.7 us  [place(): gathered = lax.dynamic_update_slice(gathered, block, (0, slot * width, 0))]
    ppermute x15, waiting for transfers between devices: 46 us -> 50.6 us  [moved(): lax.ppermute(block, 'inp', [(p, mapping(p)) for p in range(lax.axis_size(...]
    dot_general x1, matrix products: 2.52 us -> 5.9 us  [shards(): jnp.einsum('cik,cjk->cij', own_rows, piece, preferred_element_type=jnp.fl...]
    dot_general x1, matrix products: 2.54 us -> 5.92 us  [shards(): jnp.einsum('cik,cjk->cij', swapped, piece, preferred_element_type=jnp.flo...]
    broadcast_in_dim x1, local copies, waits for them, and re-layouts: 0.94 us -> 4.19 us  [gather_inputs(): gathered = jnp.zeros((own.shape[0], 16 * width, own.shape[2]), own.dtype)]
  transfers between devices with their start and end apart: 17 -> 17, of which waited for: 5 -> 5; matrix products, arithmetic and copies ran while one was open for 12% -> 16% of each run, Pallas kernels for 0% -> 0%
where the time goes in v10:
time: 258 us; the launch traced here: 257 us
  starting transfers between devices  67.7 us (26%)
  waiting for transfers between devices  65.3 us (25%)
  blocking collectives  36.9 us (14%)
  local copies, waits for them, and re-layouts  34.8 us (13%)
  other arithmetic  25.1 us (10%)
  matrix products  20.3 us (8%)
  Pallas kernels  6.69 us (3%)
    ppermute x15, waiting for transfers between devices, moved(): lax.ppermute(block, 'inp', [(p, mapping(p)) for p in range(lax.axis_size(...  50.6 us
    ppermute x15, starting transfers between devices, moved(): lax.ppermute(block, 'inp', [(p, mapping(p)) for p in range(lax.axis_size(...  50.2 us
    all_to_all x1, blocking collectives, shards(): lax.all_to_all(spectra, 'chan', split_axis=3, concat_axis=0, tiled=True)  36.9 us
    ppermute x1, starting transfers between devices, shards(): lax.ppermute(samples, 'chan', [(i, (i - 1) % count) for i in range(count)])  15.3 us
    ppermute x1, waiting for transfers between devices, shifted(): return lax.ppermute(block, axis, route)  14.8 us
    dynamic_update_slice x16, local copies, waits for them, and re-layouts, place(): gathered = lax.dynamic_update_slice(gathered, block, (0, slot * width, 0))  13.7 us
    dot_general x1, matrix products, shards(): jnp.dot(filtered, dft_table(), preferred_element_type=jnp.float32)  8.44 us
    convert_element_type x1, other arithmetic, dft_table(): return lax.optimization_barrier(both.astype(jnp.bfloat16))  8.04 us
  transfers between devices with their start and end apart: 17, of which 5 were waited for; matrix products, arithmetic and copies ran while one was open for 16% of the time, Pallas kernels for 0%

profile of v10, /device:TPU:7, one launch (start us, length us, event | category | flops | bytes accessed | tf_op | source)
XLA Modules:
  0.0 257.3 jit_solution(7617408893075129171)
XLA Ops:
  0.0 1.7 convert_element_type.54
  1.7 1.1 copy.25
  2.8 15.3 %collective-permute-start.1 = (bf16[4,32,4096]{2,1,0:T(8,128)(2,1)}, bf16[4,32,4096]{2,1,0:T(8,128)(2,1)}, u32[]{:S(2)}, u32[]{:S(2)}) collective-permute-start(bf16[4,32,4096]{2,1,0:T(8,128)(2,1)} %bitcast.33), channel_id=1, source_target_pairs={{0,496},{16,0},{32,16},{48,32},{64,48},{80,64},{96,80},{112,96},{1... | collective-permute-start | bytes 3145736 | tf_op jit(solution)/shard_map/ppermute | solution.py:130
  18.1 2.1 slice.12
  20.2 2.2 collective-permute-start
  22.3 1.8 sine_negate_fusion
  24.1 1.1 fusion.26
  25.2 6.1 %multiply_subtract_fusion = (f32[64,64,1024]{2,1,0:T(8,128)S(1)}, f32[64,64,1024]{2,1,0:T(8,128)S(1)}) fusion(f32[64,1024]{1,0:T(8,128)} %get-tuple-element.15, f32[64,1024]{1,0:T(8,128)S(1)} %get-tuple-element.14, f32[64,1024]{1,0:T(8,128)} %get-tuple-element.16, f32[64,1024]{1,0:T(8,128)S(1)} %get-tuple-element.13), kind=kLoop, calls=%fused_computation.3 | loop fusion | flops 25165824 | bytes 34603008 | tf_op jit(solution)/shard_map/sub | solution.py:49
  31.3 8.0 %fusion = bf16[4096,2048]{1,0:T(8,128)(2,1)} fusion(f32[4096,1024]{1,0:T(8,128)S(1)} %bitcast.35, f32[4096,1024]{1,0:T(8,128)S(1)} %bitcast.34), kind=kLoop, calls=%fused_computation.1 | loop fusion | flops 25165824 | bytes 50331648 | tf_op jit(solution)/shard_map/convert_element_type | solution.py:52
  39.4 1.0 broadcast_select_fusion.refs_1_
  40.4 1.3 fusion.21.refs_3_
  41.7 0.7 copy.14.refs_4_
  42.4 14.8 %collective-permute-done = bf16[3,32,4096]{2,1,0:T(8,128)(2,1)} collective-permute-done((bf16[3,32,4096]{2,1,0:T(8,128)(2,1)}, bf16[3,32,4096]{2,1,0:T(8,128)(2,1)}, u32[]{:S(2)}, u32[]{:S(2)}) %collective-permute-start) | collective-permute-done | bytes 786464 | tf_op jit(solution)/shard_map/ppermute | solution.py:19
  57.2 2.1 broadcast_select_fusion.1.refs_0_
  59.2 6.7 %shard_map.28 = bf16[4,32,4096]{2,1,0:T(8,128)(2,1)} custom-call(bf16[3,32,4096]{2,1,0:T(8,128)(2,1)} %broadcast_select_fusion.1.refs_0_, bf16[4,32,4096]{2,1,0:T(8,128)(2,1)} %broadcast_select_fusion.refs_1_, bf16[4,32,4096]{2,1,0:T(8,128)(2,1)} %collective-permute-done.1.refs_2_, f32[8,4096]{1,0:T(8,128)} %fusion.21.refs_3_, f32[32,1]{1,0:T(8,128)} %copy.14.refs_4_), custom_call_target="tpu_custom_call" | custom-call | tf_op jit(solution)/shard_map/pallas_call | solution.py:69
  65.9 8.4 %convolution_convert_fusion = bf16[128,2048]{1,0:T(8,128)(2,1)S(1)} fusion(bf16[128,4096]{1,0:T(8,128)(2,1)} %bitcast.41, bf16[4096,2048]{1,0:T(8,128)(2,1)} %fusion), kind=kOutput, calls=%fused_computation.6 | convolution fusion | flops 2147745792 | bytes 18350080 | tf_op jit(solution)/shard_map/dot_general | solution.py:136
  74.4 0.4 reshape.118
  74.7 1.9 copy.15
  76.7 2.0 reshape.120
  78.7 36.9 %all_to_all.18 = bf16[32,2,4096]{2,1,0:T(2,128)(2,1)S(1)} all-to-all(bf16[32,2,4096]{2,1,0:T(2,128)(2,1)S(1)} %reshape.120), channel_id=1, replica_groups=mesh['chan'=32,'inp'=16] {'chan'}, dimensions={0} | all-to-all | bytes 1048576 | tf_op jit(solution)/shard_map/all_to_all | solution.py:138
  115.6 1.0 reshape.121
  116.6 3.8 %copy.20 = bf16[4,32,2,32,32]{4,1,2,0,3:T(8,128)(2,1)} copy(bf16[4,32,2,32,32]{1,2,0,4,3:T(2,128)(2,1)S(1)} %bitcast.39) | data formatting | bytes 1048576 | tf_op jit(solution)/shard_map/all_to_all | solution.py:138
  120.4 3.7 %copy.18 = bf16[32,32,2,128]{3,2,1,0:T(2,128)(2,1)S(1)} copy(bf16[32,32,2,128]{0,1,2,3:T(8,128)(2,1)} %bitcast.40) | data formatting | bytes 1048576 | tf_op jit(solution)/shard_map/transpose | solution.py:141
  124.1 0.3 reshape.119
  124.4 2.1 collective-permute-start.2
  126.6 3.2 %collective-permute-start.3 = (bf16[32,32,256]{2,1,0:T(8,128)(2,1)S(1)}, bf16[32,32,256]{2,1,0:T(8,128)(2,1)S(1)}, u32[]{:S(2)}, u32[]{:S(2)}) collective-permute-start(bf16[32,32,256]{2,1,0:T(8,128)(2,1)S(1)} %reshape.119), channel_id=1, source_target_pairs={{0,6},{1,7},{2,0},{3,1},{4,2},{5,3},{6,4},{7,5},{8,14},{9,15},{10,... | collective-permute-start | bytes 1572872 | tf_op jit(solution)/shard_map/ppermute | solution.py:23
  129.7 8.2 %collective-permute-done.2 = bf16[32,32,256]{2,1,0:T(8,128)(2,1)S(1)} collective-permute-done((bf16[32,32,256]{2,1,0:T(8,128)(2,1)S(1)}, bf16[32,32,256]{2,1,0:T(8,128)(2,1)S(1)}, u32[]{:S(2)}, u32[]{:S(2)}) %collective-permute-start.2) | collective-permute-done | bytes 524320 | tf_op jit(solution)/shard_map/ppermute | solution.py:23
  137.9 3.3 %collective-permute-start.4 = (bf16[32,32,256]{2,1,0:T(8,128)(2,1)S(1)}, bf16[32,32,256]{2,1,0:T(8,128)(2,1)S(1)}, u32[]{:S(2)}, u32[]{:S(2)}) collective-permute-start(bf16[32,32,256]{2,1,0:T(8,128)(2,1)S(1)} %collective-permute-done.2), channel_id=1, source_target_pairs={{0,2},{1,3},{2,4},{3,5},{4,6},{5,7},{6,0},{7,1},{8,10},{9,11},{10,... | collective-permute-start | bytes 1572872 | tf_op jit(solution)/shard_map/ppermute | solution.py:23
  141.2 4.9 %collective-permute-start.5 = (bf16[32,32,256]{2,1,0:T(8,128)(2,1)S(1)}, bf16[32,32,256]{2,1,0:T(8,128)(2,1)S(1)}, u32[]{:S(2)}, u32[]{:S(2)}) collective-permute-start(bf16[32,32,256]{2,1,0:T(8,128)(2,1)S(1)} %reshape.119), channel_id=1, source_target_pairs={{0,1},{1,0},{2,3},{3,2},{4,5},{5,4},{6,7},{7,6},{8,9},{9,8},{10,11... | collective-permute-start | bytes 1572872 | tf_op jit(solution)/shard_map/ppermute | solution.py:23
  146.4 9.1 %collective-permute-start.9 = (bf16[32,32,256]{2,1,0:T(8,128)(2,1)S(1)}, bf16[32,32,256]{2,1,0:T(8,128)(2,1)S(1)}, u32[]{:S(2)}, u32[]{:S(2)}) collective-permute-start(bf16[32,32,256]{2,1,0:T(8,128)(2,1)S(1)} %reshape.119), channel_id=1, source_target_pairs={{0,8},{1,9},{2,10},{3,11},{4,12},{5,13},{6,14},{7,15},{8,0},{9,1},... | collective-permute-start | bytes 1572872 | tf_op jit(solution)/shard_map/ppermute | solution.py:23
  155.4 2.4 collective-permute-start.6
  157.8 4.2 %broadcast_in_dim.56 = bf16[32,512,256]{2,1,0:T(8,128)(2,1)} broadcast(bf16[]{:T(256)} %constant.230.clone.1), dimensions={} | broadcast | bytes 8388610 | tf_op jit(solution)/shard_map/broadcast_in_dim | solution.py:111
  162.0 0.8 constant_dynamic-update-slice_fusion.15
  162.8 2.1 collective-permute-start.7
  165.0 0.9 constant_dynamic-update-slice_fusion.14
  165.8 2.2 collective-permute-start.8
  168.0 0.9 constant_dynamic-update-slice_fusion.13
  168.9 0.8 constant_dynamic-update-slice_fusion.12
  169.7 0.8 constant_dynamic-update-slice_fusion.11
  170.6 0.8 constant_dynamic-update-slice_fusion.10
  171.4 0.9 constant_dynamic-update-slice_fusion.9
  172.3 0.8 constant_dynamic-update-slice_fusion.8
  173.1 30.2 %collective-permute-done.9 = bf16[32,32,256]{2,1,0:T(8,128)(2,1)S(1)} collective-permute-done((bf16[32,32,256]{2,1,0:T(8,128)(2,1)S(1)}, bf16[32,32,256]{2,1,0:T(8,128)(2,1)S(1)}, u32[]{:S(2)}, u32[]{:S(2)}) %collective-permute-start.9) | collective-permute-done | bytes 524320 | tf_op jit(solution)/shard_map/ppermute | solution.py:23
  203.3 2.0 collective-permute-start.11
  205.3 4.5 %collective-permute-start.10 = (bf16[32,32,256]{2,1,0:T(8,128)(2,1)S(1)}, bf16[32,32,256]{2,1,0:T(8,128)(2,1)S(1)}, u32[]{:S(2)}, u32[]{:S(2)}) collective-permute-start(bf16[32,32,256]{2,1,0:T(8,128)(2,1)S(1)} %collective-permute-done.9), channel_id=1, source_target_pairs={{0,2},{1,3},{2,4},{3,5},{4,6},{5,7},{6,0},{7,1},{8,10},{9,11},{10,... | collective-permute-start | bytes 1572872 | tf_op jit(solution)/shard_map/ppermute | solution.py:23
  209.8 9.2 %collective-permute-done.11 = bf16[32,32,256]{2,1,0:T(8,128)(2,1)S(1)} collective-permute-done((bf16[32,32,256]{2,1,0:T(8,128)(2,1)S(1)}, bf16[32,32,256]{2,1,0:T(8,128)(2,1)S(1)}, u32[]{:S(2)}, u32[]{:S(2)}) %collective-permute-start.11) | collective-permute-done | bytes 524320 | tf_op jit(solution)/shard_map/ppermute | solution.py:23
  219.0 1.9 collective-permute-start.12
  221.0 3.7 %collective-permute-start.13 = (bf16[32,32,256]{2,1,0:T(8,128)(2,1)S(1)}, bf16[32,32,256]{2,1,0:T(8,128)(2,1)S(1)}, u32[]{:S(2)}, u32[]{:S(2)}) collective-permute-start(bf16[32,32,256]{2,1,0:T(8,128)(2,1)S(1)} %collective-permute-done.9), channel_id=1, source_target_pairs={{0,1},{1,0},{2,3},{3,2},{4,5},{5,4},{6,7},{7,6},{8,9},{9,8},{10,11... | collective-permute-start | bytes 1572872 | tf_op jit(solution)/shard_map/ppermute | solution.py:23
  224.7 0.1 fusion.33
  224.8 1.9 collective-permute-start.14
  226.7 0.8 constant_dynamic-update-slice_fusion.7
  227.6 2.4 collective-permute-start.15
  230.0 0.9 constant_dynamic-update-slice_fusion.6
  230.8 2.9 %collective-permute-done.12 = bf16[32,32,256]{2,1,0:T(8,128)(2,1)S(1)} collective-permute-done((bf16[32,32,256]{2,1,0:T(8,128)(2,1)S(1)}, bf16[32,32,256]{2,1,0:T(8,128)(2,1)S(1)}, u32[]{:S(2)}, u32[]{:S(2)}) %collective-permute-start.12) | collective-permute-done | bytes 524320 | tf_op jit(solution)/shard_map/ppermute | solution.py:23
  233.8 4.6 %collective-permute-start.16 = (bf16[32,32,256]{2,1,0:T(8,128)(2,1)S(1)}, bf16[32,32,256]{2,1,0:T(8,128)(2,1)S(1)}, u32[]{:S(2)}, u32[]{:S(2)}) collective-permute-start(bf16[32,32,256]{2,1,0:T(8,128)(2,1)S(1)} %collective-permute-done.12), channel_id=1, source_target_pairs={{0,1},{1,0},{2,3},{3,2},{4,5},{5,4},{6,7},{7,6},{8,9},{9,8},{10,11... | collective-permute-start | bytes 1572872 | tf_op jit(solution)/shard_map/ppermute | solution.py:23
  238.4 0.9 constant_dynamic-update-slice_fusion.5
  239.2 0.9 constant_dynamic-update-slice_fusion.4
  240.1 0.8 constant_dynamic-update-slice_fusion.3
  240.9 0.9 constant_dynamic-update-slice_fusion.2
  241.8 0.9 constant_dynamic-update-slice_fusion.1
  242.7 0.9 constant_dynamic-update-slice_fusion
  243.5 5.9 %convolution_bitcast_fusion.1 = f32[1,32,32,512]{3,2,1,0:T(8,128)S(1)} fusion(bf16[32,32,256]{2,1,0:T(8,128)(2,1)S(1)} %reshape.119, bf16[32,512,256]{2,1,0:T(8,128)(2,1)} %constant_dynamic-update-slice_fusion), kind=kOutput, calls=%fused_computation.8 | convolution fusion | flops 268435456 | bytes 11010048 | tf_op jit(solution)/shard_map/cik,cjk->cij/dot_general | solution.py:144
  249.4 5.9 %convolution_bitcast_fusion = f32[1,32,32,512]{3,2,1,0:T(8,128)S(1)} fusion(bf16[32,512,256]{2,1,0:T(8,128)(2,1)} %constant_dynamic-update-slice_fusion, bf16[32,32,128]{2,1,0:T(8,128)(2,1)S(1)} %get-tuple-element.12, bf16[32,32,128]{2,1,0:T(8,128)(2,1)S(1)} %get-tuple-element.11), kind=kOutput, calls=%fused_computation.7 | convolution fusion | flops 269484032 | bytes 11010048 | tf_op jit(solution)/shard_map/cik,cjk->cij/dot_general | solution.py:145
  255.4 2.0 fusion.1
  (16 shorter events, 0.0 us)
Async XLA Ops:
  2.8 56.5 %collective-permute-start.1 = (bf16[4,32,4096]{2,1,0:T(8,128)(2,1)}, bf16[4,32,4096]{2,1,0:T(8,128)(2,1)}, u32[]{:S(2)}, u32[]{:S(2)}) collective-permute-start(bf16[4,32,4096]{2,1,0:T(8,128)(2,1)} %bitcast.33), channel_id=1, source_target_pairs={{0,496},{16,0},{32,16},{48,32},{64,48},{80,64},{96,80},{112,96},{1... | collective-permute-start | bytes 3145736 | tf_op jit(solution)/shard_map/ppermute | solution.py:130
  20.2 37.0 %collective-permute-start = (bf16[3,32,4096]{2,1,0:T(8,128)(2,1)}, bf16[3,32,4096]{2,1,0:T(8,128)(2,1)}, u32[]{:S(2)}, u32[]{:S(2)}) collective-permute-start(bf16[3,32,4096]{2,1,0:T(8,128)(2,1)} %slice.12), channel_id=1, source_target_pairs={{0,16},{16,32},{32,48},{48,64},{64,80},{80,96},{96,112},{112,128},... | collective-permute-start | bytes 2359304 | tf_op jit(solution)/shard_map/ppermute | solution.py:19
  31.3 10.4 %copy-start = (s32[32]{0:T(128)S(1)}, s32[32]{0:T(128)}, u32[]{:S(2)}) copy-start(s32[32]{0:T(128)} %param.3) | copy-start | bytes 388
  124.4 13.5 %collective-permute-start.2 = (bf16[32,32,256]{2,1,0:T(8,128)(2,1)S(1)}, bf16[32,32,256]{2,1,0:T(8,128)(2,1)S(1)}, u32[]{:S(2)}, u32[]{:S(2)}) collective-permute-start(bf16[32,32,256]{2,1,0:T(8,128)(2,1)S(1)} %reshape.119), channel_id=1, source_target_pairs={{0,2},{1,3},{2,4},{3,5},{4,6},{5,7},{6,0},{7,1},{8,10},{9,11},{10,... | collective-permute-start | bytes 1572872 | tf_op jit(solution)/shard_map/ppermute | solution.py:23
  126.6 36.3 %collective-permute-start.3 = (bf16[32,32,256]{2,1,0:T(8,128)(2,1)S(1)}, bf16[32,32,256]{2,1,0:T(8,128)(2,1)S(1)}, u32[]{:S(2)}, u32[]{:S(2)}) collective-permute-start(bf16[32,32,256]{2,1,0:T(8,128)(2,1)S(1)} %reshape.119), channel_id=1, source_target_pairs={{0,6},{1,7},{2,0},{3,1},{4,2},{5,3},{6,4},{7,5},{8,14},{9,15},{10,... | collective-permute-start | bytes 1572872 | tf_op jit(solution)/shard_map/ppermute | solution.py:23
  137.9 27.9 %collective-permute-start.4 = (bf16[32,32,256]{2,1,0:T(8,128)(2,1)S(1)}, bf16[32,32,256]{2,1,0:T(8,128)(2,1)S(1)}, u32[]{:S(2)}, u32[]{:S(2)}) collective-permute-start(bf16[32,32,256]{2,1,0:T(8,128)(2,1)S(1)} %collective-permute-done.2), channel_id=1, source_target_pairs={{0,2},{1,3},{2,4},{3,5},{4,6},{5,7},{6,0},{7,1},{8,10},{9,11},{10,... | collective-permute-start | bytes 1572872 | tf_op jit(solution)/shard_map/ppermute | solution.py:23
  141.2 28.5 %collective-permute-start.5 = (bf16[32,32,256]{2,1,0:T(8,128)(2,1)S(1)}, bf16[32,32,256]{2,1,0:T(8,128)(2,1)S(1)}, u32[]{:S(2)}, u32[]{:S(2)}) collective-permute-start(bf16[32,32,256]{2,1,0:T(8,128)(2,1)S(1)} %reshape.119), channel_id=1, source_target_pairs={{0,1},{1,0},{2,3},{3,2},{4,5},{5,4},{6,7},{7,6},{8,9},{9,8},{10,11... | collective-permute-start | bytes 1572872 | tf_op jit(solution)/shard_map/ppermute | solution.py:23
  146.4 57.0 %collective-permute-start.9 = (bf16[32,32,256]{2,1,0:T(8,128)(2,1)S(1)}, bf16[32,32,256]{2,1,0:T(8,128)(2,1)S(1)}, u32[]{:S(2)}, u32[]{:S(2)}) collective-permute-start(bf16[32,32,256]{2,1,0:T(8,128)(2,1)S(1)} %reshape.119), channel_id=1, source_target_pairs={{0,8},{1,9},{2,10},{3,11},{4,12},{5,13},{6,14},{7,15},{8,0},{9,1},... | collective-permute-start | bytes 1572872 | tf_op jit(solution)/shard_map/ppermute | solution.py:23
  155.4 15.2 %collective-permute-start.6 = (bf16[32,32,256]{2,1,0:T(8,128)(2,1)S(1)}, bf16[32,32,256]{2,1,0:T(8,128)(2,1)S(1)}, u32[]{:S(2)}, u32[]{:S(2)}) collective-permute-start(bf16[32,32,256]{2,1,0:T(8,128)(2,1)S(1)} %collective-permute-done.2), channel_id=1, source_target_pairs={{0,1},{1,0},{2,3},{3,2},{4,5},{5,4},{6,7},{7,6},{8,9},{9,8},{10,11... | collective-permute-start | bytes 1572872 | tf_op jit(solution)/shard_map/ppermute | solution.py:23
  162.8 8.6 %collective-permute-start.7 = (bf16[32,32,256]{2,1,0:T(8,128)(2,1)S(1)}, bf16[32,32,256]{2,1,0:T(8,128)(2,1)S(1)}, u32[]{:S(2)}, u32[]{:S(2)}) collective-permute-start(bf16[32,32,256]{2,1,0:T(8,128)(2,1)S(1)} %collective-permute-done.3), channel_id=1, source_target_pairs={{0,1},{1,0},{2,3},{3,2},{4,5},{5,4},{6,7},{7,6},{8,9},{9,8},{10,11... | collective-permute-start | bytes 1572872 | tf_op jit(solution)/shard_map/ppermute | solution.py:23
  165.8 6.5 %collective-permute-start.8 = (bf16[32,32,256]{2,1,0:T(8,128)(2,1)S(1)}, bf16[32,32,256]{2,1,0:T(8,128)(2,1)S(1)}, u32[]{:S(2)}, u32[]{:S(2)}) collective-permute-start(bf16[32,32,256]{2,1,0:T(8,128)(2,1)S(1)} %collective-permute-done.4), channel_id=1, source_target_pairs={{0,1},{1,0},{2,3},{3,2},{4,5},{5,4},{6,7},{7,6},{8,9},{9,8},{10,11... | collective-permute-start | bytes 1572872 | tf_op jit(solution)/shard_map/ppermute | solution.py:23
  203.3 15.7 %collective-permute-start.11 = (bf16[32,32,256]{2,1,0:T(8,128)(2,1)S(1)}, bf16[32,32,256]{2,1,0:T(8,128)(2,1)S(1)}, u32[]{:S(2)}, u32[]{:S(2)}) collective-permute-start(bf16[32,32,256]{2,1,0:T(8,128)(2,1)S(1)} %collective-permute-done.9), channel_id=1, source_target_pairs={{0,6},{1,7},{2,0},{3,1},{4,2},{5,3},{6,4},{7,5},{8,14},{9,15},{10,... | collective-permute-start | bytes 1572872 | tf_op jit(solution)/shard_map/ppermute | solution.py:23
  205.3 19.5 %collective-permute-start.10 = (bf16[32,32,256]{2,1,0:T(8,128)(2,1)S(1)}, bf16[32,32,256]{2,1,0:T(8,128)(2,1)S(1)}, u32[]{:S(2)}, u32[]{:S(2)}) collective-permute-start(bf16[32,32,256]{2,1,0:T(8,128)(2,1)S(1)} %collective-permute-done.9), channel_id=1, source_target_pairs={{0,2},{1,3},{2,4},{3,5},{4,6},{5,7},{6,0},{7,1},{8,10},{9,11},{10,... | collective-permute-start | bytes 1572872 | tf_op jit(solution)/shard_map/ppermute | solution.py:23
  219.0 14.8 %collective-permute-start.12 = (bf16[32,32,256]{2,1,0:T(8,128)(2,1)S(1)}, bf16[32,32,256]{2,1,0:T(8,128)(2,1)S(1)}, u32[]{:S(2)}, u32[]{:S(2)}) collective-permute-start(bf16[32,32,256]{2,1,0:T(8,128)(2,1)S(1)} %collective-permute-done.11), channel_id=1, source_target_pairs={{0,6},{1,7},{2,0},{3,1},{4,2},{5,3},{6,4},{7,5},{8,14},{9,15},{10,... | collective-permute-start | bytes 1572872 | tf_op jit(solution)/shard_map/ppermute | solution.py:23
  221.0 19.1 %collective-permute-start.13 = (bf16[32,32,256]{2,1,0:T(8,128)(2,1)S(1)}, bf16[32,32,256]{2,1,0:T(8,128)(2,1)S(1)}, u32[]{:S(2)}, u32[]{:S(2)}) collective-permute-start(bf16[32,32,256]{2,1,0:T(8,128)(2,1)S(1)} %collective-permute-done.9), channel_id=1, source_target_pairs={{0,1},{1,0},{2,3},{3,2},{4,5},{5,4},{6,7},{7,6},{8,9},{9,8},{10,11... | collective-permute-start | bytes 1572872 | tf_op jit(solution)/shard_map/ppermute | solution.py:23
  224.8 16.1 %collective-permute-start.14 = (bf16[32,32,256]{2,1,0:T(8,128)(2,1)S(1)}, bf16[32,32,256]{2,1,0:T(8,128)(2,1)S(1)}, u32[]{:S(2)}, u32[]{:S(2)}) collective-permute-start(bf16[32,32,256]{2,1,0:T(8,128)(2,1)S(1)} %collective-permute-done.10), channel_id=1, source_target_pairs={{0,1},{1,0},{2,3},{3,2},{4,5},{5,4},{6,7},{7,6},{8,9},{9,8},{10,11... | collective-permute-start | bytes 1572872 | tf_op jit(solution)/shard_map/ppermute | solution.py:23
  227.6 14.3 %collective-permute-start.15 = (bf16[32,32,256]{2,1,0:T(8,128)(2,1)S(1)}, bf16[32,32,256]{2,1,0:T(8,128)(2,1)S(1)}, u32[]{:S(2)}, u32[]{:S(2)}) collective-permute-start(bf16[32,32,256]{2,1,0:T(8,128)(2,1)S(1)} %collective-permute-done.11), channel_id=1, source_target_pairs={{0,1},{1,0},{2,3},{3,2},{4,5},{5,4},{6,7},{7,6},{8,9},{9,8},{10,11... | collective-permute-start | bytes 1572872 | tf_op jit(solution)/shard_map/ppermute | solution.py:23
  233.8 8.9 %collective-permute-start.16 = (bf16[32,32,256]{2,1,0:T(8,128)(2,1)S(1)}, bf16[32,32,256]{2,1,0:T(8,128)(2,1)S(1)}, u32[]{:S(2)}, u32[]{:S(2)}) collective-permute-start(bf16[32,32,256]{2,1,0:T(8,128)(2,1)S(1)} %collective-permute-done.12), channel_id=1, source_target_pairs={{0,1},{1,0},{2,3},{3,2},{4,5},{5,4},{6,7},{7,6},{8,9},{9,8},{10,11... | collective-permute-start | bytes 1572872 | tf_op jit(solution)/shard_map/ppermute | solution.py:23

commit v11 on v8

--- a/solution.py
+++ b/solution.py
@@ -142,9 +142,9 @@
     own_rows = local_block.transpose(3, 1, 2, 0).reshape(chan_count, inp_count, 2 * spec_total)
     swapped = jnp.concatenate([own_rows[..., spec_total:], -own_rows[..., :spec_total]], axis=-1)
     piece = gather_inputs(own_rows)
-    real_part = jnp.einsum("cik,cjk->cij", own_rows, piece, preferred_element_type=jnp.float32)
-    imag_part = jnp.einsum("cik,cjk->cij", swapped, piece, preferred_element_type=jnp.float32)
-    result = jnp.stack([real_part, imag_part]) * (1.0 / spec_total)
+    lhs = jnp.concatenate([own_rows, swapped], axis=1)
+    both = jnp.einsum("cik,cjk->cij", lhs, piece, preferred_element_type=jnp.float32)
+    result = both.reshape(chan_count, 2, inp_count, -1).transpose(1, 0, 2, 3) * (1.0 / spec_total)
     return result.astype(jnp.bfloat16)
 
 

time: 230 us -> 227 us (0.987)
  matrix products: 13.5 us -> 11.1 us
    dot_general x2 -> x1, matrix products: 5.07 us -> 2.65 us  [shards(): jnp.einsum('cik,cjk->cij', lhs, piece, preferred_element_type=jnp.float32)]
where the time goes in v11:
time: 227 us; the launch traced here: 226 us
  starting transfers between devices  65.2 us (29%)
  waiting for transfers between devices  60.8 us (27%)
  blocking collectives  36.9 us (16%)
  other arithmetic  23.1 us (10%)
  local copies, waits for them, and re-layouts  21.2 us (9%)
  matrix products  11.1 us (5%)
  Pallas kernels  6.69 us (3%)
    ppermute x15, starting transfers between devices, moved(): lax.ppermute(block, 'inp', [(p, mapping(p)) for p in range(lax.axis_size(...  47.7 us
    ppermute x15, waiting for transfers between devices, moved(): lax.ppermute(block, 'inp', [(p, mapping(p)) for p in range(lax.axis_size(...  46.1 us
    all_to_all x1, blocking collectives, shards(): lax.all_to_all(spectra, 'chan', split_axis=3, concat_axis=0, tiled=True)  36.9 us
    ppermute x1, starting transfers between devices, shards(): lax.ppermute(samples, 'chan', [(i, (i - 1) % count) for i in range(count)])  15.3 us
    ppermute x1, waiting for transfers between devices, shifted(): return lax.ppermute(block, axis, route)  14.8 us
    dot_general x1, matrix products, shards(): jnp.dot(filtered, dft_table(), preferred_element_type=jnp.float32)  8.44 us
    convert_element_type x1, other arithmetic, dft_table(): return lax.optimization_barrier(both.astype(jnp.bfloat16))  8.04 us
    pallas_call x1, Pallas kernels, polyphase(): pl.pallas_call(functools.partial(polyphase_kernel, spec_count), out_shape...  6.69 us
  transfers between devices with their start and end apart: 17, of which 5 were waited for; matrix products, arithmetic and copies ran while one was open for 12% of the time, Pallas kernels for 0%

profile of v11, /device:TPU:7, one launch (start us, length us, event | category | flops | bytes accessed | tf_op | source)
XLA Modules:
  0.0 225.8 jit_solution(1568400789672711033)
XLA Ops:
  0.0 1.7 convert_element_type.60
  1.7 1.1 copy.31
  2.8 15.3 %collective-permute-start.1 = (bf16[4,32,4096]{2,1,0:T(8,128)(2,1)}, bf16[4,32,4096]{2,1,0:T(8,128)(2,1)}, u32[]{:S(2)}, u32[]{:S(2)}) collective-permute-start(bf16[4,32,4096]{2,1,0:T(8,128)(2,1)} %bitcast.31), channel_id=1, source_target_pairs={{0,496},{16,0},{32,16},{48,32},{64,48},{80,64},{96,80},{112,96},{1... | collective-permute-start | bytes 3145736 | tf_op jit(solution)/shard_map/ppermute | solution.py:131
  18.1 2.1 slice.12
  20.2 2.2 collective-permute-start
  22.3 1.8 sine_negate_fusion
  24.1 1.1 fusion.27
  25.2 6.1 %multiply_subtract_fusion = (f32[64,64,1024]{2,1,0:T(8,128)S(1)}, f32[64,64,1024]{2,1,0:T(8,128)S(1)}) fusion(f32[64,1024]{1,0:T(8,128)} %get-tuple-element.11, f32[64,1024]{1,0:T(8,128)S(1)} %get-tuple-element.10, f32[64,1024]{1,0:T(8,128)} %get-tuple-element.12, f32[64,1024]{1,0:T(8,128)S(1)} %get-tuple-element.9), kind=kLoop, calls=%fused_computation.3 | loop fusion | flops 25165824 | bytes 34603008 | tf_op jit(solution)/shard_map/sub | solution.py:49
  31.3 0.0 copy-start
  31.3 8.0 %fusion = bf16[4096,2048]{1,0:T(8,128)(2,1)} fusion(f32[4096,1024]{1,0:T(8,128)S(1)} %bitcast.33, f32[4096,1024]{1,0:T(8,128)S(1)} %bitcast.32), kind=kLoop, calls=%fused_computation.1 | loop fusion | flops 25165824 | bytes 50331648 | tf_op jit(solution)/shard_map/convert_element_type | solution.py:52
  39.4 1.0 broadcast_select_fusion.refs_1_
  40.4 1.3 fusion.22.refs_3_
  41.7 0.7 copy.17.refs_4_
  42.4 14.8 %collective-permute-done = bf16[3,32,4096]{2,1,0:T(8,128)(2,1)} collective-permute-done((bf16[3,32,4096]{2,1,0:T(8,128)(2,1)}, bf16[3,32,4096]{2,1,0:T(8,128)(2,1)}, u32[]{:S(2)}, u32[]{:S(2)}) %collective-permute-start) | collective-permute-done | bytes 786464 | tf_op jit(solution)/shard_map/ppermute | solution.py:19
  57.2 2.1 broadcast_select_fusion.1.refs_0_
  59.2 0.0 collective-permute-done.1.refs_2_
  59.2 6.7 %shard_map.28 = bf16[4,32,4096]{2,1,0:T(8,128)(2,1)} custom-call(bf16[3,32,4096]{2,1,0:T(8,128)(2,1)} %broadcast_select_fusion.1.refs_0_, bf16[4,32,4096]{2,1,0:T(8,128)(2,1)} %broadcast_select_fusion.refs_1_, bf16[4,32,4096]{2,1,0:T(8,128)(2,1)} %collective-permute-done.1.refs_2_, f32[8,4096]{1,0:T(8,128)} %fusion.22.refs_3_, f32[32,1]{1,0:T(8,128)} %copy.17.refs_4_), custom_call_target="tpu_custom_call" | custom-call | tf_op jit(solution)/shard_map/pallas_call | solution.py:69
  65.9 8.4 %convolution_convert_fusion = bf16[128,2048]{1,0:T(8,128)(2,1)S(1)} fusion(bf16[128,4096]{1,0:T(8,128)(2,1)} %bitcast.40, bf16[4096,2048]{1,0:T(8,128)(2,1)} %fusion), kind=kOutput, calls=%fused_computation.5 | convolution fusion | flops 2147745792 | bytes 18350080 | tf_op jit(solution)/shard_map/dot_general | solution.py:137
  74.4 0.4 reshape.122
  74.7 1.9 copy.18
  76.7 2.0 reshape.124
  78.7 36.9 %all_to_all.18 = bf16[32,2,4096]{2,1,0:T(2,128)(2,1)S(1)} all-to-all(bf16[32,2,4096]{2,1,0:T(2,128)(2,1)S(1)} %reshape.124), channel_id=1, replica_groups=mesh['chan'=32,'inp'=16] {'chan'}, dimensions={0} | all-to-all | bytes 1048576 | tf_op jit(solution)/shard_map/all_to_all | solution.py:139
  115.6 1.0 reshape.125
  116.6 3.8 %copy.24 = bf16[4,32,2,32,32]{4,1,2,0,3:T(8,128)(2,1)} copy(bf16[4,32,2,32,32]{1,2,0,4,3:T(2,128)(2,1)S(1)} %bitcast.37) | data formatting | bytes 1048576 | tf_op jit(solution)/shard_map/all_to_all | solution.py:139
  120.4 3.7 %copy.21 = bf16[32,32,2,128]{3,2,1,0:T(2,128)(2,1)S(1)} copy(bf16[32,32,2,128]{0,1,2,3:T(8,128)(2,1)} %bitcast.38) | data formatting | bytes 1048576 | tf_op jit(solution)/shard_map/transpose | solution.py:142
  124.1 0.3 reshape.123
  124.4 9.1 %collective-permute-start.3 = (bf16[32,32,256]{2,1,0:T(8,128)(2,1)S(1)}, bf16[32,32,256]{2,1,0:T(8,128)(2,1)S(1)}, u32[]{:S(2)}, u32[]{:S(2)}) collective-permute-start(bf16[32,32,256]{2,1,0:T(8,128)(2,1)S(1)} %reshape.123), channel_id=1, source_target_pairs={{0,8},{1,9},{2,10},{3,11},{4,12},{5,13},{6,14},{7,15},{8,0},{9,1},... | collective-permute-start | bytes 1572872 | tf_op jit(solution)/shard_map/ppermute | solution.py:23
  133.5 4.0 %collective-permute-start.2 = (bf16[32,32,256]{2,1,0:T(8,128)(2,1)S(1)}, bf16[32,32,256]{2,1,0:T(8,128)(2,1)}, u32[]{:S(2)}, u32[]{:S(2)}) collective-permute-start(bf16[32,32,256]{2,1,0:T(8,128)(2,1)S(1)} %reshape.123), channel_id=1, source_target_pairs={{0,1},{1,0},{2,3},{3,2},{4,5},{5,4},{6,7},{7,6},{8,9},{9,8},{10,11... | collective-permute-start | bytes 1572872 | tf_op jit(solution)/shard_map/ppermute | solution.py:23
  137.5 2.1 collective-permute-start.5
  139.6 3.2 %collective-permute-start.9 = (bf16[32,32,256]{2,1,0:T(8,128)(2,1)S(1)}, bf16[32,32,256]{2,1,0:T(8,128)(2,1)S(1)}, u32[]{:S(2)}, u32[]{:S(2)}) collective-permute-start(bf16[32,32,256]{2,1,0:T(8,128)(2,1)S(1)} %reshape.123), channel_id=1, source_target_pairs={{0,6},{1,7},{2,0},{3,1},{4,2},{5,3},{6,4},{7,5},{8,14},{9,15},{10,... | collective-permute-start | bytes 1572872 | tf_op jit(solution)/shard_map/ppermute | solution.py:23
  142.8 38.2 %collective-permute-done.3 = bf16[32,32,256]{2,1,0:T(8,128)(2,1)S(1)} collective-permute-done((bf16[32,32,256]{2,1,0:T(8,128)(2,1)S(1)}, bf16[32,32,256]{2,1,0:T(8,128)(2,1)S(1)}, u32[]{:S(2)}, u32[]{:S(2)}) %collective-permute-start.3) | collective-permute-done | bytes 524320 | tf_op jit(solution)/shard_map/ppermute | solution.py:23
  181.0 2.1 collective-permute-start.7
  183.1 3.2 %collective-permute-start.11 = (bf16[32,32,256]{2,1,0:T(8,128)(2,1)S(1)}, bf16[32,32,256]{2,1,0:T(8,128)(2,1)S(1)}, u32[]{:S(2)}, u32[]{:S(2)}) collective-permute-start(bf16[32,32,256]{2,1,0:T(8,128)(2,1)S(1)} %collective-permute-done.3), channel_id=1, source_target_pairs={{0,6},{1,7},{2,0},{3,1},{4,2},{5,3},{6,4},{7,5},{8,14},{9,15},{10,... | collective-permute-start | bytes 1572872 | tf_op jit(solution)/shard_map/ppermute | solution.py:23
  186.6 0.0 collective-permute-done.2
  186.6 3.7 %collective-permute-start.4 = (bf16[32,32,256]{2,1,0:T(8,128)(2,1)S(1)}, bf16[32,32,256]{2,1,0:T(8,128)(2,1)S(1)}, u32[]{:S(2)}, u32[]{:S(2)}) collective-permute-start(bf16[32,32,256]{2,1,0:T(8,128)(2,1)S(1)} %collective-permute-done.3), channel_id=1, source_target_pairs={{0,1},{1,0},{2,3},{3,2},{4,5},{5,4},{6,7},{7,6},{8,9},{9,8},{10,11... | collective-permute-start | bytes 1572872 | tf_op jit(solution)/shard_map/ppermute | solution.py:23
  190.3 0.1 fusion.34
  190.4 0.0 collective-permute-done.5
  190.4 1.9 collective-permute-start.6
  192.3 0.0 collective-permute-done.9
  192.3 3.5 %collective-permute-start.13 = (bf16[32,32,256]{2,1,0:T(8,128)(2,1)S(1)}, bf16[32,32,256]{2,1,0:T(8,128)(2,1)S(1)}, u32[]{:S(2)}, u32[]{:S(2)}) collective-permute-start(bf16[32,32,256]{2,1,0:T(8,128)(2,1)S(1)} %collective-permute-done.5), channel_id=1, source_target_pairs={{0,2},{1,3},{2,4},{3,5},{4,6},{5,7},{6,0},{7,1},{8,10},{9,11},{10,... | collective-permute-start | bytes 1572872 | tf_op jit(solution)/shard_map/ppermute | solution.py:23
  195.8 0.9 broadcast_in_dim.56
  196.8 1.1 constant_dynamic-update-slice_fusion.14
  197.9 0.0 collective-permute-done.7
  197.9 2.7 %collective-permute-start.8 = (bf16[32,32,256]{2,1,0:T(8,128)(2,1)S(1)}, bf16[32,32,256]{2,1,0:T(8,128)(2,1)S(1)}, u32[]{:S(2)}, u32[]{:S(2)}) collective-permute-start(bf16[32,32,256]{2,1,0:T(8,128)(2,1)S(1)} %collective-permute-done.7), channel_id=1, source_target_pairs={{0,1},{1,0},{2,3},{3,2},{4,5},{5,4},{6,7},{7,6},{8,9},{9,8},{10,11... | collective-permute-start | bytes 1572872 | tf_op jit(solution)/shard_map/ppermute | solution.py:23
  200.6 0.0 collective-permute-done.11
  200.6 2.0 collective-permute-start.15
  202.7 0.0 collective-permute-done.4
  202.7 2.2 collective-permute-start.10
  204.9 0.1 constant_dynamic-update-slice_fusion.12
  205.0 2.1 collective-permute-start.12
  207.1 0.1 collective-permute-done.13
  207.2 3.2 %collective-permute-start.14 = (bf16[32,32,256]{2,1,0:T(8,128)(2,1)S(1)}, bf16[32,32,256]{2,1,0:T(8,128)(2,1)S(1)}, u32[]{:S(2)}, u32[]{:S(2)}) collective-permute-start(bf16[32,32,256]{2,1,0:T(8,128)(2,1)S(1)} %collective-permute-done.13), channel_id=1, source_target_pairs={{0,1},{1,0},{2,3},{3,2},{4,5},{5,4},{6,7},{7,6},{8,9},{9,8},{10,11... | collective-permute-start | bytes 1572872 | tf_op jit(solution)/shard_map/ppermute | solution.py:23
  210.6 6.7 %collective-permute-done.15 = bf16[32,32,256]{2,1,0:T(8,128)(2,1)S(1)} collective-permute-done((bf16[32,32,256]{2,1,0:T(8,128)(2,1)S(1)}, bf16[32,32,256]{2,1,0:T(8,128)(2,1)S(1)}, u32[]{:S(2)}, u32[]{:S(2)}) %collective-permute-start.15) | collective-permute-done | bytes 524320 | tf_op jit(solution)/shard_map/ppermute | solution.py:23
  217.3 2.7 %collective-permute-start.16 = (bf16[32,32,256]{2,1,0:T(8,128)(2,1)S(1)}, bf16[32,32,256]{2,1,0:T(8,128)(2,1)S(1)}, u32[]{:S(2)}, u32[]{:S(2)}) collective-permute-start(bf16[32,32,256]{2,1,0:T(8,128)(2,1)S(1)} %collective-permute-done.15), channel_id=1, source_target_pairs={{0,1},{1,0},{2,3},{3,2},{4,5},{5,4},{6,7},{7,6},{8,9},{9,8},{10,11... | collective-permute-start | bytes 1572872 | tf_op jit(solution)/shard_map/ppermute | solution.py:23
  220.0 0.0 collective-permute-done.8
  220.0 0.1 constant_dynamic-update-slice_fusion.8
  220.1 0.0 collective-permute-done.10
  220.1 0.1 constant_dynamic-update-slice_fusion.6
  220.2 0.0 collective-permute-done.12
  220.2 0.1 constant_dynamic-update-slice_fusion.4
  220.3 0.1 constant_dynamic-update-slice_fusion.2
  220.5 1.0 collective-permute-done.16
  221.5 2.6 %multiply_convert_fusion = bf16[32,64,512]{2,1,0:T(8,128)(2,1)S(1)} fusion(bf16[32,512,256]{2,1,0:T(8,128)(2,1)S(1)} %constant_dynamic-update-slice_fusion, bf16[32,32,128]{2,1,0:T(8,128)(2,1)S(1)} %get-tuple-element.8, bf16[32,32,128]{2,1,0:T(8,128)(2,1)S(1)} %get-tuple-element.7, bf16[32,32,256]{2,1,0:T(8,128)(2,1)S(1)} %reshape.123), kind=kOutput, calls=%fused_computation.4 | convolution fusion | flops 542113792 | bytes 11534336 | tf_op jit(solution)/shard_map/cik,cjk->cij/dot_general | solution.py:146
  224.2 1.6 copy.30
  (15 shorter events, 0.5 us)
Async XLA Ops:
  2.8 56.5 %collective-permute-start.1 = (bf16[4,32,4096]{2,1,0:T(8,128)(2,1)}, bf16[4,32,4096]{2,1,0:T(8,128)(2,1)}, u32[]{:S(2)}, u32[]{:S(2)}) collective-permute-start(bf16[4,32,4096]{2,1,0:T(8,128)(2,1)} %bitcast.31), channel_id=1, source_target_pairs={{0,496},{16,0},{32,16},{48,32},{64,48},{80,64},{96,80},{112,96},{1... | collective-permute-start | bytes 3145736 | tf_op jit(solution)/shard_map/ppermute | solution.py:131
  20.2 37.0 %collective-permute-start = (bf16[3,32,4096]{2,1,0:T(8,128)(2,1)}, bf16[3,32,4096]{2,1,0:T(8,128)(2,1)}, u32[]{:S(2)}, u32[]{:S(2)}) collective-permute-start(bf16[3,32,4096]{2,1,0:T(8,128)(2,1)} %slice.12), channel_id=1, source_target_pairs={{0,16},{16,32},{32,48},{48,64},{64,80},{80,96},{96,112},{112,128},... | collective-permute-start | bytes 2359304 | tf_op jit(solution)/shard_map/ppermute | solution.py:19
  31.3 10.4 %copy-start = (s32[32]{0:T(128)S(1)}, s32[32]{0:T(128)}, u32[]{:S(2)}) copy-start(s32[32]{0:T(128)} %param.3) | copy-start | bytes 388
  124.4 56.6 %collective-permute-start.3 = (bf16[32,32,256]{2,1,0:T(8,128)(2,1)S(1)}, bf16[32,32,256]{2,1,0:T(8,128)(2,1)S(1)}, u32[]{:S(2)}, u32[]{:S(2)}) collective-permute-start(bf16[32,32,256]{2,1,0:T(8,128)(2,1)S(1)} %reshape.123), channel_id=1, source_target_pairs={{0,8},{1,9},{2,10},{3,11},{4,12},{5,13},{6,14},{7,15},{8,0},{9,1},... | collective-permute-start | bytes 1572872 | tf_op jit(solution)/shard_map/ppermute | solution.py:23
  133.5 53.0 %collective-permute-start.2 = (bf16[32,32,256]{2,1,0:T(8,128)(2,1)S(1)}, bf16[32,32,256]{2,1,0:T(8,128)(2,1)}, u32[]{:S(2)}, u32[]{:S(2)}) collective-permute-start(bf16[32,32,256]{2,1,0:T(8,128)(2,1)S(1)} %reshape.123), channel_id=1, source_target_pairs={{0,1},{1,0},{2,3},{3,2},{4,5},{5,4},{6,7},{7,6},{8,9},{9,8},{10,11... | collective-permute-start | bytes 1572872 | tf_op jit(solution)/shard_map/ppermute | solution.py:23
  137.5 52.8 %collective-permute-start.5 = (bf16[32,32,256]{2,1,0:T(8,128)(2,1)S(1)}, bf16[32,32,256]{2,1,0:T(8,128)(2,1)S(1)}, u32[]{:S(2)}, u32[]{:S(2)}) collective-permute-start(bf16[32,32,256]{2,1,0:T(8,128)(2,1)S(1)} %reshape.123), channel_id=1, source_target_pairs={{0,2},{1,3},{2,4},{3,5},{4,6},{5,7},{6,0},{7,1},{8,10},{9,11},{10,... | collective-permute-start | bytes 1572872 | tf_op jit(solution)/shard_map/ppermute | solution.py:23
  139.6 52.7 %collective-permute-start.9 = (bf16[32,32,256]{2,1,0:T(8,128)(2,1)S(1)}, bf16[32,32,256]{2,1,0:T(8,128)(2,1)S(1)}, u32[]{:S(2)}, u32[]{:S(2)}) collective-permute-start(bf16[32,32,256]{2,1,0:T(8,128)(2,1)S(1)} %reshape.123), channel_id=1, source_target_pairs={{0,6},{1,7},{2,0},{3,1},{4,2},{5,3},{6,4},{7,5},{8,14},{9,15},{10,... | collective-permute-start | bytes 1572872 | tf_op jit(solution)/shard_map/ppermute | solution.py:23
  181.0 16.9 %collective-permute-start.7 = (bf16[32,32,256]{2,1,0:T(8,128)(2,1)S(1)}, bf16[32,32,256]{2,1,0:T(8,128)(2,1)S(1)}, u32[]{:S(2)}, u32[]{:S(2)}) collective-permute-start(bf16[32,32,256]{2,1,0:T(8,128)(2,1)S(1)} %collective-permute-done.3), channel_id=1, source_target_pairs={{0,2},{1,3},{2,4},{3,5},{4,6},{5,7},{6,0},{7,1},{8,10},{9,11},{10,... | collective-permute-start | bytes 1572872 | tf_op jit(solution)/shard_map/ppermute | solution.py:23
  183.1 17.5 %collective-permute-start.11 = (bf16[32,32,256]{2,1,0:T(8,128)(2,1)S(1)}, bf16[32,32,256]{2,1,0:T(8,128)(2,1)S(1)}, u32[]{:S(2)}, u32[]{:S(2)}) collective-permute-start(bf16[32,32,256]{2,1,0:T(8,128)(2,1)S(1)} %collective-permute-done.3), channel_id=1, source_target_pairs={{0,6},{1,7},{2,0},{3,1},{4,2},{5,3},{6,4},{7,5},{8,14},{9,15},{10,... | collective-permute-start | bytes 1572872 | tf_op jit(solution)/shard_map/ppermute | solution.py:23
  186.6 16.1 %collective-permute-start.4 = (bf16[32,32,256]{2,1,0:T(8,128)(2,1)S(1)}, bf16[32,32,256]{2,1,0:T(8,128)(2,1)S(1)}, u32[]{:S(2)}, u32[]{:S(2)}) collective-permute-start(bf16[32,32,256]{2,1,0:T(8,128)(2,1)S(1)} %collective-permute-done.3), channel_id=1, source_target_pairs={{0,1},{1,0},{2,3},{3,2},{4,5},{5,4},{6,7},{7,6},{8,9},{9,8},{10,11... | collective-permute-start | bytes 1572872 | tf_op jit(solution)/shard_map/ppermute | solution.py:23
  190.4 14.6 %collective-permute-start.6 = (bf16[32,32,256]{2,1,0:T(8,128)(2,1)S(1)}, bf16[32,32,256]{2,1,0:T(8,128)(2,1)S(1)}, u32[]{:S(2)}, u32[]{:S(2)}) collective-permute-start(bf16[32,32,256]{2,1,0:T(8,128)(2,1)S(1)} %collective-permute-done.5), channel_id=1, source_target_pairs={{0,1},{1,0},{2,3},{3,2},{4,5},{5,4},{6,7},{7,6},{8,9},{9,8},{10,11... | collective-permute-start | bytes 1572872 | tf_op jit(solution)/shard_map/ppermute | solution.py:23
  192.3 14.9 %collective-permute-start.13 = (bf16[32,32,256]{2,1,0:T(8,128)(2,1)S(1)}, bf16[32,32,256]{2,1,0:T(8,128)(2,1)S(1)}, u32[]{:S(2)}, u32[]{:S(2)}) collective-permute-start(bf16[32,32,256]{2,1,0:T(8,128)(2,1)S(1)} %collective-permute-done.5), channel_id=1, source_target_pairs={{0,2},{1,3},{2,4},{3,5},{4,6},{5,7},{6,0},{7,1},{8,10},{9,11},{10,... | collective-permute-start | bytes 1572872 | tf_op jit(solution)/shard_map/ppermute | solution.py:23
  197.9 22.1 %collective-permute-start.8 = (bf16[32,32,256]{2,1,0:T(8,128)(2,1)S(1)}, bf16[32,32,256]{2,1,0:T(8,128)(2,1)S(1)}, u32[]{:S(2)}, u32[]{:S(2)}) collective-permute-start(bf16[32,32,256]{2,1,0:T(8,128)(2,1)S(1)} %collective-permute-done.7), channel_id=1, source_target_pairs={{0,1},{1,0},{2,3},{3,2},{4,5},{5,4},{6,7},{7,6},{8,9},{9,8},{10,11... | collective-permute-start | bytes 1572872 | tf_op jit(solution)/shard_map/ppermute | solution.py:23
  200.6 16.6 %collective-permute-start.15 = (bf16[32,32,256]{2,1,0:T(8,128)(2,1)S(1)}, bf16[32,32,256]{2,1,0:T(8,128)(2,1)S(1)}, u32[]{:S(2)}, u32[]{:S(2)}) collective-permute-start(bf16[32,32,256]{2,1,0:T(8,128)(2,1)S(1)} %collective-permute-done.11), channel_id=1, source_target_pairs={{0,6},{1,7},{2,0},{3,1},{4,2},{5,3},{6,4},{7,5},{8,14},{9,15},{10,... | collective-permute-start | bytes 1572872 | tf_op jit(solution)/shard_map/ppermute | solution.py:23
  202.7 17.4 %collective-permute-start.10 = (bf16[32,32,256]{2,1,0:T(8,128)(2,1)S(1)}, bf16[32,32,256]{2,1,0:T(8,128)(2,1)S(1)}, u32[]{:S(2)}, u32[]{:S(2)}) collective-permute-start(bf16[32,32,256]{2,1,0:T(8,128)(2,1)S(1)} %collective-permute-done.9), channel_id=1, source_target_pairs={{0,1},{1,0},{2,3},{3,2},{4,5},{5,4},{6,7},{7,6},{8,9},{9,8},{10,11... | collective-permute-start | bytes 1572872 | tf_op jit(solution)/shard_map/ppermute | solution.py:23
  205.0 15.2 %collective-permute-start.12 = (bf16[32,32,256]{2,1,0:T(8,128)(2,1)S(1)}, bf16[32,32,256]{2,1,0:T(8,128)(2,1)S(1)}, u32[]{:S(2)}, u32[]{:S(2)}) collective-permute-start(bf16[32,32,256]{2,1,0:T(8,128)(2,1)S(1)} %collective-permute-done.11), channel_id=1, source_target_pairs={{0,1},{1,0},{2,3},{3,2},{4,5},{5,4},{6,7},{7,6},{8,9},{9,8},{10,11... | collective-permute-start | bytes 1572872 | tf_op jit(solution)/shard_map/ppermute | solution.py:23
  207.2 13.1 %collective-permute-start.14 = (bf16[32,32,256]{2,1,0:T(8,128)(2,1)S(1)}, bf16[32,32,256]{2,1,0:T(8,128)(2,1)S(1)}, u32[]{:S(2)}, u32[]{:S(2)}) collective-permute-start(bf16[32,32,256]{2,1,0:T(8,128)(2,1)S(1)} %collective-permute-done.13), channel_id=1, source_target_pairs={{0,1},{1,0},{2,3},{3,2},{4,5},{5,4},{6,7},{7,6},{8,9},{9,8},{10,11... | collective-permute-start | bytes 1572872 | tf_op jit(solution)/shard_map/ppermute | solution.py:23
  217.3 4.2 %collective-permute-start.16 = (bf16[32,32,256]{2,1,0:T(8,128)(2,1)S(1)}, bf16[32,32,256]{2,1,0:T(8,128)(2,1)S(1)}, u32[]{:S(2)}, u32[]{:S(2)}) collective-permute-start(bf16[32,32,256]{2,1,0:T(8,128)(2,1)S(1)} %collective-permute-done.15), channel_id=1, source_target_pairs={{0,1},{1,0},{2,3},{3,2},{4,5},{5,4},{6,7},{7,6},{8,9},{9,8},{10,11... | collective-permute-start | bytes 1572872 | tf_op jit(solution)/shard_map/ppermute | solution.py:23

commit v12 on v11

--- a/solution.py
+++ b/solution.py
@@ -65,7 +65,7 @@
 
 def polyphase(pieces, window, gain, spec_count):
     inputs, length = pieces[0].shape[1:]
-    lanes = 512
+    lanes = 2048
     return pl.pallas_call(
         functools.partial(polyphase_kernel, spec_count),
         out_shape=jax.ShapeDtypeStruct((spec_count, inputs, length), jnp.bfloat16),

time: 227 us -> 225 us (level)
  no operation moved by 1% of the time
where the time goes in v12:
time: 225 us; the launch traced here: 224 us
  starting transfers between devices  65.3 us (29%)
  waiting for transfers between devices  60.5 us (27%)
  blocking collectives  36.9 us (16%)
  other arithmetic  23.1 us (10%)
  local copies, waits for them, and re-layouts  21.2 us (9%)
  matrix products  11.1 us (5%)
  Pallas kernels  4.97 us (2%)
    ppermute x15, starting transfers between devices, moved(): lax.ppermute(block, 'inp', [(p, mapping(p)) for p in range(lax.axis_size(...  47.8 us
    ppermute x15, waiting for transfers between devices, moved(): lax.ppermute(block, 'inp', [(p, mapping(p)) for p in range(lax.axis_size(...  45.7 us
    all_to_all x1, blocking collectives, shards(): lax.all_to_all(spectra, 'chan', split_axis=3, concat_axis=0, tiled=True)  36.9 us
    ppermute x1, starting transfers between devices, shards(): lax.ppermute(samples, 'chan', [(i, (i - 1) % count) for i in range(count)])  15.3 us
    ppermute x1, waiting for transfers between devices, shifted(): return lax.ppermute(block, axis, route)  14.8 us
    dot_general x1, matrix products, shards(): jnp.dot(filtered, dft_table(), preferred_element_type=jnp.float32)  8.44 us
    convert_element_type x1, other arithmetic, dft_table(): return lax.optimization_barrier(both.astype(jnp.bfloat16))  8.04 us
    sub x1, other arithmetic, dft_table(): real = hr * lr - hi * li  6.11 us
  transfers between devices with their start and end apart: 17, of which 5 were waited for; matrix products, arithmetic and copies ran while one was open for 12% of the time, Pallas kernels for 0%

profile of v12, /device:TPU:7, one launch (start us, length us, event | category | flops | bytes accessed | tf_op | source)
XLA Modules:
  0.0 223.9 jit_solution(2681951102814189065)
XLA Ops:
  0.0 1.7 convert_element_type.60
  1.7 1.1 copy.31
  2.8 15.3 %collective-permute-start.1 = (bf16[4,32,4096]{2,1,0:T(8,128)(2,1)}, bf16[4,32,4096]{2,1,0:T(8,128)(2,1)}, u32[]{:S(2)}, u32[]{:S(2)}) collective-permute-start(bf16[4,32,4096]{2,1,0:T(8,128)(2,1)} %bitcast.31), channel_id=1, source_target_pairs={{0,496},{16,0},{32,16},{48,32},{64,48},{80,64},{96,80},{112,96},{1... | collective-permute-start | bytes 3145736 | tf_op jit(solution)/shard_map/ppermute | solution.py:131
  18.1 2.1 slice.12
  20.2 2.2 collective-permute-start
  22.3 1.8 sine_negate_fusion
  24.1 1.1 fusion.27
  25.2 6.1 %multiply_subtract_fusion = (f32[64,64,1024]{2,1,0:T(8,128)S(1)}, f32[64,64,1024]{2,1,0:T(8,128)S(1)}) fusion(f32[64,1024]{1,0:T(8,128)} %get-tuple-element.11, f32[64,1024]{1,0:T(8,128)S(1)} %get-tuple-element.10, f32[64,1024]{1,0:T(8,128)} %get-tuple-element.12, f32[64,1024]{1,0:T(8,128)S(1)} %get-tuple-element.9), kind=kLoop, calls=%fused_computation.3 | loop fusion | flops 25165824 | bytes 34603008 | tf_op jit(solution)/shard_map/sub | solution.py:49
  31.3 0.0 copy-start
  31.3 8.0 %fusion = bf16[4096,2048]{1,0:T(8,128)(2,1)} fusion(f32[4096,1024]{1,0:T(8,128)S(1)} %bitcast.33, f32[4096,1024]{1,0:T(8,128)S(1)} %bitcast.32), kind=kLoop, calls=%fused_computation.1 | loop fusion | flops 25165824 | bytes 50331648 | tf_op jit(solution)/shard_map/convert_element_type | solution.py:52
  39.4 1.0 broadcast_select_fusion.refs_1_
  40.4 1.3 fusion.22.refs_3_
  41.7 0.7 copy.17.refs_4_
  42.4 14.8 %collective-permute-done = bf16[3,32,4096]{2,1,0:T(8,128)(2,1)} collective-permute-done((bf16[3,32,4096]{2,1,0:T(8,128)(2,1)}, bf16[3,32,4096]{2,1,0:T(8,128)(2,1)}, u32[]{:S(2)}, u32[]{:S(2)}) %collective-permute-start) | collective-permute-done | bytes 786464 | tf_op jit(solution)/shard_map/ppermute | solution.py:19
  57.2 2.1 broadcast_select_fusion.1.refs_0_
  59.2 0.0 collective-permute-done.1.refs_2_
  59.2 5.0 %shard_map.28 = bf16[4,32,4096]{2,1,0:T(8,128)(2,1)} custom-call(bf16[3,32,4096]{2,1,0:T(8,128)(2,1)} %broadcast_select_fusion.1.refs_0_, bf16[4,32,4096]{2,1,0:T(8,128)(2,1)} %broadcast_select_fusion.refs_1_, bf16[4,32,4096]{2,1,0:T(8,128)(2,1)} %collective-permute-done.1.refs_2_, f32[8,4096]{1,0:T(8,128)} %fusion.22.refs_3_, f32[32,1]{1,0:T(8,128)} %copy.17.refs_4_), custom_call_target="tpu_custom_call" | custom-call | tf_op jit(solution)/shard_map/pallas_call | solution.py:69
  64.2 8.4 %convolution_convert_fusion = bf16[128,2048]{1,0:T(8,128)(2,1)S(1)} fusion(bf16[128,4096]{1,0:T(8,128)(2,1)} %bitcast.40, bf16[4096,2048]{1,0:T(8,128)(2,1)} %fusion), kind=kOutput, calls=%fused_computation.5 | convolution fusion | flops 2147745792 | bytes 18350080 | tf_op jit(solution)/shard_map/dot_general | solution.py:137
  72.6 0.4 reshape.122
  73.0 1.9 copy.18
  74.9 2.0 reshape.124
  76.9 36.9 %all_to_all.18 = bf16[32,2,4096]{2,1,0:T(2,128)(2,1)S(1)} all-to-all(bf16[32,2,4096]{2,1,0:T(2,128)(2,1)S(1)} %reshape.124), channel_id=1, replica_groups=mesh['chan'=32,'inp'=16] {'chan'}, dimensions={0} | all-to-all | bytes 1048576 | tf_op jit(solution)/shard_map/all_to_all | solution.py:139
  113.9 1.0 reshape.125
  114.9 3.8 %copy.24 = bf16[4,32,2,32,32]{4,1,2,0,3:T(8,128)(2,1)} copy(bf16[4,32,2,32,32]{1,2,0,4,3:T(2,128)(2,1)S(1)} %bitcast.37) | data formatting | bytes 1048576 | tf_op jit(solution)/shard_map/all_to_all | solution.py:139
  118.7 3.7 %copy.21 = bf16[32,32,2,128]{3,2,1,0:T(2,128)(2,1)S(1)} copy(bf16[32,32,2,128]{0,1,2,3:T(8,128)(2,1)} %bitcast.38) | data formatting | bytes 1048576 | tf_op jit(solution)/shard_map/transpose | solution.py:142
  122.4 0.3 reshape.123
  122.7 9.2 %collective-permute-start.3 = (bf16[32,32,256]{2,1,0:T(8,128)(2,1)S(1)}, bf16[32,32,256]{2,1,0:T(8,128)(2,1)S(1)}, u32[]{:S(2)}, u32[]{:S(2)}) collective-permute-start(bf16[32,32,256]{2,1,0:T(8,128)(2,1)S(1)} %reshape.123), channel_id=1, source_target_pairs={{0,8},{1,9},{2,10},{3,11},{4,12},{5,13},{6,14},{7,15},{8,0},{9,1},... | collective-permute-start | bytes 1572872 | tf_op jit(solution)/shard_map/ppermute | solution.py:23
  132.0 4.0 %collective-permute-start.2 = (bf16[32,32,256]{2,1,0:T(8,128)(2,1)S(1)}, bf16[32,32,256]{2,1,0:T(8,128)(2,1)}, u32[]{:S(2)}, u32[]{:S(2)}) collective-permute-start(bf16[32,32,256]{2,1,0:T(8,128)(2,1)S(1)} %reshape.123), channel_id=1, source_target_pairs={{0,1},{1,0},{2,3},{3,2},{4,5},{5,4},{6,7},{7,6},{8,9},{9,8},{10,11... | collective-permute-start | bytes 1572872 | tf_op jit(solution)/shard_map/ppermute | solution.py:23
  136.0 2.1 collective-permute-start.5
  138.1 3.2 %collective-permute-start.9 = (bf16[32,32,256]{2,1,0:T(8,128)(2,1)S(1)}, bf16[32,32,256]{2,1,0:T(8,128)(2,1)S(1)}, u32[]{:S(2)}, u32[]{:S(2)}) collective-permute-start(bf16[32,32,256]{2,1,0:T(8,128)(2,1)S(1)} %reshape.123), channel_id=1, source_target_pairs={{0,6},{1,7},{2,0},{3,1},{4,2},{5,3},{6,4},{7,5},{8,14},{9,15},{10,... | collective-permute-start | bytes 1572872 | tf_op jit(solution)/shard_map/ppermute | solution.py:23
  141.3 38.0 %collective-permute-done.3 = bf16[32,32,256]{2,1,0:T(8,128)(2,1)S(1)} collective-permute-done((bf16[32,32,256]{2,1,0:T(8,128)(2,1)S(1)}, bf16[32,32,256]{2,1,0:T(8,128)(2,1)S(1)}, u32[]{:S(2)}, u32[]{:S(2)}) %collective-permute-start.3) | collective-permute-done | bytes 524320 | tf_op jit(solution)/shard_map/ppermute | solution.py:23
  179.3 2.1 collective-permute-start.7
  181.4 3.2 %collective-permute-start.11 = (bf16[32,32,256]{2,1,0:T(8,128)(2,1)S(1)}, bf16[32,32,256]{2,1,0:T(8,128)(2,1)S(1)}, u32[]{:S(2)}, u32[]{:S(2)}) collective-permute-start(bf16[32,32,256]{2,1,0:T(8,128)(2,1)S(1)} %collective-permute-done.3), channel_id=1, source_target_pairs={{0,6},{1,7},{2,0},{3,1},{4,2},{5,3},{6,4},{7,5},{8,14},{9,15},{10,... | collective-permute-start | bytes 1572872 | tf_op jit(solution)/shard_map/ppermute | solution.py:23
  184.8 0.0 collective-permute-done.2
  184.8 3.7 %collective-permute-start.4 = (bf16[32,32,256]{2,1,0:T(8,128)(2,1)S(1)}, bf16[32,32,256]{2,1,0:T(8,128)(2,1)S(1)}, u32[]{:S(2)}, u32[]{:S(2)}) collective-permute-start(bf16[32,32,256]{2,1,0:T(8,128)(2,1)S(1)} %collective-permute-done.3), channel_id=1, source_target_pairs={{0,1},{1,0},{2,3},{3,2},{4,5},{5,4},{6,7},{7,6},{8,9},{9,8},{10,11... | collective-permute-start | bytes 1572872 | tf_op jit(solution)/shard_map/ppermute | solution.py:23
  188.6 0.1 fusion.34
  188.7 0.0 collective-permute-done.5
  188.7 1.9 collective-permute-start.6
  190.6 0.0 collective-permute-done.9
  190.6 3.3 %collective-permute-start.13 = (bf16[32,32,256]{2,1,0:T(8,128)(2,1)S(1)}, bf16[32,32,256]{2,1,0:T(8,128)(2,1)S(1)}, u32[]{:S(2)}, u32[]{:S(2)}) collective-permute-start(bf16[32,32,256]{2,1,0:T(8,128)(2,1)S(1)} %collective-permute-done.5), channel_id=1, source_target_pairs={{0,2},{1,3},{2,4},{3,5},{4,6},{5,7},{6,0},{7,1},{8,10},{9,11},{10,... | collective-permute-start | bytes 1572872 | tf_op jit(solution)/shard_map/ppermute | solution.py:23
  193.9 0.9 broadcast_in_dim.56
  194.9 1.1 constant_dynamic-update-slice_fusion.14
  196.0 0.0 collective-permute-done.7
  196.0 2.7 %collective-permute-start.8 = (bf16[32,32,256]{2,1,0:T(8,128)(2,1)S(1)}, bf16[32,32,256]{2,1,0:T(8,128)(2,1)S(1)}, u32[]{:S(2)}, u32[]{:S(2)}) collective-permute-start(bf16[32,32,256]{2,1,0:T(8,128)(2,1)S(1)} %collective-permute-done.7), channel_id=1, source_target_pairs={{0,1},{1,0},{2,3},{3,2},{4,5},{5,4},{6,7},{7,6},{8,9},{9,8},{10,11... | collective-permute-start | bytes 1572872 | tf_op jit(solution)/shard_map/ppermute | solution.py:23
  198.7 0.0 collective-permute-done.11
  198.7 2.0 collective-permute-start.15
  200.8 2.3 %collective-permute-start.10 = (bf16[32,32,256]{2,1,0:T(8,128)(2,1)S(1)}, bf16[32,32,256]{2,1,0:T(8,128)(2,1)S(1)}, u32[]{:S(2)}, u32[]{:S(2)}) collective-permute-start(bf16[32,32,256]{2,1,0:T(8,128)(2,1)S(1)} %collective-permute-done.9), channel_id=1, source_target_pairs={{0,1},{1,0},{2,3},{3,2},{4,5},{5,4},{6,7},{7,6},{8,9},{9,8},{10,11... | collective-permute-start | bytes 1572872 | tf_op jit(solution)/shard_map/ppermute | solution.py:23
  203.1 0.1 constant_dynamic-update-slice_fusion.12
  203.2 0.0 collective-permute-done.6
  203.2 2.0 collective-permute-start.12
  205.2 0.3 collective-permute-done.13
  205.5 3.2 %collective-permute-start.14 = (bf16[32,32,256]{2,1,0:T(8,128)(2,1)S(1)}, bf16[32,32,256]{2,1,0:T(8,128)(2,1)S(1)}, u32[]{:S(2)}, u32[]{:S(2)}) collective-permute-start(bf16[32,32,256]{2,1,0:T(8,128)(2,1)S(1)} %collective-permute-done.13), channel_id=1, source_target_pairs={{0,1},{1,0},{2,3},{3,2},{4,5},{5,4},{6,7},{7,6},{8,9},{9,8},{10,11... | collective-permute-start | bytes 1572872 | tf_op jit(solution)/shard_map/ppermute | solution.py:23
  208.8 6.4 %collective-permute-done.15 = bf16[32,32,256]{2,1,0:T(8,128)(2,1)S(1)} collective-permute-done((bf16[32,32,256]{2,1,0:T(8,128)(2,1)S(1)}, bf16[32,32,256]{2,1,0:T(8,128)(2,1)S(1)}, u32[]{:S(2)}, u32[]{:S(2)}) %collective-permute-start.15) | collective-permute-done | bytes 524320 | tf_op jit(solution)/shard_map/ppermute | solution.py:23
  215.2 2.8 %collective-permute-start.16 = (bf16[32,32,256]{2,1,0:T(8,128)(2,1)S(1)}, bf16[32,32,256]{2,1,0:T(8,128)(2,1)S(1)}, u32[]{:S(2)}, u32[]{:S(2)}) collective-permute-start(bf16[32,32,256]{2,1,0:T(8,128)(2,1)S(1)} %collective-permute-done.15), channel_id=1, source_target_pairs={{0,1},{1,0},{2,3},{3,2},{4,5},{5,4},{6,7},{7,6},{8,9},{9,8},{10,11... | collective-permute-start | bytes 1572872 | tf_op jit(solution)/shard_map/ppermute | solution.py:23
  218.1 0.0 collective-permute-done.8
  218.1 0.1 constant_dynamic-update-slice_fusion.8
  218.2 0.0 collective-permute-done.10
  218.2 0.1 constant_dynamic-update-slice_fusion.6
  218.3 0.0 collective-permute-done.12
  218.3 0.1 constant_dynamic-update-slice_fusion.4
  218.4 0.1 constant_dynamic-update-slice_fusion.2
  218.6 1.0 collective-permute-done.16
  219.6 2.6 %multiply_convert_fusion = bf16[32,64,512]{2,1,0:T(8,128)(2,1)S(1)} fusion(bf16[32,512,256]{2,1,0:T(8,128)(2,1)S(1)} %constant_dynamic-update-slice_fusion, bf16[32,32,128]{2,1,0:T(8,128)(2,1)S(1)} %get-tuple-element.8, bf16[32,32,128]{2,1,0:T(8,128)(2,1)S(1)} %get-tuple-element.7, bf16[32,32,256]{2,1,0:T(8,128)(2,1)S(1)} %reshape.123), kind=kOutput, calls=%fused_computation.4 | convolution fusion | flops 542113792 | bytes 11534336 | tf_op jit(solution)/shard_map/cik,cjk->cij/dot_general | solution.py:146
  222.3 1.6 copy.30
  (15 shorter events, 0.5 us)
Async XLA Ops:
  2.8 56.5 %collective-permute-start.1 = (bf16[4,32,4096]{2,1,0:T(8,128)(2,1)}, bf16[4,32,4096]{2,1,0:T(8,128)(2,1)}, u32[]{:S(2)}, u32[]{:S(2)}) collective-permute-start(bf16[4,32,4096]{2,1,0:T(8,128)(2,1)} %bitcast.31), channel_id=1, source_target_pairs={{0,496},{16,0},{32,16},{48,32},{64,48},{80,64},{96,80},{112,96},{1... | collective-permute-start | bytes 3145736 | tf_op jit(solution)/shard_map/ppermute | solution.py:131
  20.2 37.0 %collective-permute-start = (bf16[3,32,4096]{2,1,0:T(8,128)(2,1)}, bf16[3,32,4096]{2,1,0:T(8,128)(2,1)}, u32[]{:S(2)}, u32[]{:S(2)}) collective-permute-start(bf16[3,32,4096]{2,1,0:T(8,128)(2,1)} %slice.12), channel_id=1, source_target_pairs={{0,16},{16,32},{32,48},{48,64},{64,80},{80,96},{96,112},{112,128},... | collective-permute-start | bytes 2359304 | tf_op jit(solution)/shard_map/ppermute | solution.py:19
  31.3 10.4 %copy-start = (s32[32]{0:T(128)S(1)}, s32[32]{0:T(128)}, u32[]{:S(2)}) copy-start(s32[32]{0:T(128)} %param.3) | copy-start | bytes 388
  122.7 56.6 %collective-permute-start.3 = (bf16[32,32,256]{2,1,0:T(8,128)(2,1)S(1)}, bf16[32,32,256]{2,1,0:T(8,128)(2,1)S(1)}, u32[]{:S(2)}, u32[]{:S(2)}) collective-permute-start(bf16[32,32,256]{2,1,0:T(8,128)(2,1)S(1)} %reshape.123), channel_id=1, source_target_pairs={{0,8},{1,9},{2,10},{3,11},{4,12},{5,13},{6,14},{7,15},{8,0},{9,1},... | collective-permute-start | bytes 1572872 | tf_op jit(solution)/shard_map/ppermute | solution.py:23
  132.0 52.9 %collective-permute-start.2 = (bf16[32,32,256]{2,1,0:T(8,128)(2,1)S(1)}, bf16[32,32,256]{2,1,0:T(8,128)(2,1)}, u32[]{:S(2)}, u32[]{:S(2)}) collective-permute-start(bf16[32,32,256]{2,1,0:T(8,128)(2,1)S(1)} %reshape.123), channel_id=1, source_target_pairs={{0,1},{1,0},{2,3},{3,2},{4,5},{5,4},{6,7},{7,6},{8,9},{9,8},{10,11... | collective-permute-start | bytes 1572872 | tf_op jit(solution)/shard_map/ppermute | solution.py:23
  136.0 52.7 %collective-permute-start.5 = (bf16[32,32,256]{2,1,0:T(8,128)(2,1)S(1)}, bf16[32,32,256]{2,1,0:T(8,128)(2,1)S(1)}, u32[]{:S(2)}, u32[]{:S(2)}) collective-permute-start(bf16[32,32,256]{2,1,0:T(8,128)(2,1)S(1)} %reshape.123), channel_id=1, source_target_pairs={{0,2},{1,3},{2,4},{3,5},{4,6},{5,7},{6,0},{7,1},{8,10},{9,11},{10,... | collective-permute-start | bytes 1572872 | tf_op jit(solution)/shard_map/ppermute | solution.py:23
  138.1 52.5 %collective-permute-start.9 = (bf16[32,32,256]{2,1,0:T(8,128)(2,1)S(1)}, bf16[32,32,256]{2,1,0:T(8,128)(2,1)S(1)}, u32[]{:S(2)}, u32[]{:S(2)}) collective-permute-start(bf16[32,32,256]{2,1,0:T(8,128)(2,1)S(1)} %reshape.123), channel_id=1, source_target_pairs={{0,6},{1,7},{2,0},{3,1},{4,2},{5,3},{6,4},{7,5},{8,14},{9,15},{10,... | collective-permute-start | bytes 1572872 | tf_op jit(solution)/shard_map/ppermute | solution.py:23
  179.3 16.7 %collective-permute-start.7 = (bf16[32,32,256]{2,1,0:T(8,128)(2,1)S(1)}, bf16[32,32,256]{2,1,0:T(8,128)(2,1)S(1)}, u32[]{:S(2)}, u32[]{:S(2)}) collective-permute-start(bf16[32,32,256]{2,1,0:T(8,128)(2,1)S(1)} %collective-permute-done.3), channel_id=1, source_target_pairs={{0,2},{1,3},{2,4},{3,5},{4,6},{5,7},{6,0},{7,1},{8,10},{9,11},{10,... | collective-permute-start | bytes 1572872 | tf_op jit(solution)/shard_map/ppermute | solution.py:23
  181.4 17.3 %collective-permute-start.11 = (bf16[32,32,256]{2,1,0:T(8,128)(2,1)S(1)}, bf16[32,32,256]{2,1,0:T(8,128)(2,1)S(1)}, u32[]{:S(2)}, u32[]{:S(2)}) collective-permute-start(bf16[32,32,256]{2,1,0:T(8,128)(2,1)S(1)} %collective-permute-done.3), channel_id=1, source_target_pairs={{0,6},{1,7},{2,0},{3,1},{4,2},{5,3},{6,4},{7,5},{8,14},{9,15},{10,... | collective-permute-start | bytes 1572872 | tf_op jit(solution)/shard_map/ppermute | solution.py:23
  184.8 15.9 %collective-permute-start.4 = (bf16[32,32,256]{2,1,0:T(8,128)(2,1)S(1)}, bf16[32,32,256]{2,1,0:T(8,128)(2,1)S(1)}, u32[]{:S(2)}, u32[]{:S(2)}) collective-permute-start(bf16[32,32,256]{2,1,0:T(8,128)(2,1)S(1)} %collective-permute-done.3), channel_id=1, source_target_pairs={{0,1},{1,0},{2,3},{3,2},{4,5},{5,4},{6,7},{7,6},{8,9},{9,8},{10,11... | collective-permute-start | bytes 1572872 | tf_op jit(solution)/shard_map/ppermute | solution.py:23
  188.7 14.6 %collective-permute-start.6 = (bf16[32,32,256]{2,1,0:T(8,128)(2,1)S(1)}, bf16[32,32,256]{2,1,0:T(8,128)(2,1)S(1)}, u32[]{:S(2)}, u32[]{:S(2)}) collective-permute-start(bf16[32,32,256]{2,1,0:T(8,128)(2,1)S(1)} %collective-permute-done.5), channel_id=1, source_target_pairs={{0,1},{1,0},{2,3},{3,2},{4,5},{5,4},{6,7},{7,6},{8,9},{9,8},{10,11... | collective-permute-start | bytes 1572872 | tf_op jit(solution)/shard_map/ppermute | solution.py:23
  190.6 14.9 %collective-permute-start.13 = (bf16[32,32,256]{2,1,0:T(8,128)(2,1)S(1)}, bf16[32,32,256]{2,1,0:T(8,128)(2,1)S(1)}, u32[]{:S(2)}, u32[]{:S(2)}) collective-permute-start(bf16[32,32,256]{2,1,0:T(8,128)(2,1)S(1)} %collective-permute-done.5), channel_id=1, source_target_pairs={{0,2},{1,3},{2,4},{3,5},{4,6},{5,7},{6,0},{7,1},{8,10},{9,11},{10,... | collective-permute-start | bytes 1572872 | tf_op jit(solution)/shard_map/ppermute | solution.py:23
  196.0 22.1 %collective-permute-start.8 = (bf16[32,32,256]{2,1,0:T(8,128)(2,1)S(1)}, bf16[32,32,256]{2,1,0:T(8,128)(2,1)S(1)}, u32[]{:S(2)}, u32[]{:S(2)}) collective-permute-start(bf16[32,32,256]{2,1,0:T(8,128)(2,1)S(1)} %collective-permute-done.7), channel_id=1, source_target_pairs={{0,1},{1,0},{2,3},{3,2},{4,5},{5,4},{6,7},{7,6},{8,9},{9,8},{10,11... | collective-permute-start | bytes 1572872 | tf_op jit(solution)/shard_map/ppermute | solution.py:23
  198.7 16.5 %collective-permute-start.15 = (bf16[32,32,256]{2,1,0:T(8,128)(2,1)S(1)}, bf16[32,32,256]{2,1,0:T(8,128)(2,1)S(1)}, u32[]{:S(2)}, u32[]{:S(2)}) collective-permute-start(bf16[32,32,256]{2,1,0:T(8,128)(2,1)S(1)} %collective-permute-done.11), channel_id=1, source_target_pairs={{0,6},{1,7},{2,0},{3,1},{4,2},{5,3},{6,4},{7,5},{8,14},{9,15},{10,... | collective-permute-start | bytes 1572872 | tf_op jit(solution)/shard_map/ppermute | solution.py:23
  200.8 17.4 %collective-permute-start.10 = (bf16[32,32,256]{2,1,0:T(8,128)(2,1)S(1)}, bf16[32,32,256]{2,1,0:T(8,128)(2,1)S(1)}, u32[]{:S(2)}, u32[]{:S(2)}) collective-permute-start(bf16[32,32,256]{2,1,0:T(8,128)(2,1)S(1)} %collective-permute-done.9), channel_id=1, source_target_pairs={{0,1},{1,0},{2,3},{3,2},{4,5},{5,4},{6,7},{7,6},{8,9},{9,8},{10,11... | collective-permute-start | bytes 1572872 | tf_op jit(solution)/shard_map/ppermute | solution.py:23
  203.2 15.1 %collective-permute-start.12 = (bf16[32,32,256]{2,1,0:T(8,128)(2,1)S(1)}, bf16[32,32,256]{2,1,0:T(8,128)(2,1)S(1)}, u32[]{:S(2)}, u32[]{:S(2)}) collective-permute-start(bf16[32,32,256]{2,1,0:T(8,128)(2,1)S(1)} %collective-permute-done.11), channel_id=1, source_target_pairs={{0,1},{1,0},{2,3},{3,2},{4,5},{5,4},{6,7},{7,6},{8,9},{9,8},{10,11... | collective-permute-start | bytes 1572872 | tf_op jit(solution)/shard_map/ppermute | solution.py:23
  205.5 13.0 %collective-permute-start.14 = (bf16[32,32,256]{2,1,0:T(8,128)(2,1)S(1)}, bf16[32,32,256]{2,1,0:T(8,128)(2,1)S(1)}, u32[]{:S(2)}, u32[]{:S(2)}) collective-permute-start(bf16[32,32,256]{2,1,0:T(8,128)(2,1)S(1)} %collective-permute-done.13), channel_id=1, source_target_pairs={{0,1},{1,0},{2,3},{3,2},{4,5},{5,4},{6,7},{7,6},{8,9},{9,8},{10,11... | collective-permute-start | bytes 1572872 | tf_op jit(solution)/shard_map/ppermute | solution.py:23
  215.2 4.4 %collective-permute-start.16 = (bf16[32,32,256]{2,1,0:T(8,128)(2,1)S(1)}, bf16[32,32,256]{2,1,0:T(8,128)(2,1)S(1)}, u32[]{:S(2)}, u32[]{:S(2)}) collective-permute-start(bf16[32,32,256]{2,1,0:T(8,128)(2,1)S(1)} %collective-permute-done.15), channel_id=1, source_target_pairs={{0,1},{1,0},{2,3},{3,2},{4,5},{5,4},{6,7},{7,6},{8,9},{9,8},{10,11... | collective-permute-start | bytes 1572872 | tf_op jit(solution)/shard_map/ppermute | solution.py:23

commit v13 on v12

--- a/solution.py
+++ b/solution.py
@@ -53,9 +53,9 @@
 
 
 def polyphase_kernel(spec_count, *refs):
-    pieces, (w_ref, g_ref, o_ref) = refs[:-3], refs[-3:]
-    gain = g_ref[...]
-    rows = [p[k].astype(jnp.float32) * gain for p in pieces for k in range(p.shape[0])]
+    pieces, (w_ref, c_ref, g_ref, o_ref) = refs[:-4], refs[-4:]
+    gains = [c_ref[...]] * (len(pieces) - 1) + [g_ref[...]]
+    rows = [p[k].astype(jnp.float32) * g for p, g in zip(pieces, gains) for k in range(p.shape[0])]
     for s in range(spec_count):
         total = jnp.zeros(o_ref.shape[1:], jnp.float32)
         for tap in range(TAPS):
@@ -63,7 +63,7 @@
         o_ref[s] = total.astype(o_ref.dtype)
 
 
-def polyphase(pieces, window, gain, spec_count):
+def polyphase(pieces, window, context_gain, gain, spec_count):
     inputs, length = pieces[0].shape[1:]
     lanes = 2048
     return pl.pallas_call(
@@ -74,9 +74,10 @@
         + [
             pl.BlockSpec((TAPS, lanes), lambda k: (0, k)),
             pl.BlockSpec((inputs, 1), lambda k: (0, 0)),
+            pl.BlockSpec((inputs, 1), lambda k: (0, 0)),
         ],
         out_specs=pl.BlockSpec((spec_count, inputs, lanes), lambda k: (0, 0, k)),
-    )(*pieces, window, gain)
+    )(*pieces, window, context_gain, gain)
 
 
 def gather_inputs(own):
@@ -129,10 +130,9 @@
     last = lax.axis_index("chan") == count - 1
     from_prev = shifted(samples[spec_count - behind :], "chan", 1)
     from_next = lax.ppermute(samples, "chan", [(i, (i - 1) % count) for i in range(count)])
-    earlier = [jnp.where(last, jnp.zeros_like(from_prev), from_prev), jnp.where(last, jnp.zeros_like(samples), samples)]
-    samples = from_next
     gain = (scales.astype(jnp.float32) * (1.0 / 256.0)).reshape(inp_count, 1)
-    filtered = polyphase(earlier + [samples], window_table(), gain, spec_count)
+    context_gain = jnp.where(last, jnp.zeros_like(gain), gain)
+    filtered = polyphase([from_prev, samples, from_next], window_table(), context_gain, gain, spec_count)
     filtered = filtered.reshape(spec_count * inp_count, NFFT)
     spectra = jnp.dot(filtered, dft_table(), preferred_element_type=jnp.float32).astype(jnp.bfloat16)
     spectra = spectra.reshape(spec_count, inp_count, 2, CHANS)

time: 225 us -> 220 us (0.978)
  other arithmetic: 23.1 us -> 18 us
    ppermute x1, waiting for transfers between devices: 14.8 us -> 18.1 us  [shifted(): return lax.ppermute(block, axis, route)]
    select_n x2 -> x0, other arithmetic: 3.09 us -> none  [the longest x1 2.06 us: shards(): jnp.where(last, jnp.zeros_like(from_prev), from_prev)]
  transfers between devices with their start and end apart: 17 -> 17, of which waited for: 5 -> 5; matrix products, arithmetic and copies ran while one was open for 12% -> 10% of each run, Pallas kernels for 0% -> 0%
where the time goes in v13:
time: 220 us
  starting transfers between devices  67.2 us (31%)
  waiting for transfers between devices  61.8 us (28%)
  blocking collectives  36.1 us (16%)
  local copies, waits for them, and re-layouts  19.8 us (9%)
  other arithmetic  18 us (8%)
  matrix products  11.1 us (5%)
  Pallas kernels  5 us (2%)
    ppermute x15, starting transfers between devices, moved(): lax.ppermute(block, 'inp', [(p, mapping(p)) for p in range(lax.axis_size(...  49.7 us
    ppermute x15, waiting for transfers between devices, moved(): lax.ppermute(block, 'inp', [(p, mapping(p)) for p in range(lax.axis_size(...  43.7 us
    all_to_all x1, blocking collectives, shards(): lax.all_to_all(spectra, 'chan', split_axis=3, concat_axis=0, tiled=True)  36.1 us
    ppermute x1, waiting for transfers between devices, shifted(): return lax.ppermute(block, axis, route)  18.1 us
    ppermute x1, starting transfers between devices, shards(): lax.ppermute(samples, 'chan', [(i, (i - 1) % count) for i in range(count)])  15.3 us
    dot_general x1, matrix products, shards(): jnp.dot(filtered, dft_table(), preferred_element_type=jnp.float32)  8.44 us
    convert_element_type x1, other arithmetic, dft_table(): return lax.optimization_barrier(both.astype(jnp.bfloat16))  8.03 us
    pallas_call x1, Pallas kernels, polyphase(): pl.pallas_call(functools.partial(polyphase_kernel, spec_count), out_shape...  5 us
  transfers between devices with their start and end apart: 17, of which 5 were waited for; matrix products, arithmetic and copies ran while one was open for 10% of the time, Pallas kernels for 0%

profile of v13, /device:TPU:7, one launch (start us, length us, event | category | flops | bytes accessed | tf_op | source)
XLA Modules:
  0.0 219.6 jit_solution(8929451644346776697)
XLA Ops:
  0.0 1.7 convert_element_type.58
  1.7 0.1 copy.33
  1.8 0.0 copy-start
  1.8 15.3 %collective-permute-start.1 = (bf16[4,32,4096]{2,1,0:T(8,128)(2,1)S(1)}, bf16[4,32,4096]{2,1,0:T(8,128)(2,1)}, u32[]{:S(2)}, u32[]{:S(2)}) collective-permute-start(bf16[4,32,4096]{2,1,0:T(8,128)(2,1)S(1)} %bitcast.36), channel_id=1, source_target_pairs={{0,496},{16,0},{32,16},{48,32},{64,48},{80,64},{96,80},{112,96},{1... | collective-permute-start | bytes 3145736 | tf_op jit(solution)/shard_map/ppermute | solution.py:132
  17.1 1.0 slice.12
  18.1 2.2 collective-permute-start
  20.3 1.0 sine_negate_fusion
  21.3 1.1 fusion.27
  22.4 4.8 %multiply_subtract_fusion = (f32[64,64,1024]{2,1,0:T(8,128)S(1)}, f32[64,64,1024]{2,1,0:T(8,128)S(1)}) fusion(f32[64,1024]{1,0:T(8,128)S(1)} %get-tuple-element.13, f32[64,1024]{1,0:T(8,128)S(1)} %get-tuple-element.10, f32[64,1024]{1,0:T(8,128)S(1)} %get-tuple-element.14, f32[64,1024]{1,0:T(8,128)S(1)} %get-tuple-element.9), kind=kLoop, calls=%fused_computation.3 | loop fusion | flops 25165824 | bytes 34603008 | tf_op jit(solution)/shard_map/sub | solution.py:49
  27.2 0.0 copy-start.1
  27.3 8.0 %fusion = bf16[4096,2048]{1,0:T(8,128)(2,1)} fusion(f32[4096,1024]{1,0:T(8,128)S(1)} %bitcast.31, f32[4096,1024]{1,0:T(8,128)S(1)} %bitcast.30), kind=kLoop, calls=%fused_computation.1 | loop fusion | flops 25165824 | bytes 50331648 | tf_op jit(solution)/shard_map/convert_element_type | solution.py:52
  35.3 0.7 copy.20.refs_4_
  36.0 0.7 copy.21.refs_5_
  36.7 1.3 fusion.22.refs_3_
  37.9 18.1 %collective-permute-done.refs_0_ = bf16[3,32,4096]{2,1,0:T(8,128)(2,1)} collective-permute-done((bf16[3,32,4096]{2,1,0:T(8,128)(2,1)}, bf16[3,32,4096]{2,1,0:T(8,128)(2,1)}, u32[]{:S(2)}, u32[]{:S(2)}) %collective-permute-start) | collective-permute-done | bytes 786464 | tf_op jit(solution)/shard_map/ppermute | solution.py:19
  56.0 0.0 collective-permute-done.1.refs_2_
  56.0 5.0 %shard_map.28 = bf16[4,32,4096]{2,1,0:T(8,128)(2,1)} custom-call(bf16[3,32,4096]{2,1,0:T(8,128)(2,1)} %collective-permute-done.refs_0_, bf16[4,32,4096]{2,1,0:T(8,128)(2,1)} %bitcast.38, bf16[4,32,4096]{2,1,0:T(8,128)(2,1)} %collective-permute-done.1.refs_2_, f32[8,4096]{1,0:T(8,128)} %fusion.22.refs_3_, f32[32,1]{1,0:T(8,128)} %copy.20.refs_4_, ...), custom_call_target="tpu_custom_call" | custom-call | tf_op jit(solution)/shard_map/pallas_call | solution.py:69
  61.0 8.4 %convolution_convert_fusion = bf16[128,2048]{1,0:T(8,128)(2,1)S(1)} fusion(bf16[128,4096]{1,0:T(8,128)(2,1)} %bitcast.39, bf16[4096,2048]{1,0:T(8,128)(2,1)} %fusion), kind=kOutput, calls=%fused_computation.5 | convolution fusion | flops 2147745792 | bytes 18350080 | tf_op jit(solution)/shard_map/dot_general | solution.py:137
  69.4 0.4 reshape.123
  69.8 1.9 copy.22
  71.7 2.0 reshape.125
  73.7 36.1 %all_to_all.18 = bf16[32,2,4096]{2,1,0:T(2,128)(2,1)S(1)} all-to-all(bf16[32,2,4096]{2,1,0:T(2,128)(2,1)S(1)} %reshape.125), channel_id=1, replica_groups=mesh['chan'=32,'inp'=16] {'chan'}, dimensions={0} | all-to-all | bytes 1048576 | tf_op jit(solution)/shard_map/all_to_all | solution.py:139
  109.8 1.0 reshape.126
  110.8 3.8 %copy.28 = bf16[4,32,2,32,32]{4,1,2,0,3:T(8,128)(2,1)} copy(bf16[4,32,2,32,32]{1,2,0,4,3:T(2,128)(2,1)S(1)} %bitcast.33) | data formatting | bytes 1048576 | tf_op jit(solution)/shard_map/all_to_all | solution.py:139
  114.6 3.7 %copy.25 = bf16[32,32,2,128]{3,2,1,0:T(2,128)(2,1)S(1)} copy(bf16[32,32,2,128]{0,1,2,3:T(8,128)(2,1)} %bitcast.34) | data formatting | bytes 1048576 | tf_op jit(solution)/shard_map/transpose | solution.py:142
  118.3 0.3 reshape.124
  118.6 10.0 %collective-permute-start.3 = (bf16[32,32,256]{2,1,0:T(8,128)(2,1)S(1)}, bf16[32,32,256]{2,1,0:T(8,128)(2,1)S(1)}, u32[]{:S(2)}, u32[]{:S(2)}) collective-permute-start(bf16[32,32,256]{2,1,0:T(8,128)(2,1)S(1)} %reshape.124), channel_id=1, source_target_pairs={{0,8},{1,9},{2,10},{3,11},{4,12},{5,13},{6,14},{7,15},{8,0},{9,1},... | collective-permute-start | bytes 1572872 | tf_op jit(solution)/shard_map/ppermute | solution.py:23
  128.6 4.0 %collective-permute-start.2 = (bf16[32,32,256]{2,1,0:T(8,128)(2,1)S(1)}, bf16[32,32,256]{2,1,0:T(8,128)(2,1)}, u32[]{:S(2)}, u32[]{:S(2)}) collective-permute-start(bf16[32,32,256]{2,1,0:T(8,128)(2,1)S(1)} %reshape.124), channel_id=1, source_target_pairs={{0,1},{1,0},{2,3},{3,2},{4,5},{5,4},{6,7},{7,6},{8,9},{9,8},{10,11... | collective-permute-start | bytes 1572872 | tf_op jit(solution)/shard_map/ppermute | solution.py:23
  132.6 2.1 collective-permute-start.5
  134.7 3.2 %collective-permute-start.9 = (bf16[32,32,256]{2,1,0:T(8,128)(2,1)S(1)}, bf16[32,32,256]{2,1,0:T(8,128)(2,1)S(1)}, u32[]{:S(2)}, u32[]{:S(2)}) collective-permute-start(bf16[32,32,256]{2,1,0:T(8,128)(2,1)S(1)} %reshape.124), channel_id=1, source_target_pairs={{0,6},{1,7},{2,0},{3,1},{4,2},{5,3},{6,4},{7,5},{8,14},{9,15},{10,... | collective-permute-start | bytes 1572872 | tf_op jit(solution)/shard_map/ppermute | solution.py:23
  137.9 35.9 %collective-permute-done.3 = bf16[32,32,256]{2,1,0:T(8,128)(2,1)S(1)} collective-permute-done((bf16[32,32,256]{2,1,0:T(8,128)(2,1)S(1)}, bf16[32,32,256]{2,1,0:T(8,128)(2,1)S(1)}, u32[]{:S(2)}, u32[]{:S(2)}) %collective-permute-start.3) | collective-permute-done | bytes 524320 | tf_op jit(solution)/shard_map/ppermute | solution.py:23
  173.8 2.0 collective-permute-start.7
  175.9 3.3 %collective-permute-start.11 = (bf16[32,32,256]{2,1,0:T(8,128)(2,1)S(1)}, bf16[32,32,256]{2,1,0:T(8,128)(2,1)S(1)}, u32[]{:S(2)}, u32[]{:S(2)}) collective-permute-start(bf16[32,32,256]{2,1,0:T(8,128)(2,1)S(1)} %collective-permute-done.3), channel_id=1, source_target_pairs={{0,6},{1,7},{2,0},{3,1},{4,2},{5,3},{6,4},{7,5},{8,14},{9,15},{10,... | collective-permute-start | bytes 1572872 | tf_op jit(solution)/shard_map/ppermute | solution.py:23
  179.4 0.0 collective-permute-done.2
  179.4 5.0 %collective-permute-start.4 = (bf16[32,32,256]{2,1,0:T(8,128)(2,1)S(1)}, bf16[32,32,256]{2,1,0:T(8,128)(2,1)S(1)}, u32[]{:S(2)}, u32[]{:S(2)}) collective-permute-start(bf16[32,32,256]{2,1,0:T(8,128)(2,1)S(1)} %collective-permute-done.3), channel_id=1, source_target_pairs={{0,1},{1,0},{2,3},{3,2},{4,5},{5,4},{6,7},{7,6},{8,9},{9,8},{10,11... | collective-permute-start | bytes 1572872 | tf_op jit(solution)/shard_map/ppermute | solution.py:23
  184.4 0.1 fusion.36
  184.5 0.0 collective-permute-done.5
  184.5 1.9 collective-permute-start.6
  186.4 0.0 collective-permute-done.9
  186.4 3.2 %collective-permute-start.13 = (bf16[32,32,256]{2,1,0:T(8,128)(2,1)S(1)}, bf16[32,32,256]{2,1,0:T(8,128)(2,1)S(1)}, u32[]{:S(2)}, u32[]{:S(2)}) collective-permute-start(bf16[32,32,256]{2,1,0:T(8,128)(2,1)S(1)} %collective-permute-done.5), channel_id=1, source_target_pairs={{0,2},{1,3},{2,4},{3,5},{4,6},{5,7},{6,0},{7,1},{8,10},{9,11},{10,... | collective-permute-start | bytes 1572872 | tf_op jit(solution)/shard_map/ppermute | solution.py:23
  189.7 0.9 broadcast_in_dim.52
  190.6 1.1 constant_dynamic-update-slice_fusion.14
  191.7 0.0 collective-permute-done.7
  191.7 2.7 %collective-permute-start.8 = (bf16[32,32,256]{2,1,0:T(8,128)(2,1)S(1)}, bf16[32,32,256]{2,1,0:T(8,128)(2,1)S(1)}, u32[]{:S(2)}, u32[]{:S(2)}) collective-permute-start(bf16[32,32,256]{2,1,0:T(8,128)(2,1)S(1)} %collective-permute-done.7), channel_id=1, source_target_pairs={{0,1},{1,0},{2,3},{3,2},{4,5},{5,4},{6,7},{7,6},{8,9},{9,8},{10,11... | collective-permute-start | bytes 1572872 | tf_op jit(solution)/shard_map/ppermute | solution.py:23
  194.4 0.0 collective-permute-done.11
  194.5 2.0 collective-permute-start.15
  196.6 0.0 collective-permute-done.4
  196.6 2.2 %collective-permute-start.10 = (bf16[32,32,256]{2,1,0:T(8,128)(2,1)S(1)}, bf16[32,32,256]{2,1,0:T(8,128)(2,1)S(1)}, u32[]{:S(2)}, u32[]{:S(2)}) collective-permute-start(bf16[32,32,256]{2,1,0:T(8,128)(2,1)S(1)} %collective-permute-done.9), channel_id=1, source_target_pairs={{0,1},{1,0},{2,3},{3,2},{4,5},{5,4},{6,7},{7,6},{8,9},{9,8},{10,11... | collective-permute-start | bytes 1572872 | tf_op jit(solution)/shard_map/ppermute | solution.py:23
  198.8 0.1 constant_dynamic-update-slice_fusion.12
  198.9 0.0 collective-permute-done.6
  198.9 2.1 collective-permute-start.12
  201.0 0.3 collective-permute-done.13
  201.3 3.2 %collective-permute-start.14 = (bf16[32,32,256]{2,1,0:T(8,128)(2,1)S(1)}, bf16[32,32,256]{2,1,0:T(8,128)(2,1)S(1)}, u32[]{:S(2)}, u32[]{:S(2)}) collective-permute-start(bf16[32,32,256]{2,1,0:T(8,128)(2,1)S(1)} %collective-permute-done.13), channel_id=1, source_target_pairs={{0,1},{1,0},{2,3},{3,2},{4,5},{5,4},{6,7},{7,6},{8,9},{9,8},{10,11... | collective-permute-start | bytes 1572872 | tf_op jit(solution)/shard_map/ppermute | solution.py:23
  204.6 6.5 %collective-permute-done.15 = bf16[32,32,256]{2,1,0:T(8,128)(2,1)S(1)} collective-permute-done((bf16[32,32,256]{2,1,0:T(8,128)(2,1)S(1)}, bf16[32,32,256]{2,1,0:T(8,128)(2,1)S(1)}, u32[]{:S(2)}, u32[]{:S(2)}) %collective-permute-start.15) | collective-permute-done | bytes 524320 | tf_op jit(solution)/shard_map/ppermute | solution.py:23
  211.1 2.7 %collective-permute-start.16 = (bf16[32,32,256]{2,1,0:T(8,128)(2,1)S(1)}, bf16[32,32,256]{2,1,0:T(8,128)(2,1)S(1)}, u32[]{:S(2)}, u32[]{:S(2)}) collective-permute-start(bf16[32,32,256]{2,1,0:T(8,128)(2,1)S(1)} %collective-permute-done.15), channel_id=1, source_target_pairs={{0,1},{1,0},{2,3},{3,2},{4,5},{5,4},{6,7},{7,6},{8,9},{9,8},{10,11... | collective-permute-start | bytes 1572872 | tf_op jit(solution)/shard_map/ppermute | solution.py:23
  213.8 0.0 collective-permute-done.8
  213.8 0.1 constant_dynamic-update-slice_fusion.8
  213.9 0.0 collective-permute-done.10
  213.9 0.1 constant_dynamic-update-slice_fusion.6
  214.0 0.1 constant_dynamic-update-slice_fusion.4
  214.2 0.1 constant_dynamic-update-slice_fusion.2
  214.3 1.0 collective-permute-done.16
  215.4 2.6 %multiply_convert_fusion = bf16[32,64,512]{2,1,0:T(8,128)(2,1)S(1)} fusion(bf16[32,512,256]{2,1,0:T(8,128)(2,1)S(1)} %constant_dynamic-update-slice_fusion, bf16[32,32,128]{2,1,0:T(8,128)(2,1)S(1)} %get-tuple-element.8, bf16[32,32,128]{2,1,0:T(8,128)(2,1)S(1)} %get-tuple-element.7, bf16[32,32,256]{2,1,0:T(8,128)(2,1)S(1)} %reshape.124), kind=kOutput, calls=%fused_computation.4 | convolution fusion | flops 542113792 | bytes 11534336 | tf_op jit(solution)/shard_map/cik,cjk->cij/dot_general | solution.py:146
  218.0 1.6 copy.32
  (16 shorter events, 0.5 us)
Async XLA Ops:
  1.8 25.5 %copy-start = (bf16[4,4,8,4096]{3,2,0,1:T(8,128)(2,1)}, bf16[4,4,8,4096]{3,2,0,1:T(8,128)(2,1)S(1)}, u32[]{:S(2)}) copy-start(bf16[4,4,8,4096]{3,2,0,1:T(8,128)(2,1)S(1)} %copy.33) | copy-start | bytes 3145732
  1.8 54.2 %collective-permute-start.1 = (bf16[4,32,4096]{2,1,0:T(8,128)(2,1)S(1)}, bf16[4,32,4096]{2,1,0:T(8,128)(2,1)}, u32[]{:S(2)}, u32[]{:S(2)}) collective-permute-start(bf16[4,32,4096]{2,1,0:T(8,128)(2,1)S(1)} %bitcast.36), channel_id=1, source_target_pairs={{0,496},{16,0},{32,16},{48,32},{64,48},{80,64},{96,80},{112,96},{1... | collective-permute-start | bytes 3145736 | tf_op jit(solution)/shard_map/ppermute | solution.py:132
  18.1 37.9 %collective-permute-start = (bf16[3,32,4096]{2,1,0:T(8,128)(2,1)}, bf16[3,32,4096]{2,1,0:T(8,128)(2,1)}, u32[]{:S(2)}, u32[]{:S(2)}) collective-permute-start(bf16[3,32,4096]{2,1,0:T(8,128)(2,1)} %slice.12), channel_id=1, source_target_pairs={{0,16},{16,32},{32,48},{48,64},{64,80},{80,96},{96,112},{112,128},... | collective-permute-start | bytes 2359304 | tf_op jit(solution)/shard_map/ppermute | solution.py:19
  27.2 8.0 %copy-start.1 = (s32[32]{0:T(128)S(1)}, s32[32]{0:T(128)}, u32[]{:S(2)}) copy-start(s32[32]{0:T(128)} %param.3) | copy-start | bytes 388
  118.6 55.2 %collective-permute-start.3 = (bf16[32,32,256]{2,1,0:T(8,128)(2,1)S(1)}, bf16[32,32,256]{2,1,0:T(8,128)(2,1)S(1)}, u32[]{:S(2)}, u32[]{:S(2)}) collective-permute-start(bf16[32,32,256]{2,1,0:T(8,128)(2,1)S(1)} %reshape.124), channel_id=1, source_target_pairs={{0,8},{1,9},{2,10},{3,11},{4,12},{5,13},{6,14},{7,15},{8,0},{9,1},... | collective-permute-start | bytes 1572872 | tf_op jit(solution)/shard_map/ppermute | solution.py:23
  128.6 50.7 %collective-permute-start.2 = (bf16[32,32,256]{2,1,0:T(8,128)(2,1)S(1)}, bf16[32,32,256]{2,1,0:T(8,128)(2,1)}, u32[]{:S(2)}, u32[]{:S(2)}) collective-permute-start(bf16[32,32,256]{2,1,0:T(8,128)(2,1)S(1)} %reshape.124), channel_id=1, source_target_pairs={{0,1},{1,0},{2,3},{3,2},{4,5},{5,4},{6,7},{7,6},{8,9},{9,8},{10,11... | collective-permute-start | bytes 1572872 | tf_op jit(solution)/shard_map/ppermute | solution.py:23
  132.6 51.8 %collective-permute-start.5 = (bf16[32,32,256]{2,1,0:T(8,128)(2,1)S(1)}, bf16[32,32,256]{2,1,0:T(8,128)(2,1)S(1)}, u32[]{:S(2)}, u32[]{:S(2)}) collective-permute-start(bf16[32,32,256]{2,1,0:T(8,128)(2,1)S(1)} %reshape.124), channel_id=1, source_target_pairs={{0,2},{1,3},{2,4},{3,5},{4,6},{5,7},{6,0},{7,1},{8,10},{9,11},{10,... | collective-permute-start | bytes 1572872 | tf_op jit(solution)/shard_map/ppermute | solution.py:23
  134.7 51.7 %collective-permute-start.9 = (bf16[32,32,256]{2,1,0:T(8,128)(2,1)S(1)}, bf16[32,32,256]{2,1,0:T(8,128)(2,1)S(1)}, u32[]{:S(2)}, u32[]{:S(2)}) collective-permute-start(bf16[32,32,256]{2,1,0:T(8,128)(2,1)S(1)} %reshape.124), channel_id=1, source_target_pairs={{0,6},{1,7},{2,0},{3,1},{4,2},{5,3},{6,4},{7,5},{8,14},{9,15},{10,... | collective-permute-start | bytes 1572872 | tf_op jit(solution)/shard_map/ppermute | solution.py:23
  173.8 17.9 %collective-permute-start.7 = (bf16[32,32,256]{2,1,0:T(8,128)(2,1)S(1)}, bf16[32,32,256]{2,1,0:T(8,128)(2,1)S(1)}, u32[]{:S(2)}, u32[]{:S(2)}) collective-permute-start(bf16[32,32,256]{2,1,0:T(8,128)(2,1)S(1)} %collective-permute-done.3), channel_id=1, source_target_pairs={{0,2},{1,3},{2,4},{3,5},{4,6},{5,7},{6,0},{7,1},{8,10},{9,11},{10,... | collective-permute-start | bytes 1572872 | tf_op jit(solution)/shard_map/ppermute | solution.py:23
  175.9 18.6 %collective-permute-start.11 = (bf16[32,32,256]{2,1,0:T(8,128)(2,1)S(1)}, bf16[32,32,256]{2,1,0:T(8,128)(2,1)S(1)}, u32[]{:S(2)}, u32[]{:S(2)}) collective-permute-start(bf16[32,32,256]{2,1,0:T(8,128)(2,1)S(1)} %collective-permute-done.3), channel_id=1, source_target_pairs={{0,6},{1,7},{2,0},{3,1},{4,2},{5,3},{6,4},{7,5},{8,14},{9,15},{10,... | collective-permute-start | bytes 1572872 | tf_op jit(solution)/shard_map/ppermute | solution.py:23
  179.4 17.2 %collective-permute-start.4 = (bf16[32,32,256]{2,1,0:T(8,128)(2,1)S(1)}, bf16[32,32,256]{2,1,0:T(8,128)(2,1)S(1)}, u32[]{:S(2)}, u32[]{:S(2)}) collective-permute-start(bf16[32,32,256]{2,1,0:T(8,128)(2,1)S(1)} %collective-permute-done.3), channel_id=1, source_target_pairs={{0,1},{1,0},{2,3},{3,2},{4,5},{5,4},{6,7},{7,6},{8,9},{9,8},{10,11... | collective-permute-start | bytes 1572872 | tf_op jit(solution)/shard_map/ppermute | solution.py:23
  184.5 14.4 %collective-permute-start.6 = (bf16[32,32,256]{2,1,0:T(8,128)(2,1)S(1)}, bf16[32,32,256]{2,1,0:T(8,128)(2,1)S(1)}, u32[]{:S(2)}, u32[]{:S(2)}) collective-permute-start(bf16[32,32,256]{2,1,0:T(8,128)(2,1)S(1)} %collective-permute-done.5), channel_id=1, source_target_pairs={{0,1},{1,0},{2,3},{3,2},{4,5},{5,4},{6,7},{7,6},{8,9},{9,8},{10,11... | collective-permute-start | bytes 1572872 | tf_op jit(solution)/shard_map/ppermute | solution.py:23
  186.4 14.9 %collective-permute-start.13 = (bf16[32,32,256]{2,1,0:T(8,128)(2,1)S(1)}, bf16[32,32,256]{2,1,0:T(8,128)(2,1)S(1)}, u32[]{:S(2)}, u32[]{:S(2)}) collective-permute-start(bf16[32,32,256]{2,1,0:T(8,128)(2,1)S(1)} %collective-permute-done.5), channel_id=1, source_target_pairs={{0,2},{1,3},{2,4},{3,5},{4,6},{5,7},{6,0},{7,1},{8,10},{9,11},{10,... | collective-permute-start | bytes 1572872 | tf_op jit(solution)/shard_map/ppermute | solution.py:23
  191.7 22.1 %collective-permute-start.8 = (bf16[32,32,256]{2,1,0:T(8,128)(2,1)S(1)}, bf16[32,32,256]{2,1,0:T(8,128)(2,1)S(1)}, u32[]{:S(2)}, u32[]{:S(2)}) collective-permute-start(bf16[32,32,256]{2,1,0:T(8,128)(2,1)S(1)} %collective-permute-done.7), channel_id=1, source_target_pairs={{0,1},{1,0},{2,3},{3,2},{4,5},{5,4},{6,7},{7,6},{8,9},{9,8},{10,11... | collective-permute-start | bytes 1572872 | tf_op jit(solution)/shard_map/ppermute | solution.py:23
  194.5 16.6 %collective-permute-start.15 = (bf16[32,32,256]{2,1,0:T(8,128)(2,1)S(1)}, bf16[32,32,256]{2,1,0:T(8,128)(2,1)S(1)}, u32[]{:S(2)}, u32[]{:S(2)}) collective-permute-start(bf16[32,32,256]{2,1,0:T(8,128)(2,1)S(1)} %collective-permute-done.11), channel_id=1, source_target_pairs={{0,6},{1,7},{2,0},{3,1},{4,2},{5,3},{6,4},{7,5},{8,14},{9,15},{10,... | collective-permute-start | bytes 1572872 | tf_op jit(solution)/shard_map/ppermute | solution.py:23
  196.6 17.4 %collective-permute-start.10 = (bf16[32,32,256]{2,1,0:T(8,128)(2,1)S(1)}, bf16[32,32,256]{2,1,0:T(8,128)(2,1)S(1)}, u32[]{:S(2)}, u32[]{:S(2)}) collective-permute-start(bf16[32,32,256]{2,1,0:T(8,128)(2,1)S(1)} %collective-permute-done.9), channel_id=1, source_target_pairs={{0,1},{1,0},{2,3},{3,2},{4,5},{5,4},{6,7},{7,6},{8,9},{9,8},{10,11... | collective-permute-start | bytes 1572872 | tf_op jit(solution)/shard_map/ppermute | solution.py:23
  198.9 15.2 %collective-permute-start.12 = (bf16[32,32,256]{2,1,0:T(8,128)(2,1)S(1)}, bf16[32,32,256]{2,1,0:T(8,128)(2,1)S(1)}, u32[]{:S(2)}, u32[]{:S(2)}) collective-permute-start(bf16[32,32,256]{2,1,0:T(8,128)(2,1)S(1)} %collective-permute-done.11), channel_id=1, source_target_pairs={{0,1},{1,0},{2,3},{3,2},{4,5},{5,4},{6,7},{7,6},{8,9},{9,8},{10,11... | collective-permute-start | bytes 1572872 | tf_op jit(solution)/shard_map/ppermute | solution.py:23
  201.3 12.9 %collective-permute-start.14 = (bf16[32,32,256]{2,1,0:T(8,128)(2,1)S(1)}, bf16[32,32,256]{2,1,0:T(8,128)(2,1)S(1)}, u32[]{:S(2)}, u32[]{:S(2)}) collective-permute-start(bf16[32,32,256]{2,1,0:T(8,128)(2,1)S(1)} %collective-permute-done.13), channel_id=1, source_target_pairs={{0,1},{1,0},{2,3},{3,2},{4,5},{5,4},{6,7},{7,6},{8,9},{9,8},{10,11... | collective-permute-start | bytes 1572872 | tf_op jit(solution)/shard_map/ppermute | solution.py:23
  211.1 4.2 %collective-permute-start.16 = (bf16[32,32,256]{2,1,0:T(8,128)(2,1)S(1)}, bf16[32,32,256]{2,1,0:T(8,128)(2,1)S(1)}, u32[]{:S(2)}, u32[]{:S(2)}) collective-permute-start(bf16[32,32,256]{2,1,0:T(8,128)(2,1)S(1)} %collective-permute-done.15), channel_id=1, source_target_pairs={{0,1},{1,0},{2,3},{3,2},{4,5},{5,4},{6,7},{7,6},{8,9},{9,8},{10,11... | collective-permute-start | bytes 1572872 | tf_op jit(solution)/shard_map/ppermute | solution.py:23

commit v14 on v13

--- a/solution.py
+++ b/solution.py
@@ -65,7 +65,7 @@
 
 def polyphase(pieces, window, context_gain, gain, spec_count):
     inputs, length = pieces[0].shape[1:]
-    lanes = 2048
+    lanes = 1024
     return pl.pallas_call(
         functools.partial(polyphase_kernel, spec_count),
         out_shape=jax.ShapeDtypeStruct((spec_count, inputs, length), jnp.bfloat16),

time: 220 us -> 221 us (level)
  no operation moved by 1% of the time
where the time goes in v14:
time: 221 us; the launch traced here: 220 us
  starting transfers between devices  67 us (30%)
  waiting for transfers between devices  62.4 us (28%)
  blocking collectives  36.1 us (16%)
  local copies, waits for them, and re-layouts  19.8 us (9%)
  other arithmetic  18 us (8%)
  matrix products  11.1 us (5%)
  Pallas kernels  4.89 us (2%)
    ppermute x15, starting transfers between devices, moved(): lax.ppermute(block, 'inp', [(p, mapping(p)) for p in range(lax.axis_size(...  49.5 us
    ppermute x15, waiting for transfers between devices, moved(): lax.ppermute(block, 'inp', [(p, mapping(p)) for p in range(lax.axis_size(...  44.3 us
    all_to_all x1, blocking collectives, shards(): lax.all_to_all(spectra, 'chan', split_axis=3, concat_axis=0, tiled=True)  36.1 us
    ppermute x1, waiting for transfers between devices, shifted(): return lax.ppermute(block, axis, route)  18.1 us
    ppermute x1, starting transfers between devices, shards(): lax.ppermute(samples, 'chan', [(i, (i - 1) % count) for i in range(count)])  15.3 us
    dot_general x1, matrix products, shards(): jnp.dot(filtered, dft_table(), preferred_element_type=jnp.float32)  8.44 us
    convert_element_type x1, other arithmetic, dft_table(): return lax.optimization_barrier(both.astype(jnp.bfloat16))  8.03 us
    pallas_call x1, Pallas kernels, polyphase(): pl.pallas_call(functools.partial(polyphase_kernel, spec_count), out_shape...  4.89 us
  transfers between devices with their start and end apart: 17, of which 5 were waited for; matrix products, arithmetic and copies ran while one was open for 10% of the time, Pallas kernels for 0%

profile of v14, /device:TPU:7, one launch (start us, length us, event | category | flops | bytes accessed | tf_op | source)
XLA Modules:
  0.0 219.9 jit_solution(891621538305210136)
XLA Ops:
  0.0 1.7 convert_element_type.58
  1.7 0.1 copy.33
  1.8 0.0 copy-start
  1.8 15.3 %collective-permute-start.1 = (bf16[4,32,4096]{2,1,0:T(8,128)(2,1)S(1)}, bf16[4,32,4096]{2,1,0:T(8,128)(2,1)}, u32[]{:S(2)}, u32[]{:S(2)}) collective-permute-start(bf16[4,32,4096]{2,1,0:T(8,128)(2,1)S(1)} %bitcast.36), channel_id=1, source_target_pairs={{0,496},{16,0},{32,16},{48,32},{64,48},{80,64},{96,80},{112,96},{1... | collective-permute-start | bytes 3145736 | tf_op jit(solution)/shard_map/ppermute | solution.py:132
  17.1 1.0 slice.12
  18.1 2.2 collective-permute-start
  20.3 1.0 sine_negate_fusion
  21.3 1.1 fusion.27
  22.4 4.8 %multiply_subtract_fusion = (f32[64,64,1024]{2,1,0:T(8,128)S(1)}, f32[64,64,1024]{2,1,0:T(8,128)S(1)}) fusion(f32[64,1024]{1,0:T(8,128)S(1)} %get-tuple-element.13, f32[64,1024]{1,0:T(8,128)S(1)} %get-tuple-element.10, f32[64,1024]{1,0:T(8,128)S(1)} %get-tuple-element.14, f32[64,1024]{1,0:T(8,128)S(1)} %get-tuple-element.9), kind=kLoop, calls=%fused_computation.3 | loop fusion | flops 25165824 | bytes 34603008 | tf_op jit(solution)/shard_map/sub | solution.py:49
  27.2 0.0 copy-start.1
  27.3 8.0 %fusion = bf16[4096,2048]{1,0:T(8,128)(2,1)} fusion(f32[4096,1024]{1,0:T(8,128)S(1)} %bitcast.31, f32[4096,1024]{1,0:T(8,128)S(1)} %bitcast.30), kind=kLoop, calls=%fused_computation.1 | loop fusion | flops 25165824 | bytes 50331648 | tf_op jit(solution)/shard_map/convert_element_type | solution.py:52
  35.3 0.7 copy.20.refs_4_
  36.0 0.7 copy.21.refs_5_
  36.7 1.3 fusion.22.refs_3_
  37.9 18.1 %collective-permute-done.refs_0_ = bf16[3,32,4096]{2,1,0:T(8,128)(2,1)} collective-permute-done((bf16[3,32,4096]{2,1,0:T(8,128)(2,1)}, bf16[3,32,4096]{2,1,0:T(8,128)(2,1)}, u32[]{:S(2)}, u32[]{:S(2)}) %collective-permute-start) | collective-permute-done | bytes 786464 | tf_op jit(solution)/shard_map/ppermute | solution.py:19
  56.0 0.0 collective-permute-done.1.refs_2_
  56.0 4.9 %shard_map.28 = bf16[4,32,4096]{2,1,0:T(8,128)(2,1)} custom-call(bf16[3,32,4096]{2,1,0:T(8,128)(2,1)} %collective-permute-done.refs_0_, bf16[4,32,4096]{2,1,0:T(8,128)(2,1)} %bitcast.38, bf16[4,32,4096]{2,1,0:T(8,128)(2,1)} %collective-permute-done.1.refs_2_, f32[8,4096]{1,0:T(8,128)} %fusion.22.refs_3_, f32[32,1]{1,0:T(8,128)} %copy.20.refs_4_, ...), custom_call_target="tpu_custom_call" | custom-call | tf_op jit(solution)/shard_map/pallas_call | solution.py:69
  60.9 8.4 %convolution_convert_fusion = bf16[128,2048]{1,0:T(8,128)(2,1)S(1)} fusion(bf16[128,4096]{1,0:T(8,128)(2,1)} %bitcast.39, bf16[4096,2048]{1,0:T(8,128)(2,1)} %fusion), kind=kOutput, calls=%fused_computation.5 | convolution fusion | flops 2147745792 | bytes 18350080 | tf_op jit(solution)/shard_map/dot_general | solution.py:137
  69.3 0.4 reshape.123
  69.7 1.9 copy.22
  71.6 2.0 reshape.125
  73.6 36.1 %all_to_all.18 = bf16[32,2,4096]{2,1,0:T(2,128)(2,1)S(1)} all-to-all(bf16[32,2,4096]{2,1,0:T(2,128)(2,1)S(1)} %reshape.125), channel_id=1, replica_groups=mesh['chan'=32,'inp'=16] {'chan'}, dimensions={0} | all-to-all | bytes 1048576 | tf_op jit(solution)/shard_map/all_to_all | solution.py:139
  109.7 1.0 reshape.126
  110.7 3.8 %copy.28 = bf16[4,32,2,32,32]{4,1,2,0,3:T(8,128)(2,1)} copy(bf16[4,32,2,32,32]{1,2,0,4,3:T(2,128)(2,1)S(1)} %bitcast.33) | data formatting | bytes 1048576 | tf_op jit(solution)/shard_map/all_to_all | solution.py:139
  114.5 3.7 %copy.25 = bf16[32,32,2,128]{3,2,1,0:T(2,128)(2,1)S(1)} copy(bf16[32,32,2,128]{0,1,2,3:T(8,128)(2,1)} %bitcast.34) | data formatting | bytes 1048576 | tf_op jit(solution)/shard_map/transpose | solution.py:142
  118.2 0.3 reshape.124
  118.5 10.0 %collective-permute-start.3 = (bf16[32,32,256]{2,1,0:T(8,128)(2,1)S(1)}, bf16[32,32,256]{2,1,0:T(8,128)(2,1)S(1)}, u32[]{:S(2)}, u32[]{:S(2)}) collective-permute-start(bf16[32,32,256]{2,1,0:T(8,128)(2,1)S(1)} %reshape.124), channel_id=1, source_target_pairs={{0,8},{1,9},{2,10},{3,11},{4,12},{5,13},{6,14},{7,15},{8,0},{9,1},... | collective-permute-start | bytes 1572872 | tf_op jit(solution)/shard_map/ppermute | solution.py:23
  128.5 4.0 %collective-permute-start.2 = (bf16[32,32,256]{2,1,0:T(8,128)(2,1)S(1)}, bf16[32,32,256]{2,1,0:T(8,128)(2,1)}, u32[]{:S(2)}, u32[]{:S(2)}) collective-permute-start(bf16[32,32,256]{2,1,0:T(8,128)(2,1)S(1)} %reshape.124), channel_id=1, source_target_pairs={{0,1},{1,0},{2,3},{3,2},{4,5},{5,4},{6,7},{7,6},{8,9},{9,8},{10,11... | collective-permute-start | bytes 1572872 | tf_op jit(solution)/shard_map/ppermute | solution.py:23
  132.5 2.1 collective-permute-start.5
  134.6 3.2 %collective-permute-start.9 = (bf16[32,32,256]{2,1,0:T(8,128)(2,1)S(1)}, bf16[32,32,256]{2,1,0:T(8,128)(2,1)S(1)}, u32[]{:S(2)}, u32[]{:S(2)}) collective-permute-start(bf16[32,32,256]{2,1,0:T(8,128)(2,1)S(1)} %reshape.124), channel_id=1, source_target_pairs={{0,6},{1,7},{2,0},{3,1},{4,2},{5,3},{6,4},{7,5},{8,14},{9,15},{10,... | collective-permute-start | bytes 1572872 | tf_op jit(solution)/shard_map/ppermute | solution.py:23
  137.8 36.4 %collective-permute-done.3 = bf16[32,32,256]{2,1,0:T(8,128)(2,1)S(1)} collective-permute-done((bf16[32,32,256]{2,1,0:T(8,128)(2,1)S(1)}, bf16[32,32,256]{2,1,0:T(8,128)(2,1)S(1)}, u32[]{:S(2)}, u32[]{:S(2)}) %collective-permute-start.3) | collective-permute-done | bytes 524320 | tf_op jit(solution)/shard_map/ppermute | solution.py:23
  174.2 2.1 collective-permute-start.7
  176.3 3.4 %collective-permute-start.11 = (bf16[32,32,256]{2,1,0:T(8,128)(2,1)S(1)}, bf16[32,32,256]{2,1,0:T(8,128)(2,1)S(1)}, u32[]{:S(2)}, u32[]{:S(2)}) collective-permute-start(bf16[32,32,256]{2,1,0:T(8,128)(2,1)S(1)} %collective-permute-done.3), channel_id=1, source_target_pairs={{0,6},{1,7},{2,0},{3,1},{4,2},{5,3},{6,4},{7,5},{8,14},{9,15},{10,... | collective-permute-start | bytes 1572872 | tf_op jit(solution)/shard_map/ppermute | solution.py:23
  179.9 0.0 collective-permute-done.2
  180.0 4.7 %collective-permute-start.4 = (bf16[32,32,256]{2,1,0:T(8,128)(2,1)S(1)}, bf16[32,32,256]{2,1,0:T(8,128)(2,1)S(1)}, u32[]{:S(2)}, u32[]{:S(2)}) collective-permute-start(bf16[32,32,256]{2,1,0:T(8,128)(2,1)S(1)} %collective-permute-done.3), channel_id=1, source_target_pairs={{0,1},{1,0},{2,3},{3,2},{4,5},{5,4},{6,7},{7,6},{8,9},{9,8},{10,11... | collective-permute-start | bytes 1572872 | tf_op jit(solution)/shard_map/ppermute | solution.py:23
  184.7 0.1 fusion.36
  184.7 0.0 collective-permute-done.5
  184.8 1.9 collective-permute-start.6
  186.7 0.0 collective-permute-done.9
  186.7 3.3 %collective-permute-start.13 = (bf16[32,32,256]{2,1,0:T(8,128)(2,1)S(1)}, bf16[32,32,256]{2,1,0:T(8,128)(2,1)S(1)}, u32[]{:S(2)}, u32[]{:S(2)}) collective-permute-start(bf16[32,32,256]{2,1,0:T(8,128)(2,1)S(1)} %collective-permute-done.5), channel_id=1, source_target_pairs={{0,2},{1,3},{2,4},{3,5},{4,6},{5,7},{6,0},{7,1},{8,10},{9,11},{10,... | collective-permute-start | bytes 1572872 | tf_op jit(solution)/shard_map/ppermute | solution.py:23
  190.0 0.9 broadcast_in_dim.52
  191.0 1.1 constant_dynamic-update-slice_fusion.14
  192.1 0.0 collective-permute-done.7
  192.1 2.7 %collective-permute-start.8 = (bf16[32,32,256]{2,1,0:T(8,128)(2,1)S(1)}, bf16[32,32,256]{2,1,0:T(8,128)(2,1)S(1)}, u32[]{:S(2)}, u32[]{:S(2)}) collective-permute-start(bf16[32,32,256]{2,1,0:T(8,128)(2,1)S(1)} %collective-permute-done.7), channel_id=1, source_target_pairs={{0,1},{1,0},{2,3},{3,2},{4,5},{5,4},{6,7},{7,6},{8,9},{9,8},{10,11... | collective-permute-start | bytes 1572872 | tf_op jit(solution)/shard_map/ppermute | solution.py:23
  194.8 0.0 collective-permute-done.11
  194.8 2.0 collective-permute-start.15
  196.9 2.2 %collective-permute-start.10 = (bf16[32,32,256]{2,1,0:T(8,128)(2,1)S(1)}, bf16[32,32,256]{2,1,0:T(8,128)(2,1)S(1)}, u32[]{:S(2)}, u32[]{:S(2)}) collective-permute-start(bf16[32,32,256]{2,1,0:T(8,128)(2,1)S(1)} %collective-permute-done.9), channel_id=1, source_target_pairs={{0,1},{1,0},{2,3},{3,2},{4,5},{5,4},{6,7},{7,6},{8,9},{9,8},{10,11... | collective-permute-start | bytes 1572872 | tf_op jit(solution)/shard_map/ppermute | solution.py:23
  199.1 0.1 constant_dynamic-update-slice_fusion.12
  199.2 0.0 collective-permute-done.6
  199.2 2.1 collective-permute-start.12
  201.3 0.3 collective-permute-done.13
  201.6 3.2 %collective-permute-start.14 = (bf16[32,32,256]{2,1,0:T(8,128)(2,1)S(1)}, bf16[32,32,256]{2,1,0:T(8,128)(2,1)S(1)}, u32[]{:S(2)}, u32[]{:S(2)}) collective-permute-start(bf16[32,32,256]{2,1,0:T(8,128)(2,1)S(1)} %collective-permute-done.13), channel_id=1, source_target_pairs={{0,1},{1,0},{2,3},{3,2},{4,5},{5,4},{6,7},{7,6},{8,9},{9,8},{10,11... | collective-permute-start | bytes 1572872 | tf_op jit(solution)/shard_map/ppermute | solution.py:23
  204.9 6.5 %collective-permute-done.15 = bf16[32,32,256]{2,1,0:T(8,128)(2,1)S(1)} collective-permute-done((bf16[32,32,256]{2,1,0:T(8,128)(2,1)S(1)}, bf16[32,32,256]{2,1,0:T(8,128)(2,1)S(1)}, u32[]{:S(2)}, u32[]{:S(2)}) %collective-permute-start.15) | collective-permute-done | bytes 524320 | tf_op jit(solution)/shard_map/ppermute | solution.py:23
  211.5 2.7 %collective-permute-start.16 = (bf16[32,32,256]{2,1,0:T(8,128)(2,1)S(1)}, bf16[32,32,256]{2,1,0:T(8,128)(2,1)S(1)}, u32[]{:S(2)}, u32[]{:S(2)}) collective-permute-start(bf16[32,32,256]{2,1,0:T(8,128)(2,1)S(1)} %collective-permute-done.15), channel_id=1, source_target_pairs={{0,1},{1,0},{2,3},{3,2},{4,5},{5,4},{6,7},{7,6},{8,9},{9,8},{10,11... | collective-permute-start | bytes 1572872 | tf_op jit(solution)/shard_map/ppermute | solution.py:23
  214.2 0.0 collective-permute-done.8
  214.2 0.1 constant_dynamic-update-slice_fusion.8
  214.3 0.0 collective-permute-done.10
  214.3 0.1 constant_dynamic-update-slice_fusion.6
  214.4 0.0 collective-permute-done.12
  214.4 0.1 constant_dynamic-update-slice_fusion.4
  214.5 0.1 constant_dynamic-update-slice_fusion.2
  214.6 1.0 collective-permute-done.16
  215.7 2.6 %multiply_convert_fusion = bf16[32,64,512]{2,1,0:T(8,128)(2,1)S(1)} fusion(bf16[32,512,256]{2,1,0:T(8,128)(2,1)S(1)} %constant_dynamic-update-slice_fusion, bf16[32,32,128]{2,1,0:T(8,128)(2,1)S(1)} %get-tuple-element.8, bf16[32,32,128]{2,1,0:T(8,128)(2,1)S(1)} %get-tuple-element.7, bf16[32,32,256]{2,1,0:T(8,128)(2,1)S(1)} %reshape.124), kind=kOutput, calls=%fused_computation.4 | convolution fusion | flops 542113792 | bytes 11534336 | tf_op jit(solution)/shard_map/cik,cjk->cij/dot_general | solution.py:146
  218.4 1.6 copy.32
  (16 shorter events, 0.5 us)
Async XLA Ops:
  1.8 25.5 %copy-start = (bf16[4,4,8,4096]{3,2,0,1:T(8,128)(2,1)}, bf16[4,4,8,4096]{3,2,0,1:T(8,128)(2,1)S(1)}, u32[]{:S(2)}) copy-start(bf16[4,4,8,4096]{3,2,0,1:T(8,128)(2,1)S(1)} %copy.33) | copy-start | bytes 3145732
  1.8 54.2 %collective-permute-start.1 = (bf16[4,32,4096]{2,1,0:T(8,128)(2,1)S(1)}, bf16[4,32,4096]{2,1,0:T(8,128)(2,1)}, u32[]{:S(2)}, u32[]{:S(2)}) collective-permute-start(bf16[4,32,4096]{2,1,0:T(8,128)(2,1)S(1)} %bitcast.36), channel_id=1, source_target_pairs={{0,496},{16,0},{32,16},{48,32},{64,48},{80,64},{96,80},{112,96},{1... | collective-permute-start | bytes 3145736 | tf_op jit(solution)/shard_map/ppermute | solution.py:132
  18.1 37.9 %collective-permute-start = (bf16[3,32,4096]{2,1,0:T(8,128)(2,1)}, bf16[3,32,4096]{2,1,0:T(8,128)(2,1)}, u32[]{:S(2)}, u32[]{:S(2)}) collective-permute-start(bf16[3,32,4096]{2,1,0:T(8,128)(2,1)} %slice.12), channel_id=1, source_target_pairs={{0,16},{16,32},{32,48},{48,64},{64,80},{80,96},{96,112},{112,128},... | collective-permute-start | bytes 2359304 | tf_op jit(solution)/shard_map/ppermute | solution.py:19
  27.2 8.0 %copy-start.1 = (s32[32]{0:T(128)S(1)}, s32[32]{0:T(128)}, u32[]{:S(2)}) copy-start(s32[32]{0:T(128)} %param.3) | copy-start | bytes 388
  118.5 55.7 %collective-permute-start.3 = (bf16[32,32,256]{2,1,0:T(8,128)(2,1)S(1)}, bf16[32,32,256]{2,1,0:T(8,128)(2,1)S(1)}, u32[]{:S(2)}, u32[]{:S(2)}) collective-permute-start(bf16[32,32,256]{2,1,0:T(8,128)(2,1)S(1)} %reshape.124), channel_id=1, source_target_pairs={{0,8},{1,9},{2,10},{3,11},{4,12},{5,13},{6,14},{7,15},{8,0},{9,1},... | collective-permute-start | bytes 1572872 | tf_op jit(solution)/shard_map/ppermute | solution.py:23
  128.5 51.4 %collective-permute-start.2 = (bf16[32,32,256]{2,1,0:T(8,128)(2,1)S(1)}, bf16[32,32,256]{2,1,0:T(8,128)(2,1)}, u32[]{:S(2)}, u32[]{:S(2)}) collective-permute-start(bf16[32,32,256]{2,1,0:T(8,128)(2,1)S(1)} %reshape.124), channel_id=1, source_target_pairs={{0,1},{1,0},{2,3},{3,2},{4,5},{5,4},{6,7},{7,6},{8,9},{9,8},{10,11... | collective-permute-start | bytes 1572872 | tf_op jit(solution)/shard_map/ppermute | solution.py:23
  132.5 52.2 %collective-permute-start.5 = (bf16[32,32,256]{2,1,0:T(8,128)(2,1)S(1)}, bf16[32,32,256]{2,1,0:T(8,128)(2,1)S(1)}, u32[]{:S(2)}, u32[]{:S(2)}) collective-permute-start(bf16[32,32,256]{2,1,0:T(8,128)(2,1)S(1)} %reshape.124), channel_id=1, source_target_pairs={{0,2},{1,3},{2,4},{3,5},{4,6},{5,7},{6,0},{7,1},{8,10},{9,11},{10,... | collective-permute-start | bytes 1572872 | tf_op jit(solution)/shard_map/ppermute | solution.py:23
  134.6 52.1 %collective-permute-start.9 = (bf16[32,32,256]{2,1,0:T(8,128)(2,1)S(1)}, bf16[32,32,256]{2,1,0:T(8,128)(2,1)S(1)}, u32[]{:S(2)}, u32[]{:S(2)}) collective-permute-start(bf16[32,32,256]{2,1,0:T(8,128)(2,1)S(1)} %reshape.124), channel_id=1, source_target_pairs={{0,6},{1,7},{2,0},{3,1},{4,2},{5,3},{6,4},{7,5},{8,14},{9,15},{10,... | collective-permute-start | bytes 1572872 | tf_op jit(solution)/shard_map/ppermute | solution.py:23
  174.2 17.9 %collective-permute-start.7 = (bf16[32,32,256]{2,1,0:T(8,128)(2,1)S(1)}, bf16[32,32,256]{2,1,0:T(8,128)(2,1)S(1)}, u32[]{:S(2)}, u32[]{:S(2)}) collective-permute-start(bf16[32,32,256]{2,1,0:T(8,128)(2,1)S(1)} %collective-permute-done.3), channel_id=1, source_target_pairs={{0,2},{1,3},{2,4},{3,5},{4,6},{5,7},{6,0},{7,1},{8,10},{9,11},{10,... | collective-permute-start | bytes 1572872 | tf_op jit(solution)/shard_map/ppermute | solution.py:23
  176.3 18.5 %collective-permute-start.11 = (bf16[32,32,256]{2,1,0:T(8,128)(2,1)S(1)}, bf16[32,32,256]{2,1,0:T(8,128)(2,1)S(1)}, u32[]{:S(2)}, u32[]{:S(2)}) collective-permute-start(bf16[32,32,256]{2,1,0:T(8,128)(2,1)S(1)} %collective-permute-done.3), channel_id=1, source_target_pairs={{0,6},{1,7},{2,0},{3,1},{4,2},{5,3},{6,4},{7,5},{8,14},{9,15},{10,... | collective-permute-start | bytes 1572872 | tf_op jit(solution)/shard_map/ppermute | solution.py:23
  180.0 16.9 %collective-permute-start.4 = (bf16[32,32,256]{2,1,0:T(8,128)(2,1)S(1)}, bf16[32,32,256]{2,1,0:T(8,128)(2,1)S(1)}, u32[]{:S(2)}, u32[]{:S(2)}) collective-permute-start(bf16[32,32,256]{2,1,0:T(8,128)(2,1)S(1)} %collective-permute-done.3), channel_id=1, source_target_pairs={{0,1},{1,0},{2,3},{3,2},{4,5},{5,4},{6,7},{7,6},{8,9},{9,8},{10,11... | collective-permute-start | bytes 1572872 | tf_op jit(solution)/shard_map/ppermute | solution.py:23
  184.8 14.4 %collective-permute-start.6 = (bf16[32,32,256]{2,1,0:T(8,128)(2,1)S(1)}, bf16[32,32,256]{2,1,0:T(8,128)(2,1)S(1)}, u32[]{:S(2)}, u32[]{:S(2)}) collective-permute-start(bf16[32,32,256]{2,1,0:T(8,128)(2,1)S(1)} %collective-permute-done.5), channel_id=1, source_target_pairs={{0,1},{1,0},{2,3},{3,2},{4,5},{5,4},{6,7},{7,6},{8,9},{9,8},{10,11... | collective-permute-start | bytes 1572872 | tf_op jit(solution)/shard_map/ppermute | solution.py:23
  186.7 14.9 %collective-permute-start.13 = (bf16[32,32,256]{2,1,0:T(8,128)(2,1)S(1)}, bf16[32,32,256]{2,1,0:T(8,128)(2,1)S(1)}, u32[]{:S(2)}, u32[]{:S(2)}) collective-permute-start(bf16[32,32,256]{2,1,0:T(8,128)(2,1)S(1)} %collective-permute-done.5), channel_id=1, source_target_pairs={{0,2},{1,3},{2,4},{3,5},{4,6},{5,7},{6,0},{7,1},{8,10},{9,11},{10,... | collective-permute-start | bytes 1572872 | tf_op jit(solution)/shard_map/ppermute | solution.py:23
  192.1 22.1 %collective-permute-start.8 = (bf16[32,32,256]{2,1,0:T(8,128)(2,1)S(1)}, bf16[32,32,256]{2,1,0:T(8,128)(2,1)S(1)}, u32[]{:S(2)}, u32[]{:S(2)}) collective-permute-start(bf16[32,32,256]{2,1,0:T(8,128)(2,1)S(1)} %collective-permute-done.7), channel_id=1, source_target_pairs={{0,1},{1,0},{2,3},{3,2},{4,5},{5,4},{6,7},{7,6},{8,9},{9,8},{10,11... | collective-permute-start | bytes 1572872 | tf_op jit(solution)/shard_map/ppermute | solution.py:23
  194.8 16.6 %collective-permute-start.15 = (bf16[32,32,256]{2,1,0:T(8,128)(2,1)S(1)}, bf16[32,32,256]{2,1,0:T(8,128)(2,1)S(1)}, u32[]{:S(2)}, u32[]{:S(2)}) collective-permute-start(bf16[32,32,256]{2,1,0:T(8,128)(2,1)S(1)} %collective-permute-done.11), channel_id=1, source_target_pairs={{0,6},{1,7},{2,0},{3,1},{4,2},{5,3},{6,4},{7,5},{8,14},{9,15},{10,... | collective-permute-start | bytes 1572872 | tf_op jit(solution)/shard_map/ppermute | solution.py:23
  196.9 17.4 %collective-permute-start.10 = (bf16[32,32,256]{2,1,0:T(8,128)(2,1)S(1)}, bf16[32,32,256]{2,1,0:T(8,128)(2,1)S(1)}, u32[]{:S(2)}, u32[]{:S(2)}) collective-permute-start(bf16[32,32,256]{2,1,0:T(8,128)(2,1)S(1)} %collective-permute-done.9), channel_id=1, source_target_pairs={{0,1},{1,0},{2,3},{3,2},{4,5},{5,4},{6,7},{7,6},{8,9},{9,8},{10,11... | collective-permute-start | bytes 1572872 | tf_op jit(solution)/shard_map/ppermute | solution.py:23
  199.2 15.2 %collective-permute-start.12 = (bf16[32,32,256]{2,1,0:T(8,128)(2,1)S(1)}, bf16[32,32,256]{2,1,0:T(8,128)(2,1)S(1)}, u32[]{:S(2)}, u32[]{:S(2)}) collective-permute-start(bf16[32,32,256]{2,1,0:T(8,128)(2,1)S(1)} %collective-permute-done.11), channel_id=1, source_target_pairs={{0,1},{1,0},{2,3},{3,2},{4,5},{5,4},{6,7},{7,6},{8,9},{9,8},{10,11... | collective-permute-start | bytes 1572872 | tf_op jit(solution)/shard_map/ppermute | solution.py:23
  201.6 13.0 %collective-permute-start.14 = (bf16[32,32,256]{2,1,0:T(8,128)(2,1)S(1)}, bf16[32,32,256]{2,1,0:T(8,128)(2,1)S(1)}, u32[]{:S(2)}, u32[]{:S(2)}) collective-permute-start(bf16[32,32,256]{2,1,0:T(8,128)(2,1)S(1)} %collective-permute-done.13), channel_id=1, source_target_pairs={{0,1},{1,0},{2,3},{3,2},{4,5},{5,4},{6,7},{7,6},{8,9},{9,8},{10,11... | collective-permute-start | bytes 1572872 | tf_op jit(solution)/shard_map/ppermute | solution.py:23
  211.5 4.2 %collective-permute-start.16 = (bf16[32,32,256]{2,1,0:T(8,128)(2,1)S(1)}, bf16[32,32,256]{2,1,0:T(8,128)(2,1)S(1)}, u32[]{:S(2)}, u32[]{:S(2)}) collective-permute-start(bf16[32,32,256]{2,1,0:T(8,128)(2,1)S(1)} %collective-permute-done.15), channel_id=1, source_target_pairs={{0,1},{1,0},{2,3},{3,2},{4,5},{5,4},{6,7},{7,6},{8,9},{9,8},{10,11... | collective-permute-start | bytes 1572872 | tf_op jit(solution)/shard_map/ppermute | solution.py:23

commit v15 on v14

--- a/solution.py
+++ b/solution.py
@@ -65,7 +65,7 @@
 
 def polyphase(pieces, window, context_gain, gain, spec_count):
     inputs, length = pieces[0].shape[1:]
-    lanes = 1024
+    lanes = 4096
     return pl.pallas_call(
         functools.partial(polyphase_kernel, spec_count),
         out_shape=jax.ShapeDtypeStruct((spec_count, inputs, length), jnp.bfloat16),

time: 221 us -> 221 us (level)
  no operation moved by 1% of the time
where the time goes in v15:
time: 221 us
  starting transfers between devices  67.2 us (30%)
  waiting for transfers between devices  61.9 us (28%)
  blocking collectives  36.1 us (16%)
  local copies, waits for them, and re-layouts  19.8 us (9%)
  other arithmetic  18 us (8%)
  matrix products  11.1 us (5%)
  Pallas kernels  5.84 us (3%)
    ppermute x15, starting transfers between devices, moved(): lax.ppermute(block, 'inp', [(p, mapping(p)) for p in range(lax.axis_size(...  49.7 us
    ppermute x15, waiting for transfers between devices, moved(): lax.ppermute(block, 'inp', [(p, mapping(p)) for p in range(lax.axis_size(...  43.8 us
    all_to_all x1, blocking collectives, shards(): lax.all_to_all(spectra, 'chan', split_axis=3, concat_axis=0, tiled=True)  36.1 us
    ppermute x1, waiting for transfers between devices, shifted(): return lax.ppermute(block, axis, route)  18.1 us
    ppermute x1, starting transfers between devices, shards(): lax.ppermute(samples, 'chan', [(i, (i - 1) % count) for i in range(count)])  15.3 us
    dot_general x1, matrix products, shards(): jnp.dot(filtered, dft_table(), preferred_element_type=jnp.float32)  8.44 us
    convert_element_type x1, other arithmetic, dft_table(): return lax.optimization_barrier(both.astype(jnp.bfloat16))  8.03 us
    pallas_call x1, Pallas kernels, polyphase(): pl.pallas_call(functools.partial(polyphase_kernel, spec_count), out_shape...  5.84 us
  transfers between devices with their start and end apart: 17, of which 5 were waited for; matrix products, arithmetic and copies ran while one was open for 10% of the time, Pallas kernels for 0%

profile of v15, /device:TPU:7, one launch (start us, length us, event | category | flops | bytes accessed | tf_op | source)
XLA Modules:
  0.0 220.5 jit_solution(1526539360722520648)
XLA Ops:
  0.0 1.7 convert_element_type.58
  1.7 0.1 copy.33
  1.8 0.0 copy-start
  1.8 15.3 %collective-permute-start.1 = (bf16[4,32,4096]{2,1,0:T(8,128)(2,1)S(1)}, bf16[4,32,4096]{2,1,0:T(8,128)(2,1)}, u32[]{:S(2)}, u32[]{:S(2)}) collective-permute-start(bf16[4,32,4096]{2,1,0:T(8,128)(2,1)S(1)} %bitcast.36), channel_id=1, source_target_pairs={{0,496},{16,0},{32,16},{48,32},{64,48},{80,64},{96,80},{112,96},{1... | collective-permute-start | bytes 3145736 | tf_op jit(solution)/shard_map/ppermute | solution.py:132
  17.1 1.0 slice.12
  18.1 2.2 collective-permute-start
  20.3 1.0 sine_negate_fusion
  21.3 1.1 fusion.27
  22.4 4.8 %multiply_subtract_fusion = (f32[64,64,1024]{2,1,0:T(8,128)S(1)}, f32[64,64,1024]{2,1,0:T(8,128)S(1)}) fusion(f32[64,1024]{1,0:T(8,128)S(1)} %get-tuple-element.13, f32[64,1024]{1,0:T(8,128)S(1)} %get-tuple-element.10, f32[64,1024]{1,0:T(8,128)S(1)} %get-tuple-element.14, f32[64,1024]{1,0:T(8,128)S(1)} %get-tuple-element.9), kind=kLoop, calls=%fused_computation.3 | loop fusion | flops 25165824 | bytes 34603008 | tf_op jit(solution)/shard_map/sub | solution.py:49
  27.2 0.0 copy-start.1
  27.3 8.0 %fusion = bf16[4096,2048]{1,0:T(8,128)(2,1)} fusion(f32[4096,1024]{1,0:T(8,128)S(1)} %bitcast.31, f32[4096,1024]{1,0:T(8,128)S(1)} %bitcast.30), kind=kLoop, calls=%fused_computation.1 | loop fusion | flops 25165824 | bytes 50331648 | tf_op jit(solution)/shard_map/convert_element_type | solution.py:52
  35.3 0.7 copy.20.refs_4_
  36.0 0.7 copy.21.refs_5_
  36.7 1.3 fusion.22.refs_3_
  37.9 18.1 %collective-permute-done.refs_0_ = bf16[3,32,4096]{2,1,0:T(8,128)(2,1)} collective-permute-done((bf16[3,32,4096]{2,1,0:T(8,128)(2,1)}, bf16[3,32,4096]{2,1,0:T(8,128)(2,1)}, u32[]{:S(2)}, u32[]{:S(2)}) %collective-permute-start) | collective-permute-done | bytes 786464 | tf_op jit(solution)/shard_map/ppermute | solution.py:19
  56.0 0.0 collective-permute-done.1.refs_2_
  56.0 5.8 %shard_map.28 = bf16[4,32,4096]{2,1,0:T(8,128)(2,1)} custom-call(bf16[3,32,4096]{2,1,0:T(8,128)(2,1)} %collective-permute-done.refs_0_, bf16[4,32,4096]{2,1,0:T(8,128)(2,1)} %bitcast.38, bf16[4,32,4096]{2,1,0:T(8,128)(2,1)} %collective-permute-done.1.refs_2_, f32[8,4096]{1,0:T(8,128)} %fusion.22.refs_3_, f32[32,1]{1,0:T(8,128)} %copy.20.refs_4_, ...), custom_call_target="tpu_custom_call" | custom-call | tf_op jit(solution)/shard_map/pallas_call | solution.py:69
  61.8 8.4 %convolution_convert_fusion = bf16[128,2048]{1,0:T(8,128)(2,1)S(1)} fusion(bf16[128,4096]{1,0:T(8,128)(2,1)} %bitcast.39, bf16[4096,2048]{1,0:T(8,128)(2,1)} %fusion), kind=kOutput, calls=%fused_computation.5 | convolution fusion | flops 2147745792 | bytes 18350080 | tf_op jit(solution)/shard_map/dot_general | solution.py:137
  70.3 0.4 reshape.123
  70.7 1.9 copy.22
  72.6 2.0 reshape.125
  74.6 36.1 %all_to_all.18 = bf16[32,2,4096]{2,1,0:T(2,128)(2,1)S(1)} all-to-all(bf16[32,2,4096]{2,1,0:T(2,128)(2,1)S(1)} %reshape.125), channel_id=1, replica_groups=mesh['chan'=32,'inp'=16] {'chan'}, dimensions={0} | all-to-all | bytes 1048576 | tf_op jit(solution)/shard_map/all_to_all | solution.py:139
  110.6 1.0 reshape.126
  111.7 3.8 %copy.28 = bf16[4,32,2,32,32]{4,1,2,0,3:T(8,128)(2,1)} copy(bf16[4,32,2,32,32]{1,2,0,4,3:T(2,128)(2,1)S(1)} %bitcast.33) | data formatting | bytes 1048576 | tf_op jit(solution)/shard_map/all_to_all | solution.py:139
  115.5 3.7 %copy.25 = bf16[32,32,2,128]{3,2,1,0:T(2,128)(2,1)S(1)} copy(bf16[32,32,2,128]{0,1,2,3:T(8,128)(2,1)} %bitcast.34) | data formatting | bytes 1048576 | tf_op jit(solution)/shard_map/transpose | solution.py:142
  119.1 0.3 reshape.124
  119.5 10.0 %collective-permute-start.3 = (bf16[32,32,256]{2,1,0:T(8,128)(2,1)S(1)}, bf16[32,32,256]{2,1,0:T(8,128)(2,1)S(1)}, u32[]{:S(2)}, u32[]{:S(2)}) collective-permute-start(bf16[32,32,256]{2,1,0:T(8,128)(2,1)S(1)} %reshape.124), channel_id=1, source_target_pairs={{0,8},{1,9},{2,10},{3,11},{4,12},{5,13},{6,14},{7,15},{8,0},{9,1},... | collective-permute-start | bytes 1572872 | tf_op jit(solution)/shard_map/ppermute | solution.py:23
  129.5 4.0 %collective-permute-start.2 = (bf16[32,32,256]{2,1,0:T(8,128)(2,1)S(1)}, bf16[32,32,256]{2,1,0:T(8,128)(2,1)}, u32[]{:S(2)}, u32[]{:S(2)}) collective-permute-start(bf16[32,32,256]{2,1,0:T(8,128)(2,1)S(1)} %reshape.124), channel_id=1, source_target_pairs={{0,1},{1,0},{2,3},{3,2},{4,5},{5,4},{6,7},{7,6},{8,9},{9,8},{10,11... | collective-permute-start | bytes 1572872 | tf_op jit(solution)/shard_map/ppermute | solution.py:23
  133.5 2.1 collective-permute-start.5
  135.6 3.2 %collective-permute-start.9 = (bf16[32,32,256]{2,1,0:T(8,128)(2,1)S(1)}, bf16[32,32,256]{2,1,0:T(8,128)(2,1)S(1)}, u32[]{:S(2)}, u32[]{:S(2)}) collective-permute-start(bf16[32,32,256]{2,1,0:T(8,128)(2,1)S(1)} %reshape.124), channel_id=1, source_target_pairs={{0,6},{1,7},{2,0},{3,1},{4,2},{5,3},{6,4},{7,5},{8,14},{9,15},{10,... | collective-permute-start | bytes 1572872 | tf_op jit(solution)/shard_map/ppermute | solution.py:23
  138.8 35.9 %collective-permute-done.3 = bf16[32,32,256]{2,1,0:T(8,128)(2,1)S(1)} collective-permute-done((bf16[32,32,256]{2,1,0:T(8,128)(2,1)S(1)}, bf16[32,32,256]{2,1,0:T(8,128)(2,1)S(1)}, u32[]{:S(2)}, u32[]{:S(2)}) %collective-permute-start.3) | collective-permute-done | bytes 524320 | tf_op jit(solution)/shard_map/ppermute | solution.py:23
  174.7 2.1 collective-permute-start.7
  176.8 3.2 %collective-permute-start.11 = (bf16[32,32,256]{2,1,0:T(8,128)(2,1)S(1)}, bf16[32,32,256]{2,1,0:T(8,128)(2,1)S(1)}, u32[]{:S(2)}, u32[]{:S(2)}) collective-permute-start(bf16[32,32,256]{2,1,0:T(8,128)(2,1)S(1)} %collective-permute-done.3), channel_id=1, source_target_pairs={{0,6},{1,7},{2,0},{3,1},{4,2},{5,3},{6,4},{7,5},{8,14},{9,15},{10,... | collective-permute-start | bytes 1572872 | tf_op jit(solution)/shard_map/ppermute | solution.py:23
  180.2 0.0 collective-permute-done.2
  180.2 5.0 %collective-permute-start.4 = (bf16[32,32,256]{2,1,0:T(8,128)(2,1)S(1)}, bf16[32,32,256]{2,1,0:T(8,128)(2,1)S(1)}, u32[]{:S(2)}, u32[]{:S(2)}) collective-permute-start(bf16[32,32,256]{2,1,0:T(8,128)(2,1)S(1)} %collective-permute-done.3), channel_id=1, source_target_pairs={{0,1},{1,0},{2,3},{3,2},{4,5},{5,4},{6,7},{7,6},{8,9},{9,8},{10,11... | collective-permute-start | bytes 1572872 | tf_op jit(solution)/shard_map/ppermute | solution.py:23
  185.2 0.1 fusion.36
  185.3 0.0 collective-permute-done.5
  185.3 1.9 collective-permute-start.6
  187.2 0.0 collective-permute-done.9
  187.2 3.3 %collective-permute-start.13 = (bf16[32,32,256]{2,1,0:T(8,128)(2,1)S(1)}, bf16[32,32,256]{2,1,0:T(8,128)(2,1)S(1)}, u32[]{:S(2)}, u32[]{:S(2)}) collective-permute-start(bf16[32,32,256]{2,1,0:T(8,128)(2,1)S(1)} %collective-permute-done.5), channel_id=1, source_target_pairs={{0,2},{1,3},{2,4},{3,5},{4,6},{5,7},{6,0},{7,1},{8,10},{9,11},{10,... | collective-permute-start | bytes 1572872 | tf_op jit(solution)/shard_map/ppermute | solution.py:23
  190.6 0.9 broadcast_in_dim.52
  191.6 1.1 constant_dynamic-update-slice_fusion.14
  192.7 0.0 collective-permute-done.7
  192.7 2.7 %collective-permute-start.8 = (bf16[32,32,256]{2,1,0:T(8,128)(2,1)S(1)}, bf16[32,32,256]{2,1,0:T(8,128)(2,1)S(1)}, u32[]{:S(2)}, u32[]{:S(2)}) collective-permute-start(bf16[32,32,256]{2,1,0:T(8,128)(2,1)S(1)} %collective-permute-done.7), channel_id=1, source_target_pairs={{0,1},{1,0},{2,3},{3,2},{4,5},{5,4},{6,7},{7,6},{8,9},{9,8},{10,11... | collective-permute-start | bytes 1572872 | tf_op jit(solution)/shard_map/ppermute | solution.py:23
  195.4 0.0 collective-permute-done.11
  195.4 2.0 collective-permute-start.15
  197.4 0.0 collective-permute-done.4
  197.4 2.2 collective-permute-start.10
  199.6 0.1 constant_dynamic-update-slice_fusion.12
  199.7 2.1 collective-permute-start.12
  201.9 0.3 collective-permute-done.13
  202.1 3.2 %collective-permute-start.14 = (bf16[32,32,256]{2,1,0:T(8,128)(2,1)S(1)}, bf16[32,32,256]{2,1,0:T(8,128)(2,1)S(1)}, u32[]{:S(2)}, u32[]{:S(2)}) collective-permute-start(bf16[32,32,256]{2,1,0:T(8,128)(2,1)S(1)} %collective-permute-done.13), channel_id=1, source_target_pairs={{0,1},{1,0},{2,3},{3,2},{4,5},{5,4},{6,7},{7,6},{8,9},{9,8},{10,11... | collective-permute-start | bytes 1572872 | tf_op jit(solution)/shard_map/ppermute | solution.py:23
  205.5 6.5 %collective-permute-done.15 = bf16[32,32,256]{2,1,0:T(8,128)(2,1)S(1)} collective-permute-done((bf16[32,32,256]{2,1,0:T(8,128)(2,1)S(1)}, bf16[32,32,256]{2,1,0:T(8,128)(2,1)S(1)}, u32[]{:S(2)}, u32[]{:S(2)}) %collective-permute-start.15) | collective-permute-done | bytes 524320 | tf_op jit(solution)/shard_map/ppermute | solution.py:23
  212.0 2.7 %collective-permute-start.16 = (bf16[32,32,256]{2,1,0:T(8,128)(2,1)S(1)}, bf16[32,32,256]{2,1,0:T(8,128)(2,1)S(1)}, u32[]{:S(2)}, u32[]{:S(2)}) collective-permute-start(bf16[32,32,256]{2,1,0:T(8,128)(2,1)S(1)} %collective-permute-done.15), channel_id=1, source_target_pairs={{0,1},{1,0},{2,3},{3,2},{4,5},{5,4},{6,7},{7,6},{8,9},{9,8},{10,11... | collective-permute-start | bytes 1572872 | tf_op jit(solution)/shard_map/ppermute | solution.py:23
  214.7 0.0 collective-permute-done.8
  214.7 0.1 constant_dynamic-update-slice_fusion.8
  214.8 0.0 collective-permute-done.10
  214.9 0.1 constant_dynamic-update-slice_fusion.6
  215.0 0.0 collective-permute-done.12
  215.0 0.1 constant_dynamic-update-slice_fusion.4
  215.1 0.1 constant_dynamic-update-slice_fusion.2
  215.2 1.0 collective-permute-done.16
  216.3 2.6 %multiply_convert_fusion = bf16[32,64,512]{2,1,0:T(8,128)(2,1)S(1)} fusion(bf16[32,512,256]{2,1,0:T(8,128)(2,1)S(1)} %constant_dynamic-update-slice_fusion, bf16[32,32,128]{2,1,0:T(8,128)(2,1)S(1)} %get-tuple-element.8, bf16[32,32,128]{2,1,0:T(8,128)(2,1)S(1)} %get-tuple-element.7, bf16[32,32,256]{2,1,0:T(8,128)(2,1)S(1)} %reshape.124), kind=kOutput, calls=%fused_computation.4 | convolution fusion | flops 542113792 | bytes 11534336 | tf_op jit(solution)/shard_map/cik,cjk->cij/dot_general | solution.py:146
  218.9 1.6 copy.32
  (16 shorter events, 0.5 us)
Async XLA Ops:
  1.8 25.5 %copy-start = (bf16[4,4,8,4096]{3,2,0,1:T(8,128)(2,1)}, bf16[4,4,8,4096]{3,2,0,1:T(8,128)(2,1)S(1)}, u32[]{:S(2)}) copy-start(bf16[4,4,8,4096]{3,2,0,1:T(8,128)(2,1)S(1)} %copy.33) | copy-start | bytes 3145732
  1.8 54.2 %collective-permute-start.1 = (bf16[4,32,4096]{2,1,0:T(8,128)(2,1)S(1)}, bf16[4,32,4096]{2,1,0:T(8,128)(2,1)}, u32[]{:S(2)}, u32[]{:S(2)}) collective-permute-start(bf16[4,32,4096]{2,1,0:T(8,128)(2,1)S(1)} %bitcast.36), channel_id=1, source_target_pairs={{0,496},{16,0},{32,16},{48,32},{64,48},{80,64},{96,80},{112,96},{1... | collective-permute-start | bytes 3145736 | tf_op jit(solution)/shard_map/ppermute | solution.py:132
  18.1 37.9 %collective-permute-start = (bf16[3,32,4096]{2,1,0:T(8,128)(2,1)}, bf16[3,32,4096]{2,1,0:T(8,128)(2,1)}, u32[]{:S(2)}, u32[]{:S(2)}) collective-permute-start(bf16[3,32,4096]{2,1,0:T(8,128)(2,1)} %slice.12), channel_id=1, source_target_pairs={{0,16},{16,32},{32,48},{48,64},{64,80},{80,96},{96,112},{112,128},... | collective-permute-start | bytes 2359304 | tf_op jit(solution)/shard_map/ppermute | solution.py:19
  27.2 8.0 %copy-start.1 = (s32[32]{0:T(128)S(1)}, s32[32]{0:T(128)}, u32[]{:S(2)}) copy-start(s32[32]{0:T(128)} %param.3) | copy-start | bytes 388
  119.5 55.2 %collective-permute-start.3 = (bf16[32,32,256]{2,1,0:T(8,128)(2,1)S(1)}, bf16[32,32,256]{2,1,0:T(8,128)(2,1)S(1)}, u32[]{:S(2)}, u32[]{:S(2)}) collective-permute-start(bf16[32,32,256]{2,1,0:T(8,128)(2,1)S(1)} %reshape.124), channel_id=1, source_target_pairs={{0,8},{1,9},{2,10},{3,11},{4,12},{5,13},{6,14},{7,15},{8,0},{9,1},... | collective-permute-start | bytes 1572872 | tf_op jit(solution)/shard_map/ppermute | solution.py:23
  129.5 50.7 %collective-permute-start.2 = (bf16[32,32,256]{2,1,0:T(8,128)(2,1)S(1)}, bf16[32,32,256]{2,1,0:T(8,128)(2,1)}, u32[]{:S(2)}, u32[]{:S(2)}) collective-permute-start(bf16[32,32,256]{2,1,0:T(8,128)(2,1)S(1)} %reshape.124), channel_id=1, source_target_pairs={{0,1},{1,0},{2,3},{3,2},{4,5},{5,4},{6,7},{7,6},{8,9},{9,8},{10,11... | collective-permute-start | bytes 1572872 | tf_op jit(solution)/shard_map/ppermute | solution.py:23
  133.5 51.8 %collective-permute-start.5 = (bf16[32,32,256]{2,1,0:T(8,128)(2,1)S(1)}, bf16[32,32,256]{2,1,0:T(8,128)(2,1)S(1)}, u32[]{:S(2)}, u32[]{:S(2)}) collective-permute-start(bf16[32,32,256]{2,1,0:T(8,128)(2,1)S(1)} %reshape.124), channel_id=1, source_target_pairs={{0,2},{1,3},{2,4},{3,5},{4,6},{5,7},{6,0},{7,1},{8,10},{9,11},{10,... | collective-permute-start | bytes 1572872 | tf_op jit(solution)/shard_map/ppermute | solution.py:23
  135.6 51.7 %collective-permute-start.9 = (bf16[32,32,256]{2,1,0:T(8,128)(2,1)S(1)}, bf16[32,32,256]{2,1,0:T(8,128)(2,1)S(1)}, u32[]{:S(2)}, u32[]{:S(2)}) collective-permute-start(bf16[32,32,256]{2,1,0:T(8,128)(2,1)S(1)} %reshape.124), channel_id=1, source_target_pairs={{0,6},{1,7},{2,0},{3,1},{4,2},{5,3},{6,4},{7,5},{8,14},{9,15},{10,... | collective-permute-start | bytes 1572872 | tf_op jit(solution)/shard_map/ppermute | solution.py:23
  174.7 18.0 %collective-permute-start.7 = (bf16[32,32,256]{2,1,0:T(8,128)(2,1)S(1)}, bf16[32,32,256]{2,1,0:T(8,128)(2,1)S(1)}, u32[]{:S(2)}, u32[]{:S(2)}) collective-permute-start(bf16[32,32,256]{2,1,0:T(8,128)(2,1)S(1)} %collective-permute-done.3), channel_id=1, source_target_pairs={{0,2},{1,3},{2,4},{3,5},{4,6},{5,7},{6,0},{7,1},{8,10},{9,11},{10,... | collective-permute-start | bytes 1572872 | tf_op jit(solution)/shard_map/ppermute | solution.py:23
  176.8 18.6 %collective-permute-start.11 = (bf16[32,32,256]{2,1,0:T(8,128)(2,1)S(1)}, bf16[32,32,256]{2,1,0:T(8,128)(2,1)S(1)}, u32[]{:S(2)}, u32[]{:S(2)}) collective-permute-start(bf16[32,32,256]{2,1,0:T(8,128)(2,1)S(1)} %collective-permute-done.3), channel_id=1, source_target_pairs={{0,6},{1,7},{2,0},{3,1},{4,2},{5,3},{6,4},{7,5},{8,14},{9,15},{10,... | collective-permute-start | bytes 1572872 | tf_op jit(solution)/shard_map/ppermute | solution.py:23
  180.2 17.2 %collective-permute-start.4 = (bf16[32,32,256]{2,1,0:T(8,128)(2,1)S(1)}, bf16[32,32,256]{2,1,0:T(8,128)(2,1)S(1)}, u32[]{:S(2)}, u32[]{:S(2)}) collective-permute-start(bf16[32,32,256]{2,1,0:T(8,128)(2,1)S(1)} %collective-permute-done.3), channel_id=1, source_target_pairs={{0,1},{1,0},{2,3},{3,2},{4,5},{5,4},{6,7},{7,6},{8,9},{9,8},{10,11... | collective-permute-start | bytes 1572872 | tf_op jit(solution)/shard_map/ppermute | solution.py:23
  185.3 14.4 %collective-permute-start.6 = (bf16[32,32,256]{2,1,0:T(8,128)(2,1)S(1)}, bf16[32,32,256]{2,1,0:T(8,128)(2,1)S(1)}, u32[]{:S(2)}, u32[]{:S(2)}) collective-permute-start(bf16[32,32,256]{2,1,0:T(8,128)(2,1)S(1)} %collective-permute-done.5), channel_id=1, source_target_pairs={{0,1},{1,0},{2,3},{3,2},{4,5},{5,4},{6,7},{7,6},{8,9},{9,8},{10,11... | collective-permute-start | bytes 1572872 | tf_op jit(solution)/shard_map/ppermute | solution.py:23
  187.2 14.9 %collective-permute-start.13 = (bf16[32,32,256]{2,1,0:T(8,128)(2,1)S(1)}, bf16[32,32,256]{2,1,0:T(8,128)(2,1)S(1)}, u32[]{:S(2)}, u32[]{:S(2)}) collective-permute-start(bf16[32,32,256]{2,1,0:T(8,128)(2,1)S(1)} %collective-permute-done.5), channel_id=1, source_target_pairs={{0,2},{1,3},{2,4},{3,5},{4,6},{5,7},{6,0},{7,1},{8,10},{9,11},{10,... | collective-permute-start | bytes 1572872 | tf_op jit(solution)/shard_map/ppermute | solution.py:23
  192.7 22.1 %collective-permute-start.8 = (bf16[32,32,256]{2,1,0:T(8,128)(2,1)S(1)}, bf16[32,32,256]{2,1,0:T(8,128)(2,1)S(1)}, u32[]{:S(2)}, u32[]{:S(2)}) collective-permute-start(bf16[32,32,256]{2,1,0:T(8,128)(2,1)S(1)} %collective-permute-done.7), channel_id=1, source_target_pairs={{0,1},{1,0},{2,3},{3,2},{4,5},{5,4},{6,7},{7,6},{8,9},{9,8},{10,11... | collective-permute-start | bytes 1572872 | tf_op jit(solution)/shard_map/ppermute | solution.py:23
  195.4 16.6 %collective-permute-start.15 = (bf16[32,32,256]{2,1,0:T(8,128)(2,1)S(1)}, bf16[32,32,256]{2,1,0:T(8,128)(2,1)S(1)}, u32[]{:S(2)}, u32[]{:S(2)}) collective-permute-start(bf16[32,32,256]{2,1,0:T(8,128)(2,1)S(1)} %collective-permute-done.11), channel_id=1, source_target_pairs={{0,6},{1,7},{2,0},{3,1},{4,2},{5,3},{6,4},{7,5},{8,14},{9,15},{10,... | collective-permute-start | bytes 1572872 | tf_op jit(solution)/shard_map/ppermute | solution.py:23
  197.4 17.4 %collective-permute-start.10 = (bf16[32,32,256]{2,1,0:T(8,128)(2,1)S(1)}, bf16[32,32,256]{2,1,0:T(8,128)(2,1)S(1)}, u32[]{:S(2)}, u32[]{:S(2)}) collective-permute-start(bf16[32,32,256]{2,1,0:T(8,128)(2,1)S(1)} %collective-permute-done.9), channel_id=1, source_target_pairs={{0,1},{1,0},{2,3},{3,2},{4,5},{5,4},{6,7},{7,6},{8,9},{9,8},{10,11... | collective-permute-start | bytes 1572872 | tf_op jit(solution)/shard_map/ppermute | solution.py:23
  199.7 15.2 %collective-permute-start.12 = (bf16[32,32,256]{2,1,0:T(8,128)(2,1)S(1)}, bf16[32,32,256]{2,1,0:T(8,128)(2,1)S(1)}, u32[]{:S(2)}, u32[]{:S(2)}) collective-permute-start(bf16[32,32,256]{2,1,0:T(8,128)(2,1)S(1)} %collective-permute-done.11), channel_id=1, source_target_pairs={{0,1},{1,0},{2,3},{3,2},{4,5},{5,4},{6,7},{7,6},{8,9},{9,8},{10,11... | collective-permute-start | bytes 1572872 | tf_op jit(solution)/shard_map/ppermute | solution.py:23
  202.1 13.0 %collective-permute-start.14 = (bf16[32,32,256]{2,1,0:T(8,128)(2,1)S(1)}, bf16[32,32,256]{2,1,0:T(8,128)(2,1)S(1)}, u32[]{:S(2)}, u32[]{:S(2)}) collective-permute-start(bf16[32,32,256]{2,1,0:T(8,128)(2,1)S(1)} %collective-permute-done.13), channel_id=1, source_target_pairs={{0,1},{1,0},{2,3},{3,2},{4,5},{5,4},{6,7},{7,6},{8,9},{9,8},{10,11... | collective-permute-start | bytes 1572872 | tf_op jit(solution)/shard_map/ppermute | solution.py:23
  212.0 4.2 %collective-permute-start.16 = (bf16[32,32,256]{2,1,0:T(8,128)(2,1)S(1)}, bf16[32,32,256]{2,1,0:T(8,128)(2,1)S(1)}, u32[]{:S(2)}, u32[]{:S(2)}) collective-permute-start(bf16[32,32,256]{2,1,0:T(8,128)(2,1)S(1)} %collective-permute-done.15), channel_id=1, source_target_pairs={{0,1},{1,0},{2,3},{3,2},{4,5},{5,4},{6,7},{7,6},{8,9},{9,8},{10,11... | collective-permute-start | bytes 1572872 | tf_op jit(solution)/shard_map/ppermute | solution.py:23
